TPU v7x, 32 devices: a whole 2x2x4 slice. The times are simulated.
32 devices in a mesh: grp: 1, dap: 32 (over z, y, x, core).
Axes of the slice: x: 2, y: 2, z: 4, core: 2. Of those that a mesh axis runs over, the one named last changes fastest.
Arguments:
- alignment: bfloat16 [64, 128, 256], P(('grp', 'dap')), may hold values from -6 to 6
- pairwise: bfloat16 [128, 128, 128], P(('grp', 'dap')), may hold values from -6 to 6
- sequence_mask: int32 [64], P('grp'), may hold values from 0 to 1, as said below
- residue_mask: int32 [128], P('grp'), may hold values from 0 to 1, as said below
- row_project: bfloat16 [4, 256, 256], replicated, may hold values from -0.375 to 0.375
- row_bias_map: bfloat16 [128, 8], replicated, as said below
- row_output: bfloat16 [256, 256], replicated, may hold values from -0.375 to 0.375
- column_project: bfloat16 [4, 256, 256], replicated, as said below
- column_output: bfloat16 [256, 256], replicated, may hold values from -0.375 to 0.375
- start_project: bfloat16 [4, 128, 128], replicated, may hold values from -0.5 to 0.5
- start_bias_map: bfloat16 [128, 4], replicated, as said below
- start_output: bfloat16 [128, 128], replicated, may hold values from -0.5 to 0.5
- end_project: bfloat16 [4, 128, 128], replicated, may hold values from -0.5 to 0.5
- end_bias_map: bfloat16 [128, 4], replicated, as said below
- end_output: bfloat16 [128, 128], replicated, may hold values from -0.5 to 0.5
- outer_left: bfloat16 [256, 32], replicated, may hold values from -0.375 to 0.375
- outer_right: bfloat16 [256, 32], replicated, may hold values from -0.375 to 0.375
- outer_output: bfloat16 [1024, 128], replicated, may hold values from -1 to 1
Outputs:
- alignment_out: bfloat16 [64, 128, 256], P('grp', 'dap')
- pairwise_out: bfloat16 [128, 128, 128], P('grp', 'dap')
Inputs may be any that keep to these rules, and one draw needn't show every extreme that they name: `sequence_mask`: 0 or 1; entry 0, the query sequence, is always 1. `residue_mask`: 1 on a prefix of the residues of 64 positions or more, 0 after it. `row_bias_map`: a weight matrix. `start_bias_map`: a weight matrix. `end_bias_map`: a weight matrix. `column_project`: weight matrices.
All inputs are finite; a program needn't handle non-finite values.
Results may differ from a plain program's by a relative error of at most 0.02.
The roundings to bfloat16 on the way count: a program that leaves them out, or rounds other values in their place, can miss the bound.
Values may be sent and summed in bfloat16 or wider, within the bound.
No kernel may reach another device: no remote copies, remote signals or barrier semaphores. Data moves between devices by JAX's collectives and lax.ppermute only.
A program may use at most 128 MiB of HBM per device.

v0:
```python
import jax
import jax.numpy as jnp
from jax import lax
from jax.sharding import PartitionSpec as P

H_M = 8
H_Z = 4


norm_epsilon = 1e-05
mask_scale = 1000000000.0


def layer_norm(values):
    widened = values.astype(jnp.float32)
    center = widened - jnp.mean(widened, axis=-1, keepdims=True)
    spread = jnp.mean(center * center, axis=-1, keepdims=True)
    return (center * lax.rsqrt(spread + norm_epsilon)).astype(jnp.bfloat16)


def key_offsets(mask_values):
    return (mask_values.astype(jnp.float32) - 1.0) * mask_scale


def project(inputs, weight_table):
    return jnp.einsum("bqc,cf->bqf", inputs, weight_table, preferred_element_type=jnp.float32)


def attend(inputs, weights, bias_table, key_bias, output_map, head_count):
    batch_size, query_count, width = inputs.shape
    query_all = project(inputs, weights[0]).astype(jnp.bfloat16)
    key_all = project(inputs, weights[1]).astype(jnp.bfloat16)
    value_all = project(inputs, weights[2]).astype(jnp.bfloat16)
    gating = jax.nn.sigmoid(project(inputs, weights[3]))
    head_size = query_all.shape[-1] // head_count
    query_heads = query_all.reshape(batch_size, query_count, head_count, head_size)
    key_heads = key_all.reshape(batch_size, query_count, head_count, head_size)
    value_heads = value_all.reshape(batch_size, query_count, head_count, head_size)
    scores = jnp.einsum(
        "bqhd,bkhd->bhqk", query_heads, key_heads, preferred_element_type=jnp.float32
    ) * head_size ** (-0.5)
    if bias_table is not None:
        scores = scores + bias_table.astype(jnp.float32)[None]
    scores = scores + key_bias
    softened = jax.nn.softmax(scores, axis=-1).astype(jnp.bfloat16)
    mixed = jnp.einsum("bhqk,bkhd->bqhd", softened, value_heads, preferred_element_type=jnp.float32)
    mixed = mixed.reshape(batch_size, query_count, head_count * head_size)
    gated = (mixed * gating).astype(jnp.bfloat16)
    return jnp.einsum("bqf,fc->bqc", gated, output_map, preferred_element_type=jnp.float32)


def per_device(
    alignment,
    pairwise,
    sequence_mask,
    residue_mask,
    row_project,
    row_bias_map,
    row_output,
    column_project,
    column_output,
    start_project,
    start_bias_map,
    start_output,
    end_project,
    end_bias_map,
    end_output,
    outer_left,
    outer_right,
    outer_output,
):
    residue_keys = key_offsets(residue_mask)
    sequence_keys = key_offsets(sequence_mask)
    pair_norm = layer_norm(pairwise)
    row_local = jnp.einsum(
        "ijc,ch->hij", pair_norm, row_bias_map, preferred_element_type=jnp.float32
    ).astype(jnp.bfloat16)
    start_local = jnp.einsum(
        "ijc,ch->hij", pair_norm, start_bias_map, preferred_element_type=jnp.float32
    ).astype(jnp.bfloat16)
    row_bias, start_bias = (
        lax.all_gather(row_local, "dap", axis=1, tiled=True),
        lax.all_gather(start_local, "dap", axis=1, tiled=True),
    )
    row_update = attend(layer_norm(alignment), row_project, row_bias, residue_keys, row_output, H_M)
    alignment_one = (alignment.astype(jnp.float32) + row_update).astype(jnp.bfloat16)
    alignment_cols = lax.all_to_all(alignment_one, "dap", split_axis=1, concat_axis=0, tiled=True)
    start_update = attend(pair_norm, start_project, start_bias, residue_keys, start_output, H_Z)
    pair_one = (pairwise.astype(jnp.float32) + start_update).astype(jnp.bfloat16)
    pair_cols = lax.all_to_all(pair_one, "dap", split_axis=1, concat_axis=0, tiled=True)
    rows_norm_one = layer_norm(pair_one)
    end_local = jnp.einsum(
        "kic,ch->hki", rows_norm_one, end_bias_map, preferred_element_type=jnp.float32
    ).astype(jnp.bfloat16)
    end_bias = jnp.swapaxes(lax.all_gather(end_local, "dap", axis=1, tiled=True), 1, 2)
    column_norm = jnp.swapaxes(layer_norm(alignment_cols), 0, 1)
    column_update = attend(column_norm, column_project, None, sequence_keys, column_output, H_M)
    alignment_out = (alignment_cols.astype(jnp.float32) + jnp.swapaxes(column_update, 0, 1)).astype(
        jnp.bfloat16
    )
    end_norm = jnp.swapaxes(layer_norm(pair_cols), 0, 1)
    end_update = jnp.swapaxes(
        attend(end_norm, end_project, end_bias, residue_keys, end_output, H_Z), 0, 1
    )
    last_norm = layer_norm(alignment_out)
    weighting = sequence_mask.astype(jnp.float32)[:, None, None]
    left = (
        jnp.einsum("sic,co->sio", last_norm, outer_left, preferred_element_type=jnp.float32)
        * weighting
    ).astype(jnp.bfloat16)
    right = (
        jnp.einsum("sic,co->sio", last_norm, outer_right, preferred_element_type=jnp.float32)
        * weighting
    ).astype(jnp.bfloat16)
    row_count = jnp.sum(sequence_mask.astype(jnp.float32))
    outer_sum = (
        jnp.einsum(
            "sic,sje->ijce",
            left,
            lax.all_gather(right, "dap", axis=1, tiled=True),
            preferred_element_type=jnp.float32,
        )
        / row_count
    )
    flattened = outer_sum.astype(jnp.bfloat16).reshape(outer_sum.shape[0], outer_sum.shape[1], -1)
    rows_update = jnp.einsum(
        "ijf,fc->ijc", flattened, outer_output, preferred_element_type=jnp.float32
    )
    outer_update = lax.all_to_all(
        rows_update.astype(jnp.bfloat16), "dap", split_axis=1, concat_axis=0, tiled=True
    ).astype(rows_update.dtype)
    pairwise_out = (pair_cols.astype(jnp.float32) + end_update + outer_update).astype(jnp.bfloat16)
    return (alignment_out, pairwise_out)


def solution(mesh):
    return jax.shard_map(
        per_device,
        mesh=mesh,
        in_specs=(
            P(("grp", "dap"), None, None),
            P(("grp", "dap"), None, None),
            P("grp"),
            P("grp"),
            P(),
            P(),
            P(),
            P(),
            P(),
            P(),
            P(),
            P(),
            P(),
            P(),
            P(),
            P(),
            P(),
            P(),
        ),
        out_specs=(P("grp", "dap", None), P("grp", "dap", None)),
        check_vma=False,
    )
```

profile of v0, /device:TPU:0, one launch (start us, length us, event | category | flops | bytes accessed | tf_op | source)
XLA Modules:
  0.0 216.3 jit_solution(3972832571887352512)
XLA Ops:
  0.7 1.1 convert_reduce_fusion.1
  1.8 1.1 fusion.68
  2.9 1.2 convolution_convert_fusion.12
  4.2 1.2 convolution_convert_fusion.11
  6.4 43.9 %all_gather.12 = bf16[8,128,128]{2,0,1:T(8,128)(2,1)S(1)} all-gather(bf16[8,4,128]{2,0,1:T(8,128)(2,1)S(1)} %fusion.50), channel_id=1, replica_groups=mesh['grp'=1,'dap'=32] {'dap'}, dimensions={1}, use_global_device_ids=true | all-gather | bytes 270336 | tf_op jit(solution)/shard_map/all_gather | solution.py:82
  50.5 0.5 fusion.174
  52.9 0.8 copy.215
  53.6 2.6 %all-to-all-start = ((bf16[2,128,256]{2,0,1:T(2,128)(2,1)}), bf16[2,128,256]{2,0,1:T(2,128)(2,1)S(1)}, u32[]{:S(2)}, u32[]{:S(2)}) async-start(bf16[2,128,256]{2,0,1:T(2,128)(2,1)} %copy.215), calls=%async_computation | async-start | bytes 262144 | tf_op jit(solution)/shard_map/all_to_all | solution.py:87
  57.0 42.1 %all_gather.13 = bf16[4,128,128]{2,0,1:T(4,128)(2,1)S(1)} all-gather(bf16[4,4,128]{2,0,1:T(4,128)(2,1)S(1)} %fusion.51), channel_id=1, replica_groups=mesh['grp'=1,'dap'=32] {'dap'}, dimensions={1}, use_global_device_ids=true | all-gather | bytes 135168 | tf_op jit(solution)/shard_map/all_gather | solution.py:83
  99.3 0.6 fusion.180
  101.7 37.0 %all_gather.14 = bf16[4,128,128]{2,0,1:T(4,128)(2,1)S(1)} all-gather(bf16[4,4,128]{2,0,1:T(4,128)(2,1)S(1)} %fusion.52), channel_id=1, replica_groups=mesh['grp'=1,'dap'=32] {'dap'}, dimensions={1}, use_global_device_ids=true | all-gather | bytes 135168 | tf_op jit(solution)/shard_map/all_gather | solution.py:95
  138.7 0.8 copy.243
  139.4 0.6 convert_element_type.230
  140.1 0.6 convert_reduce_fusion.4
  140.7 2.8 %all-to-all-start.1 = ((bf16[4,128,128]{2,0,1:T(4,128)(2,1)}), bf16[4,128,128]{2,0,1:T(4,128)(2,1)S(1)}, u32[]{:S(2)}, u32[]{:S(2)}) async-start(bf16[4,128,128]{2,0,1:T(4,128)(2,1)} %copy.243), calls=%async_computation.1 | async-start | bytes 262144 | tf_op jit(solution)/shard_map/all_to_all | solution.py:90
  145.8 1.2 fusion.175
  147.4 4.1 %all-to-all-done.1 = bf16[4,128,128]{2,0,1:T(4,128)(2,1)S(1)} async-done(((bf16[4,128,128]{2,0,1:T(4,128)(2,1)}), bf16[4,128,128]{2,0,1:T(4,128)(2,1)S(1)}, u32[]{:S(2)}, u32[]{:S(2)}) %all-to-all-start.1) | async-done | bytes 131104 | tf_op jit(solution)/shard_map/all_to_all | solution.py:90
  153.3 1.0 convolution_convert_fusion.6
  155.1 0.8 copy.225
  155.9 1.3 fusion.54
  157.4 1.4 convert_reduce_fusion.2
  159.3 40.9 %all_gather.15 = bf16[64,128,32]{0,2,1:T(8,128)(2,1)S(1)} all-gather(bf16[64,4,32]{0,2,1:T(8,128)(2,1)S(1)} %fusion.47), channel_id=1, replica_groups=mesh['grp'=1,'dap'=32] {'dap'}, dimensions={1}, use_global_device_ids=true | all-gather | bytes 540672 | tf_op jit(solution)/shard_map/all_gather | solution.py:120
  200.2 1.3 fusion.12
  201.5 0.7 copy.259
  202.2 0.5 convolution_convert_fusion.3
  202.7 0.8 copy.261
  203.5 2.6 %all-to-all-start.2 = ((bf16[4,128,128]{2,0,1:T(4,128)(2,1)}), bf16[4,128,128]{2,0,1:T(4,128)(2,1)S(1)}, u32[]{:S(2)}, u32[]{:S(2)}) async-start(bf16[4,128,128]{2,0,1:T(4,128)(2,1)} %copy.261), calls=%async_computation.2 | async-start | bytes 262144 | tf_op jit(solution)/shard_map/all_to_all | solution.py:129
  206.4 0.6 fusion.185
  207.0 0.8 copy.263
  208.3 6.0 %all-to-all-done.2 = bf16[4,128,128]{2,0,1:T(4,128)(2,1)S(1)} async-done(((bf16[4,128,128]{2,0,1:T(4,128)(2,1)}), bf16[4,128,128]{2,0,1:T(4,128)(2,1)S(1)}, u32[]{:S(2)}, u32[]{:S(2)}) %all-to-all-start.2) | async-done | bytes 131104 | tf_op jit(solution)/shard_map/all_to_all | solution.py:129
  214.3 1.2 fusion.44
  215.6 0.8 copy.264
  (119 shorter events, 12.2 us)
Async XLA Ops:
  0.6 201.6 %copy-start = (bf16[1024,128]{1,0:T(8,128)(2,1)S(1)}, bf16[1024,128]{1,0:T(8,128)(2,1)}, u32[]{:S(2)}) copy-start(bf16[1024,128]{1,0:T(8,128)(2,1)} %param.35) | copy-start | bytes 786436
  0.6 4.8 %copy-start.1 = (bf16[2,128,256]{2,1,0:T(8,128)(2,1)S(1)}, bf16[2,128,256]{2,1,0:T(8,128)(2,1)}, u32[]{:S(2)}) copy-start(bf16[2,128,256]{2,1,0:T(8,128)(2,1)} %param.18) | copy-start | bytes 393220
  0.7 4.8 %copy-start.9 = (bf16[4,256,256]{2,1,0:T(8,128)(2,1)S(1)}, bf16[4,256,256]{2,1,0:T(8,128)(2,1)}, u32[]{:S(2)}) copy-start(bf16[4,256,256]{2,1,0:T(8,128)(2,1)} %param.22) | copy-start | bytes 1572868
  1.8 4.2 %copy-start.18 = (s32[128]{0:T(128)S(1)}, s32[128]{0:T(128)}, u32[]{:S(2)}) copy-start(s32[128]{0:T(128)} %param.21) | copy-start | bytes 1540
  1.8 4.2 %copy-start.3 = (bf16[4,128,128]{2,1,0:T(8,128)(2,1)S(1)}, bf16[4,128,128]{2,1,0:T(8,128)(2,1)}, u32[]{:S(2)}) copy-start(bf16[4,128,128]{2,1,0:T(8,128)(2,1)} %param.19) | copy-start | bytes 393220
  4.2 2.1 copy-start.15
  6.0 93.9 %copy-start.7 = (f32[128]{0:T(128)}, f32[128]{0:T(128)S(1)}, u32[]{:S(2)}) copy-start(f32[128]{0:T(128)S(1)} %add_multiply_fusion.1) | copy-start | bytes 1540
  51.5 0.9 copy-start.10
  52.4 3.8 %copy-start.5 = (bf16[4,128,128]{2,1,0:T(8,128)(2,1)S(1)}, bf16[4,128,128]{2,1,0:T(8,128)(2,1)}, u32[]{:S(2)}) copy-start(bf16[4,128,128]{2,1,0:T(8,128)(2,1)} %param.27) | copy-start | bytes 393220
  52.8 4.0 %copy-start.16 = (bf16[128,4]{0,1:T(4,128)(2,1)S(1)}, bf16[128,4]{0,1:T(4,128)(2,1)}, u32[]{:S(2)}) copy-start(bf16[128,4]{0,1:T(4,128)(2,1)} %param.28) | copy-start | bytes 3076
  53.6 87.0 %all-to-all-start = ((bf16[2,128,256]{2,0,1:T(2,128)(2,1)}), bf16[2,128,256]{2,0,1:T(2,128)(2,1)S(1)}, u32[]{:S(2)}, u32[]{:S(2)}) async-start(bf16[2,128,256]{2,0,1:T(2,128)(2,1)} %copy.215), calls=%async_computation | async-start | bytes 262144 | tf_op jit(solution)/shard_map/all_to_all | solution.py:87
  100.2 0.8 copy-start.11
  100.6 0.9 copy-start.17
  101.0 38.5 %copy-start.19 = (s32[64]{0:T(128)S(1)}, s32[64]{0:T(128)}, u32[]{:S(2)}) copy-start(s32[64]{0:T(128)} %param.20) | copy-start | bytes 772
  140.7 10.8 %all-to-all-start.1 = ((bf16[4,128,128]{2,0,1:T(4,128)(2,1)}), bf16[4,128,128]{2,0,1:T(4,128)(2,1)S(1)}, u32[]{:S(2)}, u32[]{:S(2)}) async-start(bf16[4,128,128]{2,0,1:T(4,128)(2,1)} %copy.243), calls=%async_computation.1 | async-start | bytes 262144 | tf_op jit(solution)/shard_map/all_to_all | solution.py:90
  143.6 1.1 copy-start.2
  151.5 1.8 copy-start.6
  157.4 1.6 copy-start.13
  157.4 1.6 copy-start.20
  158.8 41.4 %copy-start.14 = (bf16[256,32]{0,1:T(8,128)(2,1)S(1)}, bf16[256,32]{0,1:T(8,128)(2,1)}, u32[]{:S(2)}) copy-start(bf16[256,32]{0,1:T(8,128)(2,1)} %param.33) | copy-start | bytes 49156
  158.8 41.4 %copy-start.21 = (f32[64]{0:T(128)S(1)}, f32[64]{0:T(128)}, u32[]{:S(2)}) copy-start(f32[64]{0:T(128)} %convert_element_type.230) | copy-start | bytes 772
  202.2 3.9 %copy-start.8 = (f32[128]{0:T(128)S(1)}, f32[128]{0:T(128)}, u32[]{:S(2)}) copy-start(f32[128]{0:T(128)} %copy-done.7) | copy-start | bytes 1540
  203.5 10.8 %all-to-all-start.2 = ((bf16[4,128,128]{2,0,1:T(4,128)(2,1)}), bf16[4,128,128]{2,0,1:T(4,128)(2,1)S(1)}, u32[]{:S(2)}, u32[]{:S(2)}) async-start(bf16[4,128,128]{2,0,1:T(4,128)(2,1)} %copy.261), calls=%async_computation.2 | async-start | bytes 262144 | tf_op jit(solution)/shard_map/all_to_all | solution.py:129
  206.4 1.3 copy-start.4
  207.8 6.6 %copy-start.12 = (bf16[128,128]{1,0:T(8,128)(2,1)S(1)}, bf16[128,128]{1,0:T(8,128)(2,1)}, u32[]{:S(2)}) copy-start(bf16[128,128]{1,0:T(8,128)(2,1)} %param.32) | copy-start | bytes 98308
where the time goes:
time: 217 us; the launch traced here: 216 us
  blocking collectives  164 us (76%)
  matrix products  18.4 us (8%)
  waiting for transfers between devices  10.2 us (5%)
  local copies, waits for them, and re-layouts  9.69 us (4%)
  starting transfers between devices  7.91 us (4%)
  other arithmetic  4.96 us (2%)
    all_gather x1, blocking collectives, per_device(): lax.all_gather(row_local, 'dap', axis=1, tiled=True)  43.9 us
    all_gather x1, blocking collectives, per_device(): lax.all_gather(start_local, 'dap', axis=1, tiled=True)  42.1 us
    all_gather x1, blocking collectives, per_device(): lax.all_gather(right, 'dap', axis=1, tiled=True)  40.9 us
    all_gather x1, blocking collectives, per_device(): lax.all_gather(end_local, 'dap', axis=1, tiled=True)  37 us
    all_to_all x1, waiting for transfers between devices, per_device(): lax.all_to_all(rows_update.astype(jnp.bfloat16), 'dap', split_axis=1, con...  6.03 us
    dot_general x12, matrix products, project(): jnp.einsum('bqc,cf->bqf', inputs, weight_table, preferred_element_type=jn...  5.88 us
  transfers between devices with their start and end apart: 3, of which 2 were waited for; matrix products, arithmetic and copies ran while one was open for 5% of the time, Pallas kernels for 0%

commit v1 on v0

--- a/solution.py
+++ b/solution.py
@@ -1,3 +1,5 @@
+import functools
+
 import jax
 import jax.numpy as jnp
 from jax import lax
@@ -49,6 +51,14 @@
     return jnp.einsum("bqf,fc->bqc", gated, output_map, preferred_element_type=jnp.float32)
 
 
+def gather_blocks(block, axis, count):
+    spread = jnp.broadcast_to(block[None], (count,) + block.shape)
+    received = lax.all_to_all(spread, "dap", 0, 0, tiled=True)
+    received = jnp.moveaxis(received, 0, axis)
+    shape = block.shape[:axis] + (count * block.shape[axis],) + block.shape[axis + 1 :]
+    return received.reshape(shape)
+
+
 def per_device(
     alignment,
     pairwise,
@@ -68,20 +78,18 @@
     outer_left,
     outer_right,
     outer_output,
+    count=1,
 ):
     residue_keys = key_offsets(residue_mask)
     sequence_keys = key_offsets(sequence_mask)
     pair_norm = layer_norm(pairwise)
-    row_local = jnp.einsum(
-        "ijc,ch->hij", pair_norm, row_bias_map, preferred_element_type=jnp.float32
+    both_maps = jnp.concatenate([row_bias_map, start_bias_map], axis=1)
+    both_local = jnp.einsum(
+        "ijc,ch->hij", pair_norm, both_maps, preferred_element_type=jnp.float32
     ).astype(jnp.bfloat16)
-    start_local = jnp.einsum(
-        "ijc,ch->hij", pair_norm, start_bias_map, preferred_element_type=jnp.float32
-    ).astype(jnp.bfloat16)
-    row_bias, start_bias = (
-        lax.all_gather(row_local, "dap", axis=1, tiled=True),
-        lax.all_gather(start_local, "dap", axis=1, tiled=True),
-    )
+    both_bias = gather_blocks(both_local, 1, count)
+    row_bias = both_bias[:H_M]
+    start_bias = both_bias[H_M:]
     row_update = attend(layer_norm(alignment), row_project, row_bias, residue_keys, row_output, H_M)
     alignment_one = (alignment.astype(jnp.float32) + row_update).astype(jnp.bfloat16)
     alignment_cols = lax.all_to_all(alignment_one, "dap", split_axis=1, concat_axis=0, tiled=True)
@@ -92,7 +100,7 @@
     end_local = jnp.einsum(
         "kic,ch->hki", rows_norm_one, end_bias_map, preferred_element_type=jnp.float32
     ).astype(jnp.bfloat16)
-    end_bias = jnp.swapaxes(lax.all_gather(end_local, "dap", axis=1, tiled=True), 1, 2)
+    end_bias = jnp.swapaxes(gather_blocks(end_local, 1, count), 1, 2)
     column_norm = jnp.swapaxes(layer_norm(alignment_cols), 0, 1)
     column_update = attend(column_norm, column_project, None, sequence_keys, column_output, H_M)
     alignment_out = (alignment_cols.astype(jnp.float32) + jnp.swapaxes(column_update, 0, 1)).astype(
@@ -116,26 +124,23 @@
     outer_sum = (
         jnp.einsum(
             "sic,sje->ijce",
-            left,
-            lax.all_gather(right, "dap", axis=1, tiled=True),
+            gather_blocks(left, 1, count),
+            right,
             preferred_element_type=jnp.float32,
         )
         / row_count
     )
     flattened = outer_sum.astype(jnp.bfloat16).reshape(outer_sum.shape[0], outer_sum.shape[1], -1)
-    rows_update = jnp.einsum(
+    outer_update = jnp.einsum(
         "ijf,fc->ijc", flattened, outer_output, preferred_element_type=jnp.float32
     )
-    outer_update = lax.all_to_all(
-        rows_update.astype(jnp.bfloat16), "dap", split_axis=1, concat_axis=0, tiled=True
-    ).astype(rows_update.dtype)
     pairwise_out = (pair_cols.astype(jnp.float32) + end_update + outer_update).astype(jnp.bfloat16)
     return (alignment_out, pairwise_out)
 
 
 def solution(mesh):
     return jax.shard_map(
-        per_device,
+        functools.partial(per_device, count=mesh.shape["dap"]),
         mesh=mesh,
         in_specs=(
             P(("grp", "dap"), None, None),

time: 217 us -> 92.7 us (0.43)
  blocking collectives: 164 us -> 0 us
  waiting for transfers between devices: 10.2 us -> 34.4 us
  starting transfers between devices: 7.91 us -> 20.9 us
  local copies, waits for them, and re-layouts: 9.69 us -> 14.7 us
    all_gather x4 -> x0, blocking collectives: 164 us -> none  [the longest x1 43.9 us: per_device(): lax.all_gather(row_local, 'dap', axis=1, tiled=True)]
    all_to_all x1 -> x3, waiting for transfers between devices: 6.03 us -> 22.1 us  [gather_blocks(): received = lax.all_to_all(spread, 'dap', 0, 0, tiled=True)]
    all_to_all x1 -> x3, starting transfers between devices: 2.58 us -> 15.7 us  [gather_blocks(): received = lax.all_to_all(spread, 'dap', 0, 0, tiled=True)]
    all_to_all x1, waiting for transfers between devices: 0.01 us -> 7.22 us  [per_device(): lax.all_to_all(alignment_one, 'dap', split_axis=1, concat_axis=0, tiled=T...]
    unnamed x47 -> x48, local copies, waits for them, and re-layouts: 2.45 us -> 6.29 us
    dot_general x12, matrix products: 5.88 us -> 3.25 us  [project(): jnp.einsum('bqc,cf->bqf', inputs, weight_table, preferred_element_type=jn...]
  transfers between devices with their start and end apart: 3 -> 5, of which waited for: 2 -> 4; matrix products, arithmetic and copies ran while one was open for 5% -> 20% of each run, Pallas kernels for 0% -> 0%
where the time goes in v1:
time: 92.7 us; the launch traced here: 91.8 us
  waiting for transfers between devices  34.4 us (37%)
  starting transfers between devices  20.9 us (23%)
  matrix products  16.7 us (18%)
  local copies, waits for them, and re-layouts  14.7 us (16%)
  other arithmetic  3.68 us (4%)
  between operations  1.43 us (2%)
    all_to_all x3, waiting for transfers between devices, gather_blocks(): received = lax.all_to_all(spread, 'dap', 0, 0, tiled=True)  22.1 us
    all_to_all x3, starting transfers between devices, gather_blocks(): received = lax.all_to_all(spread, 'dap', 0, 0, tiled=True)  15.7 us
    all_to_all x1, waiting for transfers between devices, per_device(): lax.all_to_all(alignment_one, 'dap', split_axis=1, concat_axis=0, tiled=T...  7.22 us
    unnamed x48, local copies, waits for them, and re-layouts  6.29 us
    all_to_all x1, waiting for transfers between devices, per_device(): lax.all_to_all(pair_one, 'dap', split_axis=1, concat_axis=0, tiled=True)  5.12 us
    sub x4, matrix products, attend(): softened = jax.nn.softmax(scores, axis=-1).astype(jnp.bfloat16)  3.43 us
    dot_general x4, matrix products, attend(): jnp.einsum('bqf,fc->bqc', gated, output_map, preferred_element_type=jnp.f...  3.41 us
    dot_general x12, matrix products, project(): jnp.einsum('bqc,cf->bqf', inputs, weight_table, preferred_element_type=jn...  3.25 us
  transfers between devices with their start and end apart: 5, of which 4 were waited for; matrix products, arithmetic and copies ran while one was open for 20% of the time, Pallas kernels for 0%

profile of v1, /device:TPU:0, one launch (start us, length us, event | category | flops | bytes accessed | tf_op | source)
XLA Modules:
  0.0 91.8 jit_solution(12809701294136405967)
XLA Ops:
  0.7 1.1 %copy.205 = bf16[4,128,128]{1,2,0:T(8,128)(2,1)S(1)} copy(bf16[4,128,128]{2,1,0:T(8,128)(2,1)} %param.19) | data formatting | bytes 262144 | tf_op args[1]
  1.9 0.9 convolution_convert_fusion.12
  2.8 0.8 broadcast_in_dim.6
  3.6 7.3 %all-to-all-start = ((bf16[32,12,4,128]{3,2,1,0:T(4,128)(2,1)}), bf16[32,12,4,128]{3,2,1,0:T(4,128)(2,1)S(1)}, u32[]{:S(2)}, u32[]{:S(2)}) async-start(bf16[32,12,4,128]{3,2,1,0:T(4,128)(2,1)} %broadcast_in_dim.6), calls=%async_computation | async-start | bytes 786432 | tf_op jit(solution)/shard_map/all_to_all | solution.py:56
  12.1 1.2 %convert_reduce_fusion.4 = (f32[]{:T(128)}, f32[64]{0:T(128)}) fusion(s32[64]{0:T(128)S(1)} %copy-done.18), kind=kLoop, calls=%fused_computation.195 | loop fusion | flops 255 | bytes 516 | tf_op jit(solution)/shard_map/reduce_sum | solution.py:123
  13.3 0.6 convert_element_type.226
  14.9 9.2 %all-to-all-done = bf16[32,12,4,128]{3,2,1,0:T(4,128)(2,1)S(1)} async-done(((bf16[32,12,4,128]{3,2,1,0:T(4,128)(2,1)}), bf16[32,12,4,128]{3,2,1,0:T(4,128)(2,1)S(1)}, u32[]{:S(2)}, u32[]{:S(2)}) %all-to-all-start) | async-done | bytes 393248 | tf_op jit(solution)/shard_map/all_to_all | solution.py:56
  24.9 1.2 %fusion.178 = f32[4,4,128]{2,1,0:T(4,128)} fusion(bf16[4,128,4,32]{1,3,2,0:T(8,128)(2,1)S(1)} %bitcast.267, bf16[4,128,4,32]{1,3,2,0:T(8,128)(2,1)S(1)} %bitcast.269, f32[128]{0:T(128)S(1)} %add_multiply_fusion.1, f32[4,128,128]{1,2,0:T(8,128)S(1)} %copy.235), kind=kOutput, calls=%fused_computation.207 | convolution fusion | flops 18088064 | bytes 532992 | tf_op jit(solution)/shard_map/sub | solution.py:47
  27.0 1.2 %fusion.172 = f32[2,8,128]{2,1,0:T(8,128)} fusion(bf16[2,128,8,32]{1,3,2,0:T(8,128)(2,1)S(1)} %bitcast.276, bf16[2,128,8,32]{1,3,2,0:T(8,128)(2,1)S(1)} %bitcast.278, f32[128]{0:T(128)S(1)} %add_multiply_fusion.1, f32[8,128,128]{1,2,0:T(8,128)S(1)} %copy.210), kind=kOutput, calls=%fused_computation.205 | convolution fusion | flops 18088064 | bytes 795136 | tf_op jit(solution)/shard_map/sub | solution.py:47
  28.2 1.0 %fusion.53 = f32[4,4,32,128]{3,2,1,0:T(8,128)S(1)} fusion(bf16[4,128,4,32]{1,3,2,0:T(8,128)(2,1)S(1)} %bitcast.283, f32[4,4,128]{2,1,0:T(4,128)} %fusion.178, f32[4,4,128,128]{2,3,1,0:T(8,128)S(1)} %fusion.15), kind=kOutput, calls=%fused_computation.86 | convolution fusion | flops 17565824 | bytes 1449984 | tf_op jit(solution)/shard_map/bhqk,bkhd->bqhd/dot_general | solution.py:48
  29.4 1.2 %convert_reduce_fusion.3 = (f32[4,128]{1,0:T(4,128)S(1)}, bf16[4,128,128]{1,2,0:T(8,128)(2,1)S(1)}) fusion(bf16[128,128]{1,0:T(8,128)(2,1)S(1)} %copy-done.12, f32[4,128,128]{2,1,0:T(8,128)S(1)} %copy.238, bf16[4,128,128]{1,2,0:T(8,128)(2,1)S(1)} %copy.205, f32[4,128]{1,0:T(4,128)S(1)} %add_rsqrt_fusion.4, f32[4,128]{1,0:T(4,128)S(1)} %broadcast_multiply_fusion.4, ...), kind=kOutput, calls=%fused_computation.96 | convolution fusion | flops 34471424 | bytes 727040 | tf_op jit(solution)/shard_map/bqf,fc->bqc/dot_general | solution.py:51
  30.6 0.8 copy.240
  31.4 2.6 %all-to-all-start.2 = ((bf16[4,128,128]{2,0,1:T(4,128)(2,1)}), bf16[4,128,128]{2,0,1:T(4,128)(2,1)S(1)}, u32[]{:S(2)}, u32[]{:S(2)}) async-start(bf16[4,128,128]{2,0,1:T(4,128)(2,1)} %copy.240), calls=%async_computation.2 | async-start | bytes 262144 | tf_op jit(solution)/shard_map/all_to_all | solution.py:98
  35.1 1.3 %fusion.44 = bf16[2,128,256]{2,1,0:T(8,128)(2,1)S(1)} fusion(f32[2,128,256]{2,1,0:T(8,128)S(1)} %copy.212, bf16[2,128,256]{2,1,0:T(8,128)(2,1)S(1)} %copy-done.2, bf16[256,256]{1,0:T(8,128)(2,1)S(1)} %copy-done.10, bf16[4,256,256]{2,1,0:T(8,128)(2,1)} %param.22, f32[2,128]{1,0:T(2,128)S(1)} %copy-done.7, f32[2,128]{1,0:T(2,128)S(1)} %broadcast_multiply_fusion.5), kind=kOutput, calls=%fused_computation.57 | convolution fusion | flops 67895296 | bytes 919552 | tf_op jit(solution)/shard_map/bqf,fc->bqc/dot_general | solution.py:51
  36.4 0.8 copy.213
  37.2 5.1 %all-to-all-done.2 = bf16[4,128,128]{2,0,1:T(4,128)(2,1)S(1)} async-done(((bf16[4,128,128]{2,0,1:T(4,128)(2,1)}), bf16[4,128,128]{2,0,1:T(4,128)(2,1)S(1)}, u32[]{:S(2)}, u32[]{:S(2)}) %all-to-all-start.2) | async-done | bytes 131104 | tf_op jit(solution)/shard_map/all_to_all | solution.py:98
  42.3 2.6 %all-to-all-start.1 = ((bf16[2,128,256]{2,0,1:T(2,128)(2,1)}), bf16[2,128,256]{2,0,1:T(2,128)(2,1)S(1)}, u32[]{:S(2)}, u32[]{:S(2)}) async-start(bf16[2,128,256]{2,0,1:T(2,128)(2,1)} %copy.213), calls=%async_computation.1 | async-start | bytes 262144 | tf_op jit(solution)/shard_map/all_to_all | solution.py:95
  45.9 7.2 %all-to-all-done.1 = bf16[2,128,256]{2,0,1:T(2,128)(2,1)S(1)} async-done(((bf16[2,128,256]{2,0,1:T(2,128)(2,1)}), bf16[2,128,256]{2,0,1:T(2,128)(2,1)S(1)}, u32[]{:S(2)}, u32[]{:S(2)}) %all-to-all-start.1) | async-done | bytes 131104 | tf_op jit(solution)/shard_map/all_to_all | solution.py:95
  53.1 0.7 broadcast_in_dim.7
  53.8 2.8 %all-to-all-start.3 = ((bf16[32,4,4,128]{3,2,1,0:T(4,128)(2,1)}), bf16[32,4,4,128]{3,2,1,0:T(4,128)(2,1)S(1)}, u32[]{:S(2)}, u32[]{:S(2)}) async-start(bf16[32,4,4,128]{3,2,1,0:T(4,128)(2,1)} %broadcast_in_dim.7), calls=%async_computation.3 | async-start | bytes 262144 | tf_op jit(solution)/shard_map/all_to_all | solution.py:56
  59.1 0.6 fusion.173
  61.8 0.5 convert_reduce_fusion.2
  63.6 1.5 %reshape.265 = bf16[32,2,4096]{2,1,0:T(2,128)(2,1)} reshape(bf16[32,4,32,64]{3,2,1,0:T(8,128)(2,1)S(1)} %broadcast_bitcast_fusion) | data formatting | bytes 1048576
  65.5 5.7 %all-to-all-start.4 = ((bf16[32,2,4096]{2,1,0:T(2,128)(2,1)}), bf16[32,2,4096]{2,1,0:T(2,128)(2,1)S(1)}, u32[]{:S(2)}, u32[]{:S(2)}) async-start(bf16[32,2,4096]{2,1,0:T(2,128)(2,1)} %reshape.265), calls=%async_computation.4 | async-start | bytes 1048576 | tf_op jit(solution)/shard_map/all_to_all | solution.py:56
  71.2 0.8 copy.258
  72.0 0.6 fusion.183
  73.8 12.9 %all-to-all-done.4 = bf16[32,2,4096]{2,1,0:T(2,128)(2,1)S(1)} async-done(((bf16[32,2,4096]{2,1,0:T(2,128)(2,1)}), bf16[32,2,4096]{2,1,0:T(2,128)(2,1)S(1)}, u32[]{:S(2)}, u32[]{:S(2)}) %all-to-all-start.4) | async-done | bytes 524320 | tf_op jit(solution)/shard_map/all_to_all | solution.py:56
  86.7 0.7 reshape.266
  87.4 1.1 %copy.256 = bf16[64,128,32]{1,0,2:T(8,128)(2,1)S(1)} copy(bf16[64,128,32]{0,2,1:T(8,128)(2,1)S(1)} %bitcast.246) | data formatting | bytes 1048576 | tf_op jit(solution)/shard_map/reshape | solution.py:59
  88.5 1.3 %divide_convert_fusion = bf16[4,32,128,32]{2,1,3,0:T(8,128)(2,1)S(1)} fusion(f32[]{:T(128)} %get-tuple-element.12, bf16[64,128,32]{1,0,2:T(8,128)(2,1)S(1)} %copy.256, bf16[64,4,256]{2,0,1:T(8,128)(2,1)S(1)} %get-tuple-element.15, f32[64,4]{0,1:T(4,128)S(1)} %add_rsqrt_fusion.2, f32[64,4]{0,1:T(4,128)S(1)} %broadcast_multiply_fusion.2, ...), kind=kOutput, calls=%fused_computation.4 | convolution fusion | flops 72630272 | bytes 1722628 | tf_op jit(solution)/shard_map/sic,sje->ijce/dot_general | solution.py:125
  89.9 0.5 fusion.71
  91.1 0.8 copy.259
  (125 shorter events, 14.1 us)
Async XLA Ops:
  0.6 89.2 %copy-start = (bf16[1024,128]{1,0:T(8,128)(2,1)S(1)}, bf16[1024,128]{1,0:T(8,128)(2,1)}, u32[]{:S(2)}) copy-start(bf16[1024,128]{1,0:T(8,128)(2,1)} %param.35) | copy-start | bytes 786436
  0.6 10.3 %copy-start.1 = (bf16[2,128,256]{2,1,0:T(8,128)(2,1)S(1)}, bf16[2,128,256]{2,1,0:T(8,128)(2,1)}, u32[]{:S(2)}) copy-start(bf16[2,128,256]{2,1,0:T(8,128)(2,1)} %param.18) | copy-start | bytes 393220
  0.7 10.6 %copy-start.9 = (bf16[4,256,256]{2,1,0:T(8,128)(2,1)S(1)}, bf16[4,256,256]{2,1,0:T(8,128)(2,1)}, u32[]{:S(2)}) copy-start(bf16[4,256,256]{2,1,0:T(8,128)(2,1)} %param.22) | copy-start | bytes 1572868
  3.6 8.5 %copy-start.17 = (s32[128]{0:T(128)S(1)}, s32[128]{0:T(128)}, u32[]{:S(2)}) copy-start(s32[128]{0:T(128)} %param.21) | copy-start | bytes 1540
  3.6 8.5 %copy-start.18 = (s32[64]{0:T(128)S(1)}, s32[64]{0:T(128)}, u32[]{:S(2)}) copy-start(s32[64]{0:T(128)} %param.20) | copy-start | bytes 772
  3.6 20.5 %all-to-all-start = ((bf16[32,12,4,128]{3,2,1,0:T(4,128)(2,1)}), bf16[32,12,4,128]{3,2,1,0:T(4,128)(2,1)S(1)}, u32[]{:S(2)}, u32[]{:S(2)}) async-start(bf16[32,12,4,128]{3,2,1,0:T(4,128)(2,1)} %broadcast_in_dim.6), calls=%async_computation | async-start | bytes 786432 | tf_op jit(solution)/shard_map/all_to_all | solution.py:56
  11.2 2.8 %copy-start.6 = (f32[2,128]{1,0:T(2,128)}, f32[2,128]{1,0:T(2,128)S(1)}, u32[]{:S(2)}) copy-start(f32[2,128]{1,0:T(2,128)S(1)} %add_rsqrt_fusion.5) | copy-start | bytes 3076
  11.3 3.0 %copy-start.4 = (bf16[4,128,128]{2,1,0:T(8,128)(2,1)S(1)}, bf16[4,128,128]{2,1,0:T(8,128)(2,1)}, u32[]{:S(2)}) copy-start(bf16[4,128,128]{2,1,0:T(8,128)(2,1)} %param.27) | copy-start | bytes 393220
  28.2 1.2 %copy-start.12 = (bf16[128,128]{1,0:T(8,128)(2,1)S(1)}, bf16[128,128]{1,0:T(8,128)(2,1)}, u32[]{:S(2)}) copy-start(bf16[128,128]{1,0:T(8,128)(2,1)} %param.29) | copy-start | bytes 98308
  29.4 4.7 %copy-start.20 = (f32[2,8,128]{2,1,0:T(8,128)S(1)}, f32[2,8,128]{2,1,0:T(8,128)}, u32[]{:S(2)}) copy-start(f32[2,8,128]{2,1,0:T(8,128)} %fusion.172) | copy-start | bytes 24580
  31.4 10.9 %all-to-all-start.2 = ((bf16[4,128,128]{2,0,1:T(4,128)(2,1)}), bf16[4,128,128]{2,0,1:T(4,128)(2,1)S(1)}, u32[]{:S(2)}, u32[]{:S(2)}) async-start(bf16[4,128,128]{2,0,1:T(4,128)(2,1)} %copy.240), calls=%async_computation.2 | async-start | bytes 262144 | tf_op jit(solution)/shard_map/all_to_all | solution.py:98
  34.1 0.7 copy-start.16
  34.1 1.0 %copy-start.2 = (bf16[2,128,256]{2,1,0:T(8,128)(2,1)S(1)}, bf16[2,128,256]{2,1,0:T(8,128)(2,1)}, u32[]{:S(2)}) copy-start(bf16[2,128,256]{2,1,0:T(8,128)(2,1)} %param.18) | copy-start | bytes 393220
  34.1 1.0 %copy-start.7 = (f32[2,128]{1,0:T(2,128)S(1)}, f32[2,128]{1,0:T(2,128)}, u32[]{:S(2)}) copy-start(f32[2,128]{1,0:T(2,128)} %copy-done.6) | copy-start | bytes 3076
  34.1 1.0 %copy-start.10 = (bf16[256,256]{1,0:T(8,128)(2,1)S(1)}, bf16[256,256]{1,0:T(8,128)(2,1)}, u32[]{:S(2)}) copy-start(bf16[256,256]{1,0:T(8,128)(2,1)} %param.24) | copy-start | bytes 393220
  42.3 10.8 %all-to-all-start.1 = ((bf16[2,128,256]{2,0,1:T(2,128)(2,1)}), bf16[2,128,256]{2,0,1:T(2,128)(2,1)S(1)}, u32[]{:S(2)}, u32[]{:S(2)}) async-start(bf16[2,128,256]{2,0,1:T(2,128)(2,1)} %copy.213), calls=%async_computation.1 | async-start | bytes 262144 | tf_op jit(solution)/shard_map/all_to_all | solution.py:95
  53.8 11.7 %all-to-all-start.3 = ((bf16[32,4,4,128]{3,2,1,0:T(4,128)(2,1)}), bf16[32,4,4,128]{3,2,1,0:T(4,128)(2,1)S(1)}, u32[]{:S(2)}, u32[]{:S(2)}) async-start(bf16[32,4,4,128]{3,2,1,0:T(4,128)(2,1)} %broadcast_in_dim.7), calls=%async_computation.3 | async-start | bytes 262144 | tf_op jit(solution)/shard_map/all_to_all | solution.py:56
  56.9 1.0 %copy-start.3 = (bf16[4,256,256]{2,1,0:T(8,128)(2,1)S(1)}, bf16[4,256,256]{2,1,0:T(8,128)(2,1)}, u32[]{:S(2)}) copy-start(bf16[4,256,256]{2,1,0:T(8,128)(2,1)} %param.25) | copy-start | bytes 1572868
  57.9 0.9 copy-start.8
  60.9 0.9 copy-start.11
  61.8 0.7 copy-start.14
  61.8 0.7 copy-start.19
  62.3 0.9 copy-start.5
  65.5 21.2 %all-to-all-start.4 = ((bf16[32,2,4096]{2,1,0:T(2,128)(2,1)}), bf16[32,2,4096]{2,1,0:T(2,128)(2,1)S(1)}, u32[]{:S(2)}, u32[]{:S(2)}) async-start(bf16[32,2,4096]{2,1,0:T(2,128)(2,1)} %reshape.265), calls=%async_computation.4 | async-start | bytes 1048576 | tf_op jit(solution)/shard_map/all_to_all | solution.py:56
  87.4 1.1 %copy-start.15 = (bf16[256,32]{0,1:T(8,128)(2,1)S(1)}, bf16[256,32]{0,1:T(8,128)(2,1)}, u32[]{:S(2)}) copy-start(bf16[256,32]{0,1:T(8,128)(2,1)} %param.34) | copy-start | bytes 49156
  89.9 0.8 copy-start.13

commit v2 on v1

--- a/solution.py
+++ b/solution.py
@@ -59,6 +59,35 @@
     return received.reshape(shape)
 
 
+def split_for_all(values, count):
+    lead, width = values.shape[0], values.shape[1]
+    pieces = values.reshape((lead, count, width // count) + values.shape[2:])
+    return jnp.moveaxis(pieces, 1, 0).reshape(count, -1)
+
+
+def exchange(alignment_one, pair_one, end_local, count):
+    parts = [
+        split_for_all(alignment_one, count),
+        split_for_all(pair_one, count),
+        jnp.broadcast_to(end_local.reshape(1, -1), (count, end_local.size)),
+    ]
+    sizes = [part.shape[1] for part in parts]
+    received = lax.all_to_all(jnp.concatenate(parts, axis=1), "dap", 0, 0, tiled=True)
+    first, second = sizes[0], sizes[0] + sizes[1]
+    block = alignment_one.shape[1] // count
+    alignment_cols = received[:, :first].reshape(
+        (count * alignment_one.shape[0], block) + alignment_one.shape[2:]
+    )
+    pair_cols = received[:, first:second].reshape(
+        (count * pair_one.shape[0], block) + pair_one.shape[2:]
+    )
+    end_all = jnp.moveaxis(received[:, second:].reshape((count,) + end_local.shape), 0, 1)
+    end_all = end_all.reshape(
+        (end_local.shape[0], count * end_local.shape[1]) + end_local.shape[2:]
+    )
+    return alignment_cols, pair_cols, end_all
+
+
 def per_device(
     alignment,
     pairwise,
@@ -92,15 +121,14 @@
     start_bias = both_bias[H_M:]
     row_update = attend(layer_norm(alignment), row_project, row_bias, residue_keys, row_output, H_M)
     alignment_one = (alignment.astype(jnp.float32) + row_update).astype(jnp.bfloat16)
-    alignment_cols = lax.all_to_all(alignment_one, "dap", split_axis=1, concat_axis=0, tiled=True)
     start_update = attend(pair_norm, start_project, start_bias, residue_keys, start_output, H_Z)
     pair_one = (pairwise.astype(jnp.float32) + start_update).astype(jnp.bfloat16)
-    pair_cols = lax.all_to_all(pair_one, "dap", split_axis=1, concat_axis=0, tiled=True)
     rows_norm_one = layer_norm(pair_one)
     end_local = jnp.einsum(
         "kic,ch->hki", rows_norm_one, end_bias_map, preferred_element_type=jnp.float32
     ).astype(jnp.bfloat16)
-    end_bias = jnp.swapaxes(gather_blocks(end_local, 1, count), 1, 2)
+    alignment_cols, pair_cols, end_all = exchange(alignment_one, pair_one, end_local, count)
+    end_bias = jnp.swapaxes(end_all, 1, 2)
     column_norm = jnp.swapaxes(layer_norm(alignment_cols), 0, 1)
     column_update = attend(column_norm, column_project, None, sequence_keys, column_output, H_M)
     alignment_out = (alignment_cols.astype(jnp.float32) + jnp.swapaxes(column_update, 0, 1)).astype(

time: 92.7 us -> 87.6 us (0.945)
  starting transfers between devices: 20.9 us -> 12.8 us
  other arithmetic: 3.68 us -> 6.29 us
  matrix products: 16.7 us -> 18.6 us
  local copies, waits for them, and re-layouts: 14.7 us -> 13 us
    all_to_all x3 -> x2, starting transfers between devices: 15.7 us -> 9.94 us  [gather_blocks(): received = lax.all_to_all(spread, 'dap', 0, 0, tiled=True)]
    all_to_all x2 -> x1, starting transfers between devices: 5.22 us -> 2.83 us  [exchange(): lax.all_to_all(jnp.concatenate(parts, axis=1), 'dap', 0, 0, tiled=True)]
    convert_element_type x2 -> x0, local copies, waits for them, and re-layouts: 1.58 us -> none  [the longest x1 0.79 us: per_device(): (alignment.astype(jnp.float32) + row_update).astype(jnp.bfloat16)]
    reduce_sum x6, other arithmetic: 1.09 us -> 2.33 us  [layer_norm(): spread = jnp.mean(center * center, axis=-1, keepdims=True)]
    reduce_sum x4, other arithmetic: 0.5 us -> 1.55 us  [layer_norm(): center = widened - jnp.mean(widened, axis=-1, keepdims=True)]
    dot_general x4, matrix products: 2.09 us -> 3.07 us  [attend(): jnp.einsum('bhqk,bkhd->bqhd', softened, value_heads, preferred_element_ty...]
    all_to_all x0 -> x2, other arithmetic: none -> 0.95 us  [exchange(): lax.all_to_all(jnp.concatenate(parts, axis=1), 'dap', 0, 0, tiled=True)]
    all_to_all x3 -> x2, waiting for transfers between devices: 22.1 us -> 22.5 us  [gather_blocks(): received = lax.all_to_all(spread, 'dap', 0, 0, tiled=True)]
  transfers between devices with their start and end apart: 5 -> 3, of which waited for: 4 -> 3; matrix products, arithmetic and copies ran while one was open for 20% -> 8% of each run, Pallas kernels for 0% -> 0%
where the time goes in v2:
time: 87.6 us; the launch traced here: 86.9 us
  waiting for transfers between devices  34.8 us (40%)
  matrix products  18.6 us (21%)
  local copies, waits for them, and re-layouts  13 us (15%)
  starting transfers between devices  12.8 us (15%)
  other arithmetic  6.29 us (7%)
  between operations  1.43 us (2%)
    all_to_all x2, waiting for transfers between devices, gather_blocks(): received = lax.all_to_all(spread, 'dap', 0, 0, tiled=True)  22.5 us
    all_to_all x1, waiting for transfers between devices, exchange(): lax.all_to_all(jnp.concatenate(parts, axis=1), 'dap', 0, 0, tiled=True)  12.3 us
    all_to_all x2, starting transfers between devices, gather_blocks(): received = lax.all_to_all(spread, 'dap', 0, 0, tiled=True)  9.94 us
    unnamed x48, local copies, waits for them, and re-layouts  6.57 us
    sub x4, matrix products, attend(): softened = jax.nn.softmax(scores, axis=-1).astype(jnp.bfloat16)  4.04 us
    dot_general x4, matrix products, attend(): jnp.einsum('bqf,fc->bqc', gated, output_map, preferred_element_type=jnp.f...  3.36 us
    dot_general x12, matrix products, project(): jnp.einsum('bqc,cf->bqf', inputs, weight_table, preferred_element_type=jn...  3.1 us
    dot_general x4, matrix products, attend(): jnp.einsum('bhqk,bkhd->bqhd', softened, value_heads, preferred_element_ty...  3.07 us
  transfers between devices with their start and end apart: 3, of which 3 were waited for; matrix products, arithmetic and copies ran while one was open for 8% of the time, Pallas kernels for 0%

profile of v2, /device:TPU:0, one launch (start us, length us, event | category | flops | bytes accessed | tf_op | source)
XLA Modules:
  0.0 86.9 jit_solution(13699129986304387362)
XLA Ops:
  0.7 1.1 %convert_reduce_fusion = f32[4,128]{1,0:T(4,128)S(1)} fusion(bf16[4,128,128]{2,1,0:T(8,128)(2,1)} %param.19), kind=kLoop, calls=%fused_computation.92 | loop fusion | flops 130560 | bytes 133120 | tf_op jit(solution)/shard_map/reduce_sum | solution.py:18
  1.8 1.1 %fusion.63 = f32[4,128]{1,0:T(4,128)S(1)} fusion(bf16[4,128,128]{2,1,0:T(8,128)(2,1)} %param.19, f32[4,128]{1,0:T(4,128)S(1)} %broadcast_multiply_fusion.4), kind=kLoop, calls=%fused_computation.107 | loop fusion | flops 261632 | bytes 135168 | tf_op jit(solution)/shard_map/reduce_sum | solution.py:19
  2.9 1.3 %convolution_convert_fusion.12 = bf16[12,4,128]{2,0,1:T(8,128)(2,1)S(1)} fusion(bf16[4,128,128]{2,1,0:T(8,128)(2,1)} %param.19, f32[4,128]{1,0:T(4,128)S(1)} %add_rsqrt_fusion.4, f32[4,128]{1,0:T(4,128)S(1)} %broadcast_multiply_fusion.4, bf16[128,4]{0,1:T(4,128)(2,1)} %param.28, bf16[128,8]{0,1:T(8,128)(2,1)} %param.23), kind=kOutput, calls=%fused_computation.76 | convolution fusion | flops 1847296 | bytes 150528 | tf_op jit(solution)/shard_map/ijc,ch->hij/dot_general | solution.py:116
  4.2 0.8 broadcast_in_dim.8
  5.1 7.3 %all-to-all-start = ((bf16[32,12,4,128]{3,2,1,0:T(4,128)(2,1)}), bf16[32,12,4,128]{3,2,1,0:T(4,128)(2,1)S(1)}, u32[]{:S(2)}, u32[]{:S(2)}) async-start(bf16[32,12,4,128]{3,2,1,0:T(4,128)(2,1)} %broadcast_in_dim.8), calls=%async_computation | async-start | bytes 786432 | tf_op jit(solution)/shard_map/all_to_all | solution.py:56
  15.1 10.4 %all-to-all-done = bf16[32,12,4,128]{3,2,1,0:T(4,128)(2,1)S(1)} async-done(((bf16[32,12,4,128]{3,2,1,0:T(4,128)(2,1)}), bf16[32,12,4,128]{3,2,1,0:T(4,128)(2,1)S(1)}, u32[]{:S(2)}, u32[]{:S(2)}) %all-to-all-start) | async-done | bytes 393248 | tf_op jit(solution)/shard_map/all_to_all | solution.py:56
  26.0 1.2 %fusion.170 = f32[4,4,128]{2,1,0:T(4,128)} fusion(bf16[4,128,4,32]{1,3,2,0:T(8,128)(2,1)S(1)} %bitcast.233, bf16[4,128,4,32]{1,3,2,0:T(8,128)(2,1)S(1)} %bitcast.235, f32[128]{0:T(128)S(1)} %add_multiply_fusion.1, f32[4,128,128]{1,2,0:T(8,128)S(1)} %copy.324), kind=kOutput, calls=%fused_computation.215 | convolution fusion | flops 18088064 | bytes 532992 | tf_op jit(solution)/shard_map/sub | solution.py:47
  28.1 1.1 %fusion.171 = f32[2,8,128]{2,1,0:T(8,128)} fusion(bf16[2,128,8,32]{1,3,2,0:T(8,128)(2,1)S(1)} %bitcast.245, bf16[2,128,8,32]{1,3,2,0:T(8,128)(2,1)S(1)} %bitcast.247, f32[128]{0:T(128)S(1)} %add_multiply_fusion.1, f32[8,128,128]{1,2,0:T(8,128)S(1)} %copy.316), kind=kOutput, calls=%fused_computation.216 | convolution fusion | flops 18088064 | bytes 795136 | tf_op jit(solution)/shard_map/sub | solution.py:47
  29.6 1.0 %fusion.53 = f32[4,4,32,128]{3,2,1,0:T(8,128)S(1)} fusion(bf16[4,128,4,32]{1,3,2,0:T(8,128)(2,1)S(1)} %bitcast.253, f32[4,4,128]{2,1,0:T(4,128)} %fusion.170, f32[4,4,128,128]{2,3,1,0:T(8,128)S(1)} %fusion.15), kind=kOutput, calls=%fused_computation.86 | convolution fusion | flops 17565824 | bytes 1449984 | tf_op jit(solution)/shard_map/bhqk,bkhd->bqhd/dot_general | solution.py:48
  30.8 1.3 %convert_reduce_fusion.3 = (f32[4,128]{1,0:T(4,128)S(1)}, bf16[4,128,128]{2,1,0:T(8,128)(2,1)S(1)}) fusion(bf16[128,128]{1,0:T(8,128)(2,1)S(1)} %copy-done.12, f32[4,128,128]{2,1,0:T(8,128)S(1)} %copy.326, bf16[4,128,128]{2,1,0:T(8,128)(2,1)S(1)} %copy-done.1, f32[4,128]{1,0:T(4,128)S(1)} %add_rsqrt_fusion.4, f32[4,128]{1,0:T(4,128)S(1)} %broadcast_multiply_fusion.4, ...), kind=kOutput, calls=%fused_computation.98 | convolution fusion | flops 34471424 | bytes 727040 | tf_op jit(solution)/shard_map/bqf,fc->bqc/dot_general | solution.py:51
  32.8 0.4 copy-done.3
  33.3 1.3 %fusion.44 = bf16[2,128,256]{2,1,0:T(8,128)(2,1)S(1)} fusion(f32[2,128,256]{2,1,0:T(8,128)S(1)} %copy.318, bf16[2,128,256]{2,1,0:T(8,128)(2,1)S(1)} %copy-done.3, bf16[256,256]{1,0:T(8,128)(2,1)S(1)} %copy-done.10, bf16[4,256,256]{2,1,0:T(8,128)(2,1)} %param.22, f32[2,128]{1,0:T(2,128)S(1)} %copy-done.8, f32[2,128]{1,0:T(2,128)S(1)} %broadcast_multiply_fusion.5), kind=kOutput, calls=%fused_computation.57 | convolution fusion | flops 67895296 | bytes 919552 | tf_op jit(solution)/shard_map/bqf,fc->bqc/dot_general | solution.py:51
  35.4 0.5 broadcast.220
  35.9 0.9 %reduce = bf16[32,6144]{1,0:T(8,128)(2,1)S(1)} reduce(bf16[32,1,6144]{2,0,1:T(8,128)(2,1)S(1)} %maximum_bitcast_fusion, bf16[]{:T(256)} %broadcast.220), dimensions={1}, to_apply=%copy.329.reduce_sub_computation | reduce | bytes 786434 | tf_op jit(solution)/shard_map/all_to_all | solution.py:75
  36.8 1.0 %reshape.245 = bf16[32,2,3072]{2,1,0:T(2,128)(2,1)} reshape(bf16[32,6144]{1,0:T(8,128)(2,1)S(1)} %reduce) | data formatting | bytes 786432
  37.9 2.8 %all-to-all-start.1 = ((bf16[32,2,3072]{2,1,0:T(2,128)(2,1)}), bf16[32,2,3072]{2,1,0:T(2,128)(2,1)S(1)}, u32[]{:S(2)}, u32[]{:S(2)}) async-start(bf16[32,2,3072]{2,1,0:T(2,128)(2,1)} %reshape.245), calls=%async_computation.1 | async-start | bytes 786432 | tf_op jit(solution)/shard_map/all_to_all | solution.py:75
  40.7 0.7 convert_reduce_fusion.4
  41.4 12.3 %all-to-all-done.1 = bf16[32,2,3072]{2,1,0:T(2,128)(2,1)S(1)} async-done(((bf16[32,2,3072]{2,1,0:T(2,128)(2,1)}), bf16[32,2,3072]{2,1,0:T(2,128)(2,1)S(1)}, u32[]{:S(2)}, u32[]{:S(2)}) %all-to-all-start.1) | async-done | bytes 393248 | tf_op jit(solution)/shard_map/all_to_all | solution.py:75
  56.3 1.2 %fusion.176 = f32[4,8,64]{2,1,0:T(8,128)} fusion(bf16[4,64,8,32]{1,3,2,0:T(8,128)(2,1)S(1)} %bitcast.229, bf16[4,64,8,32]{1,3,2,0:T(8,128)(2,1)S(1)} %bitcast.231, f32[64]{0:T(128)S(1)} %get-tuple-element.22), kind=kOutput, calls=%fused_computation.217 | convolution fusion | flops 8912959 | bytes 270592 | tf_op jit(solution)/shard_map/sub | solution.py:47
  57.8 0.8 copy.335
  58.7 1.3 %fusion.51 = f32[4,8,32,64]{3,2,1,0:T(8,128)S(1)} fusion(bf16[4,64,8,32]{1,3,2,0:T(8,128)(2,1)} %bitcast.249, f32[4,8,64]{2,1,0:T(8,128)} %fusion.176, f32[4,8,64,64]{2,3,1,0:T(8,128)S(1)} %fusion.18), kind=kOutput, calls=%fused_computation.84 | convolution fusion | flops 8783935 | bytes 925696 | tf_op jit(solution)/shard_map/bhqk,bkhd->bqhd/dot_general | solution.py:48
  60.2 0.4 convert_reduce_fusion.2
  60.6 0.8 copy.357
  62.1 1.5 %reshape.247 = bf16[32,2,4096]{2,1,0:T(2,128)(2,1)} reshape(bf16[32,4,32,64]{3,2,1,0:T(8,128)(2,1)S(1)} %broadcast_bitcast_fusion) | data formatting | bytes 1048576
  63.7 2.6 %all-to-all-start.2 = ((bf16[32,2,4096]{2,1,0:T(2,128)(2,1)}), bf16[32,2,4096]{2,1,0:T(2,128)(2,1)S(1)}, u32[]{:S(2)}, u32[]{:S(2)}) async-start(bf16[32,2,4096]{2,1,0:T(2,128)(2,1)} %reshape.247), calls=%async_computation.2 | async-start | bytes 1048576 | tf_op jit(solution)/shard_map/all_to_all | solution.py:56
  68.2 0.6 fusion.181
  69.8 12.0 %all-to-all-done.2 = bf16[32,2,4096]{2,1,0:T(2,128)(2,1)S(1)} async-done(((bf16[32,2,4096]{2,1,0:T(2,128)(2,1)}), bf16[32,2,4096]{2,1,0:T(2,128)(2,1)S(1)}, u32[]{:S(2)}, u32[]{:S(2)}) %all-to-all-start.2) | async-done | bytes 524320 | tf_op jit(solution)/shard_map/all_to_all | solution.py:56
  81.9 0.7 reshape.248
  82.5 1.1 %copy.355 = bf16[64,128,32]{1,0,2:T(8,128)(2,1)S(1)} copy(bf16[64,128,32]{0,2,1:T(8,128)(2,1)S(1)} %bitcast.219) | data formatting | bytes 1048576 | tf_op jit(solution)/shard_map/reshape | solution.py:59
  83.7 1.3 %divide_convert_fusion = bf16[4,32,128,32]{2,1,3,0:T(8,128)(2,1)S(1)} fusion(f32[]{:T(128)} %get-tuple-element.21, bf16[64,128,32]{1,0,2:T(8,128)(2,1)S(1)} %copy.355, bf16[64,4,256]{2,0,1:T(8,128)(2,1)S(1)} %get-tuple-element.26, f32[64,4]{0,1:T(4,128)S(1)} %add_rsqrt_fusion.2, f32[64,4]{0,1:T(4,128)S(1)} %broadcast_multiply_fusion.2, ...), kind=kOutput, calls=%fused_computation.4 | convolution fusion | flops 72630272 | bytes 1722628 | tf_op jit(solution)/shard_map/sic,sje->ijce/dot_general | solution.py:153
  85.0 0.5 fusion.71
  86.1 0.8 copy.358
  (117 shorter events, 13.1 us)
Async XLA Ops:
  0.6 84.4 %copy-start = (bf16[1024,128]{1,0:T(8,128)(2,1)S(1)}, bf16[1024,128]{1,0:T(8,128)(2,1)}, u32[]{:S(2)}) copy-start(bf16[1024,128]{1,0:T(8,128)(2,1)} %param.35) | copy-start | bytes 786436
  0.6 11.7 %copy-start.2 = (bf16[2,128,256]{2,1,0:T(8,128)(2,1)S(1)}, bf16[2,128,256]{2,1,0:T(8,128)(2,1)}, u32[]{:S(2)}) copy-start(bf16[2,128,256]{2,1,0:T(8,128)(2,1)} %param.18) | copy-start | bytes 393220
  0.7 12.0 %copy-start.9 = (bf16[4,256,256]{2,1,0:T(8,128)(2,1)S(1)}, bf16[4,256,256]{2,1,0:T(8,128)(2,1)}, u32[]{:S(2)}) copy-start(bf16[4,256,256]{2,1,0:T(8,128)(2,1)} %param.22) | copy-start | bytes 1572868
  5.1 8.5 %copy-start.17 = (s32[128]{0:T(128)S(1)}, s32[128]{0:T(128)}, u32[]{:S(2)}) copy-start(s32[128]{0:T(128)} %param.21) | copy-start | bytes 1540
  5.1 20.5 %all-to-all-start = ((bf16[32,12,4,128]{3,2,1,0:T(4,128)(2,1)}), bf16[32,12,4,128]{3,2,1,0:T(4,128)(2,1)S(1)}, u32[]{:S(2)}, u32[]{:S(2)}) async-start(bf16[32,12,4,128]{3,2,1,0:T(4,128)(2,1)} %broadcast_in_dim.8), calls=%async_computation | async-start | bytes 786432 | tf_op jit(solution)/shard_map/all_to_all | solution.py:56
  12.7 1.2 %copy-start.7 = (f32[2,128]{1,0:T(2,128)}, f32[2,128]{1,0:T(2,128)S(1)}, u32[]{:S(2)}) copy-start(f32[2,128]{1,0:T(2,128)S(1)} %add_rsqrt_fusion.5) | copy-start | bytes 3076
  12.7 1.2 %copy-start.1 = (bf16[4,128,128]{2,1,0:T(8,128)(2,1)S(1)}, bf16[4,128,128]{2,1,0:T(8,128)(2,1)}, u32[]{:S(2)}) copy-start(bf16[4,128,128]{2,1,0:T(8,128)(2,1)} %param.19) | copy-start | bytes 393220
  12.7 1.2 %copy-start.5 = (bf16[4,128,128]{2,1,0:T(8,128)(2,1)S(1)}, bf16[4,128,128]{2,1,0:T(8,128)(2,1)}, u32[]{:S(2)}) copy-start(bf16[4,128,128]{2,1,0:T(8,128)(2,1)} %param.27) | copy-start | bytes 393220
  29.6 1.2 %copy-start.12 = (bf16[128,128]{1,0:T(8,128)(2,1)S(1)}, bf16[128,128]{1,0:T(8,128)(2,1)}, u32[]{:S(2)}) copy-start(bf16[128,128]{1,0:T(8,128)(2,1)} %param.29) | copy-start | bytes 98308
  30.8 1.5 %copy-start.19 = (f32[2,8,128]{2,1,0:T(8,128)S(1)}, f32[2,8,128]{2,1,0:T(8,128)}, u32[]{:S(2)}) copy-start(f32[2,8,128]{2,1,0:T(8,128)} %fusion.171) | copy-start | bytes 24580
  32.3 0.9 %copy-start.3 = (bf16[2,128,256]{2,1,0:T(8,128)(2,1)S(1)}, bf16[2,128,256]{2,1,0:T(8,128)(2,1)}, u32[]{:S(2)}) copy-start(bf16[2,128,256]{2,1,0:T(8,128)(2,1)} %param.18) | copy-start | bytes 393220
  32.3 0.9 %copy-start.8 = (f32[2,128]{1,0:T(2,128)S(1)}, f32[2,128]{1,0:T(2,128)}, u32[]{:S(2)}) copy-start(f32[2,128]{1,0:T(2,128)} %copy-done.7) | copy-start | bytes 3076
  32.3 1.0 %copy-start.10 = (bf16[256,256]{1,0:T(8,128)(2,1)S(1)}, bf16[256,256]{1,0:T(8,128)(2,1)}, u32[]{:S(2)}) copy-start(bf16[256,256]{1,0:T(8,128)(2,1)} %param.24) | copy-start | bytes 393220
  33.3 1.8 %copy-start.16 = (bf16[128,4]{0,1:T(4,128)(2,1)S(1)}, bf16[128,4]{0,1:T(4,128)(2,1)}, u32[]{:S(2)}) copy-start(bf16[128,4]{0,1:T(4,128)(2,1)} %param.31) | copy-start | bytes 3076
  35.9 4.7 %copy-start.18 = (s32[64]{0:T(128)S(1)}, s32[64]{0:T(128)}, u32[]{:S(2)}) copy-start(s32[64]{0:T(128)} %param.20) | copy-start | bytes 772
  37.9 15.8 %all-to-all-start.1 = ((bf16[32,2,3072]{2,1,0:T(2,128)(2,1)}), bf16[32,2,3072]{2,1,0:T(2,128)(2,1)S(1)}, u32[]{:S(2)}, u32[]{:S(2)}) async-start(bf16[32,2,3072]{2,1,0:T(2,128)(2,1)} %reshape.245), calls=%async_computation.1 | async-start | bytes 786432 | tf_op jit(solution)/shard_map/all_to_all | solution.py:75
  54.3 1.0 %copy-start.4 = (bf16[4,256,256]{2,1,0:T(8,128)(2,1)S(1)}, bf16[4,256,256]{2,1,0:T(8,128)(2,1)}, u32[]{:S(2)}) copy-start(bf16[4,256,256]{2,1,0:T(8,128)(2,1)} %param.25) | copy-start | bytes 1572868
  58.7 1.5 %copy-start.11 = (bf16[256,256]{1,0:T(8,128)(2,1)S(1)}, bf16[256,256]{1,0:T(8,128)(2,1)}, u32[]{:S(2)}) copy-start(bf16[256,256]{1,0:T(8,128)(2,1)} %param.26) | copy-start | bytes 393220
  60.2 1.4 %copy-start.14 = (bf16[256,32]{0,1:T(8,128)(2,1)S(1)}, bf16[256,32]{0,1:T(8,128)(2,1)}, u32[]{:S(2)}) copy-start(bf16[256,32]{0,1:T(8,128)(2,1)} %param.33) | copy-start | bytes 49156
  63.7 18.2 %all-to-all-start.2 = ((bf16[32,2,4096]{2,1,0:T(2,128)(2,1)}), bf16[32,2,4096]{2,1,0:T(2,128)(2,1)S(1)}, u32[]{:S(2)}, u32[]{:S(2)}) async-start(bf16[32,2,4096]{2,1,0:T(2,128)(2,1)} %reshape.247), calls=%async_computation.2 | async-start | bytes 1048576 | tf_op jit(solution)/shard_map/all_to_all | solution.py:56
  66.7 1.0 %copy-start.6 = (bf16[4,128,128]{2,1,0:T(8,128)(2,1)S(1)}, bf16[4,128,128]{2,1,0:T(8,128)(2,1)}, u32[]{:S(2)}) copy-start(bf16[4,128,128]{2,1,0:T(8,128)(2,1)} %param.30) | copy-start | bytes 393220
  82.5 1.1 %copy-start.15 = (bf16[256,32]{0,1:T(8,128)(2,1)S(1)}, bf16[256,32]{0,1:T(8,128)(2,1)}, u32[]{:S(2)}) copy-start(bf16[256,32]{0,1:T(8,128)(2,1)} %param.34) | copy-start | bytes 49156
  85.0 0.8 copy-start.13

commit v3 on v1

--- a/solution.py
+++ b/solution.py
@@ -59,6 +59,31 @@
     return received.reshape(shape)
 
 
+def split_for_all(values, count):
+    lead, width = values.shape[0], values.shape[1]
+    pieces = values.reshape((lead, count, width // count) + values.shape[2:])
+    return jnp.moveaxis(pieces, 1, 0).reshape(count, -1)
+
+
+def exchange(blocks, broadcast, count):
+    parts = [split_for_all(values, count) for values in blocks]
+    if broadcast is not None:
+        parts.append(jnp.broadcast_to(broadcast.reshape(1, -1), (count, broadcast.size)))
+    received = lax.all_to_all(jnp.concatenate(parts, axis=1), "dap", 0, 0, tiled=True)
+    results, offset = [], 0
+    for values, part in zip(blocks, parts):
+        block = values.shape[1] // count
+        piece = received[:, offset : offset + part.shape[1]]
+        results.append(piece.reshape((count * values.shape[0], block) + values.shape[2:]))
+        offset += part.shape[1]
+    if broadcast is not None:
+        gathered = jnp.moveaxis(received[:, offset:].reshape((count,) + broadcast.shape), 0, 1)
+        results.append(
+            gathered.reshape((broadcast.shape[0], count * broadcast.shape[1]) + broadcast.shape[2:])
+        )
+    return results
+
+
 def per_device(
     alignment,
     pairwise,
@@ -92,15 +117,15 @@
     start_bias = both_bias[H_M:]
     row_update = attend(layer_norm(alignment), row_project, row_bias, residue_keys, row_output, H_M)
     alignment_one = (alignment.astype(jnp.float32) + row_update).astype(jnp.bfloat16)
-    alignment_cols = lax.all_to_all(alignment_one, "dap", split_axis=1, concat_axis=0, tiled=True)
+    (alignment_cols,) = exchange([alignment_one], None, count)
     start_update = attend(pair_norm, start_project, start_bias, residue_keys, start_output, H_Z)
     pair_one = (pairwise.astype(jnp.float32) + start_update).astype(jnp.bfloat16)
-    pair_cols = lax.all_to_all(pair_one, "dap", split_axis=1, concat_axis=0, tiled=True)
     rows_norm_one = layer_norm(pair_one)
     end_local = jnp.einsum(
         "kic,ch->hki", rows_norm_one, end_bias_map, preferred_element_type=jnp.float32
     ).astype(jnp.bfloat16)
-    end_bias = jnp.swapaxes(gather_blocks(end_local, 1, count), 1, 2)
+    pair_cols, end_all = exchange([pair_one], end_local, count)
+    end_bias = jnp.swapaxes(end_all, 1, 2)
     column_norm = jnp.swapaxes(layer_norm(alignment_cols), 0, 1)
     column_update = attend(column_norm, column_project, None, sequence_keys, column_output, H_M)
     alignment_out = (alignment_cols.astype(jnp.float32) + jnp.swapaxes(column_update, 0, 1)).astype(

time: 92.7 us -> 83.8 us (0.904)
  waiting for transfers between devices: 34.4 us -> 24.3 us
  other arithmetic: 3.68 us -> 8.86 us
  starting transfers between devices: 20.9 us -> 17.1 us
    all_to_all x2, waiting for transfers between devices: 12.3 us -> 4.93 us  [exchange(): lax.all_to_all(jnp.concatenate(parts, axis=1), 'dap', 0, 0, tiled=True)]
    all_to_all x3 -> x2, starting transfers between devices: 15.7 us -> 11.7 us  [gather_blocks(): received = lax.all_to_all(spread, 'dap', 0, 0, tiled=True)]
    all_to_all x3 -> x2, waiting for transfers between devices: 22.1 us -> 19.4 us  [gather_blocks(): received = lax.all_to_all(spread, 'dap', 0, 0, tiled=True)]
    all_to_all x0 -> x3, other arithmetic: none -> 2.29 us  [exchange(): lax.all_to_all(jnp.concatenate(parts, axis=1), 'dap', 0, 0, tiled=True)]
    convert_element_type x2 -> x0, local copies, waits for them, and re-layouts: 1.58 us -> none  [the longest x1 0.79 us: per_device(): (alignment.astype(jnp.float32) + row_update).astype(jnp.bfloat16)]
    unnamed x48 -> x52, local copies, waits for them, and re-layouts: 6.29 us -> 7.86 us
    reduce_sum x6, other arithmetic: 1.09 us -> 2.34 us  [layer_norm(): spread = jnp.mean(center * center, axis=-1, keepdims=True)]
    reduce_sum x4, other arithmetic: 0.5 us -> 1.55 us  [layer_norm(): center = widened - jnp.mean(widened, axis=-1, keepdims=True)]
  transfers between devices with their start and end apart: 5 -> 4, of which waited for: 4 -> 4; matrix products, arithmetic and copies ran while one was open for 20% -> 27% of each run, Pallas kernels for 0% -> 0%
where the time goes in v3:
time: 83.8 us; the launch traced here: 83.1 us
  waiting for transfers between devices  24.3 us (29%)
  matrix products  17.1 us (20%)
  starting transfers between devices  17.1 us (20%)
  local copies, waits for them, and re-layouts  14.3 us (17%)
  other arithmetic  8.86 us (11%)
  between operations  1.44 us (2%)
    all_to_all x2, waiting for transfers between devices, gather_blocks(): received = lax.all_to_all(spread, 'dap', 0, 0, tiled=True)  19.4 us
    all_to_all x2, starting transfers between devices, gather_blocks(): received = lax.all_to_all(spread, 'dap', 0, 0, tiled=True)  11.7 us
    unnamed x52, local copies, waits for them, and re-layouts  7.86 us
    all_to_all x2, starting transfers between devices, exchange(): lax.all_to_all(jnp.concatenate(parts, axis=1), 'dap', 0, 0, tiled=True)  5.4 us
    all_to_all x2, waiting for transfers between devices, exchange(): lax.all_to_all(jnp.concatenate(parts, axis=1), 'dap', 0, 0, tiled=True)  4.93 us
    dot_general x12, matrix products, project(): jnp.einsum('bqc,cf->bqf', inputs, weight_table, preferred_element_type=jn...  3.76 us
    dot_general x4, matrix products, attend(): jnp.einsum('bqf,fc->bqc', gated, output_map, preferred_element_type=jnp.f...  3.36 us
    sub x4, matrix products, attend(): softened = jax.nn.softmax(scores, axis=-1).astype(jnp.bfloat16)  2.86 us
  transfers between devices with their start and end apart: 4, of which 4 were waited for; matrix products, arithmetic and copies ran while one was open for 27% of the time, Pallas kernels for 0%

profile of v3, /device:TPU:0, one launch (start us, length us, event | category | flops | bytes accessed | tf_op | source)
XLA Modules:
  0.0 83.1 jit_solution(11254363685020840818)
XLA Ops:
  0.7 1.1 %convert_reduce_fusion = f32[4,128]{1,0:T(4,128)S(1)} fusion(bf16[4,128,128]{2,1,0:T(8,128)(2,1)} %param.19), kind=kLoop, calls=%fused_computation.90 | loop fusion | flops 130560 | bytes 133120 | tf_op jit(solution)/shard_map/reduce_sum | solution.py:18
  1.8 1.1 %fusion.63 = f32[4,128]{1,0:T(4,128)S(1)} fusion(bf16[4,128,128]{2,1,0:T(8,128)(2,1)} %param.19, f32[4,128]{1,0:T(4,128)S(1)} %broadcast_multiply_fusion.4), kind=kLoop, calls=%fused_computation.105 | loop fusion | flops 261632 | bytes 135168 | tf_op jit(solution)/shard_map/reduce_sum | solution.py:19
  2.9 1.3 %convolution_convert_fusion.12 = bf16[12,4,128]{2,0,1:T(8,128)(2,1)S(1)} fusion(bf16[4,128,128]{2,1,0:T(8,128)(2,1)} %param.19, f32[4,128]{1,0:T(4,128)S(1)} %add_rsqrt_fusion.4, f32[4,128]{1,0:T(4,128)S(1)} %broadcast_multiply_fusion.4, bf16[128,4]{0,1:T(4,128)(2,1)} %param.28, bf16[128,8]{0,1:T(8,128)(2,1)} %param.23), kind=kOutput, calls=%fused_computation.76 | convolution fusion | flops 1847296 | bytes 150528 | tf_op jit(solution)/shard_map/ijc,ch->hij/dot_general | solution.py:112
  4.2 0.8 %broadcast_in_dim.8 = bf16[32,12,4,128]{3,2,1,0:T(4,128)(2,1)} broadcast(bf16[12,4,128]{2,1,0:T(4,128)(2,1)S(1)} %copy.316), dimensions={1,2,3} | broadcast | bytes 405504 | tf_op jit(solution)/shard_map/broadcast_in_dim | solution.py:55
  5.1 7.3 %all-to-all-start = ((bf16[32,12,4,128]{3,2,1,0:T(4,128)(2,1)}), bf16[32,12,4,128]{3,2,1,0:T(4,128)(2,1)S(1)}, u32[]{:S(2)}, u32[]{:S(2)}) async-start(bf16[32,12,4,128]{3,2,1,0:T(4,128)(2,1)} %broadcast_in_dim.8), calls=%async_computation | async-start | bytes 786432 | tf_op jit(solution)/shard_map/all_to_all | solution.py:56
  13.5 1.2 %convert_reduce_fusion.5 = (f32[]{:T(128)}, f32[64]{0:T(128)}) fusion(s32[64]{0:T(128)S(1)} %copy-done.20), kind=kLoop, calls=%fused_computation.206 | loop fusion | flops 255 | bytes 516 | tf_op jit(solution)/shard_map/reduce_sum | solution.py:148
  14.7 0.8 copy.313
  15.8 1.0 %convolution_convert_fusion.5 = bf16[4,128,128]{1,2,0:T(8,128)(2,1)} fusion(bf16[4,128,128]{2,1,0:T(8,128)(2,1)S(1)} %copy-done.1, f32[4,128]{1,0:T(4,128)S(1)} %add_rsqrt_fusion.4, f32[4,128]{1,0:T(4,128)S(1)} %broadcast_multiply_fusion.4, bf16[4,128,128]{2,1,0:T(8,128)(2,1)S(1)} %copy-done.6), kind=kOutput, calls=%fused_computation.64 | convolution fusion | flops 17104896 | bytes 299008 | tf_op jit(solution)/shard_map/bqc,cf->bqf/dot_general | solution.py:28
  17.6 8.0 %all-to-all-done = bf16[32,12,4,128]{3,2,1,0:T(4,128)(2,1)S(1)} async-done(((bf16[32,12,4,128]{3,2,1,0:T(4,128)(2,1)}), bf16[32,12,4,128]{3,2,1,0:T(4,128)(2,1)S(1)}, u32[]{:S(2)}, u32[]{:S(2)}) %all-to-all-start) | async-done | bytes 393248 | tf_op jit(solution)/shard_map/all_to_all | solution.py:56
  29.9 1.3 %fusion.44 = bf16[2,128,256]{2,1,0:T(8,128)(2,1)S(1)} fusion(f32[2,128,256]{2,1,0:T(8,128)S(1)} %copy.321, bf16[2,128,256]{2,1,0:T(8,128)(2,1)S(1)} %copy-done.2, bf16[256,256]{1,0:T(8,128)(2,1)S(1)} %copy-done.12, bf16[4,256,256]{2,1,0:T(8,128)(2,1)} %param.22, f32[2,128]{1,0:T(2,128)S(1)} %copy-done.9, f32[2,128]{1,0:T(2,128)S(1)} %broadcast_multiply_fusion.5), kind=kOutput, calls=%fused_computation.57 | convolution fusion | flops 67895296 | bytes 919552 | tf_op jit(solution)/shard_map/bqf,fc->bqc/dot_general | solution.py:51
  31.4 0.6 broadcast.221
  32.0 1.4 %reduce.2 = bf16[32,2048]{1,0:T(8,128)(2,1)S(1)} reduce(bf16[32,1,2048]{2,1,0:T(2,128)(2,1)S(1)} %all_to_all.27, bf16[]{:T(256)} %broadcast.221), dimensions={1}, to_apply=%all_to_all.27.reduce_sub_computation | reduce | bytes 262146 | tf_op jit(solution)/shard_map/all_to_all | solution.py:72
  33.4 0.7 reshape.247
  34.1 2.6 %all-to-all-start.1 = ((bf16[32,2,1024]{2,1,0:T(2,128)(2,1)}), bf16[32,2,1024]{2,1,0:T(2,128)(2,1)S(1)}, u32[]{:S(2)}, u32[]{:S(2)}) async-start(bf16[32,2,1024]{2,1,0:T(2,128)(2,1)} %reshape.247), calls=%async_computation.1 | async-start | bytes 262144 | tf_op jit(solution)/shard_map/all_to_all | solution.py:72
  37.5 1.3 %convert_reduce_fusion.3 = (f32[4,128]{1,0:T(4,128)S(1)}, bf16[4,128,128]{2,1,0:T(8,128)(2,1)S(1)}) fusion(bf16[128,128]{1,0:T(8,128)(2,1)S(1)} %copy-done.14, f32[4,128,128]{2,1,0:T(8,128)S(1)} %copy.344, bf16[4,128,128]{2,1,0:T(8,128)(2,1)S(1)} %copy-done.1, f32[4,128]{1,0:T(4,128)S(1)} %add_rsqrt_fusion.4, f32[4,128]{1,0:T(4,128)S(1)} %broadcast_multiply_fusion.4, ...), kind=kOutput, calls=%fused_computation.96 | convolution fusion | flops 34471424 | bytes 727040 | tf_op jit(solution)/shard_map/bqf,fc->bqc/dot_general | solution.py:51
  39.6 0.8 %reduce.3 = bf16[32,4096]{1,0:T(8,128)(2,1)S(1)} reduce(bf16[32,1,4096]{2,0,1:T(8,128)(2,1)S(1)} %maximum_bitcast_fusion, bf16[]{:T(256)} %broadcast.221), dimensions={1}, to_apply=%copy.347.reduce_sub_computation | reduce | bytes 524290 | tf_op jit(solution)/shard_map/all_to_all | solution.py:72
  40.5 0.9 %reshape.251 = bf16[32,2,2048]{2,1,0:T(2,128)(2,1)} reshape(bf16[32,4096]{1,0:T(8,128)(2,1)S(1)} %reduce.3) | data formatting | bytes 524288
  41.4 3.6 %all-to-all-done.1 = bf16[32,2,1024]{2,1,0:T(2,128)(2,1)S(1)} async-done(((bf16[32,2,1024]{2,1,0:T(2,128)(2,1)}), bf16[32,2,1024]{2,1,0:T(2,128)(2,1)S(1)}, u32[]{:S(2)}, u32[]{:S(2)}) %all-to-all-start.1) | async-done | bytes 131104 | tf_op jit(solution)/shard_map/all_to_all | solution.py:72
  45.0 2.8 %all-to-all-start.2 = ((bf16[32,2,2048]{2,1,0:T(2,128)(2,1)}), bf16[32,2,2048]{2,1,0:T(2,128)(2,1)S(1)}, u32[]{:S(2)}, u32[]{:S(2)}) async-start(bf16[32,2,2048]{2,1,0:T(2,128)(2,1)} %reshape.251), calls=%async_computation.2 | async-start | bytes 524288 | tf_op jit(solution)/shard_map/all_to_all | solution.py:72
  47.9 0.7 convert_reduce_fusion.4
  50.4 1.2 %fusion.171 = f32[4,8,64]{2,1,0:T(8,128)} fusion(bf16[4,64,8,32]{1,3,2,0:T(8,128)(2,1)S(1)} %bitcast.229, bf16[4,64,8,32]{1,3,2,0:T(8,128)(2,1)S(1)} %bitcast.231, f32[64]{0:T(128)S(1)} %copy-done.10), kind=kOutput, calls=%fused_computation.216 | convolution fusion | flops 8912959 | bytes 270592 | tf_op jit(solution)/shard_map/sub | solution.py:47
  52.1 1.1 %fusion.51 = f32[4,8,32,64]{3,2,1,0:T(8,128)S(1)} fusion(bf16[4,64,8,32]{1,3,2,0:T(8,128)(2,1)S(1)} %bitcast.249, f32[4,8,64]{2,1,0:T(8,128)} %fusion.171, f32[4,8,64,64]{2,3,1,0:T(8,128)S(1)} %fusion.18), kind=kOutput, calls=%fused_computation.84 | convolution fusion | flops 8783935 | bytes 925696 | tf_op jit(solution)/shard_map/bhqk,bkhd->bqhd/dot_general | solution.py:48
  54.1 0.8 copy.361
  55.3 1.6 %reshape.249 = bf16[32,2,4096]{2,1,0:T(2,128)(2,1)} reshape(bf16[32,4,32,64]{3,2,1,0:T(8,128)(2,1)S(1)} %broadcast_bitcast_fusion) | data formatting | bytes 1048576
  56.9 1.3 %all-to-all-done.2 = bf16[32,2,2048]{2,1,0:T(2,128)(2,1)S(1)} async-done(((bf16[32,2,2048]{2,1,0:T(2,128)(2,1)}), bf16[32,2,2048]{2,1,0:T(2,128)(2,1)S(1)}, u32[]{:S(2)}, u32[]{:S(2)}) %all-to-all-start.2) | async-done | bytes 262176 | tf_op jit(solution)/shard_map/all_to_all | solution.py:72
  58.2 4.4 %all-to-all-start.3 = ((bf16[32,2,4096]{2,1,0:T(2,128)(2,1)}), bf16[32,2,4096]{2,1,0:T(2,128)(2,1)S(1)}, u32[]{:S(2)}, u32[]{:S(2)}) async-start(bf16[32,2,4096]{2,1,0:T(2,128)(2,1)} %reshape.249), calls=%async_computation.3 | async-start | bytes 1048576 | tf_op jit(solution)/shard_map/all_to_all | solution.py:56
  65.1 0.6 fusion.181
  66.7 11.4 %all-to-all-done.3 = bf16[32,2,4096]{2,1,0:T(2,128)(2,1)S(1)} async-done(((bf16[32,2,4096]{2,1,0:T(2,128)(2,1)}), bf16[32,2,4096]{2,1,0:T(2,128)(2,1)S(1)}, u32[]{:S(2)}, u32[]{:S(2)}) %all-to-all-start.3) | async-done | bytes 524320 | tf_op jit(solution)/shard_map/all_to_all | solution.py:56
  78.1 0.7 reshape.250
  78.8 1.1 %copy.359 = bf16[64,128,32]{1,0,2:T(8,128)(2,1)S(1)} copy(bf16[64,128,32]{0,2,1:T(8,128)(2,1)S(1)} %bitcast.219) | data formatting | bytes 1048576 | tf_op jit(solution)/shard_map/reshape | solution.py:59
  79.9 1.3 %divide_convert_fusion = bf16[4,32,128,32]{2,1,3,0:T(8,128)(2,1)S(1)} fusion(f32[]{:T(128)} %get-tuple-element.20, bf16[64,128,32]{1,0,2:T(8,128)(2,1)S(1)} %copy.359, bf16[64,4,256]{2,0,1:T(8,128)(2,1)S(1)} %get-tuple-element.23, f32[64,4]{0,1:T(4,128)S(1)} %add_rsqrt_fusion.2, f32[64,4]{0,1:T(4,128)S(1)} %broadcast_multiply_fusion.2, ...), kind=kOutput, calls=%fused_computation.4 | convolution fusion | flops 72630272 | bytes 1722628 | tf_op jit(solution)/shard_map/sic,sje->ijce/dot_general | solution.py:150
  82.3 0.8 copy.362
  (125 shorter events, 16.2 us)
Async XLA Ops:
  0.6 80.6 %copy-start = (bf16[1024,128]{1,0:T(8,128)(2,1)S(1)}, bf16[1024,128]{1,0:T(8,128)(2,1)}, u32[]{:S(2)}) copy-start(bf16[1024,128]{1,0:T(8,128)(2,1)} %param.35) | copy-start | bytes 786436
  0.6 11.7 %copy-start.2 = (bf16[2,128,256]{2,1,0:T(8,128)(2,1)S(1)}, bf16[2,128,256]{2,1,0:T(8,128)(2,1)}, u32[]{:S(2)}) copy-start(bf16[2,128,256]{2,1,0:T(8,128)(2,1)} %param.18) | copy-start | bytes 393220
  0.7 12.0 %copy-start.11 = (bf16[4,256,256]{2,1,0:T(8,128)(2,1)S(1)}, bf16[4,256,256]{2,1,0:T(8,128)(2,1)}, u32[]{:S(2)}) copy-start(bf16[4,256,256]{2,1,0:T(8,128)(2,1)} %param.22) | copy-start | bytes 1572868
  5.1 8.5 %copy-start.19 = (s32[128]{0:T(128)S(1)}, s32[128]{0:T(128)}, u32[]{:S(2)}) copy-start(s32[128]{0:T(128)} %param.21) | copy-start | bytes 1540
  5.1 8.5 %copy-start.20 = (s32[64]{0:T(128)S(1)}, s32[64]{0:T(128)}, u32[]{:S(2)}) copy-start(s32[64]{0:T(128)} %param.20) | copy-start | bytes 772
  5.1 20.5 %all-to-all-start = ((bf16[32,12,4,128]{3,2,1,0:T(4,128)(2,1)}), bf16[32,12,4,128]{3,2,1,0:T(4,128)(2,1)S(1)}, u32[]{:S(2)}, u32[]{:S(2)}) async-start(bf16[32,12,4,128]{3,2,1,0:T(4,128)(2,1)} %broadcast_in_dim.8), calls=%async_computation | async-start | bytes 786432 | tf_op jit(solution)/shard_map/all_to_all | solution.py:56
  12.7 2.0 %copy-start.8 = (f32[2,128]{1,0:T(2,128)}, f32[2,128]{1,0:T(2,128)S(1)}, u32[]{:S(2)}) copy-start(f32[2,128]{1,0:T(2,128)S(1)} %add_rsqrt_fusion.5) | copy-start | bytes 3076
  12.7 3.0 %copy-start.1 = (bf16[4,128,128]{2,1,0:T(8,128)(2,1)S(1)}, bf16[4,128,128]{2,1,0:T(8,128)(2,1)}, u32[]{:S(2)}) copy-start(bf16[4,128,128]{2,1,0:T(8,128)(2,1)} %param.19) | copy-start | bytes 393220
  12.7 3.0 %copy-start.6 = (bf16[4,128,128]{2,1,0:T(8,128)(2,1)S(1)}, bf16[4,128,128]{2,1,0:T(8,128)(2,1)}, u32[]{:S(2)}) copy-start(bf16[4,128,128]{2,1,0:T(8,128)(2,1)} %param.27) | copy-start | bytes 393220
  28.1 0.9 %copy-start.5 = (bf16[2,128,256]{1,2,0:T(8,128)(2,1)S(1)}, bf16[2,128,256]{1,2,0:T(8,128)(2,1)}, u32[]{:S(2)}) copy-start(bf16[2,128,256]{1,2,0:T(8,128)(2,1)} %copy.313) | copy-start | bytes 393220
  29.0 0.7 copy-start.9
  29.0 0.9 %copy-start.12 = (bf16[256,256]{1,0:T(8,128)(2,1)S(1)}, bf16[256,256]{1,0:T(8,128)(2,1)}, u32[]{:S(2)}) copy-start(bf16[256,256]{1,0:T(8,128)(2,1)} %param.24) | copy-start | bytes 393220
  31.2 5.6 %copy-start.4 = (bf16[4,128,128]{1,2,0:T(8,128)(2,1)S(1)}, bf16[4,128,128]{1,2,0:T(8,128)(2,1)}, u32[]{:S(2)}) copy-start(bf16[4,128,128]{1,2,0:T(8,128)(2,1)} %convolution_convert_fusion.5) | copy-start | bytes 393220
  34.1 10.9 %all-to-all-start.1 = ((bf16[32,2,1024]{2,1,0:T(2,128)(2,1)}), bf16[32,2,1024]{2,1,0:T(2,128)(2,1)S(1)}, u32[]{:S(2)}, u32[]{:S(2)}) async-start(bf16[32,2,1024]{2,1,0:T(2,128)(2,1)} %reshape.247), calls=%async_computation.1 | async-start | bytes 262144 | tf_op jit(solution)/shard_map/all_to_all | solution.py:72
  36.8 0.8 copy-start.14
  37.5 1.7 %copy-start.18 = (bf16[128,4]{0,1:T(4,128)(2,1)S(1)}, bf16[128,4]{0,1:T(4,128)(2,1)}, u32[]{:S(2)}) copy-start(bf16[128,4]{0,1:T(4,128)(2,1)} %param.31) | copy-start | bytes 3076
  45.0 13.2 %all-to-all-start.2 = ((bf16[32,2,2048]{2,1,0:T(2,128)(2,1)}), bf16[32,2,2048]{2,1,0:T(2,128)(2,1)S(1)}, u32[]{:S(2)}, u32[]{:S(2)}) async-start(bf16[32,2,2048]{2,1,0:T(2,128)(2,1)} %reshape.251), calls=%async_computation.2 | async-start | bytes 524288 | tf_op jit(solution)/shard_map/all_to_all | solution.py:72
  47.9 1.6 %copy-start.3 = (bf16[4,256,256]{2,1,0:T(8,128)(2,1)S(1)}, bf16[4,256,256]{2,1,0:T(8,128)(2,1)}, u32[]{:S(2)}) copy-start(bf16[4,256,256]{2,1,0:T(8,128)(2,1)} %param.25) | copy-start | bytes 1572868
  49.4 0.9 %copy-start.10 = (f32[64]{0:T(128)S(1)}, f32[64]{0:T(128)}, u32[]{:S(2)}) copy-start(f32[64]{0:T(128)} %get-tuple-element.21) | copy-start | bytes 772
  52.1 1.3 %copy-start.13 = (bf16[256,256]{1,0:T(8,128)(2,1)S(1)}, bf16[256,256]{1,0:T(8,128)(2,1)}, u32[]{:S(2)}) copy-start(bf16[256,256]{1,0:T(8,128)(2,1)} %param.26) | copy-start | bytes 393220
  53.4 1.4 %copy-start.16 = (bf16[256,32]{0,1:T(8,128)(2,1)S(1)}, bf16[256,32]{0,1:T(8,128)(2,1)}, u32[]{:S(2)}) copy-start(bf16[256,32]{0,1:T(8,128)(2,1)} %param.33) | copy-start | bytes 49156
  58.2 19.9 %all-to-all-start.3 = ((bf16[32,2,4096]{2,1,0:T(2,128)(2,1)}), bf16[32,2,4096]{2,1,0:T(2,128)(2,1)S(1)}, u32[]{:S(2)}, u32[]{:S(2)}) async-start(bf16[32,2,4096]{2,1,0:T(2,128)(2,1)} %reshape.249), calls=%async_computation.3 | async-start | bytes 1048576 | tf_op jit(solution)/shard_map/all_to_all | solution.py:56
  63.6 1.0 %copy-start.7 = (bf16[4,128,128]{2,1,0:T(8,128)(2,1)S(1)}, bf16[4,128,128]{2,1,0:T(8,128)(2,1)}, u32[]{:S(2)}) copy-start(bf16[4,128,128]{2,1,0:T(8,128)(2,1)} %param.30) | copy-start | bytes 393220
  78.8 1.1 %copy-start.17 = (bf16[256,32]{0,1:T(8,128)(2,1)S(1)}, bf16[256,32]{0,1:T(8,128)(2,1)}, u32[]{:S(2)}) copy-start(bf16[256,32]{0,1:T(8,128)(2,1)} %param.34) | copy-start | bytes 49156
  81.2 0.8 copy-start.15

commit v4 on v1

--- a/solution.py
+++ b/solution.py
@@ -59,6 +59,25 @@
     return received.reshape(shape)
 
 
+def exchange_pair(pair_one, end_local, count):
+    rows, width, channels = pair_one.shape
+    block = width // count
+    pair_part = jnp.moveaxis(pair_one.reshape(rows, count, block, channels), 1, 0)
+    pair_part = pair_part.reshape(count, rows * block, channels)
+    end_part = jnp.broadcast_to(
+        end_local.reshape(1, -1, channels), (count, end_local.size // channels, channels)
+    )
+    received = lax.all_to_all(
+        jnp.concatenate([pair_part, end_part], axis=1), "dap", 0, 0, tiled=True
+    )
+    pair_cols = received[:, : rows * block].reshape(count * rows, block, channels)
+    end_all = received[:, rows * block :].reshape((count,) + end_local.shape)
+    end_all = jnp.moveaxis(end_all, 0, 1).reshape(
+        (end_local.shape[0], count * end_local.shape[1]) + end_local.shape[2:]
+    )
+    return pair_cols, end_all
+
+
 def per_device(
     alignment,
     pairwise,
@@ -92,15 +111,15 @@
     start_bias = both_bias[H_M:]
     row_update = attend(layer_norm(alignment), row_project, row_bias, residue_keys, row_output, H_M)
     alignment_one = (alignment.astype(jnp.float32) + row_update).astype(jnp.bfloat16)
-    alignment_cols = lax.all_to_all(alignment_one, "dap", split_axis=1, concat_axis=0, tiled=True)
+    alignment_cols = lax.all_to_all(alignment_one, "dap", 1, 0, tiled=True)
     start_update = attend(pair_norm, start_project, start_bias, residue_keys, start_output, H_Z)
     pair_one = (pairwise.astype(jnp.float32) + start_update).astype(jnp.bfloat16)
-    pair_cols = lax.all_to_all(pair_one, "dap", split_axis=1, concat_axis=0, tiled=True)
     rows_norm_one = layer_norm(pair_one)
     end_local = jnp.einsum(
         "kic,ch->hki", rows_norm_one, end_bias_map, preferred_element_type=jnp.float32
     ).astype(jnp.bfloat16)
-    end_bias = jnp.swapaxes(gather_blocks(end_local, 1, count), 1, 2)
+    pair_cols, end_all = exchange_pair(pair_one, end_local, count)
+    end_bias = jnp.swapaxes(end_all, 1, 2)
     column_norm = jnp.swapaxes(layer_norm(alignment_cols), 0, 1)
     column_update = attend(column_norm, column_project, None, sequence_keys, column_output, H_M)
     alignment_out = (alignment_cols.astype(jnp.float32) + jnp.swapaxes(column_update, 0, 1)).astype(
@@ -121,15 +140,14 @@
         * weighting
     ).astype(jnp.bfloat16)
     row_count = jnp.sum(sequence_mask.astype(jnp.float32))
+    left_all = lax.all_to_all(
+        jnp.broadcast_to(left[None], (count,) + left.shape), "dap", 0, 0, tiled=True
+    )
     outer_sum = (
-        jnp.einsum(
-            "sic,sje->ijce",
-            gather_blocks(left, 1, count),
-            right,
-            preferred_element_type=jnp.float32,
-        )
+        jnp.einsum("dsic,sje->dijce", left_all, right, preferred_element_type=jnp.float32)
         / row_count
     )
+    outer_sum = outer_sum.reshape((-1,) + outer_sum.shape[2:])
     flattened = outer_sum.astype(jnp.bfloat16).reshape(outer_sum.shape[0], outer_sum.shape[1], -1)
     outer_update = jnp.einsum(
         "ijf,fc->ijc", flattened, outer_output, preferred_element_type=jnp.float32

time: 92.7 us -> 98.3 us (1.060)
  waiting for transfers between devices: 34.4 us -> 19.7 us
  local copies, waits for them, and re-layouts: 14.7 us -> 23.4 us
  matrix products: 16.7 us -> 24.4 us
  other arithmetic: 3.68 us -> 9.89 us
  starting transfers between devices: 20.9 us -> 18.7 us
    all_to_all x3 -> x1, waiting for transfers between devices: 22.1 us -> 1.48 us  [gather_blocks(): received = lax.all_to_all(spread, 'dap', 0, 0, tiled=True)]
    convert_element_type x2, local copies, waits for them, and re-layouts: 0.96 us -> 12.5 us  [per_device(): outer_sum.astype(jnp.bfloat16)]
    all_to_all x3 -> x1, starting transfers between devices: 15.7 us -> 7.3 us  [gather_blocks(): received = lax.all_to_all(spread, 'dap', 0, 0, tiled=True)]
    all_to_all x2 -> x3, starting transfers between devices: 5.22 us -> 11.4 us  [the longest x1 4.44 us: per_device(): lax.all_to_all(jnp.broadcast_to(left[None], (count,) + left.shape), 'dap'...]
    all_to_all x2 -> x3, waiting for transfers between devices: 12.3 us -> 18.2 us  [the longest x1 11.9 us: per_device(): lax.all_to_all(jnp.broadcast_to(left[None], (count,) + left.shape), 'dap'...]
    dot_general x12, matrix products: 3.25 us -> 6.23 us  [project(): jnp.einsum('bqc,cf->bqf', inputs, weight_table, preferred_element_type=jn...]
    dot_general x1, matrix products: 1.33 us -> 4.28 us  [per_device(): jnp.einsum('dsic,sje->dijce', left_all, right, preferred_element_type=jnp...]
    unnamed x48 -> x40, local copies, waits for them, and re-layouts: 6.29 us -> 4.2 us
  transfers between devices with their start and end apart: 5 -> 4, of which waited for: 4 -> 4; matrix products, arithmetic and copies ran while one was open for 20% -> 28% of each run, Pallas kernels for 0% -> 0%
where the time goes in v4:
time: 98.3 us; the launch traced here: 97.4 us
  matrix products  24.4 us (25%)
  local copies, waits for them, and re-layouts  23.4 us (24%)
  waiting for transfers between devices  19.7 us (20%)
  starting transfers between devices  18.7 us (19%)
  other arithmetic  9.89 us (10%)
  between operations  1.39 us (1%)
    convert_element_type x2, local copies, waits for them, and re-layouts, per_device(): outer_sum.astype(jnp.bfloat16)  12.5 us
    all_to_all x1, waiting for transfers between devices, per_device(): lax.all_to_all(jnp.broadcast_to(left[None], (count,) + left.shape), 'dap'...  11.9 us
    all_to_all x1, starting transfers between devices, gather_blocks(): received = lax.all_to_all(spread, 'dap', 0, 0, tiled=True)  7.3 us
    dot_general x12, matrix products, project(): jnp.einsum('bqc,cf->bqf', inputs, weight_table, preferred_element_type=jn...  6.23 us
    all_to_all x1, waiting for transfers between devices, per_device(): alignment_cols = lax.all_to_all(alignment_one, 'dap', 1, 0, tiled=True)  4.9 us
    all_to_all x1, starting transfers between devices, per_device(): lax.all_to_all(jnp.broadcast_to(left[None], (count,) + left.shape), 'dap'...  4.44 us
    dot_general x4, matrix products, attend(): jnp.einsum('bqf,fc->bqc', gated, output_map, preferred_element_type=jnp.f...  4.37 us
    all_to_all x1, starting transfers between devices, per_device(): alignment_cols = lax.all_to_all(alignment_one, 'dap', 1, 0, tiled=True)  4.36 us
  transfers between devices with their start and end apart: 4, of which 4 were waited for; matrix products, arithmetic and copies ran while one was open for 28% of the time, Pallas kernels for 0%

profile of v4, /device:TPU:0, one launch (start us, length us, event | category | flops | bytes accessed | tf_op | source)
XLA Modules:
  0.0 97.4 jit_solution(11071713702070016382)
XLA Ops:
  0.7 1.1 %convert_reduce_fusion = f32[4,128]{1,0:T(4,128)S(1)} fusion(bf16[4,128,128]{2,1,0:T(8,128)(2,1)} %param.19), kind=kLoop, calls=%fused_computation.91 | loop fusion | flops 130560 | bytes 133120 | tf_op jit(solution)/shard_map/reduce_sum | solution.py:18
  1.7 1.1 %fusion.64 = f32[4,128]{1,0:T(4,128)S(1)} fusion(bf16[4,128,128]{2,1,0:T(8,128)(2,1)} %param.19, f32[4,128]{1,0:T(4,128)S(1)} %broadcast_multiply_fusion.4), kind=kLoop, calls=%fused_computation.106 | loop fusion | flops 261632 | bytes 135168 | tf_op jit(solution)/shard_map/reduce_sum | solution.py:19
  2.9 1.3 %convolution_convert_fusion.12 = bf16[12,4,128]{2,0,1:T(8,128)(2,1)S(1)} fusion(bf16[4,128,128]{2,1,0:T(8,128)(2,1)} %param.19, f32[4,128]{1,0:T(4,128)S(1)} %add_rsqrt_fusion.4, f32[4,128]{1,0:T(4,128)S(1)} %broadcast_multiply_fusion.4, bf16[128,4]{0,1:T(4,128)(2,1)} %param.28, bf16[128,8]{0,1:T(8,128)(2,1)} %param.23), kind=kOutput, calls=%fused_computation.77 | convolution fusion | flops 1847296 | bytes 150528 | tf_op jit(solution)/shard_map/ijc,ch->hij/dot_general | solution.py:106
  4.2 0.8 broadcast_in_dim.8
  5.0 7.3 %all-to-all-start = ((bf16[32,12,4,128]{3,2,1,0:T(4,128)(2,1)}), bf16[32,12,4,128]{3,2,1,0:T(4,128)(2,1)S(1)}, u32[]{:S(2)}, u32[]{:S(2)}) async-start(bf16[32,12,4,128]{3,2,1,0:T(4,128)(2,1)} %broadcast_in_dim.8), calls=%async_computation | async-start | bytes 786432 | tf_op jit(solution)/shard_map/all_to_all | solution.py:56
  12.3 1.0 %convert_reduce_fusion.1 = f32[2,128]{1,0:T(2,128)S(1)} fusion(bf16[2,128,256]{2,1,0:T(8,128)(2,1)} %param.18), kind=kLoop, calls=%fused_computation.93 | loop fusion | flops 130816 | bytes 132096 | tf_op jit(solution)/shard_map/reduce_sum | solution.py:18
  13.4 1.1 %fusion.66 = f32[2,128]{1,0:T(2,128)S(1)} fusion(bf16[2,128,256]{2,1,0:T(8,128)(2,1)} %param.18, f32[2,128]{1,0:T(2,128)S(1)} %broadcast_multiply_fusion.5), kind=kLoop, calls=%fused_computation.108 | loop fusion | flops 261888 | bytes 133120 | tf_op jit(solution)/shard_map/reduce_sum | solution.py:19
  14.5 1.2 %convolution_convert_fusion.11 = bf16[2,128,256]{2,1,0:T(8,128)(2,1)S(1)} fusion(bf16[4,256,256]{2,1,0:T(8,128)(2,1)} %param.22, bf16[2,128,256]{2,1,0:T(8,128)(2,1)} %param.18, f32[2,128]{1,0:T(2,128)S(1)} %add_rsqrt_fusion.5, f32[2,128]{1,0:T(2,128)S(1)} %broadcast_multiply_fusion.5), kind=kOutput, calls=%fused_computation.71 | convolution fusion | flops 33882112 | bytes 395264 | tf_op jit(solution)/shard_map/bqc,cf->bqf/dot_general | solution.py:28
  15.7 1.2 %convolution_convert_fusion.10 = bf16[2,128,256]{2,1,0:T(8,128)(2,1)S(1)} fusion(bf16[4,256,256]{2,1,0:T(8,128)(2,1)} %param.22, bf16[2,128,256]{2,1,0:T(8,128)(2,1)} %param.18, f32[2,128]{1,0:T(2,128)S(1)} %add_rsqrt_fusion.5, f32[2,128]{1,0:T(2,128)S(1)} %broadcast_multiply_fusion.5), kind=kOutput, calls=%fused_computation.70 | convolution fusion | flops 33882112 | bytes 395264 | tf_op jit(solution)/shard_map/bqc,cf->bqf/dot_general | solution.py:28
  16.9 1.2 %convolution_convert_fusion.9 = bf16[2,128,256]{2,1,0:T(8,128)(2,1)S(1)} fusion(bf16[4,256,256]{2,1,0:T(8,128)(2,1)} %param.22, bf16[2,128,256]{2,1,0:T(8,128)(2,1)} %param.18, f32[2,128]{1,0:T(2,128)S(1)} %add_rsqrt_fusion.5, f32[2,128]{1,0:T(2,128)S(1)} %broadcast_multiply_fusion.5), kind=kOutput, calls=%fused_computation.69 | convolution fusion | flops 33882112 | bytes 395264 | tf_op jit(solution)/shard_map/bqc,cf->bqf/dot_general | solution.py:28
  18.8 1.8 %convert_reduce_fusion.4 = (f32[]{:T(128)}, f32[64]{0:T(128)}) fusion(s32[64]{0:T(128)} %param.20), kind=kLoop, calls=%fused_computation.201 | loop fusion | flops 255 | bytes 516 | tf_op jit(solution)/shard_map/reduce_sum | solution.py:142
  20.6 1.2 %convert_element_type.225 = f32[64]{0:T(128)} convert(s32[64]{0:T(128)} %param.20) | non-fusion elementwise | flops 64 | bytes 512 | tf_op jit(solution)/shard_map/convert_element_type | solution.py:24
  24.0 1.5 %all-to-all-done = bf16[32,12,4,128]{3,2,1,0:T(4,128)(2,1)S(1)} async-done(((bf16[32,12,4,128]{3,2,1,0:T(4,128)(2,1)}), bf16[32,12,4,128]{3,2,1,0:T(4,128)(2,1)S(1)}, u32[]{:S(2)}, u32[]{:S(2)}) %all-to-all-start) | async-done | bytes 393248 | tf_op jit(solution)/shard_map/all_to_all | solution.py:56
  26.2 1.1 %fusion.174 = f32[2,8,128]{2,1,0:T(8,128)} fusion(bf16[2,128,8,32]{1,3,2,0:T(8,128)(2,1)S(1)} %bitcast.265, bf16[2,128,8,32]{1,3,2,0:T(8,128)(2,1)S(1)} %bitcast.267, f32[128]{0:T(128)S(1)} %add_multiply_fusion.1, f32[8,128,128]{1,2,0:T(8,128)S(1)} %copy.220), kind=kOutput, calls=%fused_computation.212 | convolution fusion | flops 18088064 | bytes 795136 | tf_op jit(solution)/shard_map/sub | solution.py:47
  29.1 1.2 %fusion.53 = f32[2,8,32,128]{3,2,1,0:T(8,128)S(1)} fusion(bf16[2,128,8,32]{1,3,2,0:T(8,128)(2,1)} %bitcast.274, f32[2,8,128]{2,1,0:T(8,128)S(1)} %copy-done.15, f32[2,8,128,128]{2,3,1,0:T(8,128)S(1)} %fusion.14), kind=kOutput, calls=%fused_computation.86 | convolution fusion | flops 17565824 | bytes 1449984 | tf_op jit(solution)/shard_map/bhqk,bkhd->bqhd/dot_general | solution.py:48
  30.5 1.3 %fusion.45 = bf16[2,128,256]{2,1,0:T(8,128)(2,1)S(1)} fusion(f32[2,128,256]{2,1,0:T(8,128)S(1)} %copy.222, bf16[2,128,256]{2,1,0:T(8,128)(2,1)S(1)} %copy-done.2, bf16[256,256]{1,0:T(8,128)(2,1)S(1)} %copy-done.9, bf16[4,256,256]{2,1,0:T(8,128)(2,1)} %param.22, f32[2,128]{1,0:T(2,128)S(1)} %copy-done.7, f32[2,128]{1,0:T(2,128)S(1)} %broadcast_multiply_fusion.5), kind=kOutput, calls=%fused_computation.58 | convolution fusion | flops 67895296 | bytes 919552 | tf_op jit(solution)/shard_map/bqf,fc->bqc/dot_general | solution.py:51
  31.8 0.8 copy.223
  32.6 4.4 %all-to-all-start.1 = ((bf16[2,128,256]{2,0,1:T(2,128)(2,1)}), bf16[2,128,256]{2,0,1:T(2,128)(2,1)S(1)}, u32[]{:S(2)}, u32[]{:S(2)}) async-start(bf16[2,128,256]{2,0,1:T(2,128)(2,1)} %copy.223), calls=%async_computation.1 | async-start | bytes 262144 | tf_op jit(solution)/shard_map/all_to_all | solution.py:114
  37.5 1.3 %convert_reduce_fusion.3 = (f32[4,128]{1,0:T(4,128)S(1)}, bf16[4,128,128]{2,1,0:T(8,128)(2,1)S(1)}) fusion(bf16[128,128]{1,0:T(8,128)(2,1)S(1)} %copy-done.10, f32[4,128,128]{2,1,0:T(8,128)S(1)} %copy.244, bf16[4,128,128]{2,1,0:T(8,128)(2,1)S(1)} %copy-done.1, f32[4,128]{1,0:T(4,128)S(1)} %add_rsqrt_fusion.4, f32[4,128]{1,0:T(4,128)S(1)} %broadcast_multiply_fusion.4, ...), kind=kOutput, calls=%fused_computation.97 | convolution fusion | flops 34471424 | bytes 727040 | tf_op jit(solution)/shard_map/bqf,fc->bqc/dot_general | solution.py:51
  39.5 0.8 copy.247
  40.3 4.9 %all-to-all-done.1 = bf16[2,128,256]{2,0,1:T(2,128)(2,1)S(1)} async-done(((bf16[2,128,256]{2,0,1:T(2,128)(2,1)}), bf16[2,128,256]{2,0,1:T(2,128)(2,1)S(1)}, u32[]{:S(2)}, u32[]{:S(2)}) %all-to-all-start.1) | async-done | bytes 131104 | tf_op jit(solution)/shard_map/all_to_all | solution.py:114
  45.2 2.6 %all-to-all-start.2 = ((bf16[32,32,128]{2,1,0:T(8,128)(2,1)}), bf16[32,32,128]{2,1,0:T(8,128)(2,1)S(1)}, u32[]{:S(2)}, u32[]{:S(2)}) async-start(bf16[32,32,128]{2,1,0:T(8,128)(2,1)} %copy.247), calls=%async_computation.2 | async-start | bytes 524288 | tf_op jit(solution)/shard_map/all_to_all | solution.py:70
  51.8 1.4 %convert_reduce_fusion.2 = (f32[64,4]{0,1:T(4,128)S(1)}, bf16[64,4,256]{2,0,1:T(8,128)(2,1)S(1)}) fusion(f32[64,4,256]{2,0,1:T(8,128)S(1)} %reshape.235, bf16[256,256]{1,0:T(8,128)(2,1)} %param.26, f32[4,64,256]{2,1,0:T(8,128)S(1)} %copy.237, bf16[4,256,256]{2,1,0:T(8,128)(2,1)S(1)} %copy-done.3, f32[64,4]{0,1:T(4,128)S(1)} %copy.232, f32[64,4]{0,1:T(4,128)S(1)} %copy.228), kind=kOutput, calls=%fused_computation.95 | convolution fusion | flops 67895040 | bytes 1184768 | tf_op jit(solution)/shard_map/bqf,fc->bqc/dot_general | solution.py:51
  53.5 0.8 copy.266
  54.2 1.0 fusion.48
  55.5 1.5 %reshape.269 = bf16[32,2,4096]{2,1,0:T(2,128)(2,1)} reshape(bf16[32,4,32,64]{3,2,1,0:T(8,128)(2,1)S(1)} %broadcast_bitcast_fusion) | data formatting | bytes 1048576
  57.0 1.4 %all-to-all-done.2 = bf16[32,32,128]{2,1,0:T(8,128)(2,1)S(1)} async-done(((bf16[32,32,128]{2,1,0:T(8,128)(2,1)}), bf16[32,32,128]{2,1,0:T(8,128)(2,1)S(1)}, u32[]{:S(2)}, u32[]{:S(2)}) %all-to-all-start.2) | async-done | bytes 262176 | tf_op jit(solution)/shard_map/all_to_all | solution.py:70
  58.4 4.4 %all-to-all-start.3 = ((bf16[32,2,4096]{2,1,0:T(2,128)(2,1)}), bf16[32,2,4096]{2,1,0:T(2,128)(2,1)S(1)}, u32[]{:S(2)}, u32[]{:S(2)}) async-start(bf16[32,2,4096]{2,1,0:T(2,128)(2,1)} %reshape.269), calls=%async_computation.3 | async-start | bytes 1048576 | tf_op jit(solution)/shard_map/all_to_all | solution.py:143
  66.5 11.9 %all-to-all-done.3 = bf16[32,2,4096]{2,1,0:T(2,128)(2,1)S(1)} async-done(((bf16[32,2,4096]{2,1,0:T(2,128)(2,1)}), bf16[32,2,4096]{2,1,0:T(2,128)(2,1)S(1)}, u32[]{:S(2)}, u32[]{:S(2)}) %all-to-all-start.3) | async-done | bytes 524320 | tf_op jit(solution)/shard_map/all_to_all | solution.py:143
  79.1 4.3 %fusion.4 = bf16[32,4,4,32,32]{3,4,1,0,2:T(8,128)(2,1)} fusion(f32[]{:T(128)} %get-tuple-element.16, bf16[64,4,256]{2,0,1:T(8,128)(2,1)S(1)} %get-tuple-element.19, f32[64,4]{0,1:T(4,128)S(1)} %add_rsqrt_fusion.2, f32[64,4]{0,1:T(4,128)S(1)} %broadcast_multiply_fusion.2, f32[64]{0:T(128)S(1)} %copy-done.14, bf16[256,32]{0,1:T(8,128)(2,1)S(1)} %copy-done.12, ...), kind=kOutput, calls=%fused_computation.5 | convolution fusion | flops 72630272 | bytes 1722628 | tf_op jit(solution)/shard_map/dsic,sje->dijce/dot_general | solution.py:147
  83.3 6.3 %copy.265 = bf16[32,4,4,32,32]{4,3,1,0,2:T(8,128)(2,1)} copy(bf16[32,4,4,32,32]{3,4,1,0,2:T(8,128)(2,1)} %fusion.4) | data formatting | bytes 2097152 | tf_op jit(solution)/shard_map/convert_element_type | solution.py:151
  89.7 6.2 %convert_element_type.261 = bf16[128,4,1024]{2,0,1:T(8,128)(2,1)S(1)} reshape(bf16[32,4,4,32,32]{4,3,1,0,2:T(8,128)(2,1)} %copy.265) | data formatting | bytes 2097152 | tf_op jit(solution)/shard_map/convert_element_type | solution.py:151
  (117 shorter events, 16.5 us)
Async XLA Ops:
  0.6 95.2 %copy-start = (bf16[1024,128]{1,0:T(8,128)(2,1)S(1)}, bf16[1024,128]{1,0:T(8,128)(2,1)}, u32[]{:S(2)}) copy-start(bf16[1024,128]{1,0:T(8,128)(2,1)} %param.35) | copy-start | bytes 786436
  0.6 22.2 %copy-start.1 = (bf16[4,128,128]{2,1,0:T(8,128)(2,1)S(1)}, bf16[4,128,128]{2,1,0:T(8,128)(2,1)}, u32[]{:S(2)}) copy-start(bf16[4,128,128]{2,1,0:T(8,128)(2,1)} %param.19) | copy-start | bytes 393220
  0.7 22.2 %copy-start.4 = (bf16[4,128,128]{2,1,0:T(8,128)(2,1)S(1)}, bf16[4,128,128]{2,1,0:T(8,128)(2,1)}, u32[]{:S(2)}) copy-start(bf16[4,128,128]{2,1,0:T(8,128)(2,1)} %param.27) | copy-start | bytes 393220
  5.0 20.5 %all-to-all-start = ((bf16[32,12,4,128]{3,2,1,0:T(4,128)(2,1)}), bf16[32,12,4,128]{3,2,1,0:T(4,128)(2,1)S(1)}, u32[]{:S(2)}, u32[]{:S(2)}) async-start(bf16[32,12,4,128]{3,2,1,0:T(4,128)(2,1)} %broadcast_in_dim.8), calls=%async_computation | async-start | bytes 786432 | tf_op jit(solution)/shard_map/all_to_all | solution.py:56
  14.5 11.5 %copy-start.6 = (f32[2,128]{1,0:T(2,128)}, f32[2,128]{1,0:T(2,128)S(1)}, u32[]{:S(2)}) copy-start(f32[2,128]{1,0:T(2,128)S(1)} %add_rsqrt_fusion.5) | copy-start | bytes 3076
  27.7 1.3 %copy-start.15 = (f32[2,8,128]{2,1,0:T(8,128)S(1)}, f32[2,8,128]{2,1,0:T(8,128)}, u32[]{:S(2)}) copy-start(f32[2,8,128]{2,1,0:T(8,128)} %fusion.174) | copy-start | bytes 24580
  28.1 2.4 %copy-start.2 = (bf16[2,128,256]{2,1,0:T(8,128)(2,1)S(1)}, bf16[2,128,256]{2,1,0:T(8,128)(2,1)}, u32[]{:S(2)}) copy-start(bf16[2,128,256]{2,1,0:T(8,128)(2,1)} %param.18) | copy-start | bytes 393220
  28.1 2.4 %copy-start.7 = (f32[2,128]{1,0:T(2,128)S(1)}, f32[2,128]{1,0:T(2,128)}, u32[]{:S(2)}) copy-start(f32[2,128]{1,0:T(2,128)} %copy-done.6) | copy-start | bytes 3076
  28.1 2.4 %copy-start.9 = (bf16[256,256]{1,0:T(8,128)(2,1)S(1)}, bf16[256,256]{1,0:T(8,128)(2,1)}, u32[]{:S(2)}) copy-start(bf16[256,256]{1,0:T(8,128)(2,1)} %param.24) | copy-start | bytes 393220
  30.3 7.1 %copy-start.10 = (bf16[128,128]{1,0:T(8,128)(2,1)S(1)}, bf16[128,128]{1,0:T(8,128)(2,1)}, u32[]{:S(2)}) copy-start(bf16[128,128]{1,0:T(8,128)(2,1)} %param.29) | copy-start | bytes 98308
  30.5 8.6 %copy-start.13 = (bf16[128,4]{0,1:T(4,128)(2,1)S(1)}, bf16[128,4]{0,1:T(4,128)(2,1)}, u32[]{:S(2)}) copy-start(bf16[128,4]{0,1:T(4,128)(2,1)} %param.31) | copy-start | bytes 3076
  32.6 12.6 %all-to-all-start.1 = ((bf16[2,128,256]{2,0,1:T(2,128)(2,1)}), bf16[2,128,256]{2,0,1:T(2,128)(2,1)S(1)}, u32[]{:S(2)}, u32[]{:S(2)}) async-start(bf16[2,128,256]{2,0,1:T(2,128)(2,1)} %copy.223), calls=%async_computation.1 | async-start | bytes 262144 | tf_op jit(solution)/shard_map/all_to_all | solution.py:114
  37.3 11.7 %copy-start.3 = (bf16[4,256,256]{2,1,0:T(8,128)(2,1)S(1)}, bf16[4,256,256]{2,1,0:T(8,128)(2,1)}, u32[]{:S(2)}) copy-start(bf16[4,256,256]{2,1,0:T(8,128)(2,1)} %param.25) | copy-start | bytes 1572868
  38.8 11.4 %copy-start.8 = (f32[64]{0:T(128)S(1)}, f32[64]{0:T(128)}, u32[]{:S(2)}) copy-start(f32[64]{0:T(128)} %get-tuple-element.17) | copy-start | bytes 772
  45.2 13.2 %all-to-all-start.2 = ((bf16[32,32,128]{2,1,0:T(8,128)(2,1)}), bf16[32,32,128]{2,1,0:T(8,128)(2,1)S(1)}, u32[]{:S(2)}, u32[]{:S(2)}) async-start(bf16[32,32,128]{2,1,0:T(8,128)(2,1)} %copy.247), calls=%async_computation.2 | async-start | bytes 524288 | tf_op jit(solution)/shard_map/all_to_all | solution.py:70
  51.1 3.1 %copy-start.14 = (f32[64]{0:T(128)S(1)}, f32[64]{0:T(128)}, u32[]{:S(2)}) copy-start(f32[64]{0:T(128)} %convert_element_type.225) | copy-start | bytes 772
  51.8 12.5 %copy-start.5 = (bf16[4,128,128]{2,1,0:T(8,128)(2,1)S(1)}, bf16[4,128,128]{2,1,0:T(8,128)(2,1)}, u32[]{:S(2)}) copy-start(bf16[4,128,128]{2,1,0:T(8,128)(2,1)} %param.30) | copy-start | bytes 393220
  58.4 20.0 %all-to-all-start.3 = ((bf16[32,2,4096]{2,1,0:T(2,128)(2,1)}), bf16[32,2,4096]{2,1,0:T(2,128)(2,1)S(1)}, u32[]{:S(2)}, u32[]{:S(2)}) async-start(bf16[32,2,4096]{2,1,0:T(2,128)(2,1)} %reshape.269), calls=%async_computation.3 | async-start | bytes 1048576 | tf_op jit(solution)/shard_map/all_to_all | solution.py:143
  65.4 13.7 %copy-start.12 = (bf16[256,32]{0,1:T(8,128)(2,1)S(1)}, bf16[256,32]{0,1:T(8,128)(2,1)}, u32[]{:S(2)}) copy-start(bf16[256,32]{0,1:T(8,128)(2,1)} %param.34) | copy-start | bytes 49156
  89.7 6.6 %copy-start.11 = (bf16[128,128]{1,0:T(8,128)(2,1)S(1)}, bf16[128,128]{1,0:T(8,128)(2,1)}, u32[]{:S(2)}) copy-start(bf16[128,128]{1,0:T(8,128)(2,1)} %param.32) | copy-start | bytes 98308

commit v5 on v4

--- a/solution.py
+++ b/solution.py
@@ -140,14 +140,15 @@
         * weighting
     ).astype(jnp.bfloat16)
     row_count = jnp.sum(sequence_mask.astype(jnp.float32))
-    left_all = lax.all_to_all(
-        jnp.broadcast_to(left[None], (count,) + left.shape), "dap", 0, 0, tiled=True
-    )
     outer_sum = (
-        jnp.einsum("dsic,sje->dijce", left_all, right, preferred_element_type=jnp.float32)
+        jnp.einsum(
+            "sic,sje->ijce",
+            gather_blocks(left, 1, count),
+            right,
+            preferred_element_type=jnp.float32,
+        )
         / row_count
     )
-    outer_sum = outer_sum.reshape((-1,) + outer_sum.shape[2:])
     flattened = outer_sum.astype(jnp.bfloat16).reshape(outer_sum.shape[0], outer_sum.shape[1], -1)
     outer_update = jnp.einsum(
         "ijf,fc->ijc", flattened, outer_output, preferred_element_type=jnp.float32

time: 98.3 us -> 80.5 us (0.82)
  local copies, waits for them, and re-layouts: 23.4 us -> 14.1 us
  matrix products: 24.4 us -> 16 us
  waiting for transfers between devices: 19.7 us -> 27 us
  other arithmetic: 9.89 us -> 5.62 us
  starting transfers between devices: 18.7 us -> 15.7 us
    all_to_all x1 -> x2, waiting for transfers between devices: 1.48 us -> 19.6 us  [gather_blocks(): received = lax.all_to_all(spread, 'dap', 0, 0, tiled=True)]
    convert_element_type x2 -> x0, local copies, waits for them, and re-layouts: 12.5 us -> none  [per_device(): outer_sum.astype(jnp.bfloat16)]
    all_to_all x1 -> x0, waiting for transfers between devices: 11.9 us -> none  [per_device(): lax.all_to_all(jnp.broadcast_to(left[None], (count,) + left.shape), 'dap'...]
    all_to_all x1 -> x0, starting transfers between devices: 4.44 us -> none  [per_device(): lax.all_to_all(jnp.broadcast_to(left[None], (count,) + left.shape), 'dap'...]
    all_to_all x1 -> x2, starting transfers between devices: 7.3 us -> 10.4 us  [gather_blocks(): received = lax.all_to_all(spread, 'dap', 0, 0, tiled=True)]
    dot_general x1, matrix products: 4.28 us -> 1.27 us  [per_device(): jnp.einsum('sic,sje->ijce', gather_blocks(left, 1, count), right, preferr...]
    dot_general x12, matrix products: 6.23 us -> 3.99 us  [project(): jnp.einsum('bqc,cf->bqf', inputs, weight_table, preferred_element_type=jn...]
    unnamed x40 -> x50, local copies, waits for them, and re-layouts: 4.2 us -> 6.32 us
  transfers between devices with their start and end apart: 4 -> 4, of which waited for: 4 -> 4; matrix products, arithmetic and copies ran while one was open for 28% -> 24% of each run, Pallas kernels for 0% -> 0%
where the time goes in v5:
time: 80.5 us; the launch traced here: 79.7 us
  waiting for transfers between devices  27 us (34%)
  matrix products  16 us (20%)
  starting transfers between devices  15.7 us (20%)
  local copies, waits for them, and re-layouts  14.1 us (18%)
  other arithmetic  5.62 us (7%)
  between operations  1.36 us (2%)
    all_to_all x2, waiting for transfers between devices, gather_blocks(): received = lax.all_to_all(spread, 'dap', 0, 0, tiled=True)  19.6 us
    all_to_all x2, starting transfers between devices, gather_blocks(): received = lax.all_to_all(spread, 'dap', 0, 0, tiled=True)  10.4 us
    unnamed x50, local copies, waits for them, and re-layouts  6.32 us
    all_to_all x1, waiting for transfers between devices, per_device(): alignment_cols = lax.all_to_all(alignment_one, 'dap', 1, 0, tiled=True)  4.66 us
    dot_general x12, matrix products, project(): jnp.einsum('bqc,cf->bqf', inputs, weight_table, preferred_element_type=jn...  3.99 us
    dot_general x4, matrix products, attend(): jnp.einsum('bqf,fc->bqc', gated, output_map, preferred_element_type=jnp.f...  3.42 us
    all_to_all x1, waiting for transfers between devices, exchange_pair(): lax.all_to_all(jnp.concatenate([pair_part, end_part], axis=1), 'dap', 0,...  2.69 us
    all_to_all x1, starting transfers between devices, per_device(): alignment_cols = lax.all_to_all(alignment_one, 'dap', 1, 0, tiled=True)  2.63 us
  transfers between devices with their start and end apart: 4, of which 4 were waited for; matrix products, arithmetic and copies ran while one was open for 24% of the time, Pallas kernels for 0%

profile of v5, /device:TPU:0, one launch (start us, length us, event | category | flops | bytes accessed | tf_op | source)
XLA Modules:
  0.0 79.7 jit_solution(8637801387692139456)
XLA Ops:
  0.7 1.1 %convert_reduce_fusion = f32[4,128]{1,0:T(4,128)S(1)} fusion(bf16[4,128,128]{2,1,0:T(8,128)(2,1)} %param.19), kind=kLoop, calls=%fused_computation.90 | loop fusion | flops 130560 | bytes 133120 | tf_op jit(solution)/shard_map/reduce_sum | solution.py:18
  1.8 1.1 %fusion.63 = f32[4,128]{1,0:T(4,128)S(1)} fusion(bf16[4,128,128]{2,1,0:T(8,128)(2,1)} %param.19, f32[4,128]{1,0:T(4,128)S(1)} %broadcast_multiply_fusion.4), kind=kLoop, calls=%fused_computation.105 | loop fusion | flops 261632 | bytes 135168 | tf_op jit(solution)/shard_map/reduce_sum | solution.py:19
  2.9 1.3 %convolution_convert_fusion.12 = bf16[12,4,128]{2,0,1:T(8,128)(2,1)S(1)} fusion(bf16[4,128,128]{2,1,0:T(8,128)(2,1)} %param.19, f32[4,128]{1,0:T(4,128)S(1)} %add_rsqrt_fusion.4, f32[4,128]{1,0:T(4,128)S(1)} %broadcast_multiply_fusion.4, bf16[128,4]{0,1:T(4,128)(2,1)} %param.28, bf16[128,8]{0,1:T(8,128)(2,1)} %param.23), kind=kOutput, calls=%fused_computation.76 | convolution fusion | flops 1847296 | bytes 150528 | tf_op jit(solution)/shard_map/ijc,ch->hij/dot_general | solution.py:106
  4.2 0.8 %broadcast_in_dim.8 = bf16[32,12,4,128]{3,2,1,0:T(4,128)(2,1)} broadcast(bf16[12,4,128]{2,1,0:T(4,128)(2,1)S(1)} %copy.223), dimensions={1,2,3} | broadcast | bytes 405504 | tf_op jit(solution)/shard_map/broadcast_in_dim | solution.py:55
  5.1 7.3 %all-to-all-start = ((bf16[32,12,4,128]{3,2,1,0:T(4,128)(2,1)}), bf16[32,12,4,128]{3,2,1,0:T(4,128)(2,1)S(1)}, u32[]{:S(2)}, u32[]{:S(2)}) async-start(bf16[32,12,4,128]{3,2,1,0:T(4,128)(2,1)} %broadcast_in_dim.8), calls=%async_computation | async-start | bytes 786432 | tf_op jit(solution)/shard_map/all_to_all | solution.py:56
  13.5 1.2 %convert_reduce_fusion.4 = (f32[]{:T(128)}, f32[64]{0:T(128)}) fusion(s32[64]{0:T(128)S(1)} %copy-done.20), kind=kLoop, calls=%fused_computation.200 | loop fusion | flops 255 | bytes 516 | tf_op jit(solution)/shard_map/reduce_sum | solution.py:142
  14.7 0.8 copy.220
  15.8 1.0 %convolution_convert_fusion.5 = bf16[4,128,128]{1,2,0:T(8,128)(2,1)} fusion(bf16[4,128,128]{2,1,0:T(8,128)(2,1)S(1)} %copy-done.1, f32[4,128]{1,0:T(4,128)S(1)} %add_rsqrt_fusion.4, f32[4,128]{1,0:T(4,128)S(1)} %broadcast_multiply_fusion.4, bf16[4,128,128]{2,1,0:T(8,128)(2,1)S(1)} %copy-done.6), kind=kOutput, calls=%fused_computation.64 | convolution fusion | flops 17104896 | bytes 299008 | tf_op jit(solution)/shard_map/bqc,cf->bqf/dot_general | solution.py:28
  17.6 8.0 %all-to-all-done = bf16[32,12,4,128]{3,2,1,0:T(4,128)(2,1)S(1)} async-done(((bf16[32,12,4,128]{3,2,1,0:T(4,128)(2,1)}), bf16[32,12,4,128]{3,2,1,0:T(4,128)(2,1)S(1)}, u32[]{:S(2)}, u32[]{:S(2)}) %all-to-all-start) | async-done | bytes 393248 | tf_op jit(solution)/shard_map/all_to_all | solution.py:56
  26.2 0.6 fusion.173
  27.5 0.6 fusion.179
  28.4 0.5 copy-done.5
  29.9 1.3 %fusion.44 = bf16[2,128,256]{2,1,0:T(8,128)(2,1)S(1)} fusion(f32[2,128,256]{2,1,0:T(8,128)S(1)} %copy.228, bf16[2,128,256]{2,1,0:T(8,128)(2,1)S(1)} %copy-done.2, bf16[256,256]{1,0:T(8,128)(2,1)S(1)} %copy-done.12, bf16[4,256,256]{2,1,0:T(8,128)(2,1)} %param.22, f32[2,128]{1,0:T(2,128)S(1)} %copy-done.9, f32[2,128]{1,0:T(2,128)S(1)} %broadcast_multiply_fusion.5), kind=kOutput, calls=%fused_computation.57 | convolution fusion | flops 67895296 | bytes 919552 | tf_op jit(solution)/shard_map/bqf,fc->bqc/dot_general | solution.py:51
  31.2 0.8 copy.229
  32.0 2.6 %all-to-all-start.1 = ((bf16[2,128,256]{2,0,1:T(2,128)(2,1)}), bf16[2,128,256]{2,0,1:T(2,128)(2,1)S(1)}, u32[]{:S(2)}, u32[]{:S(2)}) async-start(bf16[2,128,256]{2,0,1:T(2,128)(2,1)} %copy.229), calls=%async_computation.1 | async-start | bytes 262144 | tf_op jit(solution)/shard_map/all_to_all | solution.py:114
  35.4 1.3 %convert_reduce_fusion.3 = (f32[4,128]{1,0:T(4,128)S(1)}, bf16[4,128,128]{2,1,0:T(8,128)(2,1)S(1)}) fusion(bf16[128,128]{1,0:T(8,128)(2,1)S(1)} %copy-done.14, f32[4,128,128]{2,1,0:T(8,128)S(1)} %copy.250, bf16[4,128,128]{2,1,0:T(8,128)(2,1)S(1)} %copy-done.1, f32[4,128]{1,0:T(4,128)S(1)} %add_rsqrt_fusion.4, f32[4,128]{1,0:T(4,128)S(1)} %broadcast_multiply_fusion.4, ...), kind=kOutput, calls=%fused_computation.96 | convolution fusion | flops 34471424 | bytes 727040 | tf_op jit(solution)/shard_map/bqf,fc->bqc/dot_general | solution.py:51
  37.4 0.8 %copy.253 = bf16[32,32,128]{2,1,0:T(8,128)(2,1)} copy(bf16[32,32,128]{2,0,1:T(8,128)(2,1)S(1)} %pad_maximum_fusion) | data formatting | bytes 524288 | tf_op jit(solution)/shard_map/concatenate | solution.py:71
  38.2 4.7 %all-to-all-done.1 = bf16[2,128,256]{2,0,1:T(2,128)(2,1)S(1)} async-done(((bf16[2,128,256]{2,0,1:T(2,128)(2,1)}), bf16[2,128,256]{2,0,1:T(2,128)(2,1)S(1)}, u32[]{:S(2)}, u32[]{:S(2)}) %all-to-all-start.1) | async-done | bytes 131104 | tf_op jit(solution)/shard_map/all_to_all | solution.py:114
  42.9 2.6 %all-to-all-start.2 = ((bf16[32,32,128]{2,1,0:T(8,128)(2,1)}), bf16[32,32,128]{2,1,0:T(8,128)(2,1)S(1)}, u32[]{:S(2)}, u32[]{:S(2)}) async-start(bf16[32,32,128]{2,1,0:T(8,128)(2,1)} %copy.253), calls=%async_computation.2 | async-start | bytes 524288 | tf_op jit(solution)/shard_map/all_to_all | solution.py:70
  47.9 0.6 fusion.174
  49.9 0.5 convert_reduce_fusion.2
  50.6 0.8 copy.273
  51.8 1.5 %reshape.273 = bf16[32,2,4096]{2,1,0:T(2,128)(2,1)} reshape(bf16[32,4,32,64]{3,2,1,0:T(8,128)(2,1)S(1)} %broadcast_bitcast_fusion) | data formatting | bytes 1048576
  53.4 2.7 %all-to-all-done.2 = bf16[32,32,128]{2,1,0:T(8,128)(2,1)S(1)} async-done(((bf16[32,32,128]{2,1,0:T(8,128)(2,1)}), bf16[32,32,128]{2,1,0:T(8,128)(2,1)S(1)}, u32[]{:S(2)}, u32[]{:S(2)}) %all-to-all-start.2) | async-done | bytes 262176 | tf_op jit(solution)/shard_map/all_to_all | solution.py:70
  56.1 3.1 %all-to-all-start.3 = ((bf16[32,2,4096]{2,1,0:T(2,128)(2,1)}), bf16[32,2,4096]{2,1,0:T(2,128)(2,1)S(1)}, u32[]{:S(2)}, u32[]{:S(2)}) async-start(bf16[32,2,4096]{2,1,0:T(2,128)(2,1)} %reshape.273), calls=%async_computation.3 | async-start | bytes 1048576 | tf_op jit(solution)/shard_map/all_to_all | solution.py:56
  61.5 0.6 fusion.184
  63.1 11.6 %all-to-all-done.3 = bf16[32,2,4096]{2,1,0:T(2,128)(2,1)S(1)} async-done(((bf16[32,2,4096]{2,1,0:T(2,128)(2,1)}), bf16[32,2,4096]{2,1,0:T(2,128)(2,1)S(1)}, u32[]{:S(2)}, u32[]{:S(2)}) %all-to-all-start.3) | async-done | bytes 524320 | tf_op jit(solution)/shard_map/all_to_all | solution.py:56
  74.8 0.7 reshape.274
  75.5 1.1 %copy.271 = bf16[64,128,32]{1,0,2:T(8,128)(2,1)S(1)} copy(bf16[64,128,32]{0,2,1:T(8,128)(2,1)S(1)} %bitcast.236) | data formatting | bytes 1048576 | tf_op jit(solution)/shard_map/reshape | solution.py:59
  76.6 1.3 %divide_convert_fusion = bf16[4,32,128,32]{2,1,3,0:T(8,128)(2,1)S(1)} fusion(f32[]{:T(128)} %get-tuple-element.16, bf16[64,128,32]{1,0,2:T(8,128)(2,1)S(1)} %copy.271, bf16[64,4,256]{2,0,1:T(8,128)(2,1)S(1)} %get-tuple-element.19, f32[64,4]{0,1:T(4,128)S(1)} %add_rsqrt_fusion.2, f32[64,4]{0,1:T(4,128)S(1)} %broadcast_multiply_fusion.2, ...), kind=kOutput, calls=%fused_computation.4 | convolution fusion | flops 72630272 | bytes 1722628 | tf_op jit(solution)/shard_map/sic,sje->ijce/dot_general | solution.py:144
  77.9 0.5 fusion.71
  79.0 0.8 copy.274
  (126 shorter events, 14.4 us)
Async XLA Ops:
  0.6 77.3 %copy-start = (bf16[1024,128]{1,0:T(8,128)(2,1)S(1)}, bf16[1024,128]{1,0:T(8,128)(2,1)}, u32[]{:S(2)}) copy-start(bf16[1024,128]{1,0:T(8,128)(2,1)} %param.35) | copy-start | bytes 786436
  0.6 11.7 %copy-start.2 = (bf16[2,128,256]{2,1,0:T(8,128)(2,1)S(1)}, bf16[2,128,256]{2,1,0:T(8,128)(2,1)}, u32[]{:S(2)}) copy-start(bf16[2,128,256]{2,1,0:T(8,128)(2,1)} %param.18) | copy-start | bytes 393220
  0.7 12.0 %copy-start.11 = (bf16[4,256,256]{2,1,0:T(8,128)(2,1)S(1)}, bf16[4,256,256]{2,1,0:T(8,128)(2,1)}, u32[]{:S(2)}) copy-start(bf16[4,256,256]{2,1,0:T(8,128)(2,1)} %param.22) | copy-start | bytes 1572868
  5.1 8.5 %copy-start.19 = (s32[128]{0:T(128)S(1)}, s32[128]{0:T(128)}, u32[]{:S(2)}) copy-start(s32[128]{0:T(128)} %param.21) | copy-start | bytes 1540
  5.1 8.5 %copy-start.20 = (s32[64]{0:T(128)S(1)}, s32[64]{0:T(128)}, u32[]{:S(2)}) copy-start(s32[64]{0:T(128)} %param.20) | copy-start | bytes 772
  5.1 20.5 %all-to-all-start = ((bf16[32,12,4,128]{3,2,1,0:T(4,128)(2,1)}), bf16[32,12,4,128]{3,2,1,0:T(4,128)(2,1)S(1)}, u32[]{:S(2)}, u32[]{:S(2)}) async-start(bf16[32,12,4,128]{3,2,1,0:T(4,128)(2,1)} %broadcast_in_dim.8), calls=%async_computation | async-start | bytes 786432 | tf_op jit(solution)/shard_map/all_to_all | solution.py:56
  12.7 2.0 %copy-start.8 = (f32[2,128]{1,0:T(2,128)}, f32[2,128]{1,0:T(2,128)S(1)}, u32[]{:S(2)}) copy-start(f32[2,128]{1,0:T(2,128)S(1)} %add_rsqrt_fusion.5) | copy-start | bytes 3076
  12.7 3.0 %copy-start.1 = (bf16[4,128,128]{2,1,0:T(8,128)(2,1)S(1)}, bf16[4,128,128]{2,1,0:T(8,128)(2,1)}, u32[]{:S(2)}) copy-start(bf16[4,128,128]{2,1,0:T(8,128)(2,1)} %param.19) | copy-start | bytes 393220
  12.7 3.0 %copy-start.6 = (bf16[4,128,128]{2,1,0:T(8,128)(2,1)S(1)}, bf16[4,128,128]{2,1,0:T(8,128)(2,1)}, u32[]{:S(2)}) copy-start(bf16[4,128,128]{2,1,0:T(8,128)(2,1)} %param.27) | copy-start | bytes 393220
  28.1 0.9 %copy-start.5 = (bf16[2,128,256]{1,2,0:T(8,128)(2,1)S(1)}, bf16[2,128,256]{1,2,0:T(8,128)(2,1)}, u32[]{:S(2)}) copy-start(bf16[2,128,256]{1,2,0:T(8,128)(2,1)} %copy.220) | copy-start | bytes 393220
  29.0 0.7 copy-start.9
  29.0 0.9 %copy-start.12 = (bf16[256,256]{1,0:T(8,128)(2,1)S(1)}, bf16[256,256]{1,0:T(8,128)(2,1)}, u32[]{:S(2)}) copy-start(bf16[256,256]{1,0:T(8,128)(2,1)} %param.24) | copy-start | bytes 393220
  29.9 4.8 %copy-start.4 = (bf16[4,128,128]{1,2,0:T(8,128)(2,1)S(1)}, bf16[4,128,128]{1,2,0:T(8,128)(2,1)}, u32[]{:S(2)}) copy-start(bf16[4,128,128]{1,2,0:T(8,128)(2,1)} %convolution_convert_fusion.5) | copy-start | bytes 393220
  32.0 10.9 %all-to-all-start.1 = ((bf16[2,128,256]{2,0,1:T(2,128)(2,1)}), bf16[2,128,256]{2,0,1:T(2,128)(2,1)S(1)}, u32[]{:S(2)}, u32[]{:S(2)}) async-start(bf16[2,128,256]{2,0,1:T(2,128)(2,1)} %copy.229), calls=%async_computation.1 | async-start | bytes 262144 | tf_op jit(solution)/shard_map/all_to_all | solution.py:114
  34.7 0.8 copy-start.14
  35.0 2.0 %copy-start.18 = (bf16[128,4]{0,1:T(4,128)(2,1)S(1)}, bf16[128,4]{0,1:T(4,128)(2,1)}, u32[]{:S(2)}) copy-start(bf16[128,4]{0,1:T(4,128)(2,1)} %param.31) | copy-start | bytes 3076
  42.9 13.2 %all-to-all-start.2 = ((bf16[32,32,128]{2,1,0:T(8,128)(2,1)}), bf16[32,32,128]{2,1,0:T(8,128)(2,1)S(1)}, u32[]{:S(2)}, u32[]{:S(2)}) async-start(bf16[32,32,128]{2,1,0:T(8,128)(2,1)} %copy.253), calls=%async_computation.2 | async-start | bytes 524288 | tf_op jit(solution)/shard_map/all_to_all | solution.py:70
  45.7 1.1 %copy-start.3 = (bf16[4,256,256]{2,1,0:T(8,128)(2,1)S(1)}, bf16[4,256,256]{2,1,0:T(8,128)(2,1)}, u32[]{:S(2)}) copy-start(bf16[4,256,256]{2,1,0:T(8,128)(2,1)} %param.25) | copy-start | bytes 1572868
  47.0 0.9 %copy-start.10 = (f32[64]{0:T(128)S(1)}, f32[64]{0:T(128)}, u32[]{:S(2)}) copy-start(f32[64]{0:T(128)} %get-tuple-element.17) | copy-start | bytes 772
  49.0 0.9 %copy-start.13 = (bf16[256,256]{1,0:T(8,128)(2,1)S(1)}, bf16[256,256]{1,0:T(8,128)(2,1)}, u32[]{:S(2)}) copy-start(bf16[256,256]{1,0:T(8,128)(2,1)} %param.26) | copy-start | bytes 393220
  49.9 1.5 %copy-start.16 = (bf16[256,32]{0,1:T(8,128)(2,1)S(1)}, bf16[256,32]{0,1:T(8,128)(2,1)}, u32[]{:S(2)}) copy-start(bf16[256,32]{0,1:T(8,128)(2,1)} %param.33) | copy-start | bytes 49156
  56.1 18.7 %all-to-all-start.3 = ((bf16[32,2,4096]{2,1,0:T(2,128)(2,1)}), bf16[32,2,4096]{2,1,0:T(2,128)(2,1)S(1)}, u32[]{:S(2)}, u32[]{:S(2)}) async-start(bf16[32,2,4096]{2,1,0:T(2,128)(2,1)} %reshape.273), calls=%async_computation.3 | async-start | bytes 1048576 | tf_op jit(solution)/shard_map/all_to_all | solution.py:56
  60.1 0.9 %copy-start.7 = (bf16[4,128,128]{2,1,0:T(8,128)(2,1)S(1)}, bf16[4,128,128]{2,1,0:T(8,128)(2,1)}, u32[]{:S(2)}) copy-start(bf16[4,128,128]{2,1,0:T(8,128)(2,1)} %param.30) | copy-start | bytes 393220
  75.4 1.1 %copy-start.17 = (bf16[256,32]{0,1:T(8,128)(2,1)S(1)}, bf16[256,32]{0,1:T(8,128)(2,1)}, u32[]{:S(2)}) copy-start(bf16[256,32]{0,1:T(8,128)(2,1)} %param.34) | copy-start | bytes 49156
  77.9 0.8 copy-start.15

commit v6 on v5

--- a/solution.py
+++ b/solution.py
@@ -7,6 +7,7 @@
 
 H_M = 8
 H_Z = 4
+DAP = ("chip", "core")
 
 
 norm_epsilon = 1e-05
@@ -52,8 +53,16 @@
 
 
 def gather_blocks(block, axis, count):
-    spread = jnp.broadcast_to(block[None], (count,) + block.shape)
-    received = lax.all_to_all(spread, "dap", 0, 0, tiled=True)
+    half = count // 2
+    spread = jnp.broadcast_to(block[None], (half,) + block.shape)
+    same_core = lax.all_to_all(spread, "chip", 0, 0, tiled=True)
+    other_core = lax.ppermute(same_core, "core", [(0, 1), (1, 0)])
+    first = lax.axis_index("core") == 0
+    received = jnp.where(
+        first,
+        jnp.stack([same_core, other_core], axis=1),
+        jnp.stack([other_core, same_core], axis=1),
+    ).reshape((count,) + block.shape)
     received = jnp.moveaxis(received, 0, axis)
     shape = block.shape[:axis] + (count * block.shape[axis],) + block.shape[axis + 1 :]
     return received.reshape(shape)
@@ -68,7 +77,7 @@
         end_local.reshape(1, -1, channels), (count, end_local.size // channels, channels)
     )
     received = lax.all_to_all(
-        jnp.concatenate([pair_part, end_part], axis=1), "dap", 0, 0, tiled=True
+        jnp.concatenate([pair_part, end_part], axis=1), DAP, 0, 0, tiled=True
     )
     pair_cols = received[:, : rows * block].reshape(count * rows, block, channels)
     end_all = received[:, rows * block :].reshape((count,) + end_local.shape)
@@ -111,7 +120,7 @@
     start_bias = both_bias[H_M:]
     row_update = attend(layer_norm(alignment), row_project, row_bias, residue_keys, row_output, H_M)
     alignment_one = (alignment.astype(jnp.float32) + row_update).astype(jnp.bfloat16)
-    alignment_cols = lax.all_to_all(alignment_one, "dap", 1, 0, tiled=True)
+    alignment_cols = lax.all_to_all(alignment_one, DAP, 1, 0, tiled=True)
     start_update = attend(pair_norm, start_project, start_bias, residue_keys, start_output, H_Z)
     pair_one = (pairwise.astype(jnp.float32) + start_update).astype(jnp.bfloat16)
     rows_norm_one = layer_norm(pair_one)
@@ -158,12 +167,16 @@
 
 
 def solution(mesh):
+    count = mesh.shape["dap"]
+    split_mesh = jax.sharding.Mesh(
+        mesh.devices.reshape(mesh.shape["grp"], count // 2, 2), ("grp",) + DAP
+    )
     return jax.shard_map(
-        functools.partial(per_device, count=mesh.shape["dap"]),
-        mesh=mesh,
+        functools.partial(per_device, count=count),
+        mesh=split_mesh,
         in_specs=(
-            P(("grp", "dap"), None, None),
-            P(("grp", "dap"), None, None),
+            P(("grp",) + DAP, None, None),
+            P(("grp",) + DAP, None, None),
             P("grp"),
             P("grp"),
             P(),
@@ -181,6 +194,6 @@
             P(),
             P(),
         ),
-        out_specs=(P("grp", "dap", None), P("grp", "dap", None)),
+        out_specs=(P("grp", DAP, None), P("grp", DAP, None)),
         check_vma=False,
     )

time: 80.5 us -> 77.2 us (0.959)
  waiting for transfers between devices: 27 us -> 20.4 us
  starting transfers between devices: 15.7 us -> 18.2 us
  other arithmetic: 5.62 us -> 6.61 us
  local copies, waits for them, and re-layouts: 14.1 us -> 13.2 us
    all_to_all x4, waiting for transfers between devices: 27 us -> 17.6 us  [the longest x2 9.89 us: gather_blocks(): same_core = lax.all_to_all(spread, 'chip', 0, 0, tiled=True)]
    ppermute x0 -> x2, waiting for transfers between devices: none -> 2.78 us  [gather_blocks(): other_core = lax.ppermute(same_core, 'core', [(0, 1), (1, 0)])]
    all_to_all x4, starting transfers between devices: 15.7 us -> 18 us  [the longest x2 12.2 us: gather_blocks(): same_core = lax.all_to_all(spread, 'chip', 0, 0, tiled=True)]
    unnamed x50 -> x54, local copies, waits for them, and re-layouts: 6.32 us -> 5.16 us
  transfers between devices with their start and end apart: 4 -> 6, of which waited for: 4 -> 6; matrix products, arithmetic and copies ran while one was open for 24% -> 25% of each run, Pallas kernels for 0% -> 0%
where the time goes in v6:
time: 77.2 us; the launch traced here: 76.5 us
  waiting for transfers between devices  20.4 us (26%)
  starting transfers between devices  18.2 us (24%)
  matrix products  16.7 us (22%)
  local copies, waits for them, and re-layouts  13.2 us (17%)
  other arithmetic  6.61 us (9%)
  between operations  1.43 us (2%)
    all_to_all x2, starting transfers between devices, gather_blocks(): same_core = lax.all_to_all(spread, 'chip', 0, 0, tiled=True)  12.2 us
    all_to_all x2, waiting for transfers between devices, gather_blocks(): same_core = lax.all_to_all(spread, 'chip', 0, 0, tiled=True)  9.89 us
    unnamed x54, local copies, waits for them, and re-layouts  5.16 us
    all_to_all x1, waiting for transfers between devices, per_device(): alignment_cols = lax.all_to_all(alignment_one, DAP, 1, 0, tiled=True)  4.67 us
    dot_general x12, matrix products, project(): jnp.einsum('bqc,cf->bqf', inputs, weight_table, preferred_element_type=jn...  3.98 us
    dot_general x4, matrix products, attend(): jnp.einsum('bqf,fc->bqc', gated, output_map, preferred_element_type=jnp.f...  3.42 us
    all_to_all x1, waiting for transfers between devices, exchange_pair(): lax.all_to_all(jnp.concatenate([pair_part, end_part], axis=1), DAP, 0, 0,...  3.07 us
    all_to_all x1, starting transfers between devices, per_device(): alignment_cols = lax.all_to_all(alignment_one, DAP, 1, 0, tiled=True)  3.06 us
  transfers between devices with their start and end apart: 6, of which 6 were waited for; matrix products, arithmetic and copies ran while one was open for 25% of the time, Pallas kernels for 0%

profile of v6, /device:TPU:0, one launch (start us, length us, event | category | flops | bytes accessed | tf_op | source)
XLA Modules:
  0.0 76.5 jit_solution(12945804606807061492)
XLA Ops:
  0.7 1.1 %convert_reduce_fusion = f32[4,128]{1,0:T(4,128)S(1)} fusion(bf16[4,128,128]{2,1,0:T(8,128)(2,1)} %param.19), kind=kLoop, calls=%fused_computation.91 | loop fusion | flops 130560 | bytes 133120 | tf_op jit(solution)/shard_map/reduce_sum | solution.py:19
  1.8 1.1 %fusion.63 = f32[4,128]{1,0:T(4,128)S(1)} fusion(bf16[4,128,128]{2,1,0:T(8,128)(2,1)} %param.19, f32[4,128]{1,0:T(4,128)S(1)} %broadcast_multiply_fusion.4), kind=kLoop, calls=%fused_computation.106 | loop fusion | flops 261632 | bytes 135168 | tf_op jit(solution)/shard_map/reduce_sum | solution.py:20
  2.9 1.3 %convolution_convert_fusion.12 = bf16[12,4,128]{2,0,1:T(8,128)(2,1)S(1)} fusion(bf16[4,128,128]{2,1,0:T(8,128)(2,1)} %param.19, f32[4,128]{1,0:T(4,128)S(1)} %add_rsqrt_fusion.4, f32[4,128]{1,0:T(4,128)S(1)} %broadcast_multiply_fusion.4, bf16[128,4]{0,1:T(4,128)(2,1)} %param.28, bf16[128,8]{0,1:T(8,128)(2,1)} %param.23), kind=kOutput, calls=%fused_computation.76 | convolution fusion | flops 1847296 | bytes 150528 | tf_op jit(solution)/shard_map/ijc,ch->hij/dot_general | solution.py:115
  4.2 0.7 broadcast_in_dim.8
  4.9 8.4 %all-to-all-start = ((bf16[16,12,4,128]{3,2,1,0:T(4,128)(2,1)}), bf16[16,12,4,128]{3,2,1,0:T(4,128)(2,1)S(1)}, u32[]{:S(2)}, u32[]{:S(2)}) async-start(bf16[16,12,4,128]{3,2,1,0:T(4,128)(2,1)} %broadcast_in_dim.8), calls=%async_computation | async-start | bytes 393216 | tf_op jit(solution)/shard_map/all_to_all | solution.py:58
  14.6 1.0 %convolution_convert_fusion.5 = bf16[4,128,128]{1,2,0:T(8,128)(2,1)} fusion(bf16[4,128,128]{2,1,0:T(8,128)(2,1)S(1)} %copy-done.1, f32[4,128]{1,0:T(4,128)S(1)} %add_rsqrt_fusion.4, f32[4,128]{1,0:T(4,128)S(1)} %broadcast_multiply_fusion.4, bf16[4,128,128]{2,1,0:T(8,128)(2,1)S(1)} %copy-done.6), kind=kOutput, calls=%fused_computation.64 | convolution fusion | flops 17104896 | bytes 299008 | tf_op jit(solution)/shard_map/bqc,cf->bqf/dot_general | solution.py:29
  16.0 0.8 copy.230
  17.0 0.6 convert_element_type.221
  17.6 1.2 %convert_reduce_fusion.4 = (f32[]{:T(128)}, f32[64]{0:T(128)}) fusion(s32[64]{0:T(128)S(1)} %copy-done.19), kind=kLoop, calls=%fused_computation.201 | loop fusion | flops 255 | bytes 516 | tf_op jit(solution)/shard_map/reduce_sum | solution.py:151
  19.2 2.9 %all-to-all-done = bf16[16,12,4,128]{3,2,1,0:T(4,128)(2,1)S(1)} async-done(((bf16[16,12,4,128]{3,2,1,0:T(4,128)(2,1)}), bf16[16,12,4,128]{3,2,1,0:T(4,128)(2,1)S(1)}, u32[]{:S(2)}, u32[]{:S(2)}) %all-to-all-start) | async-done | bytes 196640 | tf_op jit(solution)/shard_map/all_to_all | solution.py:58
  22.2 1.4 %collective-permute-done = bf16[16,12,4,128]{3,0,2,1:T(8,128)(2,1)S(1)} collective-permute-done((bf16[16,12,4,128]{3,0,2,1:T(8,128)(2,1)S(1)}, bf16[16,12,4,128]{3,0,2,1:T(8,128)(2,1)S(1)}, u32[]{:S(2)}, u32[]{:S(2)}) %collective-permute-start) | collective-permute-done | bytes 196640 | tf_op jit(solution)/shard_map/ppermute | solution.py:59
  24.7 1.1 %fusion.173 = f32[2,8,128]{2,1,0:T(8,128)} fusion(bf16[2,128,8,32]{1,3,2,0:T(8,128)(2,1)S(1)} %bitcast.276, bf16[2,128,8,32]{1,3,2,0:T(8,128)(2,1)S(1)} %bitcast.278, f32[128]{0:T(128)S(1)} %add_multiply_fusion.1, f32[8,128,128]{1,2,0:T(8,128)S(1)} %copy.238), kind=kOutput, calls=%fused_computation.213 | convolution fusion | flops 18088064 | bytes 795136 | tf_op jit(solution)/shard_map/sub | solution.py:48
  26.5 0.6 fusion.179
  27.5 0.5 copy-done.5
  28.9 1.3 %fusion.44 = bf16[2,128,256]{2,1,0:T(8,128)(2,1)S(1)} fusion(f32[2,128,256]{2,1,0:T(8,128)S(1)} %copy.240, bf16[2,128,256]{2,1,0:T(8,128)(2,1)S(1)} %copy-done.2, bf16[256,256]{1,0:T(8,128)(2,1)S(1)} %copy-done.12, bf16[4,256,256]{2,1,0:T(8,128)(2,1)} %param.22, f32[2,128]{1,0:T(2,128)S(1)} %copy-done.9, f32[2,128]{1,0:T(2,128)S(1)} %broadcast_multiply_fusion.5), kind=kOutput, calls=%fused_computation.57 | convolution fusion | flops 67895296 | bytes 919552 | tf_op jit(solution)/shard_map/bqf,fc->bqc/dot_general | solution.py:52
  30.2 0.8 %copy.241 = bf16[2,128,256]{2,0,1:T(2,128)(2,1)} copy(bf16[2,128,256]{2,1,0:T(8,128)(2,1)S(1)} %fusion.44) | data formatting | bytes 262144 | tf_op jit(solution)/shard_map/convert_element_type | solution.py:122
  31.0 3.1 %all-to-all-start.1 = ((bf16[2,128,256]{2,0,1:T(2,128)(2,1)}), bf16[2,128,256]{2,0,1:T(2,128)(2,1)S(1)}, u32[]{:S(2)}, u32[]{:S(2)}) async-start(bf16[2,128,256]{2,0,1:T(2,128)(2,1)} %copy.241), calls=%async_computation.1 | async-start | bytes 262144 | tf_op jit(solution)/shard_map/all_to_all | solution.py:123
  34.9 1.3 %convert_reduce_fusion.3 = (f32[4,128]{1,0:T(4,128)S(1)}, bf16[4,128,128]{2,1,0:T(8,128)(2,1)S(1)}) fusion(bf16[128,128]{1,0:T(8,128)(2,1)S(1)} %copy-done.14, f32[4,128,128]{2,1,0:T(8,128)S(1)} %copy.262, bf16[4,128,128]{2,1,0:T(8,128)(2,1)S(1)} %copy-done.1, f32[4,128]{1,0:T(4,128)S(1)} %add_rsqrt_fusion.4, f32[4,128]{1,0:T(4,128)S(1)} %broadcast_multiply_fusion.4, ...), kind=kOutput, calls=%fused_computation.97 | convolution fusion | flops 34471424 | bytes 727040 | tf_op jit(solution)/shard_map/bqf,fc->bqc/dot_general | solution.py:52
  36.8 0.8 %copy.265 = bf16[32,32,128]{2,1,0:T(8,128)(2,1)} copy(bf16[32,32,128]{2,0,1:T(8,128)(2,1)S(1)} %pad_maximum_fusion) | data formatting | bytes 524288 | tf_op jit(solution)/shard_map/concatenate | solution.py:80
  37.6 4.7 %all-to-all-done.1 = bf16[2,128,256]{2,0,1:T(2,128)(2,1)S(1)} async-done(((bf16[2,128,256]{2,0,1:T(2,128)(2,1)}), bf16[2,128,256]{2,0,1:T(2,128)(2,1)S(1)}, u32[]{:S(2)}, u32[]{:S(2)}) %all-to-all-start.1) | async-done | bytes 131104 | tf_op jit(solution)/shard_map/all_to_all | solution.py:123
  42.3 2.8 %all-to-all-start.2 = ((bf16[32,32,128]{2,1,0:T(8,128)(2,1)}), bf16[32,32,128]{2,1,0:T(8,128)(2,1)S(1)}, u32[]{:S(2)}, u32[]{:S(2)}) async-start(bf16[32,32,128]{2,1,0:T(8,128)(2,1)} %copy.265), calls=%async_computation.2 | async-start | bytes 524288 | tf_op jit(solution)/shard_map/all_to_all | solution.py:79
  47.5 0.6 fusion.174
  50.2 0.8 copy.285
  51.3 1.1 %reshape.283 = bf16[16,2,4096]{2,1,0:T(2,128)(2,1)} reshape(bf16[16,4,32,64]{3,2,1,0:T(8,128)(2,1)S(1)} %broadcast_bitcast_fusion) | data formatting | bytes 524288
  52.4 3.1 %all-to-all-done.2 = bf16[32,32,128]{2,1,0:T(8,128)(2,1)S(1)} async-done(((bf16[32,32,128]{2,1,0:T(8,128)(2,1)}), bf16[32,32,128]{2,1,0:T(8,128)(2,1)S(1)}, u32[]{:S(2)}, u32[]{:S(2)}) %all-to-all-start.2) | async-done | bytes 262176 | tf_op jit(solution)/shard_map/all_to_all | solution.py:79
  55.5 3.7 %all-to-all-start.3 = ((bf16[16,2,4096]{2,1,0:T(2,128)(2,1)}), bf16[16,2,4096]{2,1,0:T(2,128)(2,1)S(1)}, u32[]{:S(2)}, u32[]{:S(2)}) async-start(bf16[16,2,4096]{2,1,0:T(2,128)(2,1)} %reshape.283), calls=%async_computation.3 | async-start | bytes 524288 | tf_op jit(solution)/shard_map/all_to_all | solution.py:58
  61.2 0.6 fusion.184
  62.4 7.0 %all-to-all-done.3 = bf16[16,2,4096]{2,1,0:T(2,128)(2,1)S(1)} async-done(((bf16[16,2,4096]{2,1,0:T(2,128)(2,1)}), bf16[16,2,4096]{2,1,0:T(2,128)(2,1)S(1)}, u32[]{:S(2)}, u32[]{:S(2)}) %all-to-all-start.3) | async-done | bytes 262176 | tf_op jit(solution)/shard_map/all_to_all | solution.py:58
  70.4 1.4 %collective-permute-done.1 = bf16[16,64,4,32]{1,3,2,0:T(8,128)(2,1)S(1)} collective-permute-done((bf16[16,64,4,32]{1,3,2,0:T(8,128)(2,1)S(1)}, bf16[16,64,4,32]{1,3,2,0:T(8,128)(2,1)S(1)}, u32[]{:S(2)}, u32[]{:S(2)}) %collective-permute-start.1) | collective-permute-done | bytes 262176 | tf_op jit(solution)/shard_map/ppermute | solution.py:59
  72.1 1.1 %copy.283 = bf16[64,128,32]{1,0,2:T(8,128)(2,1)S(1)} copy(bf16[64,128,32]{0,2,1:T(8,128)(2,1)S(1)} %bitcast.246) | data formatting | bytes 1048576 | tf_op jit(solution)/shard_map/reshape | solution.py:68
  73.2 1.3 %divide_convert_fusion = bf16[4,32,128,32]{2,1,3,0:T(8,128)(2,1)S(1)} fusion(f32[]{:T(128)} %get-tuple-element.18, bf16[64,128,32]{1,0,2:T(8,128)(2,1)S(1)} %copy.283, bf16[64,4,256]{2,0,1:T(8,128)(2,1)S(1)} %get-tuple-element.21, f32[64,4]{0,1:T(4,128)S(1)} %add_rsqrt_fusion.2, f32[64,4]{0,1:T(4,128)S(1)} %broadcast_multiply_fusion.2, ...), kind=kOutput, calls=%fused_computation.4 | convolution fusion | flops 72630272 | bytes 1722628 | tf_op jit(solution)/shard_map/sic,sje->ijce/dot_general | solution.py:153
  75.7 0.8 copy.286
  (138 shorter events, 16.2 us)
Async XLA Ops:
  0.6 74.0 %copy-start = (bf16[1024,128]{1,0:T(8,128)(2,1)S(1)}, bf16[1024,128]{1,0:T(8,128)(2,1)}, u32[]{:S(2)}) copy-start(bf16[1024,128]{1,0:T(8,128)(2,1)} %param.35) | copy-start | bytes 786436
  0.6 12.7 %copy-start.2 = (bf16[2,128,256]{2,1,0:T(8,128)(2,1)S(1)}, bf16[2,128,256]{2,1,0:T(8,128)(2,1)}, u32[]{:S(2)}) copy-start(bf16[2,128,256]{2,1,0:T(8,128)(2,1)} %param.18) | copy-start | bytes 393220
  0.7 13.1 %copy-start.11 = (bf16[4,256,256]{2,1,0:T(8,128)(2,1)S(1)}, bf16[4,256,256]{2,1,0:T(8,128)(2,1)}, u32[]{:S(2)}) copy-start(bf16[4,256,256]{2,1,0:T(8,128)(2,1)} %param.22) | copy-start | bytes 1572868
  4.9 9.6 %copy-start.1 = (bf16[4,128,128]{2,1,0:T(8,128)(2,1)S(1)}, bf16[4,128,128]{2,1,0:T(8,128)(2,1)}, u32[]{:S(2)}) copy-start(bf16[4,128,128]{2,1,0:T(8,128)(2,1)} %param.19) | copy-start | bytes 393220
  4.9 9.6 %copy-start.6 = (bf16[4,128,128]{2,1,0:T(8,128)(2,1)S(1)}, bf16[4,128,128]{2,1,0:T(8,128)(2,1)}, u32[]{:S(2)}) copy-start(bf16[4,128,128]{2,1,0:T(8,128)(2,1)} %param.27) | copy-start | bytes 393220
  4.9 17.1 %all-to-all-start = ((bf16[16,12,4,128]{3,2,1,0:T(4,128)(2,1)}), bf16[16,12,4,128]{3,2,1,0:T(4,128)(2,1)S(1)}, u32[]{:S(2)}, u32[]{:S(2)}) async-start(bf16[16,12,4,128]{3,2,1,0:T(4,128)(2,1)} %broadcast_in_dim.8), calls=%async_computation | async-start | bytes 393216 | tf_op jit(solution)/shard_map/all_to_all | solution.py:58
  13.7 2.2 %copy-start.8 = (f32[2,128]{1,0:T(2,128)}, f32[2,128]{1,0:T(2,128)S(1)}, u32[]{:S(2)}) copy-start(f32[2,128]{1,0:T(2,128)S(1)} %add_rsqrt_fusion.5) | copy-start | bytes 3076
  14.0 3.0 %copy-start.19 = (s32[64]{0:T(128)S(1)}, s32[64]{0:T(128)}, u32[]{:S(2)}) copy-start(s32[64]{0:T(128)} %param.20) | copy-start | bytes 772
  14.5 7.6 %copy-start.20 = (s32[128]{0:T(128)S(1)}, s32[128]{0:T(128)}, u32[]{:S(2)}) copy-start(s32[128]{0:T(128)} %param.21) | copy-start | bytes 1540
  22.1 1.5 %collective-permute-start = (bf16[16,12,4,128]{3,0,2,1:T(8,128)(2,1)S(1)}, bf16[16,12,4,128]{3,0,2,1:T(8,128)(2,1)S(1)}, u32[]{:S(2)}, u32[]{:S(2)}) collective-permute-start(bf16[16,12,4,128]{3,0,2,1:T(8,128)(2,1)S(1)} %copy.324), channel_id=1, source_target_pairs={{0,1},{1,0},{2,3},{3,2},{4,5},{5,4},{6,7},{7,6},{8,9},{9,8},{10,11... | collective-permute-start | bytes 589832 | tf_op jit(solution)/shard_map/ppermute | solution.py:59
  27.1 0.9 %copy-start.5 = (bf16[2,128,256]{1,2,0:T(8,128)(2,1)S(1)}, bf16[2,128,256]{1,2,0:T(8,128)(2,1)}, u32[]{:S(2)}) copy-start(bf16[2,128,256]{1,2,0:T(8,128)(2,1)} %copy.230) | copy-start | bytes 393220
  27.1 0.9 %copy-start.22 = (f32[2,8,128]{2,1,0:T(8,128)S(1)}, f32[2,8,128]{2,1,0:T(8,128)}, u32[]{:S(2)}) copy-start(f32[2,8,128]{2,1,0:T(8,128)} %fusion.173) | copy-start | bytes 24580
  28.0 0.7 copy-start.9
  28.0 0.9 %copy-start.12 = (bf16[256,256]{1,0:T(8,128)(2,1)S(1)}, bf16[256,256]{1,0:T(8,128)(2,1)}, u32[]{:S(2)}) copy-start(bf16[256,256]{1,0:T(8,128)(2,1)} %param.24) | copy-start | bytes 393220
  28.9 5.2 %copy-start.4 = (bf16[4,128,128]{1,2,0:T(8,128)(2,1)S(1)}, bf16[4,128,128]{1,2,0:T(8,128)(2,1)}, u32[]{:S(2)}) copy-start(bf16[4,128,128]{1,2,0:T(8,128)(2,1)} %convolution_convert_fusion.5) | copy-start | bytes 393220
  31.0 11.3 %all-to-all-start.1 = ((bf16[2,128,256]{2,0,1:T(2,128)(2,1)}), bf16[2,128,256]{2,0,1:T(2,128)(2,1)S(1)}, u32[]{:S(2)}, u32[]{:S(2)}) async-start(bf16[2,128,256]{2,0,1:T(2,128)(2,1)} %copy.241), calls=%async_computation.1 | async-start | bytes 262144 | tf_op jit(solution)/shard_map/all_to_all | solution.py:123
  34.1 0.8 copy-start.14
  34.5 2.0 %copy-start.18 = (bf16[128,4]{0,1:T(4,128)(2,1)S(1)}, bf16[128,4]{0,1:T(4,128)(2,1)}, u32[]{:S(2)}) copy-start(bf16[128,4]{0,1:T(4,128)(2,1)} %param.31) | copy-start | bytes 3076
  42.3 13.2 %all-to-all-start.2 = ((bf16[32,32,128]{2,1,0:T(8,128)(2,1)}), bf16[32,32,128]{2,1,0:T(8,128)(2,1)S(1)}, u32[]{:S(2)}, u32[]{:S(2)}) async-start(bf16[32,32,128]{2,1,0:T(8,128)(2,1)} %copy.265), calls=%async_computation.2 | async-start | bytes 524288 | tf_op jit(solution)/shard_map/all_to_all | solution.py:79
  45.3 1.1 %copy-start.3 = (bf16[4,256,256]{2,1,0:T(8,128)(2,1)S(1)}, bf16[4,256,256]{2,1,0:T(8,128)(2,1)}, u32[]{:S(2)}) copy-start(bf16[4,256,256]{2,1,0:T(8,128)(2,1)} %param.25) | copy-start | bytes 1572868
  46.6 0.9 %copy-start.10 = (f32[64]{0:T(128)S(1)}, f32[64]{0:T(128)}, u32[]{:S(2)}) copy-start(f32[64]{0:T(128)} %get-tuple-element.19) | copy-start | bytes 772
  48.6 0.9 %copy-start.13 = (bf16[256,256]{1,0:T(8,128)(2,1)S(1)}, bf16[256,256]{1,0:T(8,128)(2,1)}, u32[]{:S(2)}) copy-start(bf16[256,256]{1,0:T(8,128)(2,1)} %param.26) | copy-start | bytes 393220
  49.5 1.5 %copy-start.16 = (bf16[256,32]{0,1:T(8,128)(2,1)S(1)}, bf16[256,32]{0,1:T(8,128)(2,1)}, u32[]{:S(2)}) copy-start(bf16[256,32]{0,1:T(8,128)(2,1)} %param.33) | copy-start | bytes 49156
  49.5 1.5 %copy-start.21 = (f32[64]{0:T(128)S(1)}, f32[64]{0:T(128)}, u32[]{:S(2)}) copy-start(f32[64]{0:T(128)} %convert_element_type.221) | copy-start | bytes 772
  52.4 8.1 %copy-start.7 = (bf16[4,128,128]{2,1,0:T(8,128)(2,1)S(1)}, bf16[4,128,128]{2,1,0:T(8,128)(2,1)}, u32[]{:S(2)}) copy-start(bf16[4,128,128]{2,1,0:T(8,128)(2,1)} %param.30) | copy-start | bytes 393220
  55.5 13.9 %all-to-all-start.3 = ((bf16[16,2,4096]{2,1,0:T(2,128)(2,1)}), bf16[16,2,4096]{2,1,0:T(2,128)(2,1)S(1)}, u32[]{:S(2)}, u32[]{:S(2)}) async-start(bf16[16,2,4096]{2,1,0:T(2,128)(2,1)} %reshape.283), calls=%async_computation.3 | async-start | bytes 524288 | tf_op jit(solution)/shard_map/all_to_all | solution.py:58
  69.8 2.0 %collective-permute-start.1 = (bf16[16,64,4,32]{1,3,2,0:T(8,128)(2,1)S(1)}, bf16[16,64,4,32]{1,3,2,0:T(8,128)(2,1)S(1)}, u32[]{:S(2)}, u32[]{:S(2)}) collective-permute-start(bf16[16,64,4,32]{1,3,2,0:T(8,128)(2,1)S(1)} %bitcast.247), channel_id=1, source_target_pairs={{0,1},{1,0},{2,3},{3,2},{4,5},{5,4},{6,7},{7,6},{8,9},{9,8},{10,11... | collective-permute-start | bytes 786440 | tf_op jit(solution)/shard_map/ppermute | solution.py:59
  72.1 1.1 %copy-start.17 = (bf16[256,32]{0,1:T(8,128)(2,1)S(1)}, bf16[256,32]{0,1:T(8,128)(2,1)}, u32[]{:S(2)}) copy-start(bf16[256,32]{0,1:T(8,128)(2,1)} %param.34) | copy-start | bytes 49156
  74.6 0.8 copy-start.15

commit v7 on v6

--- a/solution.py
+++ b/solution.py
@@ -141,8 +141,8 @@
     last_norm = layer_norm(alignment_out)
     weighting = sequence_mask.astype(jnp.float32)[:, None, None]
     left = (
-        jnp.einsum("sic,co->sio", last_norm, outer_left, preferred_element_type=jnp.float32)
-        * weighting
+        jnp.einsum("sic,co->ios", last_norm, outer_left, preferred_element_type=jnp.float32)
+        * sequence_mask.astype(jnp.float32)
     ).astype(jnp.bfloat16)
     right = (
         jnp.einsum("sic,co->sio", last_norm, outer_right, preferred_element_type=jnp.float32)
@@ -151,8 +151,8 @@
     row_count = jnp.sum(sequence_mask.astype(jnp.float32))
     outer_sum = (
         jnp.einsum(
-            "sic,sje->ijce",
-            gather_blocks(left, 1, count),
+            "ics,sje->ijce",
+            gather_blocks(left, 0, count),
             right,
             preferred_element_type=jnp.float32,
         )

time: 77.2 us -> 78.7 us (1.019)
  matrix products: 16.7 us -> 18.7 us
  waiting for transfers between devices: 20.4 us -> 19.6 us
    ppermute x2, waiting for transfers between devices: 2.78 us -> 1.41 us  [gather_blocks(): other_core = lax.ppermute(same_core, 'core', [(0, 1), (1, 0)])]
    select_n x1 -> x3, local copies, waits for them, and re-layouts: 0.41 us -> 1.59 us  [gather_blocks(): jnp.where(first, jnp.stack([same_core, other_core], axis=1), jnp.stack([o...]
    reshape x1 -> x0, local copies, waits for them, and re-layouts: 1.11 us -> none  [gather_blocks(): return received.reshape(shape)]
    unnamed x54 -> x53, local copies, waits for them, and re-layouts: 5.16 us -> 5.07 us
  transfers between devices with their start and end apart: 6 -> 6, of which waited for: 6 -> 5; matrix products, arithmetic and copies ran while one was open for 25% -> 26% of each run, Pallas kernels for 0% -> 0%
where the time goes in v7:
time: 78.7 us; the launch traced here: 77.7 us
  waiting for transfers between devices  19.6 us (25%)
  matrix products  18.7 us (24%)
  starting transfers between devices  18.1 us (23%)
  local copies, waits for them, and re-layouts  13.2 us (17%)
  other arithmetic  6.62 us (8%)
  between operations  1.43 us (2%)
    all_to_all x2, starting transfers between devices, gather_blocks(): same_core = lax.all_to_all(spread, 'chip', 0, 0, tiled=True)  12.2 us
    all_to_all x2, waiting for transfers between devices, gather_blocks(): same_core = lax.all_to_all(spread, 'chip', 0, 0, tiled=True)  10.5 us
    unnamed x53, local copies, waits for them, and re-layouts  5.07 us
    all_to_all x1, waiting for transfers between devices, per_device(): alignment_cols = lax.all_to_all(alignment_one, DAP, 1, 0, tiled=True)  4.67 us
    dot_general x4, matrix products, attend(): jnp.einsum('bqf,fc->bqc', gated, output_map, preferred_element_type=jnp.f...  4.17 us
    dot_general x12, matrix products, project(): jnp.einsum('bqc,cf->bqf', inputs, weight_table, preferred_element_type=jn...  3.97 us
    sub x4, matrix products, attend(): softened = jax.nn.softmax(scores, axis=-1).astype(jnp.bfloat16)  3.42 us
    all_to_all x1, waiting for transfers between devices, exchange_pair(): lax.all_to_all(jnp.concatenate([pair_part, end_part], axis=1), DAP, 0, 0,...  3.07 us
  transfers between devices with their start and end apart: 6, of which 5 were waited for; matrix products, arithmetic and copies ran while one was open for 26% of the time, Pallas kernels for 0%

profile of v7, /device:TPU:0, one launch (start us, length us, event | category | flops | bytes accessed | tf_op | source)
XLA Modules:
  0.0 77.7 jit_solution(571180827069421494)
XLA Ops:
  0.7 1.1 %convert_reduce_fusion = f32[4,128]{1,0:T(4,128)S(1)} fusion(bf16[4,128,128]{2,1,0:T(8,128)(2,1)} %param.19), kind=kLoop, calls=%fused_computation.92 | loop fusion | flops 130560 | bytes 133120 | tf_op jit(solution)/shard_map/reduce_sum | solution.py:19
  1.8 1.1 %fusion.64 = f32[4,128]{1,0:T(4,128)S(1)} fusion(bf16[4,128,128]{2,1,0:T(8,128)(2,1)} %param.19, f32[4,128]{1,0:T(4,128)S(1)} %broadcast_multiply_fusion.4), kind=kLoop, calls=%fused_computation.107 | loop fusion | flops 261632 | bytes 135168 | tf_op jit(solution)/shard_map/reduce_sum | solution.py:20
  2.9 1.3 %convolution_convert_fusion.12 = bf16[12,4,128]{2,0,1:T(8,128)(2,1)S(1)} fusion(bf16[4,128,128]{2,1,0:T(8,128)(2,1)} %param.19, f32[4,128]{1,0:T(4,128)S(1)} %add_rsqrt_fusion.4, f32[4,128]{1,0:T(4,128)S(1)} %broadcast_multiply_fusion.4, bf16[128,4]{0,1:T(4,128)(2,1)} %param.28, bf16[128,8]{0,1:T(8,128)(2,1)} %param.23), kind=kOutput, calls=%fused_computation.77 | convolution fusion | flops 1847296 | bytes 150528 | tf_op jit(solution)/shard_map/ijc,ch->hij/dot_general | solution.py:115
  4.2 0.7 broadcast_in_dim.8
  4.9 8.4 %all-to-all-start = ((bf16[16,12,4,128]{3,2,1,0:T(4,128)(2,1)}), bf16[16,12,4,128]{3,2,1,0:T(4,128)(2,1)S(1)}, u32[]{:S(2)}, u32[]{:S(2)}) async-start(bf16[16,12,4,128]{3,2,1,0:T(4,128)(2,1)} %broadcast_in_dim.8), calls=%async_computation | async-start | bytes 393216 | tf_op jit(solution)/shard_map/all_to_all | solution.py:58
  14.6 1.0 %convolution_convert_fusion.5 = bf16[4,128,128]{1,2,0:T(8,128)(2,1)} fusion(bf16[4,128,128]{2,1,0:T(8,128)(2,1)S(1)} %copy-done.1, f32[4,128]{1,0:T(4,128)S(1)} %add_rsqrt_fusion.4, f32[4,128]{1,0:T(4,128)S(1)} %broadcast_multiply_fusion.4, bf16[4,128,128]{2,1,0:T(8,128)(2,1)S(1)} %copy-done.6), kind=kOutput, calls=%fused_computation.64 | convolution fusion | flops 17104896 | bytes 299008 | tf_op jit(solution)/shard_map/bqc,cf->bqf/dot_general | solution.py:29
  16.0 0.8 copy.234
  17.0 0.6 convert_element_type.225
  17.6 1.2 %convert_reduce_fusion.4 = (f32[]{:T(128)}, f32[64]{0:T(128)}) fusion(s32[64]{0:T(128)S(1)} %copy-done.19), kind=kLoop, calls=%fused_computation.202 | loop fusion | flops 255 | bytes 516 | tf_op jit(solution)/shard_map/reduce_sum | solution.py:151
  19.2 2.9 %all-to-all-done = bf16[16,12,4,128]{3,2,1,0:T(4,128)(2,1)S(1)} async-done(((bf16[16,12,4,128]{3,2,1,0:T(4,128)(2,1)}), bf16[16,12,4,128]{3,2,1,0:T(4,128)(2,1)S(1)}, u32[]{:S(2)}, u32[]{:S(2)}) %all-to-all-start) | async-done | bytes 196640 | tf_op jit(solution)/shard_map/all_to_all | solution.py:58
  22.2 1.4 %collective-permute-done = bf16[16,12,4,128]{3,0,2,1:T(8,128)(2,1)S(1)} collective-permute-done((bf16[16,12,4,128]{3,0,2,1:T(8,128)(2,1)S(1)}, bf16[16,12,4,128]{3,0,2,1:T(8,128)(2,1)S(1)}, u32[]{:S(2)}, u32[]{:S(2)}) %collective-permute-start) | collective-permute-done | bytes 196640 | tf_op jit(solution)/shard_map/ppermute | solution.py:59
  24.7 1.1 %fusion.174 = f32[2,8,128]{2,1,0:T(8,128)} fusion(bf16[2,128,8,32]{1,3,2,0:T(8,128)(2,1)S(1)} %bitcast.269, bf16[2,128,8,32]{1,3,2,0:T(8,128)(2,1)S(1)} %bitcast.271, f32[128]{0:T(128)S(1)} %add_multiply_fusion.1, f32[8,128,128]{1,2,0:T(8,128)S(1)} %copy.242), kind=kOutput, calls=%fused_computation.214 | convolution fusion | flops 18088064 | bytes 795136 | tf_op jit(solution)/shard_map/sub | solution.py:48
  26.5 0.6 fusion.180
  28.9 1.3 %fusion.44 = bf16[2,128,256]{2,1,0:T(8,128)(2,1)S(1)} fusion(f32[2,128,256]{2,1,0:T(8,128)S(1)} %copy.244, bf16[2,128,256]{2,1,0:T(8,128)(2,1)S(1)} %copy-done.2, bf16[256,256]{1,0:T(8,128)(2,1)S(1)} %copy-done.12, bf16[4,256,256]{2,1,0:T(8,128)(2,1)} %param.22, f32[2,128]{1,0:T(2,128)S(1)} %copy-done.9, f32[2,128]{1,0:T(2,128)S(1)} %broadcast_multiply_fusion.5), kind=kOutput, calls=%fused_computation.57 | convolution fusion | flops 67895296 | bytes 919552 | tf_op jit(solution)/shard_map/bqf,fc->bqc/dot_general | solution.py:52
  30.2 0.8 %copy.245 = bf16[2,128,256]{2,0,1:T(2,128)(2,1)} copy(bf16[2,128,256]{2,1,0:T(8,128)(2,1)S(1)} %fusion.44) | data formatting | bytes 262144 | tf_op jit(solution)/shard_map/convert_element_type | solution.py:122
  31.0 3.1 %all-to-all-start.1 = ((bf16[2,128,256]{2,0,1:T(2,128)(2,1)}), bf16[2,128,256]{2,0,1:T(2,128)(2,1)S(1)}, u32[]{:S(2)}, u32[]{:S(2)}) async-start(bf16[2,128,256]{2,0,1:T(2,128)(2,1)} %copy.245), calls=%async_computation.1 | async-start | bytes 262144 | tf_op jit(solution)/shard_map/all_to_all | solution.py:123
  34.9 1.3 %convert_reduce_fusion.3 = (f32[4,128]{1,0:T(4,128)S(1)}, bf16[4,128,128]{2,1,0:T(8,128)(2,1)S(1)}) fusion(bf16[128,128]{1,0:T(8,128)(2,1)S(1)} %copy-done.14, f32[4,128,128]{2,1,0:T(8,128)S(1)} %copy.266, bf16[4,128,128]{2,1,0:T(8,128)(2,1)S(1)} %copy-done.1, f32[4,128]{1,0:T(4,128)S(1)} %add_rsqrt_fusion.4, f32[4,128]{1,0:T(4,128)S(1)} %broadcast_multiply_fusion.4, ...), kind=kOutput, calls=%fused_computation.98 | convolution fusion | flops 34471424 | bytes 727040 | tf_op jit(solution)/shard_map/bqf,fc->bqc/dot_general | solution.py:52
  36.8 0.8 %copy.269 = bf16[32,32,128]{2,1,0:T(8,128)(2,1)} copy(bf16[32,32,128]{2,0,1:T(8,128)(2,1)S(1)} %pad_maximum_fusion) | data formatting | bytes 524288 | tf_op jit(solution)/shard_map/concatenate | solution.py:80
  37.6 4.7 %all-to-all-done.1 = bf16[2,128,256]{2,0,1:T(2,128)(2,1)S(1)} async-done(((bf16[2,128,256]{2,0,1:T(2,128)(2,1)}), bf16[2,128,256]{2,0,1:T(2,128)(2,1)S(1)}, u32[]{:S(2)}, u32[]{:S(2)}) %all-to-all-start.1) | async-done | bytes 131104 | tf_op jit(solution)/shard_map/all_to_all | solution.py:123
  42.3 2.8 %all-to-all-start.2 = ((bf16[32,32,128]{2,1,0:T(8,128)(2,1)}), bf16[32,32,128]{2,1,0:T(8,128)(2,1)S(1)}, u32[]{:S(2)}, u32[]{:S(2)}) async-start(bf16[32,32,128]{2,1,0:T(8,128)(2,1)} %copy.269), calls=%async_computation.2 | async-start | bytes 524288 | tf_op jit(solution)/shard_map/all_to_all | solution.py:79
  47.5 0.6 fusion.175
  50.2 0.8 copy.290
  51.3 1.1 %reshape.279 = bf16[16,2,4096]{2,1,0:T(2,128)(2,1)} reshape(bf16[16,4,32,64]{3,2,1,0:T(8,128)(2,1)S(1)} %broadcast_in_dim.11) | data formatting | bytes 524288
  52.4 3.1 %all-to-all-done.2 = bf16[32,32,128]{2,1,0:T(8,128)(2,1)S(1)} async-done(((bf16[32,32,128]{2,1,0:T(8,128)(2,1)}), bf16[32,32,128]{2,1,0:T(8,128)(2,1)S(1)}, u32[]{:S(2)}, u32[]{:S(2)}) %all-to-all-start.2) | async-done | bytes 262176 | tf_op jit(solution)/shard_map/all_to_all | solution.py:79
  55.5 3.7 %all-to-all-start.3 = ((bf16[16,2,4096]{2,1,0:T(2,128)(2,1)}), bf16[16,2,4096]{2,1,0:T(2,128)(2,1)S(1)}, u32[]{:S(2)}, u32[]{:S(2)}) async-start(bf16[16,2,4096]{2,1,0:T(2,128)(2,1)} %reshape.279), calls=%async_computation.3 | async-start | bytes 524288 | tf_op jit(solution)/shard_map/all_to_all | solution.py:58
  61.8 7.6 %all-to-all-done.3 = bf16[16,2,4096]{2,1,0:T(2,128)(2,1)S(1)} async-done(((bf16[16,2,4096]{2,1,0:T(2,128)(2,1)}), bf16[16,2,4096]{2,1,0:T(2,128)(2,1)S(1)}, u32[]{:S(2)}, u32[]{:S(2)}) %all-to-all-start.3) | async-done | bytes 262176 | tf_op jit(solution)/shard_map/all_to_all | solution.py:58
  69.9 1.2 %fusion.185 = f32[4,4,128]{2,1,0:T(4,128)} fusion(bf16[4,128,4,32]{1,3,2,0:T(8,128)(2,1)S(1)} %bitcast.262, bf16[4,128,4,32]{1,3,2,0:T(8,128)(2,1)S(1)} %bitcast.264, f32[4,128,128]{1,2,0:T(8,128)S(1)} %bitcast.250, f32[128]{0:T(128)S(1)} %add_multiply_fusion.1), kind=kOutput, calls=%fused_computation.217 | convolution fusion | flops 18088064 | bytes 532992 | tf_op jit(solution)/shard_map/sub | solution.py:48
  71.0 1.0 %fusion.55 = f32[4,4,32,128]{3,2,1,0:T(8,128)S(1)} fusion(bf16[4,128,4,32]{1,3,2,0:T(8,128)(2,1)S(1)} %bitcast.280, f32[4,4,128]{2,1,0:T(4,128)} %fusion.185, f32[4,4,128,128]{2,3,1,0:T(8,128)S(1)} %fusion.17), kind=kOutput, calls=%fused_computation.89 | convolution fusion | flops 17565824 | bytes 1449984 | tf_op jit(solution)/shard_map/bhqk,bkhd->bqhd/dot_general | solution.py:49
  72.7 1.1 %copy.288 = bf16[128,32,64]{0,2,1:T(8,128)(2,1)S(1)} copy(bf16[128,32,64]{2,1,0:T(8,128)(2,1)S(1)} %bitcast.239) | data formatting | bytes 1048576 | tf_op jit(solution)/shard_map/jit(_where)/select_n | solution.py:61
  73.8 1.3 %divide_convert_fusion = bf16[4,32,128,32]{2,1,3,0:T(8,128)(2,1)S(1)} fusion(f32[]{:T(128)} %get-tuple-element.18, bf16[128,32,64]{0,2,1:T(8,128)(2,1)S(1)} %copy.288, bf16[64,4,256]{2,0,1:T(8,128)(2,1)S(1)} %get-tuple-element.21, f32[64,4]{0,1:T(4,128)S(1)} %add_rsqrt_fusion.2, f32[64,4]{0,1:T(4,128)S(1)} %broadcast_multiply_fusion.2, ...), kind=kOutput, calls=%fused_computation.4 | convolution fusion | flops 72630272 | bytes 1722628 | tf_op jit(solution)/shard_map/ics,sje->ijce/dot_general | solution.py:153
  75.9 1.1 %fusion.43 = bf16[128,4,128]{2,0,1:T(8,128)(2,1)S(1)} fusion(f32[128,4,128]{2,0,1:T(8,128)S(1)} %fusion.72, f32[4,128,128]{2,1,0:T(8,128)S(1)} %copy.285, f32[128,4,128]{2,1,0:T(4,128)S(1)} %bitcast.246, bf16[4,128,128]{2,0,1:T(4,128)(2,1)S(1)} %fusion.75, bf16[128,128]{1,0:T(8,128)(2,1)S(1)} %copy-done.15, bf16[4,128,128]{2,1,0:T(8,128)(2,1)} %param.30), kind=kOutput, calls=%fused_computation.56 | convolution fusion | flops 34078720 | bytes 1114112 | tf_op jit(solution)/shard_map/bqf,fc->bqc/dot_general | solution.py:52
  77.0 0.8 copy.291
  (138 shorter events, 16.1 us)
Async XLA Ops:
  0.6 74.5 %copy-start = (bf16[1024,128]{1,0:T(8,128)(2,1)S(1)}, bf16[1024,128]{1,0:T(8,128)(2,1)}, u32[]{:S(2)}) copy-start(bf16[1024,128]{1,0:T(8,128)(2,1)} %param.35) | copy-start | bytes 786436
  0.6 12.7 %copy-start.2 = (bf16[2,128,256]{2,1,0:T(8,128)(2,1)S(1)}, bf16[2,128,256]{2,1,0:T(8,128)(2,1)}, u32[]{:S(2)}) copy-start(bf16[2,128,256]{2,1,0:T(8,128)(2,1)} %param.18) | copy-start | bytes 393220
  0.7 13.1 %copy-start.11 = (bf16[4,256,256]{2,1,0:T(8,128)(2,1)S(1)}, bf16[4,256,256]{2,1,0:T(8,128)(2,1)}, u32[]{:S(2)}) copy-start(bf16[4,256,256]{2,1,0:T(8,128)(2,1)} %param.22) | copy-start | bytes 1572868
  4.9 9.6 %copy-start.1 = (bf16[4,128,128]{2,1,0:T(8,128)(2,1)S(1)}, bf16[4,128,128]{2,1,0:T(8,128)(2,1)}, u32[]{:S(2)}) copy-start(bf16[4,128,128]{2,1,0:T(8,128)(2,1)} %param.19) | copy-start | bytes 393220
  4.9 9.6 %copy-start.6 = (bf16[4,128,128]{2,1,0:T(8,128)(2,1)S(1)}, bf16[4,128,128]{2,1,0:T(8,128)(2,1)}, u32[]{:S(2)}) copy-start(bf16[4,128,128]{2,1,0:T(8,128)(2,1)} %param.27) | copy-start | bytes 393220
  4.9 17.1 %all-to-all-start = ((bf16[16,12,4,128]{3,2,1,0:T(4,128)(2,1)}), bf16[16,12,4,128]{3,2,1,0:T(4,128)(2,1)S(1)}, u32[]{:S(2)}, u32[]{:S(2)}) async-start(bf16[16,12,4,128]{3,2,1,0:T(4,128)(2,1)} %broadcast_in_dim.8), calls=%async_computation | async-start | bytes 393216 | tf_op jit(solution)/shard_map/all_to_all | solution.py:58
  13.7 2.2 %copy-start.8 = (f32[2,128]{1,0:T(2,128)}, f32[2,128]{1,0:T(2,128)S(1)}, u32[]{:S(2)}) copy-start(f32[2,128]{1,0:T(2,128)S(1)} %add_rsqrt_fusion.5) | copy-start | bytes 3076
  14.0 3.0 %copy-start.19 = (s32[64]{0:T(128)S(1)}, s32[64]{0:T(128)}, u32[]{:S(2)}) copy-start(s32[64]{0:T(128)} %param.20) | copy-start | bytes 772
  14.5 7.6 %copy-start.20 = (s32[128]{0:T(128)S(1)}, s32[128]{0:T(128)}, u32[]{:S(2)}) copy-start(s32[128]{0:T(128)} %param.21) | copy-start | bytes 1540
  22.1 1.5 %collective-permute-start = (bf16[16,12,4,128]{3,0,2,1:T(8,128)(2,1)S(1)}, bf16[16,12,4,128]{3,0,2,1:T(8,128)(2,1)S(1)}, u32[]{:S(2)}, u32[]{:S(2)}) collective-permute-start(bf16[16,12,4,128]{3,0,2,1:T(8,128)(2,1)S(1)} %copy.329), channel_id=1, source_target_pairs={{0,1},{1,0},{2,3},{3,2},{4,5},{5,4},{6,7},{7,6},{8,9},{9,8},{10,11... | collective-permute-start | bytes 589832 | tf_op jit(solution)/shard_map/ppermute | solution.py:59
  27.1 0.9 %copy-start.5 = (bf16[2,128,256]{1,2,0:T(8,128)(2,1)S(1)}, bf16[2,128,256]{1,2,0:T(8,128)(2,1)}, u32[]{:S(2)}) copy-start(bf16[2,128,256]{1,2,0:T(8,128)(2,1)} %copy.234) | copy-start | bytes 393220
  27.1 0.9 %copy-start.22 = (f32[2,8,128]{2,1,0:T(8,128)S(1)}, f32[2,8,128]{2,1,0:T(8,128)}, u32[]{:S(2)}) copy-start(f32[2,8,128]{2,1,0:T(8,128)} %fusion.174) | copy-start | bytes 24580
  28.0 0.7 copy-start.9
  28.0 0.9 %copy-start.12 = (bf16[256,256]{1,0:T(8,128)(2,1)S(1)}, bf16[256,256]{1,0:T(8,128)(2,1)}, u32[]{:S(2)}) copy-start(bf16[256,256]{1,0:T(8,128)(2,1)} %param.24) | copy-start | bytes 393220
  28.9 5.2 %copy-start.4 = (bf16[4,128,128]{1,2,0:T(8,128)(2,1)S(1)}, bf16[4,128,128]{1,2,0:T(8,128)(2,1)}, u32[]{:S(2)}) copy-start(bf16[4,128,128]{1,2,0:T(8,128)(2,1)} %convolution_convert_fusion.5) | copy-start | bytes 393220
  31.0 11.3 %all-to-all-start.1 = ((bf16[2,128,256]{2,0,1:T(2,128)(2,1)}), bf16[2,128,256]{2,0,1:T(2,128)(2,1)S(1)}, u32[]{:S(2)}, u32[]{:S(2)}) async-start(bf16[2,128,256]{2,0,1:T(2,128)(2,1)} %copy.245), calls=%async_computation.1 | async-start | bytes 262144 | tf_op jit(solution)/shard_map/all_to_all | solution.py:123
  34.1 0.8 copy-start.14
  34.5 2.0 %copy-start.18 = (bf16[128,4]{0,1:T(4,128)(2,1)S(1)}, bf16[128,4]{0,1:T(4,128)(2,1)}, u32[]{:S(2)}) copy-start(bf16[128,4]{0,1:T(4,128)(2,1)} %param.31) | copy-start | bytes 3076
  42.3 13.2 %all-to-all-start.2 = ((bf16[32,32,128]{2,1,0:T(8,128)(2,1)}), bf16[32,32,128]{2,1,0:T(8,128)(2,1)S(1)}, u32[]{:S(2)}, u32[]{:S(2)}) async-start(bf16[32,32,128]{2,1,0:T(8,128)(2,1)} %copy.269), calls=%async_computation.2 | async-start | bytes 524288 | tf_op jit(solution)/shard_map/all_to_all | solution.py:79
  45.3 1.1 %copy-start.3 = (bf16[4,256,256]{2,1,0:T(8,128)(2,1)S(1)}, bf16[4,256,256]{2,1,0:T(8,128)(2,1)}, u32[]{:S(2)}) copy-start(bf16[4,256,256]{2,1,0:T(8,128)(2,1)} %param.25) | copy-start | bytes 1572868
  46.6 0.9 %copy-start.10 = (f32[64]{0:T(128)S(1)}, f32[64]{0:T(128)}, u32[]{:S(2)}) copy-start(f32[64]{0:T(128)} %get-tuple-element.19) | copy-start | bytes 772
  48.6 0.9 %copy-start.13 = (bf16[256,256]{1,0:T(8,128)(2,1)S(1)}, bf16[256,256]{1,0:T(8,128)(2,1)}, u32[]{:S(2)}) copy-start(bf16[256,256]{1,0:T(8,128)(2,1)} %param.26) | copy-start | bytes 393220
  49.5 1.4 %copy-start.16 = (bf16[256,32]{0,1:T(8,128)(2,1)S(1)}, bf16[256,32]{0,1:T(8,128)(2,1)}, u32[]{:S(2)}) copy-start(bf16[256,32]{0,1:T(8,128)(2,1)} %param.33) | copy-start | bytes 49156
  49.5 1.4 %copy-start.21 = (f32[64]{0:T(128)S(1)}, f32[64]{0:T(128)}, u32[]{:S(2)}) copy-start(f32[64]{0:T(128)} %convert_element_type.225) | copy-start | bytes 772
  52.4 8.1 %copy-start.7 = (bf16[4,128,128]{2,1,0:T(8,128)(2,1)S(1)}, bf16[4,128,128]{2,1,0:T(8,128)(2,1)}, u32[]{:S(2)}) copy-start(bf16[4,128,128]{2,1,0:T(8,128)(2,1)} %param.30) | copy-start | bytes 393220
  55.5 13.9 %all-to-all-start.3 = ((bf16[16,2,4096]{2,1,0:T(2,128)(2,1)}), bf16[16,2,4096]{2,1,0:T(2,128)(2,1)S(1)}, u32[]{:S(2)}, u32[]{:S(2)}) async-start(bf16[16,2,4096]{2,1,0:T(2,128)(2,1)} %reshape.279), calls=%async_computation.3 | async-start | bytes 524288 | tf_op jit(solution)/shard_map/all_to_all | solution.py:58
  69.8 2.4 %collective-permute-start.1 = (bf16[16,4,32,64]{3,2,1,0:T(8,128)(2,1)S(1)}, bf16[16,4,32,64]{3,2,1,0:T(8,128)(2,1)S(1)}, u32[]{:S(2)}, u32[]{:S(2)}) collective-permute-start(bf16[16,4,32,64]{3,2,1,0:T(8,128)(2,1)S(1)} %reshape.280), channel_id=1, source_target_pairs={{0,1},{1,0},{2,3},{3,2},{4,5},{5,4},{6,7},{7,6},{8,9},{9,8},{10,11... | collective-permute-start | bytes 786440 | tf_op jit(solution)/shard_map/ppermute | solution.py:59
  72.7 1.1 %copy-start.17 = (bf16[256,32]{0,1:T(8,128)(2,1)S(1)}, bf16[256,32]{0,1:T(8,128)(2,1)}, u32[]{:S(2)}) copy-start(bf16[256,32]{0,1:T(8,128)(2,1)} %param.34) | copy-start | bytes 49156
  75.1 0.8 copy-start.15

commit v8 on v6

--- a/solution.py
+++ b/solution.py
@@ -29,7 +29,7 @@
     return jnp.einsum("bqc,cf->bqf", inputs, weight_table, preferred_element_type=jnp.float32)
 
 
-def attend(inputs, weights, bias_table, key_bias, output_map, head_count):
+def attend(inputs, weights, bias_table, key_bias, output_map, head_count, order="bqc"):
     batch_size, query_count, width = inputs.shape
     query_all = project(inputs, weights[0]).astype(jnp.bfloat16)
     key_all = project(inputs, weights[1]).astype(jnp.bfloat16)
@@ -49,7 +49,7 @@
     mixed = jnp.einsum("bhqk,bkhd->bqhd", softened, value_heads, preferred_element_type=jnp.float32)
     mixed = mixed.reshape(batch_size, query_count, head_count * head_size)
     gated = (mixed * gating).astype(jnp.bfloat16)
-    return jnp.einsum("bqf,fc->bqc", gated, output_map, preferred_element_type=jnp.float32)
+    return jnp.einsum("bqf,fc->" + order, gated, output_map, preferred_element_type=jnp.float32)
 
 
 def gather_blocks(block, axis, count):
@@ -118,9 +118,14 @@
     both_bias = gather_blocks(both_local, 1, count)
     row_bias = both_bias[:H_M]
     start_bias = both_bias[H_M:]
-    row_update = attend(layer_norm(alignment), row_project, row_bias, residue_keys, row_output, H_M)
-    alignment_one = (alignment.astype(jnp.float32) + row_update).astype(jnp.bfloat16)
-    alignment_cols = lax.all_to_all(alignment_one, DAP, 1, 0, tiled=True)
+    row_update = attend(
+        layer_norm(alignment), row_project, row_bias, residue_keys, row_output, H_M, "qbc"
+    )
+    alignment_one = (
+        jnp.swapaxes(alignment, 0, 1).astype(jnp.float32) + row_update
+    ).astype(jnp.bfloat16)
+    alignment_one, start_bias = lax.optimization_barrier((alignment_one, start_bias))
+    alignment_cols = lax.all_to_all(alignment_one, DAP, 0, 1, tiled=True)
     start_update = attend(pair_norm, start_project, start_bias, residue_keys, start_output, H_Z)
     pair_one = (pairwise.astype(jnp.float32) + start_update).astype(jnp.bfloat16)
     rows_norm_one = layer_norm(pair_one)
@@ -129,23 +134,23 @@
     ).astype(jnp.bfloat16)
     pair_cols, end_all = exchange_pair(pair_one, end_local, count)
     end_bias = jnp.swapaxes(end_all, 1, 2)
-    column_norm = jnp.swapaxes(layer_norm(alignment_cols), 0, 1)
-    column_update = attend(column_norm, column_project, None, sequence_keys, column_output, H_M)
-    alignment_out = (alignment_cols.astype(jnp.float32) + jnp.swapaxes(column_update, 0, 1)).astype(
-        jnp.bfloat16
-    )
+    column_update = attend(
+        layer_norm(alignment_cols), column_project, None, sequence_keys, column_output, H_M
+    )
+    alignment_turned = (alignment_cols.astype(jnp.float32) + column_update).astype(jnp.bfloat16)
+    alignment_out = jnp.swapaxes(alignment_turned, 0, 1)
     end_norm = jnp.swapaxes(layer_norm(pair_cols), 0, 1)
     end_update = jnp.swapaxes(
         attend(end_norm, end_project, end_bias, residue_keys, end_output, H_Z), 0, 1
     )
-    last_norm = layer_norm(alignment_out)
+    last_norm = layer_norm(alignment_turned)
     weighting = sequence_mask.astype(jnp.float32)[:, None, None]
     left = (
-        jnp.einsum("sic,co->sio", last_norm, outer_left, preferred_element_type=jnp.float32)
+        jnp.einsum("isc,co->sio", last_norm, outer_left, preferred_element_type=jnp.float32)
         * weighting
     ).astype(jnp.bfloat16)
     right = (
-        jnp.einsum("sic,co->sio", last_norm, outer_right, preferred_element_type=jnp.float32)
+        jnp.einsum("isc,co->sio", last_norm, outer_right, preferred_element_type=jnp.float32)
         * weighting
     ).astype(jnp.bfloat16)
     row_count = jnp.sum(sequence_mask.astype(jnp.float32))

time: 77.2 us -> 79.1 us (1.025)
  starting transfers between devices: 18.2 us -> 19.7 us
  matrix products: 16.7 us -> 18.1 us
  waiting for transfers between devices: 20.4 us -> 19 us
    all_to_all x2, starting transfers between devices: 12.2 us -> 14 us  [gather_blocks(): same_core = lax.all_to_all(spread, 'chip', 0, 0, tiled=True)]
    all_to_all x1, waiting for transfers between devices: 3.07 us -> 1.63 us  [exchange_pair(): lax.all_to_all(jnp.concatenate([pair_part, end_part], axis=1), DAP, 0, 0,...]
    dot_general x5, matrix products: 3.67 us -> 4.57 us  [the longest x4 4.31 us: attend(): jnp.einsum('bqf,fc->' + order, gated, output_map, preferred_element_type=...]
    optimization_barrier x0 -> x1, local copies, waits for them, and re-layouts: none -> 0.79 us  [per_device(): lax.optimization_barrier((alignment_one, start_bias))]
    unnamed x54 -> x52, local copies, waits for them, and re-layouts: 5.16 us -> 4.74 us
  transfers between devices with their start and end apart: 6 -> 6, of which waited for: 6 -> 6; matrix products, arithmetic and copies ran while one was open for 25% -> 26% of each run, Pallas kernels for 0% -> 0%
where the time goes in v8:
time: 79.1 us; the launch traced here: 78.4 us
  starting transfers between devices  19.7 us (25%)
  waiting for transfers between devices  19 us (24%)
  matrix products  18.1 us (23%)
  local copies, waits for them, and re-layouts  13 us (16%)
  other arithmetic  7.19 us (9%)
  between operations  1.43 us (2%)
    all_to_all x2, starting transfers between devices, gather_blocks(): same_core = lax.all_to_all(spread, 'chip', 0, 0, tiled=True)  14 us
    all_to_all x2, waiting for transfers between devices, gather_blocks(): same_core = lax.all_to_all(spread, 'chip', 0, 0, tiled=True)  9.93 us
    unnamed x52, local copies, waits for them, and re-layouts  4.74 us
    all_to_all x1, waiting for transfers between devices, per_device(): alignment_cols = lax.all_to_all(alignment_one, DAP, 0, 1, tiled=True)  4.67 us
    dot_general x4, matrix products, attend(): jnp.einsum('bqf,fc->' + order, gated, output_map, preferred_element_type=...  4.31 us
    dot_general x12, matrix products, project(): jnp.einsum('bqc,cf->bqf', inputs, weight_table, preferred_element_type=jn...  3.76 us
    all_to_all x1, starting transfers between devices, per_device(): alignment_cols = lax.all_to_all(alignment_one, DAP, 0, 1, tiled=True)  3.02 us
    sub x4, matrix products, attend(): softened = jax.nn.softmax(scores, axis=-1).astype(jnp.bfloat16)  2.83 us
  transfers between devices with their start and end apart: 6, of which 6 were waited for; matrix products, arithmetic and copies ran while one was open for 26% of the time, Pallas kernels for 0%

profile of v8, /device:TPU:0, one launch (start us, length us, event | category | flops | bytes accessed | tf_op | source)
XLA Modules:
  0.0 78.4 jit_solution(7116005935201491211)
XLA Ops:
  0.7 1.1 %convert_reduce_fusion = f32[4,128]{1,0:T(4,128)S(1)} fusion(bf16[4,128,128]{2,1,0:T(8,128)(2,1)} %param.19), kind=kLoop, calls=%fused_computation.92 | loop fusion | flops 130560 | bytes 133120 | tf_op jit(solution)/shard_map/reduce_sum | solution.py:19
  1.8 1.1 %fusion.64 = f32[4,128]{1,0:T(4,128)S(1)} fusion(bf16[4,128,128]{2,1,0:T(8,128)(2,1)} %param.19, f32[4,128]{1,0:T(4,128)S(1)} %broadcast_multiply_fusion.4), kind=kLoop, calls=%fused_computation.107 | loop fusion | flops 261632 | bytes 135168 | tf_op jit(solution)/shard_map/reduce_sum | solution.py:20
  2.9 1.3 %convolution_convert_fusion.12 = bf16[12,4,128]{2,0,1:T(8,128)(2,1)S(1)} fusion(bf16[4,128,128]{2,1,0:T(8,128)(2,1)} %param.19, f32[4,128]{1,0:T(4,128)S(1)} %add_rsqrt_fusion.4, f32[4,128]{1,0:T(4,128)S(1)} %broadcast_multiply_fusion.4, bf16[128,4]{0,1:T(4,128)(2,1)} %param.28, bf16[128,8]{0,1:T(8,128)(2,1)} %param.23), kind=kOutput, calls=%fused_computation.77 | convolution fusion | flops 1847296 | bytes 150528 | tf_op jit(solution)/shard_map/ijc,ch->hij/dot_general | solution.py:115
  4.2 0.7 broadcast_in_dim.8
  4.9 8.4 %all-to-all-start = ((bf16[16,12,4,128]{3,2,1,0:T(4,128)(2,1)}), bf16[16,12,4,128]{3,2,1,0:T(4,128)(2,1)S(1)}, u32[]{:S(2)}, u32[]{:S(2)}) async-start(bf16[16,12,4,128]{3,2,1,0:T(4,128)(2,1)} %broadcast_in_dim.8), calls=%async_computation | async-start | bytes 393216 | tf_op jit(solution)/shard_map/all_to_all | solution.py:58
  14.6 1.0 %convolution_convert_fusion.5 = bf16[4,128,128]{1,2,0:T(8,128)(2,1)} fusion(bf16[4,128,128]{2,1,0:T(8,128)(2,1)S(1)} %copy-done.1, f32[4,128]{1,0:T(4,128)S(1)} %add_rsqrt_fusion.4, f32[4,128]{1,0:T(4,128)S(1)} %broadcast_multiply_fusion.4, bf16[4,128,128]{2,1,0:T(8,128)(2,1)S(1)} %copy-done.6), kind=kOutput, calls=%fused_computation.63 | convolution fusion | flops 17104896 | bytes 299008 | tf_op jit(solution)/shard_map/bqc,cf->bqf/dot_general | solution.py:29
  16.0 0.8 copy.169
  17.5 1.3 %convert_reduce_fusion.4 = (f32[]{:T(128)}, f32[64]{0:T(128)}) fusion(s32[64]{0:T(128)S(1)} %copy-done.19), kind=kLoop, calls=%fused_computation.200 | loop fusion | flops 255 | bytes 516 | tf_op jit(solution)/shard_map/reduce_sum | solution.py:156
  19.1 2.9 %all-to-all-done = bf16[16,12,4,128]{3,2,1,0:T(4,128)(2,1)S(1)} async-done(((bf16[16,12,4,128]{3,2,1,0:T(4,128)(2,1)}), bf16[16,12,4,128]{3,2,1,0:T(4,128)(2,1)S(1)}, u32[]{:S(2)}, u32[]{:S(2)}) %all-to-all-start) | async-done | bytes 196640 | tf_op jit(solution)/shard_map/all_to_all | solution.py:58
  22.2 1.4 %collective-permute-done = bf16[16,12,4,128]{3,0,2,1:T(8,128)(2,1)S(1)} collective-permute-done((bf16[16,12,4,128]{3,0,2,1:T(8,128)(2,1)S(1)}, bf16[16,12,4,128]{3,0,2,1:T(8,128)(2,1)S(1)}, u32[]{:S(2)}, u32[]{:S(2)}) %collective-permute-start) | collective-permute-done | bytes 196640 | tf_op jit(solution)/shard_map/ppermute | solution.py:59
  24.7 1.1 %fusion.168 = f32[2,8,128]{2,1,0:T(8,128)} fusion(bf16[2,128,8,32]{1,3,2,0:T(8,128)(2,1)S(1)} %bitcast.271, bf16[2,128,8,32]{1,3,2,0:T(8,128)(2,1)S(1)} %bitcast.273, f32[128]{0:T(128)S(1)} %add_multiply_fusion.1, f32[8,128,128]{1,2,0:T(8,128)S(1)} %copy.177), kind=kOutput, calls=%fused_computation.212 | convolution fusion | flops 18088064 | bytes 795136 | tf_op jit(solution)/shard_map/sub | solution.py:48
  26.7 1.1 %fusion.53 = f32[2,8,32,128]{3,2,1,0:T(8,128)S(1)} fusion(bf16[2,128,8,32]{1,3,2,0:T(8,128)(2,1)S(1)} %bitcast.281, f32[2,8,128]{2,1,0:T(8,128)} %fusion.168, f32[2,8,128,128]{2,3,1,0:T(8,128)S(1)} %fusion.13), kind=kOutput, calls=%fused_computation.87 | convolution fusion | flops 17565824 | bytes 1449984 | tf_op jit(solution)/shard_map/bhqk,bkhd->bqhd/dot_general | solution.py:49
  28.0 1.3 %fusion.45 = bf16[128,2,256]{2,0,1:T(8,128)(2,1)S(1)} fusion(f32[2,128,256]{2,1,0:T(8,128)S(1)} %copy.179, bf16[2,128,256]{2,1,0:T(8,128)(2,1)S(1)} %copy-done.2, bf16[256,256]{1,0:T(8,128)(2,1)S(1)} %copy-done.12, bf16[4,256,256]{2,1,0:T(8,128)(2,1)} %param.22, f32[2,128]{1,0:T(2,128)S(1)} %copy-done.9, f32[2,128]{1,0:T(2,128)S(1)} %broadcast_multiply_fusion.5), kind=kOutput, calls=%fused_computation.70 | convolution fusion | flops 67895296 | bytes 919552 | tf_op jit(solution)/shard_map/bqf,fc->qbc/dot_general | solution.py:52
  29.5 0.6 fusion.172
  30.4 0.8 %copy.181 = bf16[128,2,256]{2,1,0:T(2,128)(2,1)} copy(bf16[128,2,256]{2,0,1:T(8,128)(2,1)S(1)} %fusion.45) | data formatting | bytes 262144 | tf_op jit(solution)/shard_map/optimization_barrier | solution.py:127
  31.2 3.0 %all-to-all-start.1 = ((bf16[128,2,256]{2,1,0:T(2,128)(2,1)}), bf16[128,2,256]{2,1,0:T(2,128)(2,1)S(1)}, u32[]{:S(2)}, u32[]{:S(2)}) async-start(bf16[128,2,256]{2,1,0:T(2,128)(2,1)} %copy.181), calls=%async_computation.1 | async-start | bytes 262144 | tf_op jit(solution)/shard_map/all_to_all | solution.py:128
  35.0 1.3 %convert_reduce_fusion.3 = (f32[4,128]{1,0:T(4,128)S(1)}, bf16[4,128,128]{2,1,0:T(8,128)(2,1)S(1)}) fusion(bf16[128,128]{1,0:T(8,128)(2,1)S(1)} %copy-done.14, f32[4,128,128]{2,1,0:T(8,128)S(1)} %copy.193, bf16[4,128,128]{2,1,0:T(8,128)(2,1)S(1)} %copy-done.1, f32[4,128]{1,0:T(4,128)S(1)} %add_rsqrt_fusion.4, f32[4,128]{1,0:T(4,128)S(1)} %broadcast_multiply_fusion.4, ...), kind=kOutput, calls=%fused_computation.98 | convolution fusion | flops 34471424 | bytes 727040 | tf_op jit(solution)/shard_map/bqf,fc->bqc/dot_general | solution.py:52
  37.0 0.8 %copy.196 = bf16[32,32,128]{2,1,0:T(8,128)(2,1)} copy(bf16[32,32,128]{2,0,1:T(8,128)(2,1)S(1)} %pad_maximum_fusion) | data formatting | bytes 524288 | tf_op jit(solution)/shard_map/concatenate | solution.py:80
  37.8 4.7 %all-to-all-done.1 = bf16[128,2,256]{2,1,0:T(2,128)(2,1)S(1)} async-done(((bf16[128,2,256]{2,1,0:T(2,128)(2,1)}), bf16[128,2,256]{2,1,0:T(2,128)(2,1)S(1)}, u32[]{:S(2)}, u32[]{:S(2)}) %all-to-all-start.1) | async-done | bytes 131104 | tf_op jit(solution)/shard_map/all_to_all | solution.py:128
  42.4 2.6 %all-to-all-start.2 = ((bf16[32,32,128]{2,1,0:T(8,128)(2,1)}), bf16[32,32,128]{2,1,0:T(8,128)(2,1)S(1)}, u32[]{:S(2)}, u32[]{:S(2)}) async-start(bf16[32,32,128]{2,1,0:T(8,128)(2,1)} %copy.196), calls=%async_computation.2 | async-start | bytes 524288 | tf_op jit(solution)/shard_map/all_to_all | solution.py:79
  47.2 0.6 fusion.169
  48.2 0.9 %reshape.254 = f32[4,64,256]{2,1,0:T(8,128)} reshape(f32[4,32,2,256]{3,2,1,0:T(2,128)S(1)} %copy_bitcast_fusion) | data formatting | bytes 524288 | tf_op jit(solution)/shard_map/convert_element_type | solution.py:140
  50.1 1.4 %convert_reduce_fusion.2 = (f32[4,64]{1,0:T(4,128)S(1)}, bf16[4,64,256]{2,1,0:T(8,128)(2,1)S(1)}) fusion(f32[4,64,256]{2,1,0:T(8,128)} %reshape.254, bf16[256,256]{1,0:T(8,128)(2,1)S(1)} %copy-done.13, f32[4,64,256]{2,1,0:T(8,128)S(1)} %copy.187, bf16[4,64,256]{2,1,0:T(8,128)(2,1)S(1)} %convert_element_type.232, bf16[4,256,256]{2,1,0:T(8,128)(2,1)S(1)} %copy-done.3), kind=kOutput, calls=%fused_computation.96 | convolution fusion | flops 67698432 | bytes 1049600 | tf_op jit(solution)/shard_map/bqf,fc->bqc/dot_general | solution.py:52
  51.8 0.8 copy.216
  52.9 1.1 %reshape.287 = bf16[16,2,4096]{2,1,0:T(2,128)(2,1)} reshape(bf16[16,4,32,64]{3,2,1,0:T(8,128)(2,1)S(1)} %broadcast_bitcast_fusion) | data formatting | bytes 524288
  54.0 1.6 %all-to-all-done.2 = bf16[32,32,128]{2,1,0:T(8,128)(2,1)S(1)} async-done(((bf16[32,32,128]{2,1,0:T(8,128)(2,1)}), bf16[32,32,128]{2,1,0:T(8,128)(2,1)S(1)}, u32[]{:S(2)}, u32[]{:S(2)}) %all-to-all-start.2) | async-done | bytes 262176 | tf_op jit(solution)/shard_map/all_to_all | solution.py:79
  55.6 5.5 %all-to-all-start.3 = ((bf16[16,2,4096]{2,1,0:T(2,128)(2,1)}), bf16[16,2,4096]{2,1,0:T(2,128)(2,1)S(1)}, u32[]{:S(2)}, u32[]{:S(2)}) async-start(bf16[16,2,4096]{2,1,0:T(2,128)(2,1)} %reshape.287), calls=%async_computation.3 | async-start | bytes 524288 | tf_op jit(solution)/shard_map/all_to_all | solution.py:58
  64.3 7.0 %all-to-all-done.3 = bf16[16,2,4096]{2,1,0:T(2,128)(2,1)S(1)} async-done(((bf16[16,2,4096]{2,1,0:T(2,128)(2,1)}), bf16[16,2,4096]{2,1,0:T(2,128)(2,1)S(1)}, u32[]{:S(2)}, u32[]{:S(2)}) %all-to-all-start.3) | async-done | bytes 262176 | tf_op jit(solution)/shard_map/all_to_all | solution.py:58
  72.3 1.4 %collective-permute-done.1 = bf16[16,64,4,32]{1,3,2,0:T(8,128)(2,1)S(1)} collective-permute-done((bf16[16,64,4,32]{1,3,2,0:T(8,128)(2,1)S(1)}, bf16[16,64,4,32]{1,3,2,0:T(8,128)(2,1)S(1)}, u32[]{:S(2)}, u32[]{:S(2)}) %collective-permute-start.1) | collective-permute-done | bytes 262176 | tf_op jit(solution)/shard_map/ppermute | solution.py:59
  74.0 1.1 %copy.214 = bf16[64,128,32]{1,0,2:T(8,128)(2,1)S(1)} copy(bf16[64,128,32]{0,2,1:T(8,128)(2,1)S(1)} %bitcast.241) | data formatting | bytes 1048576 | tf_op jit(solution)/shard_map/reshape | solution.py:68
  75.2 1.3 %divide_convert_fusion = bf16[4,32,128,32]{2,1,3,0:T(8,128)(2,1)S(1)} fusion(f32[]{:T(128)} %get-tuple-element.20, bf16[64,128,32]{1,0,2:T(8,128)(2,1)S(1)} %copy.214, bf16[4,64,256]{2,1,0:T(8,128)(2,1)S(1)} %get-tuple-element.23, f32[4,64]{1,0:T(4,128)S(1)} %add_rsqrt_fusion.2, f32[4,64]{1,0:T(4,128)S(1)} %broadcast_multiply_fusion.2, ...), kind=kOutput, calls=%fused_computation.4 | convolution fusion | flops 72630272 | bytes 1722628 | tf_op jit(solution)/shard_map/sic,sje->ijce/dot_general | solution.py:158
  77.6 0.8 copy.217
  (133 shorter events, 16.2 us)
Async XLA Ops:
  0.6 75.9 %copy-start = (bf16[1024,128]{1,0:T(8,128)(2,1)S(1)}, bf16[1024,128]{1,0:T(8,128)(2,1)}, u32[]{:S(2)}) copy-start(bf16[1024,128]{1,0:T(8,128)(2,1)} %param.35) | copy-start | bytes 786436
  0.6 12.7 %copy-start.2 = (bf16[2,128,256]{2,1,0:T(8,128)(2,1)S(1)}, bf16[2,128,256]{2,1,0:T(8,128)(2,1)}, u32[]{:S(2)}) copy-start(bf16[2,128,256]{2,1,0:T(8,128)(2,1)} %param.18) | copy-start | bytes 393220
  0.7 13.1 %copy-start.11 = (bf16[4,256,256]{2,1,0:T(8,128)(2,1)S(1)}, bf16[4,256,256]{2,1,0:T(8,128)(2,1)}, u32[]{:S(2)}) copy-start(bf16[4,256,256]{2,1,0:T(8,128)(2,1)} %param.22) | copy-start | bytes 1572868
  4.9 9.6 %copy-start.1 = (bf16[4,128,128]{2,1,0:T(8,128)(2,1)S(1)}, bf16[4,128,128]{2,1,0:T(8,128)(2,1)}, u32[]{:S(2)}) copy-start(bf16[4,128,128]{2,1,0:T(8,128)(2,1)} %param.19) | copy-start | bytes 393220
  4.9 9.6 %copy-start.6 = (bf16[4,128,128]{2,1,0:T(8,128)(2,1)S(1)}, bf16[4,128,128]{2,1,0:T(8,128)(2,1)}, u32[]{:S(2)}) copy-start(bf16[4,128,128]{2,1,0:T(8,128)(2,1)} %param.27) | copy-start | bytes 393220
  4.9 17.1 %all-to-all-start = ((bf16[16,12,4,128]{3,2,1,0:T(4,128)(2,1)}), bf16[16,12,4,128]{3,2,1,0:T(4,128)(2,1)S(1)}, u32[]{:S(2)}, u32[]{:S(2)}) async-start(bf16[16,12,4,128]{3,2,1,0:T(4,128)(2,1)} %broadcast_in_dim.8), calls=%async_computation | async-start | bytes 393216 | tf_op jit(solution)/shard_map/all_to_all | solution.py:58
  13.7 2.2 %copy-start.8 = (f32[2,128]{1,0:T(2,128)}, f32[2,128]{1,0:T(2,128)S(1)}, u32[]{:S(2)}) copy-start(f32[2,128]{1,0:T(2,128)S(1)} %add_rsqrt_fusion.5) | copy-start | bytes 3076
  14.0 3.0 %copy-start.19 = (s32[64]{0:T(128)S(1)}, s32[64]{0:T(128)}, u32[]{:S(2)}) copy-start(s32[64]{0:T(128)} %param.20) | copy-start | bytes 772
  14.5 7.6 %copy-start.20 = (s32[128]{0:T(128)S(1)}, s32[128]{0:T(128)}, u32[]{:S(2)}) copy-start(s32[128]{0:T(128)} %param.21) | copy-start | bytes 1540
  22.1 1.5 %collective-permute-start = (bf16[16,12,4,128]{3,0,2,1:T(8,128)(2,1)S(1)}, bf16[16,12,4,128]{3,0,2,1:T(8,128)(2,1)S(1)}, u32[]{:S(2)}, u32[]{:S(2)}) collective-permute-start(bf16[16,12,4,128]{3,0,2,1:T(8,128)(2,1)S(1)} %copy.252), channel_id=1, source_target_pairs={{0,1},{1,0},{2,3},{3,2},{4,5},{5,4},{6,7},{7,6},{8,9},{9,8},{10,11... | collective-permute-start | bytes 589832 | tf_op jit(solution)/shard_map/ppermute | solution.py:59
  25.8 0.9 %copy-start.5 = (bf16[2,128,256]{1,2,0:T(8,128)(2,1)S(1)}, bf16[2,128,256]{1,2,0:T(8,128)(2,1)}, u32[]{:S(2)}) copy-start(bf16[2,128,256]{1,2,0:T(8,128)(2,1)} %copy.169) | copy-start | bytes 393220
  26.7 1.3 %copy-start.9 = (f32[2,128]{1,0:T(2,128)S(1)}, f32[2,128]{1,0:T(2,128)}, u32[]{:S(2)}) copy-start(f32[2,128]{1,0:T(2,128)} %copy-done.8) | copy-start | bytes 3076
  26.7 1.3 %copy-start.12 = (bf16[256,256]{1,0:T(8,128)(2,1)S(1)}, bf16[256,256]{1,0:T(8,128)(2,1)}, u32[]{:S(2)}) copy-start(bf16[256,256]{1,0:T(8,128)(2,1)} %param.24) | copy-start | bytes 393220
  30.0 4.2 %copy-start.4 = (bf16[4,128,128]{1,2,0:T(8,128)(2,1)S(1)}, bf16[4,128,128]{1,2,0:T(8,128)(2,1)}, u32[]{:S(2)}) copy-start(bf16[4,128,128]{1,2,0:T(8,128)(2,1)} %convolution_convert_fusion.5) | copy-start | bytes 393220
  31.2 11.3 %all-to-all-start.1 = ((bf16[128,2,256]{2,1,0:T(2,128)(2,1)}), bf16[128,2,256]{2,1,0:T(2,128)(2,1)S(1)}, u32[]{:S(2)}, u32[]{:S(2)}) async-start(bf16[128,2,256]{2,1,0:T(2,128)(2,1)} %copy.181), calls=%async_computation.1 | async-start | bytes 262144 | tf_op jit(solution)/shard_map/all_to_all | solution.py:128
  34.2 0.8 copy-start.14
  34.6 2.0 %copy-start.18 = (bf16[128,4]{0,1:T(4,128)(2,1)S(1)}, bf16[128,4]{0,1:T(4,128)(2,1)}, u32[]{:S(2)}) copy-start(bf16[128,4]{0,1:T(4,128)(2,1)} %param.31) | copy-start | bytes 3076
  42.4 13.2 %all-to-all-start.2 = ((bf16[32,32,128]{2,1,0:T(8,128)(2,1)}), bf16[32,32,128]{2,1,0:T(8,128)(2,1)S(1)}, u32[]{:S(2)}, u32[]{:S(2)}) async-start(bf16[32,32,128]{2,1,0:T(8,128)(2,1)} %copy.196), calls=%async_computation.2 | async-start | bytes 524288 | tf_op jit(solution)/shard_map/all_to_all | solution.py:79
  45.0 1.2 %copy-start.3 = (bf16[4,256,256]{2,1,0:T(8,128)(2,1)S(1)}, bf16[4,256,256]{2,1,0:T(8,128)(2,1)}, u32[]{:S(2)}) copy-start(bf16[4,256,256]{2,1,0:T(8,128)(2,1)} %param.25) | copy-start | bytes 1572868
  46.2 0.9 %copy-start.10 = (f32[64]{0:T(128)S(1)}, f32[64]{0:T(128)}, u32[]{:S(2)}) copy-start(f32[64]{0:T(128)} %get-tuple-element.21) | copy-start | bytes 772
  49.2 0.9 %copy-start.13 = (bf16[256,256]{1,0:T(8,128)(2,1)S(1)}, bf16[256,256]{1,0:T(8,128)(2,1)}, u32[]{:S(2)}) copy-start(bf16[256,256]{1,0:T(8,128)(2,1)} %param.26) | copy-start | bytes 393220
  50.1 2.4 %copy-start.16 = (bf16[256,32]{0,1:T(8,128)(2,1)S(1)}, bf16[256,32]{0,1:T(8,128)(2,1)}, u32[]{:S(2)}) copy-start(bf16[256,32]{0,1:T(8,128)(2,1)} %param.33) | copy-start | bytes 49156
  50.1 2.4 %copy-start.21 = (f32[64]{0:T(128)S(1)}, f32[64]{0:T(128)}, u32[]{:S(2)}) copy-start(f32[64]{0:T(128)} %convert_element_type.236) | copy-start | bytes 772
  54.0 8.4 %copy-start.7 = (bf16[4,128,128]{2,1,0:T(8,128)(2,1)S(1)}, bf16[4,128,128]{2,1,0:T(8,128)(2,1)}, u32[]{:S(2)}) copy-start(bf16[4,128,128]{2,1,0:T(8,128)(2,1)} %param.30) | copy-start | bytes 393220
  55.6 15.7 %all-to-all-start.3 = ((bf16[16,2,4096]{2,1,0:T(2,128)(2,1)}), bf16[16,2,4096]{2,1,0:T(2,128)(2,1)S(1)}, u32[]{:S(2)}, u32[]{:S(2)}) async-start(bf16[16,2,4096]{2,1,0:T(2,128)(2,1)} %reshape.287), calls=%async_computation.3 | async-start | bytes 524288 | tf_op jit(solution)/shard_map/all_to_all | solution.py:58
  71.7 2.0 %collective-permute-start.1 = (bf16[16,64,4,32]{1,3,2,0:T(8,128)(2,1)S(1)}, bf16[16,64,4,32]{1,3,2,0:T(8,128)(2,1)S(1)}, u32[]{:S(2)}, u32[]{:S(2)}) collective-permute-start(bf16[16,64,4,32]{1,3,2,0:T(8,128)(2,1)S(1)} %bitcast.242), channel_id=1, source_target_pairs={{0,1},{1,0},{2,3},{3,2},{4,5},{5,4},{6,7},{7,6},{8,9},{9,8},{10,11... | collective-permute-start | bytes 786440 | tf_op jit(solution)/shard_map/ppermute | solution.py:59
  74.0 1.1 %copy-start.17 = (bf16[256,32]{0,1:T(8,128)(2,1)S(1)}, bf16[256,32]{0,1:T(8,128)(2,1)}, u32[]{:S(2)}) copy-start(bf16[256,32]{0,1:T(8,128)(2,1)} %param.34) | copy-start | bytes 49156
  76.5 0.8 copy-start.15

commit v9 on v6

--- a/solution.py
+++ b/solution.py
@@ -110,11 +110,11 @@
 ):
     residue_keys = key_offsets(residue_mask)
     sequence_keys = key_offsets(sequence_mask)
-    pair_norm = layer_norm(pairwise)
     both_maps = jnp.concatenate([row_bias_map, start_bias_map], axis=1)
     both_local = jnp.einsum(
-        "ijc,ch->hij", pair_norm, both_maps, preferred_element_type=jnp.float32
+        "ijc,ch->hij", layer_norm(pairwise), both_maps, preferred_element_type=jnp.float32
     ).astype(jnp.bfloat16)
+    pair_norm = layer_norm(lax.optimization_barrier(pairwise))
     both_bias = gather_blocks(both_local, 1, count)
     row_bias = both_bias[:H_M]
     start_bias = both_bias[H_M:]

time: 77.2 us -> 77.6 us (level)
    reduce_sum x6 -> x7, other arithmetic: 2.26 us -> 2.5 us  [layer_norm(): spread = jnp.mean(center * center, axis=-1, keepdims=True)]
    reduce_sum x4 -> x5, other arithmetic: 1.49 us -> 1.6 us  [layer_norm(): center = widened - jnp.mean(widened, axis=-1, keepdims=True)]
where the time goes in v9:
time: 77.6 us; the launch traced here: 76.8 us
  waiting for transfers between devices  20 us (26%)
  starting transfers between devices  18.5 us (24%)
  matrix products  16.7 us (22%)
  local copies, waits for them, and re-layouts  13.2 us (17%)
  other arithmetic  6.98 us (9%)
  between operations  1.45 us (2%)
    all_to_all x2, starting transfers between devices, gather_blocks(): same_core = lax.all_to_all(spread, 'chip', 0, 0, tiled=True)  12.2 us
    all_to_all x2, waiting for transfers between devices, gather_blocks(): same_core = lax.all_to_all(spread, 'chip', 0, 0, tiled=True)  9.5 us
    unnamed x54, local copies, waits for them, and re-layouts  5.16 us
    all_to_all x1, waiting for transfers between devices, per_device(): alignment_cols = lax.all_to_all(alignment_one, DAP, 1, 0, tiled=True)  4.67 us
    dot_general x12, matrix products, project(): jnp.einsum('bqc,cf->bqf', inputs, weight_table, preferred_element_type=jn...  3.98 us
    all_to_all x1, starting transfers between devices, per_device(): alignment_cols = lax.all_to_all(alignment_one, DAP, 1, 0, tiled=True)  3.44 us
    dot_general x4, matrix products, attend(): jnp.einsum('bqf,fc->bqc', gated, output_map, preferred_element_type=jnp.f...  3.42 us
    all_to_all x1, waiting for transfers between devices, exchange_pair(): lax.all_to_all(jnp.concatenate([pair_part, end_part], axis=1), DAP, 0, 0,...  3.07 us
  transfers between devices with their start and end apart: 6, of which 6 were waited for; matrix products, arithmetic and copies ran while one was open for 25% of the time, Pallas kernels for 0%

profile of v9, /device:TPU:0, one launch (start us, length us, event | category | flops | bytes accessed | tf_op | source)
XLA Modules:
  0.0 76.8 jit_solution(12825585861121272465)
XLA Ops:
  0.7 1.1 %convert_reduce_fusion = f32[4,128]{1,0:T(4,128)S(1)} fusion(bf16[4,128,128]{2,1,0:T(8,128)(2,1)} %param.19), kind=kLoop, calls=%fused_computation.91 | loop fusion | flops 130560 | bytes 133120 | tf_op jit(solution)/shard_map/reduce_sum | solution.py:19
  1.8 1.1 %fusion.65 = f32[4,128]{1,0:T(4,128)S(1)} fusion(bf16[4,128,128]{2,1,0:T(8,128)(2,1)} %param.19, f32[4,128]{1,0:T(4,128)S(1)} %broadcast_multiply_fusion.5), kind=kLoop, calls=%fused_computation.110 | loop fusion | flops 261632 | bytes 135168 | tf_op jit(solution)/shard_map/reduce_sum | solution.py:20
  2.9 1.3 %convolution_convert_fusion.12 = bf16[12,4,128]{2,0,1:T(8,128)(2,1)S(1)} fusion(bf16[4,128,128]{2,1,0:T(8,128)(2,1)} %param.19, f32[4,128]{1,0:T(4,128)S(1)} %add_rsqrt_fusion.5, f32[4,128]{1,0:T(4,128)S(1)} %broadcast_multiply_fusion.5, bf16[128,4]{0,1:T(4,128)(2,1)} %param.28, bf16[128,8]{0,1:T(8,128)(2,1)} %param.23), kind=kOutput, calls=%fused_computation.76 | convolution fusion | flops 1847296 | bytes 150528 | tf_op jit(solution)/shard_map/ijc,ch->hij/dot_general | solution.py:114
  4.2 0.7 broadcast_in_dim.8
  4.9 8.4 %all-to-all-start = ((bf16[16,12,4,128]{3,2,1,0:T(4,128)(2,1)}), bf16[16,12,4,128]{3,2,1,0:T(4,128)(2,1)S(1)}, u32[]{:S(2)}, u32[]{:S(2)}) async-start(bf16[16,12,4,128]{3,2,1,0:T(4,128)(2,1)} %broadcast_in_dim.8), calls=%async_computation | async-start | bytes 393216 | tf_op jit(solution)/shard_map/all_to_all | solution.py:58
  15.0 1.0 %convolution_convert_fusion.5 = bf16[4,128,128]{1,2,0:T(8,128)(2,1)} fusion(bf16[4,128,128]{2,1,0:T(8,128)(2,1)S(1)} %copy-done.6, bf16[4,128,128]{2,1,0:T(8,128)(2,1)S(1)} %copy-done.1, f32[4,128]{1,0:T(4,128)S(1)} %add_rsqrt_fusion.4, f32[4,128]{1,0:T(4,128)S(1)} %broadcast_multiply_fusion.4), kind=kOutput, calls=%fused_computation.64 | convolution fusion | flops 17104896 | bytes 299008 | tf_op jit(solution)/shard_map/bqc,cf->bqf/dot_general | solution.py:29
  16.4 0.8 copy.230
  17.4 0.6 convert_element_type.227
  18.0 1.2 %convert_reduce_fusion.5 = (f32[]{:T(128)}, f32[64]{0:T(128)}) fusion(s32[64]{0:T(128)S(1)} %copy-done.19), kind=kLoop, calls=%fused_computation.211 | loop fusion | flops 255 | bytes 516 | tf_op jit(solution)/shard_map/reduce_sum | solution.py:151
  19.6 2.5 %all-to-all-done = bf16[16,12,4,128]{3,2,1,0:T(4,128)(2,1)S(1)} async-done(((bf16[16,12,4,128]{3,2,1,0:T(4,128)(2,1)}), bf16[16,12,4,128]{3,2,1,0:T(4,128)(2,1)S(1)}, u32[]{:S(2)}, u32[]{:S(2)}) %all-to-all-start) | async-done | bytes 196640 | tf_op jit(solution)/shard_map/all_to_all | solution.py:58
  22.2 1.4 %collective-permute-done = bf16[16,12,4,128]{3,0,2,1:T(8,128)(2,1)S(1)} collective-permute-done((bf16[16,12,4,128]{3,0,2,1:T(8,128)(2,1)S(1)}, bf16[16,12,4,128]{3,0,2,1:T(8,128)(2,1)S(1)}, u32[]{:S(2)}, u32[]{:S(2)}) %collective-permute-start) | collective-permute-done | bytes 196640 | tf_op jit(solution)/shard_map/ppermute | solution.py:59
  24.7 1.1 %fusion.179 = f32[2,8,128]{2,1,0:T(8,128)} fusion(bf16[2,128,8,32]{1,3,2,0:T(8,128)(2,1)S(1)} %bitcast.276, bf16[2,128,8,32]{1,3,2,0:T(8,128)(2,1)S(1)} %bitcast.278, f32[128]{0:T(128)S(1)} %add_multiply_fusion.1, f32[8,128,128]{1,2,0:T(8,128)S(1)} %copy.238), kind=kOutput, calls=%fused_computation.223 | convolution fusion | flops 18088064 | bytes 795136 | tf_op jit(solution)/shard_map/sub | solution.py:48
  26.5 0.6 fusion.185
  27.5 0.5 copy-done.5
  28.9 1.3 %fusion.44 = bf16[2,128,256]{2,1,0:T(8,128)(2,1)S(1)} fusion(f32[2,128,256]{2,1,0:T(8,128)S(1)} %copy.240, bf16[2,128,256]{2,1,0:T(8,128)(2,1)S(1)} %copy-done.2, bf16[256,256]{1,0:T(8,128)(2,1)S(1)} %copy-done.12, bf16[4,256,256]{2,1,0:T(8,128)(2,1)} %param.22, f32[2,128]{1,0:T(2,128)S(1)} %copy-done.9, f32[2,128]{1,0:T(2,128)S(1)} %broadcast_multiply_fusion.6), kind=kOutput, calls=%fused_computation.57 | convolution fusion | flops 67895296 | bytes 919552 | tf_op jit(solution)/shard_map/bqf,fc->bqc/dot_general | solution.py:52
  30.2 0.8 %copy.241 = bf16[2,128,256]{2,0,1:T(2,128)(2,1)} copy(bf16[2,128,256]{2,1,0:T(8,128)(2,1)S(1)} %fusion.44) | data formatting | bytes 262144 | tf_op jit(solution)/shard_map/convert_element_type | solution.py:122
  31.0 3.4 %all-to-all-start.1 = ((bf16[2,128,256]{2,0,1:T(2,128)(2,1)}), bf16[2,128,256]{2,0,1:T(2,128)(2,1)S(1)}, u32[]{:S(2)}, u32[]{:S(2)}) async-start(bf16[2,128,256]{2,0,1:T(2,128)(2,1)} %copy.241), calls=%async_computation.1 | async-start | bytes 262144 | tf_op jit(solution)/shard_map/all_to_all | solution.py:123
  35.2 1.3 %convert_reduce_fusion.3 = (f32[4,128]{1,0:T(4,128)S(1)}, bf16[4,128,128]{2,1,0:T(8,128)(2,1)S(1)}) fusion(bf16[128,128]{1,0:T(8,128)(2,1)S(1)} %copy-done.14, f32[4,128,128]{2,1,0:T(8,128)S(1)} %copy.262, bf16[4,128,128]{2,1,0:T(8,128)(2,1)} %param.27, bf16[4,128,128]{2,1,0:T(8,128)(2,1)S(1)} %copy-done.1, f32[4,128]{1,0:T(4,128)S(1)} %add_rsqrt_fusion.4, ...), kind=kOutput, calls=%fused_computation.97 | convolution fusion | flops 34471424 | bytes 727040 | tf_op jit(solution)/shard_map/bqf,fc->bqc/dot_general | solution.py:52
  37.2 0.8 %copy.265 = bf16[32,32,128]{2,1,0:T(8,128)(2,1)} copy(bf16[32,32,128]{2,0,1:T(8,128)(2,1)S(1)} %pad_maximum_fusion) | data formatting | bytes 524288 | tf_op jit(solution)/shard_map/concatenate | solution.py:80
  38.0 4.7 %all-to-all-done.1 = bf16[2,128,256]{2,0,1:T(2,128)(2,1)S(1)} async-done(((bf16[2,128,256]{2,0,1:T(2,128)(2,1)}), bf16[2,128,256]{2,0,1:T(2,128)(2,1)S(1)}, u32[]{:S(2)}, u32[]{:S(2)}) %all-to-all-start.1) | async-done | bytes 131104 | tf_op jit(solution)/shard_map/all_to_all | solution.py:123
  42.7 2.8 %all-to-all-start.2 = ((bf16[32,32,128]{2,1,0:T(8,128)(2,1)}), bf16[32,32,128]{2,1,0:T(8,128)(2,1)S(1)}, u32[]{:S(2)}, u32[]{:S(2)}) async-start(bf16[32,32,128]{2,1,0:T(8,128)(2,1)} %copy.265), calls=%async_computation.2 | async-start | bytes 524288 | tf_op jit(solution)/shard_map/all_to_all | solution.py:79
  47.9 0.6 fusion.180
  50.6 0.8 copy.285
  51.7 1.1 %reshape.295 = bf16[16,2,4096]{2,1,0:T(2,128)(2,1)} reshape(bf16[16,4,32,64]{3,2,1,0:T(8,128)(2,1)S(1)} %broadcast_bitcast_fusion) | data formatting | bytes 524288
  52.8 3.1 %all-to-all-done.2 = bf16[32,32,128]{2,1,0:T(8,128)(2,1)S(1)} async-done(((bf16[32,32,128]{2,1,0:T(8,128)(2,1)}), bf16[32,32,128]{2,1,0:T(8,128)(2,1)S(1)}, u32[]{:S(2)}, u32[]{:S(2)}) %all-to-all-start.2) | async-done | bytes 262176 | tf_op jit(solution)/shard_map/all_to_all | solution.py:79
  55.9 3.7 %all-to-all-start.3 = ((bf16[16,2,4096]{2,1,0:T(2,128)(2,1)}), bf16[16,2,4096]{2,1,0:T(2,128)(2,1)S(1)}, u32[]{:S(2)}, u32[]{:S(2)}) async-start(bf16[16,2,4096]{2,1,0:T(2,128)(2,1)} %reshape.295), calls=%async_computation.3 | async-start | bytes 524288 | tf_op jit(solution)/shard_map/all_to_all | solution.py:58
  61.6 0.6 fusion.190
  62.8 7.0 %all-to-all-done.3 = bf16[16,2,4096]{2,1,0:T(2,128)(2,1)S(1)} async-done(((bf16[16,2,4096]{2,1,0:T(2,128)(2,1)}), bf16[16,2,4096]{2,1,0:T(2,128)(2,1)S(1)}, u32[]{:S(2)}, u32[]{:S(2)}) %all-to-all-start.3) | async-done | bytes 262176 | tf_op jit(solution)/shard_map/all_to_all | solution.py:58
  70.8 1.4 %collective-permute-done.1 = bf16[16,64,4,32]{1,3,2,0:T(8,128)(2,1)S(1)} collective-permute-done((bf16[16,64,4,32]{1,3,2,0:T(8,128)(2,1)S(1)}, bf16[16,64,4,32]{1,3,2,0:T(8,128)(2,1)S(1)}, u32[]{:S(2)}, u32[]{:S(2)}) %collective-permute-start.1) | collective-permute-done | bytes 262176 | tf_op jit(solution)/shard_map/ppermute | solution.py:59
  72.5 1.1 %copy.283 = bf16[64,128,32]{1,0,2:T(8,128)(2,1)S(1)} copy(bf16[64,128,32]{0,2,1:T(8,128)(2,1)S(1)} %bitcast.246) | data formatting | bytes 1048576 | tf_op jit(solution)/shard_map/reshape | solution.py:68
  73.6 1.3 %divide_convert_fusion = bf16[4,32,128,32]{2,1,3,0:T(8,128)(2,1)S(1)} fusion(f32[]{:T(128)} %get-tuple-element.18, bf16[64,128,32]{1,0,2:T(8,128)(2,1)S(1)} %copy.283, bf16[64,4,256]{2,0,1:T(8,128)(2,1)S(1)} %get-tuple-element.21, f32[64,4]{0,1:T(4,128)S(1)} %add_rsqrt_fusion.2, f32[64,4]{0,1:T(4,128)S(1)} %broadcast_multiply_fusion.2, ...), kind=kOutput, calls=%fused_computation.4 | convolution fusion | flops 72630272 | bytes 1722628 | tf_op jit(solution)/shard_map/sic,sje->ijce/dot_general | solution.py:153
  76.1 0.8 copy.286
  (142 shorter events, 16.5 us)
Async XLA Ops:
  0.6 74.4 %copy-start = (bf16[1024,128]{1,0:T(8,128)(2,1)S(1)}, bf16[1024,128]{1,0:T(8,128)(2,1)}, u32[]{:S(2)}) copy-start(bf16[1024,128]{1,0:T(8,128)(2,1)} %param.35) | copy-start | bytes 786436
  0.6 12.7 %copy-start.2 = (bf16[2,128,256]{2,1,0:T(8,128)(2,1)S(1)}, bf16[2,128,256]{2,1,0:T(8,128)(2,1)}, u32[]{:S(2)}) copy-start(bf16[2,128,256]{2,1,0:T(8,128)(2,1)} %param.18) | copy-start | bytes 393220
  0.7 13.1 %copy-start.11 = (bf16[4,256,256]{2,1,0:T(8,128)(2,1)S(1)}, bf16[4,256,256]{2,1,0:T(8,128)(2,1)}, u32[]{:S(2)}) copy-start(bf16[4,256,256]{2,1,0:T(8,128)(2,1)} %param.22) | copy-start | bytes 1572868
  4.9 9.6 %copy-start.1 = (bf16[4,128,128]{2,1,0:T(8,128)(2,1)S(1)}, bf16[4,128,128]{2,1,0:T(8,128)(2,1)}, u32[]{:S(2)}) copy-start(bf16[4,128,128]{2,1,0:T(8,128)(2,1)} %param.19) | copy-start | bytes 393220
  4.9 17.1 %all-to-all-start = ((bf16[16,12,4,128]{3,2,1,0:T(4,128)(2,1)}), bf16[16,12,4,128]{3,2,1,0:T(4,128)(2,1)S(1)}, u32[]{:S(2)}, u32[]{:S(2)}) async-start(bf16[16,12,4,128]{3,2,1,0:T(4,128)(2,1)} %broadcast_in_dim.8), calls=%async_computation | async-start | bytes 393216 | tf_op jit(solution)/shard_map/all_to_all | solution.py:58
  13.4 1.6 %copy-start.6 = (bf16[4,128,128]{2,1,0:T(8,128)(2,1)S(1)}, bf16[4,128,128]{2,1,0:T(8,128)(2,1)}, u32[]{:S(2)}) copy-start(bf16[4,128,128]{2,1,0:T(8,128)(2,1)} %param.27) | copy-start | bytes 393220
  13.7 0.8 %copy-start.8 = (f32[2,128]{1,0:T(2,128)}, f32[2,128]{1,0:T(2,128)S(1)}, u32[]{:S(2)}) copy-start(f32[2,128]{1,0:T(2,128)S(1)} %add_rsqrt_fusion.6) | copy-start | bytes 3076
  14.3 3.1 %copy-start.19 = (s32[64]{0:T(128)S(1)}, s32[64]{0:T(128)}, u32[]{:S(2)}) copy-start(s32[64]{0:T(128)} %param.20) | copy-start | bytes 772
  14.9 7.2 %copy-start.20 = (s32[128]{0:T(128)S(1)}, s32[128]{0:T(128)}, u32[]{:S(2)}) copy-start(s32[128]{0:T(128)} %param.21) | copy-start | bytes 1540
  22.1 1.5 %collective-permute-start = (bf16[16,12,4,128]{3,0,2,1:T(8,128)(2,1)S(1)}, bf16[16,12,4,128]{3,0,2,1:T(8,128)(2,1)S(1)}, u32[]{:S(2)}, u32[]{:S(2)}) collective-permute-start(bf16[16,12,4,128]{3,0,2,1:T(8,128)(2,1)S(1)} %copy.324), channel_id=1, source_target_pairs={{0,1},{1,0},{2,3},{3,2},{4,5},{5,4},{6,7},{7,6},{8,9},{9,8},{10,11... | collective-permute-start | bytes 589832 | tf_op jit(solution)/shard_map/ppermute | solution.py:59
  27.1 0.9 %copy-start.5 = (bf16[2,128,256]{1,2,0:T(8,128)(2,1)S(1)}, bf16[2,128,256]{1,2,0:T(8,128)(2,1)}, u32[]{:S(2)}) copy-start(bf16[2,128,256]{1,2,0:T(8,128)(2,1)} %copy.230) | copy-start | bytes 393220
  27.1 0.9 %copy-start.22 = (f32[2,8,128]{2,1,0:T(8,128)S(1)}, f32[2,8,128]{2,1,0:T(8,128)}, u32[]{:S(2)}) copy-start(f32[2,8,128]{2,1,0:T(8,128)} %fusion.179) | copy-start | bytes 24580
  28.0 0.7 copy-start.9
  28.0 0.9 %copy-start.12 = (bf16[256,256]{1,0:T(8,128)(2,1)S(1)}, bf16[256,256]{1,0:T(8,128)(2,1)}, u32[]{:S(2)}) copy-start(bf16[256,256]{1,0:T(8,128)(2,1)} %param.24) | copy-start | bytes 393220
  28.9 5.6 %copy-start.4 = (bf16[4,128,128]{1,2,0:T(8,128)(2,1)S(1)}, bf16[4,128,128]{1,2,0:T(8,128)(2,1)}, u32[]{:S(2)}) copy-start(bf16[4,128,128]{1,2,0:T(8,128)(2,1)} %convolution_convert_fusion.5) | copy-start | bytes 393220
  31.0 11.7 %all-to-all-start.1 = ((bf16[2,128,256]{2,0,1:T(2,128)(2,1)}), bf16[2,128,256]{2,0,1:T(2,128)(2,1)S(1)}, u32[]{:S(2)}, u32[]{:S(2)}) async-start(bf16[2,128,256]{2,0,1:T(2,128)(2,1)} %copy.241), calls=%async_computation.1 | async-start | bytes 262144 | tf_op jit(solution)/shard_map/all_to_all | solution.py:123
  34.5 0.8 copy-start.14
  34.8 2.0 %copy-start.18 = (bf16[128,4]{0,1:T(4,128)(2,1)S(1)}, bf16[128,4]{0,1:T(4,128)(2,1)}, u32[]{:S(2)}) copy-start(bf16[128,4]{0,1:T(4,128)(2,1)} %param.31) | copy-start | bytes 3076
  42.7 13.2 %all-to-all-start.2 = ((bf16[32,32,128]{2,1,0:T(8,128)(2,1)}), bf16[32,32,128]{2,1,0:T(8,128)(2,1)S(1)}, u32[]{:S(2)}, u32[]{:S(2)}) async-start(bf16[32,32,128]{2,1,0:T(8,128)(2,1)} %copy.265), calls=%async_computation.2 | async-start | bytes 524288 | tf_op jit(solution)/shard_map/all_to_all | solution.py:79
  45.7 1.1 %copy-start.3 = (bf16[4,256,256]{2,1,0:T(8,128)(2,1)S(1)}, bf16[4,256,256]{2,1,0:T(8,128)(2,1)}, u32[]{:S(2)}) copy-start(bf16[4,256,256]{2,1,0:T(8,128)(2,1)} %param.25) | copy-start | bytes 1572868
  47.0 0.9 %copy-start.10 = (f32[64]{0:T(128)S(1)}, f32[64]{0:T(128)}, u32[]{:S(2)}) copy-start(f32[64]{0:T(128)} %get-tuple-element.19) | copy-start | bytes 772
  49.0 0.9 %copy-start.13 = (bf16[256,256]{1,0:T(8,128)(2,1)S(1)}, bf16[256,256]{1,0:T(8,128)(2,1)}, u32[]{:S(2)}) copy-start(bf16[256,256]{1,0:T(8,128)(2,1)} %param.26) | copy-start | bytes 393220
  49.9 1.5 %copy-start.16 = (bf16[256,32]{0,1:T(8,128)(2,1)S(1)}, bf16[256,32]{0,1:T(8,128)(2,1)}, u32[]{:S(2)}) copy-start(bf16[256,32]{0,1:T(8,128)(2,1)} %param.33) | copy-start | bytes 49156
  49.9 1.5 %copy-start.21 = (f32[64]{0:T(128)S(1)}, f32[64]{0:T(128)}, u32[]{:S(2)}) copy-start(f32[64]{0:T(128)} %convert_element_type.227) | copy-start | bytes 772
  52.8 8.1 %copy-start.7 = (bf16[4,128,128]{2,1,0:T(8,128)(2,1)S(1)}, bf16[4,128,128]{2,1,0:T(8,128)(2,1)}, u32[]{:S(2)}) copy-start(bf16[4,128,128]{2,1,0:T(8,128)(2,1)} %param.30) | copy-start | bytes 393220
  55.9 13.9 %all-to-all-start.3 = ((bf16[16,2,4096]{2,1,0:T(2,128)(2,1)}), bf16[16,2,4096]{2,1,0:T(2,128)(2,1)S(1)}, u32[]{:S(2)}, u32[]{:S(2)}) async-start(bf16[16,2,4096]{2,1,0:T(2,128)(2,1)} %reshape.295), calls=%async_computation.3 | async-start | bytes 524288 | tf_op jit(solution)/shard_map/all_to_all | solution.py:58
  70.2 2.0 %collective-permute-start.1 = (bf16[16,64,4,32]{1,3,2,0:T(8,128)(2,1)S(1)}, bf16[16,64,4,32]{1,3,2,0:T(8,128)(2,1)S(1)}, u32[]{:S(2)}, u32[]{:S(2)}) collective-permute-start(bf16[16,64,4,32]{1,3,2,0:T(8,128)(2,1)S(1)} %bitcast.247), channel_id=1, source_target_pairs={{0,1},{1,0},{2,3},{3,2},{4,5},{5,4},{6,7},{7,6},{8,9},{9,8},{10,11... | collective-permute-start | bytes 786440 | tf_op jit(solution)/shard_map/ppermute | solution.py:59
  72.5 1.1 %copy-start.17 = (bf16[256,32]{0,1:T(8,128)(2,1)S(1)}, bf16[256,32]{0,1:T(8,128)(2,1)}, u32[]{:S(2)}) copy-start(bf16[256,32]{0,1:T(8,128)(2,1)} %param.34) | copy-start | bytes 49156
  75.0 0.8 copy-start.15

commit v10 on v9

--- a/solution.py
+++ b/solution.py
@@ -14,10 +14,10 @@
 mask_scale = 1000000000.0
 
 
-def layer_norm(values):
+def layer_norm(values, axis=-1):
     widened = values.astype(jnp.float32)
-    center = widened - jnp.mean(widened, axis=-1, keepdims=True)
-    spread = jnp.mean(center * center, axis=-1, keepdims=True)
+    center = widened - jnp.mean(widened, axis=axis, keepdims=True)
+    spread = jnp.mean(center * center, axis=axis, keepdims=True)
     return (center * lax.rsqrt(spread + norm_epsilon)).astype(jnp.bfloat16)
 
 
@@ -112,7 +112,10 @@
     sequence_keys = key_offsets(sequence_mask)
     both_maps = jnp.concatenate([row_bias_map, start_bias_map], axis=1)
     both_local = jnp.einsum(
-        "ijc,ch->hij", layer_norm(pairwise), both_maps, preferred_element_type=jnp.float32
+        "icj,ch->hij",
+        layer_norm(jnp.swapaxes(pairwise, 1, 2), axis=1),
+        both_maps,
+        preferred_element_type=jnp.float32,
     ).astype(jnp.bfloat16)
     pair_norm = layer_norm(lax.optimization_barrier(pairwise))
     both_bias = gather_blocks(both_local, 1, count)

time: 77.6 us -> 77.6 us (level)
  no operation moved by 1% of the time
where the time goes in v10:
time: 77.6 us; the launch traced here: 76.8 us
  waiting for transfers between devices  20 us (26%)
  starting transfers between devices  18.5 us (24%)
  matrix products  16.7 us (22%)
  local copies, waits for them, and re-layouts  13.2 us (17%)
  other arithmetic  6.98 us (9%)
  between operations  1.45 us (2%)
    all_to_all x2, starting transfers between devices, gather_blocks(): same_core = lax.all_to_all(spread, 'chip', 0, 0, tiled=True)  12.2 us
    all_to_all x2, waiting for transfers between devices, gather_blocks(): same_core = lax.all_to_all(spread, 'chip', 0, 0, tiled=True)  9.5 us
    unnamed x54, local copies, waits for them, and re-layouts  5.16 us
    all_to_all x1, waiting for transfers between devices, per_device(): alignment_cols = lax.all_to_all(alignment_one, DAP, 1, 0, tiled=True)  4.67 us
    dot_general x12, matrix products, project(): jnp.einsum('bqc,cf->bqf', inputs, weight_table, preferred_element_type=jn...  3.98 us
    all_to_all x1, starting transfers between devices, per_device(): alignment_cols = lax.all_to_all(alignment_one, DAP, 1, 0, tiled=True)  3.44 us
    dot_general x4, matrix products, attend(): jnp.einsum('bqf,fc->bqc', gated, output_map, preferred_element_type=jnp.f...  3.42 us
    all_to_all x1, waiting for transfers between devices, exchange_pair(): lax.all_to_all(jnp.concatenate([pair_part, end_part], axis=1), DAP, 0, 0,...  3.07 us
  transfers between devices with their start and end apart: 6, of which 6 were waited for; matrix products, arithmetic and copies ran while one was open for 25% of the time, Pallas kernels for 0%

profile of v10, /device:TPU:0, one launch (start us, length us, event | category | flops | bytes accessed | tf_op | source)
XLA Modules:
  0.0 76.8 jit_solution(12825585861121272465)
XLA Ops:
  0.7 1.1 %fusion.56 = f32[4,128]{1,0:T(4,128)S(1)} fusion(bf16[4,128,128]{2,1,0:T(8,128)(2,1)} %param.19), kind=kLoop, calls=%fused_computation.94 | loop fusion | flops 130560 | bytes 133120 | tf_op jit(solution)/shard_map/reduce_sum | solution.py:19
  1.8 1.1 %fusion.69 = f32[4,128]{1,0:T(4,128)S(1)} fusion(bf16[4,128,128]{2,1,0:T(8,128)(2,1)} %param.19, f32[4,128]{1,0:T(4,128)S(1)} %broadcast_multiply_fusion.5), kind=kLoop, calls=%fused_computation.113 | loop fusion | flops 261632 | bytes 135168 | tf_op jit(solution)/shard_map/reduce_sum | solution.py:20
  2.9 1.3 %convolution_convert_fusion.12 = bf16[12,4,128]{2,0,1:T(8,128)(2,1)S(1)} fusion(bf16[4,128,128]{2,1,0:T(8,128)(2,1)} %param.19, f32[4,128]{1,0:T(4,128)S(1)} %add_rsqrt_fusion.5, f32[4,128]{1,0:T(4,128)S(1)} %broadcast_multiply_fusion.5, bf16[128,4]{0,1:T(4,128)(2,1)} %param.28, bf16[128,8]{0,1:T(8,128)(2,1)} %param.23), kind=kOutput, calls=%fused_computation.76 | convolution fusion | flops 1847296 | bytes 150528 | tf_op jit(solution)/shard_map/icj,ch->hij/dot_general | solution.py:114
  4.2 0.7 broadcast_in_dim.8
  4.9 8.4 %all-to-all-start = ((bf16[16,12,4,128]{3,2,1,0:T(4,128)(2,1)}), bf16[16,12,4,128]{3,2,1,0:T(4,128)(2,1)S(1)}, u32[]{:S(2)}, u32[]{:S(2)}) async-start(bf16[16,12,4,128]{3,2,1,0:T(4,128)(2,1)} %broadcast_in_dim.8), calls=%async_computation | async-start | bytes 393216 | tf_op jit(solution)/shard_map/all_to_all | solution.py:58
  15.0 1.0 %convolution_convert_fusion.5 = bf16[4,128,128]{1,2,0:T(8,128)(2,1)} fusion(bf16[4,128,128]{2,1,0:T(8,128)(2,1)S(1)} %copy-done.6, bf16[4,128,128]{2,1,0:T(8,128)(2,1)S(1)} %copy-done.1, f32[4,128]{1,0:T(4,128)S(1)} %add_rsqrt_fusion.4, f32[4,128]{1,0:T(4,128)S(1)} %broadcast_multiply_fusion.4), kind=kOutput, calls=%fused_computation.64 | convolution fusion | flops 17104896 | bytes 299008 | tf_op jit(solution)/shard_map/bqc,cf->bqf/dot_general | solution.py:29
  16.4 0.8 copy.235
  17.4 0.6 convert_element_type.233
  18.0 1.2 %convert_reduce_fusion.4 = (f32[]{:T(128)}, f32[64]{0:T(128)}) fusion(s32[64]{0:T(128)S(1)} %copy-done.19), kind=kLoop, calls=%fused_computation.212 | loop fusion | flops 255 | bytes 516 | tf_op jit(solution)/shard_map/reduce_sum | solution.py:154
  19.6 2.5 %all-to-all-done = bf16[16,12,4,128]{3,2,1,0:T(4,128)(2,1)S(1)} async-done(((bf16[16,12,4,128]{3,2,1,0:T(4,128)(2,1)}), bf16[16,12,4,128]{3,2,1,0:T(4,128)(2,1)S(1)}, u32[]{:S(2)}, u32[]{:S(2)}) %all-to-all-start) | async-done | bytes 196640 | tf_op jit(solution)/shard_map/all_to_all | solution.py:58
  22.2 1.4 %collective-permute-done = bf16[16,12,4,128]{3,0,2,1:T(8,128)(2,1)S(1)} collective-permute-done((bf16[16,12,4,128]{3,0,2,1:T(8,128)(2,1)S(1)}, bf16[16,12,4,128]{3,0,2,1:T(8,128)(2,1)S(1)}, u32[]{:S(2)}, u32[]{:S(2)}) %collective-permute-start) | collective-permute-done | bytes 196640 | tf_op jit(solution)/shard_map/ppermute | solution.py:59
  24.7 1.1 %fusion.181 = f32[2,8,128]{2,1,0:T(8,128)} fusion(bf16[2,128,8,32]{1,3,2,0:T(8,128)(2,1)S(1)} %bitcast.291, bf16[2,128,8,32]{1,3,2,0:T(8,128)(2,1)S(1)} %bitcast.293, f32[128]{0:T(128)S(1)} %add_multiply_fusion.1, f32[8,128,128]{1,2,0:T(8,128)S(1)} %copy.244), kind=kOutput, calls=%fused_computation.224 | convolution fusion | flops 18088064 | bytes 795136 | tf_op jit(solution)/shard_map/sub | solution.py:48
  26.5 0.6 fusion.187
  27.5 0.5 copy-done.5
  28.9 1.3 %fusion.44 = bf16[2,128,256]{2,1,0:T(8,128)(2,1)S(1)} fusion(f32[2,128,256]{2,1,0:T(8,128)S(1)} %copy.246, bf16[2,128,256]{2,1,0:T(8,128)(2,1)S(1)} %copy-done.2, bf16[256,256]{1,0:T(8,128)(2,1)S(1)} %copy-done.12, bf16[4,256,256]{2,1,0:T(8,128)(2,1)} %param.22, f32[2,128]{1,0:T(2,128)S(1)} %copy-done.9, f32[2,128]{1,0:T(2,128)S(1)} %broadcast_multiply_fusion.6), kind=kOutput, calls=%fused_computation.57 | convolution fusion | flops 67895296 | bytes 919552 | tf_op jit(solution)/shard_map/bqf,fc->bqc/dot_general | solution.py:52
  30.2 0.8 %copy.247 = bf16[2,128,256]{2,0,1:T(2,128)(2,1)} copy(bf16[2,128,256]{2,1,0:T(8,128)(2,1)S(1)} %fusion.44) | data formatting | bytes 262144 | tf_op jit(solution)/shard_map/convert_element_type | solution.py:125
  31.0 3.4 %all-to-all-start.1 = ((bf16[2,128,256]{2,0,1:T(2,128)(2,1)}), bf16[2,128,256]{2,0,1:T(2,128)(2,1)S(1)}, u32[]{:S(2)}, u32[]{:S(2)}) async-start(bf16[2,128,256]{2,0,1:T(2,128)(2,1)} %copy.247), calls=%async_computation.1 | async-start | bytes 262144 | tf_op jit(solution)/shard_map/all_to_all | solution.py:126
  35.2 1.3 %convert_reduce_fusion.2 = (f32[4,128]{1,0:T(4,128)S(1)}, bf16[4,128,128]{2,1,0:T(8,128)(2,1)S(1)}) fusion(bf16[128,128]{1,0:T(8,128)(2,1)S(1)} %copy-done.14, f32[4,128,128]{2,1,0:T(8,128)S(1)} %copy.268, bf16[4,128,128]{2,1,0:T(8,128)(2,1)} %param.27, bf16[4,128,128]{2,1,0:T(8,128)(2,1)S(1)} %copy-done.1, f32[4,128]{1,0:T(4,128)S(1)} %add_rsqrt_fusion.4, ...), kind=kOutput, calls=%fused_computation.98 | convolution fusion | flops 34471424 | bytes 727040 | tf_op jit(solution)/shard_map/bqf,fc->bqc/dot_general | solution.py:52
  37.2 0.8 %copy.271 = bf16[32,32,128]{2,1,0:T(8,128)(2,1)} copy(bf16[32,32,128]{2,0,1:T(8,128)(2,1)S(1)} %pad_maximum_fusion) | data formatting | bytes 524288 | tf_op jit(solution)/shard_map/concatenate | solution.py:80
  38.0 4.7 %all-to-all-done.1 = bf16[2,128,256]{2,0,1:T(2,128)(2,1)S(1)} async-done(((bf16[2,128,256]{2,0,1:T(2,128)(2,1)}), bf16[2,128,256]{2,0,1:T(2,128)(2,1)S(1)}, u32[]{:S(2)}, u32[]{:S(2)}) %all-to-all-start.1) | async-done | bytes 131104 | tf_op jit(solution)/shard_map/all_to_all | solution.py:126
  42.7 2.8 %all-to-all-start.2 = ((bf16[32,32,128]{2,1,0:T(8,128)(2,1)}), bf16[32,32,128]{2,1,0:T(8,128)(2,1)S(1)}, u32[]{:S(2)}, u32[]{:S(2)}) async-start(bf16[32,32,128]{2,1,0:T(8,128)(2,1)} %copy.271), calls=%async_computation.2 | async-start | bytes 524288 | tf_op jit(solution)/shard_map/all_to_all | solution.py:79
  47.9 0.6 fusion.182
  50.6 0.8 copy.291
  51.7 1.1 %reshape.295 = bf16[16,2,4096]{2,1,0:T(2,128)(2,1)} reshape(bf16[16,4,32,64]{3,2,1,0:T(8,128)(2,1)S(1)} %broadcast_bitcast_fusion) | data formatting | bytes 524288
  52.8 3.1 %all-to-all-done.2 = bf16[32,32,128]{2,1,0:T(8,128)(2,1)S(1)} async-done(((bf16[32,32,128]{2,1,0:T(8,128)(2,1)}), bf16[32,32,128]{2,1,0:T(8,128)(2,1)S(1)}, u32[]{:S(2)}, u32[]{:S(2)}) %all-to-all-start.2) | async-done | bytes 262176 | tf_op jit(solution)/shard_map/all_to_all | solution.py:79
  55.9 3.7 %all-to-all-start.3 = ((bf16[16,2,4096]{2,1,0:T(2,128)(2,1)}), bf16[16,2,4096]{2,1,0:T(2,128)(2,1)S(1)}, u32[]{:S(2)}, u32[]{:S(2)}) async-start(bf16[16,2,4096]{2,1,0:T(2,128)(2,1)} %reshape.295), calls=%async_computation.3 | async-start | bytes 524288 | tf_op jit(solution)/shard_map/all_to_all | solution.py:58
  61.6 0.6 fusion.192
  62.8 7.0 %all-to-all-done.3 = bf16[16,2,4096]{2,1,0:T(2,128)(2,1)S(1)} async-done(((bf16[16,2,4096]{2,1,0:T(2,128)(2,1)}), bf16[16,2,4096]{2,1,0:T(2,128)(2,1)S(1)}, u32[]{:S(2)}, u32[]{:S(2)}) %all-to-all-start.3) | async-done | bytes 262176 | tf_op jit(solution)/shard_map/all_to_all | solution.py:58
  70.8 1.4 %collective-permute-done.1 = bf16[16,64,4,32]{1,3,2,0:T(8,128)(2,1)S(1)} collective-permute-done((bf16[16,64,4,32]{1,3,2,0:T(8,128)(2,1)S(1)}, bf16[16,64,4,32]{1,3,2,0:T(8,128)(2,1)S(1)}, u32[]{:S(2)}, u32[]{:S(2)}) %collective-permute-start.1) | collective-permute-done | bytes 262176 | tf_op jit(solution)/shard_map/ppermute | solution.py:59
  72.5 1.1 %copy.289 = bf16[64,128,32]{1,0,2:T(8,128)(2,1)S(1)} copy(bf16[64,128,32]{0,2,1:T(8,128)(2,1)S(1)} %bitcast.261) | data formatting | bytes 1048576 | tf_op jit(solution)/shard_map/reshape | solution.py:68
  73.6 1.3 %divide_convert_fusion = bf16[4,32,128,32]{2,1,3,0:T(8,128)(2,1)S(1)} fusion(f32[]{:T(128)} %get-tuple-element.18, bf16[64,128,32]{1,0,2:T(8,128)(2,1)S(1)} %copy.289, bf16[64,4,256]{2,0,1:T(8,128)(2,1)S(1)} %get-tuple-element.21, f32[64,4]{0,1:T(4,128)S(1)} %add_rsqrt_fusion.2, f32[64,4]{0,1:T(4,128)S(1)} %broadcast_multiply_fusion.2, ...), kind=kOutput, calls=%fused_computation.4 | convolution fusion | flops 72630272 | bytes 1722628 | tf_op jit(solution)/shard_map/sic,sje->ijce/dot_general | solution.py:156
  76.1 0.8 copy.292
  (142 shorter events, 16.5 us)
Async XLA Ops:
  0.6 74.4 %copy-start = (bf16[1024,128]{1,0:T(8,128)(2,1)S(1)}, bf16[1024,128]{1,0:T(8,128)(2,1)}, u32[]{:S(2)}) copy-start(bf16[1024,128]{1,0:T(8,128)(2,1)} %param.35) | copy-start | bytes 786436
  0.6 12.7 %copy-start.2 = (bf16[2,128,256]{2,1,0:T(8,128)(2,1)S(1)}, bf16[2,128,256]{2,1,0:T(8,128)(2,1)}, u32[]{:S(2)}) copy-start(bf16[2,128,256]{2,1,0:T(8,128)(2,1)} %param.18) | copy-start | bytes 393220
  0.7 13.1 %copy-start.11 = (bf16[4,256,256]{2,1,0:T(8,128)(2,1)S(1)}, bf16[4,256,256]{2,1,0:T(8,128)(2,1)}, u32[]{:S(2)}) copy-start(bf16[4,256,256]{2,1,0:T(8,128)(2,1)} %param.22) | copy-start | bytes 1572868
  4.9 9.6 %copy-start.1 = (bf16[4,128,128]{2,1,0:T(8,128)(2,1)S(1)}, bf16[4,128,128]{2,1,0:T(8,128)(2,1)}, u32[]{:S(2)}) copy-start(bf16[4,128,128]{2,1,0:T(8,128)(2,1)} %param.19) | copy-start | bytes 393220
  4.9 17.1 %all-to-all-start = ((bf16[16,12,4,128]{3,2,1,0:T(4,128)(2,1)}), bf16[16,12,4,128]{3,2,1,0:T(4,128)(2,1)S(1)}, u32[]{:S(2)}, u32[]{:S(2)}) async-start(bf16[16,12,4,128]{3,2,1,0:T(4,128)(2,1)} %broadcast_in_dim.8), calls=%async_computation | async-start | bytes 393216 | tf_op jit(solution)/shard_map/all_to_all | solution.py:58
  13.4 1.6 %copy-start.6 = (bf16[4,128,128]{2,1,0:T(8,128)(2,1)S(1)}, bf16[4,128,128]{2,1,0:T(8,128)(2,1)}, u32[]{:S(2)}) copy-start(bf16[4,128,128]{2,1,0:T(8,128)(2,1)} %param.27) | copy-start | bytes 393220
  13.7 0.8 %copy-start.8 = (f32[2,128]{1,0:T(2,128)}, f32[2,128]{1,0:T(2,128)S(1)}, u32[]{:S(2)}) copy-start(f32[2,128]{1,0:T(2,128)S(1)} %add_rsqrt_fusion.6) | copy-start | bytes 3076
  14.3 3.1 %copy-start.19 = (s32[64]{0:T(128)S(1)}, s32[64]{0:T(128)}, u32[]{:S(2)}) copy-start(s32[64]{0:T(128)} %param.20) | copy-start | bytes 772
  14.9 7.2 %copy-start.20 = (s32[128]{0:T(128)S(1)}, s32[128]{0:T(128)}, u32[]{:S(2)}) copy-start(s32[128]{0:T(128)} %param.21) | copy-start | bytes 1540
  22.1 1.5 %collective-permute-start = (bf16[16,12,4,128]{3,0,2,1:T(8,128)(2,1)S(1)}, bf16[16,12,4,128]{3,0,2,1:T(8,128)(2,1)S(1)}, u32[]{:S(2)}, u32[]{:S(2)}) collective-permute-start(bf16[16,12,4,128]{3,0,2,1:T(8,128)(2,1)S(1)} %copy.331), channel_id=1, source_target_pairs={{0,1},{1,0},{2,3},{3,2},{4,5},{5,4},{6,7},{7,6},{8,9},{9,8},{10,11... | collective-permute-start | bytes 589832 | tf_op jit(solution)/shard_map/ppermute | solution.py:59
  27.1 0.9 %copy-start.5 = (bf16[2,128,256]{1,2,0:T(8,128)(2,1)S(1)}, bf16[2,128,256]{1,2,0:T(8,128)(2,1)}, u32[]{:S(2)}) copy-start(bf16[2,128,256]{1,2,0:T(8,128)(2,1)} %copy.235) | copy-start | bytes 393220
  27.1 0.9 %copy-start.22 = (f32[2,8,128]{2,1,0:T(8,128)S(1)}, f32[2,8,128]{2,1,0:T(8,128)}, u32[]{:S(2)}) copy-start(f32[2,8,128]{2,1,0:T(8,128)} %fusion.181) | copy-start | bytes 24580
  28.0 0.7 copy-start.9
  28.0 0.9 %copy-start.12 = (bf16[256,256]{1,0:T(8,128)(2,1)S(1)}, bf16[256,256]{1,0:T(8,128)(2,1)}, u32[]{:S(2)}) copy-start(bf16[256,256]{1,0:T(8,128)(2,1)} %param.24) | copy-start | bytes 393220
  28.9 5.6 %copy-start.4 = (bf16[4,128,128]{1,2,0:T(8,128)(2,1)S(1)}, bf16[4,128,128]{1,2,0:T(8,128)(2,1)}, u32[]{:S(2)}) copy-start(bf16[4,128,128]{1,2,0:T(8,128)(2,1)} %convolution_convert_fusion.5) | copy-start | bytes 393220
  31.0 11.7 %all-to-all-start.1 = ((bf16[2,128,256]{2,0,1:T(2,128)(2,1)}), bf16[2,128,256]{2,0,1:T(2,128)(2,1)S(1)}, u32[]{:S(2)}, u32[]{:S(2)}) async-start(bf16[2,128,256]{2,0,1:T(2,128)(2,1)} %copy.247), calls=%async_computation.1 | async-start | bytes 262144 | tf_op jit(solution)/shard_map/all_to_all | solution.py:126
  34.5 0.8 copy-start.14
  34.8 2.0 %copy-start.18 = (bf16[128,4]{0,1:T(4,128)(2,1)S(1)}, bf16[128,4]{0,1:T(4,128)(2,1)}, u32[]{:S(2)}) copy-start(bf16[128,4]{0,1:T(4,128)(2,1)} %param.31) | copy-start | bytes 3076
  42.7 13.2 %all-to-all-start.2 = ((bf16[32,32,128]{2,1,0:T(8,128)(2,1)}), bf16[32,32,128]{2,1,0:T(8,128)(2,1)S(1)}, u32[]{:S(2)}, u32[]{:S(2)}) async-start(bf16[32,32,128]{2,1,0:T(8,128)(2,1)} %copy.271), calls=%async_computation.2 | async-start | bytes 524288 | tf_op jit(solution)/shard_map/all_to_all | solution.py:79
  45.7 1.1 %copy-start.3 = (bf16[4,256,256]{2,1,0:T(8,128)(2,1)S(1)}, bf16[4,256,256]{2,1,0:T(8,128)(2,1)}, u32[]{:S(2)}) copy-start(bf16[4,256,256]{2,1,0:T(8,128)(2,1)} %param.25) | copy-start | bytes 1572868
  47.0 0.9 %copy-start.10 = (f32[64]{0:T(128)S(1)}, f32[64]{0:T(128)}, u32[]{:S(2)}) copy-start(f32[64]{0:T(128)} %get-tuple-element.19) | copy-start | bytes 772
  49.0 0.9 %copy-start.13 = (bf16[256,256]{1,0:T(8,128)(2,1)S(1)}, bf16[256,256]{1,0:T(8,128)(2,1)}, u32[]{:S(2)}) copy-start(bf16[256,256]{1,0:T(8,128)(2,1)} %param.26) | copy-start | bytes 393220
  49.9 1.5 %copy-start.16 = (bf16[256,32]{0,1:T(8,128)(2,1)S(1)}, bf16[256,32]{0,1:T(8,128)(2,1)}, u32[]{:S(2)}) copy-start(bf16[256,32]{0,1:T(8,128)(2,1)} %param.33) | copy-start | bytes 49156
  49.9 1.5 %copy-start.21 = (f32[64]{0:T(128)S(1)}, f32[64]{0:T(128)}, u32[]{:S(2)}) copy-start(f32[64]{0:T(128)} %convert_element_type.233) | copy-start | bytes 772
  52.8 8.1 %copy-start.7 = (bf16[4,128,128]{2,1,0:T(8,128)(2,1)S(1)}, bf16[4,128,128]{2,1,0:T(8,128)(2,1)}, u32[]{:S(2)}) copy-start(bf16[4,128,128]{2,1,0:T(8,128)(2,1)} %param.30) | copy-start | bytes 393220
  55.9 13.9 %all-to-all-start.3 = ((bf16[16,2,4096]{2,1,0:T(2,128)(2,1)}), bf16[16,2,4096]{2,1,0:T(2,128)(2,1)S(1)}, u32[]{:S(2)}, u32[]{:S(2)}) async-start(bf16[16,2,4096]{2,1,0:T(2,128)(2,1)} %reshape.295), calls=%async_computation.3 | async-start | bytes 524288 | tf_op jit(solution)/shard_map/all_to_all | solution.py:58
  70.2 2.0 %collective-permute-start.1 = (bf16[16,64,4,32]{1,3,2,0:T(8,128)(2,1)S(1)}, bf16[16,64,4,32]{1,3,2,0:T(8,128)(2,1)S(1)}, u32[]{:S(2)}, u32[]{:S(2)}) collective-permute-start(bf16[16,64,4,32]{1,3,2,0:T(8,128)(2,1)S(1)} %bitcast.262), channel_id=1, source_target_pairs={{0,1},{1,0},{2,3},{3,2},{4,5},{5,4},{6,7},{7,6},{8,9},{9,8},{10,11... | collective-permute-start | bytes 786440 | tf_op jit(solution)/shard_map/ppermute | solution.py:59
  72.5 1.1 %copy-start.17 = (bf16[256,32]{0,1:T(8,128)(2,1)S(1)}, bf16[256,32]{0,1:T(8,128)(2,1)}, u32[]{:S(2)}) copy-start(bf16[256,32]{0,1:T(8,128)(2,1)} %param.34) | copy-start | bytes 49156
  75.0 0.8 copy-start.15

commit v11 on v10

--- a/solution.py
+++ b/solution.py
@@ -110,17 +110,18 @@
 ):
     residue_keys = key_offsets(residue_mask)
     sequence_keys = key_offsets(sequence_mask)
-    both_maps = jnp.concatenate([row_bias_map, start_bias_map], axis=1)
-    both_local = jnp.einsum(
+    row_local = jnp.einsum(
         "icj,ch->hij",
         layer_norm(jnp.swapaxes(pairwise, 1, 2), axis=1),
-        both_maps,
+        row_bias_map,
         preferred_element_type=jnp.float32,
     ).astype(jnp.bfloat16)
+    row_bias = gather_blocks(row_local, 1, count)
     pair_norm = layer_norm(lax.optimization_barrier(pairwise))
-    both_bias = gather_blocks(both_local, 1, count)
-    row_bias = both_bias[:H_M]
-    start_bias = both_bias[H_M:]
+    start_local = jnp.einsum(
+        "ijc,ch->hij", pair_norm, start_bias_map, preferred_element_type=jnp.float32
+    ).astype(jnp.bfloat16)
+    start_bias = gather_blocks(start_local, 1, count)
     row_update = attend(layer_norm(alignment), row_project, row_bias, residue_keys, row_output, H_M)
     alignment_one = (alignment.astype(jnp.float32) + row_update).astype(jnp.bfloat16)
     alignment_cols = lax.all_to_all(alignment_one, DAP, 1, 0, tiled=True)

time: 77.6 us -> 85.8 us (1.11)
  waiting for transfers between devices: 20 us -> 25.1 us
  starting transfers between devices: 18.5 us -> 22.7 us
  local copies, waits for them, and re-layouts: 13.2 us -> 12.1 us
    all_to_all x2 -> x3, starting transfers between devices: 12.2 us -> 17.2 us  [gather_blocks(): same_core = lax.all_to_all(spread, 'chip', 0, 0, tiled=True)]
    all_to_all x2 -> x3, waiting for transfers between devices: 9.5 us -> 12.2 us  [gather_blocks(): same_core = lax.all_to_all(spread, 'chip', 0, 0, tiled=True)]
    all_to_all x1, waiting for transfers between devices: 4.67 us -> 7 us  [per_device(): alignment_cols = lax.all_to_all(alignment_one, DAP, 1, 0, tiled=True)]
    dot_general x0 -> x1, matrix products: none -> 1.29 us  [per_device(): jnp.einsum('ijc,ch->hij', pair_norm, start_bias_map, preferred_element_ty...]
    dot_general x1, matrix products: 1.26 us -> 0.32 us  [per_device(): jnp.einsum('icj,ch->hij', layer_norm(jnp.swapaxes(pairwise, 1, 2), axis=1...]
    reduce_sum x5, other arithmetic: 1.6 us -> 2.51 us  [layer_norm(): center = widened - jnp.mean(widened, axis=axis, keepdims=True)]
    reduce_sum x7, other arithmetic: 2.5 us -> 3.4 us  [layer_norm(): spread = jnp.mean(center * center, axis=axis, keepdims=True)]
    all_to_all x1, starting transfers between devices: 3.44 us -> 2.58 us  [per_device(): alignment_cols = lax.all_to_all(alignment_one, DAP, 1, 0, tiled=True)]
  transfers between devices with their start and end apart: 6 -> 8, of which waited for: 6 -> 8; matrix products, arithmetic and copies ran while one was open for 25% -> 25% of each run, Pallas kernels for 0% -> 0%
where the time goes in v11:
time: 85.8 us; the launch traced here: 85 us
  waiting for transfers between devices  25.1 us (29%)
  starting transfers between devices  22.7 us (26%)
  matrix products  16 us (19%)
  local copies, waits for them, and re-layouts  12.1 us (14%)
  other arithmetic  7.67 us (9%)
  between operations  1.42 us (2%)
    all_to_all x3, starting transfers between devices, gather_blocks(): same_core = lax.all_to_all(spread, 'chip', 0, 0, tiled=True)  17.2 us
    all_to_all x3, waiting for transfers between devices, gather_blocks(): same_core = lax.all_to_all(spread, 'chip', 0, 0, tiled=True)  12.2 us
    all_to_all x1, waiting for transfers between devices, per_device(): alignment_cols = lax.all_to_all(alignment_one, DAP, 1, 0, tiled=True)  7 us
    unnamed x42, local copies, waits for them, and re-layouts  4.61 us
    dot_general x12, matrix products, project(): jnp.einsum('bqc,cf->bqf', inputs, weight_table, preferred_element_type=jn...  4.3 us
    reduce_sum x7, other arithmetic, layer_norm(): spread = jnp.mean(center * center, axis=axis, keepdims=True)  3.4 us
    all_to_all x1, waiting for transfers between devices, exchange_pair(): lax.all_to_all(jnp.concatenate([pair_part, end_part], axis=1), DAP, 0, 0,...  3.1 us
    ppermute x3, waiting for transfers between devices, gather_blocks(): other_core = lax.ppermute(same_core, 'core', [(0, 1), (1, 0)])  2.87 us
  transfers between devices with their start and end apart: 8, of which 8 were waited for; matrix products, arithmetic and copies ran while one was open for 25% of the time, Pallas kernels for 0%

profile of v11, /device:TPU:0, one launch (start us, length us, event | category | flops | bytes accessed | tf_op | source)
XLA Modules:
  0.0 85.0 jit_solution(1963338081948643979)
XLA Ops:
  0.7 1.1 %convert_reduce_fusion.3 = f32[4,128]{1,0:T(4,128)S(1)} fusion(bf16[4,128,128]{2,1,0:T(8,128)(2,1)} %param.19), kind=kLoop, calls=%fused_computation.102 | loop fusion | flops 130560 | bytes 133120 | tf_op jit(solution)/shard_map/reduce_sum | solution.py:19
  1.8 1.1 %fusion.77 = f32[4,128]{1,0:T(4,128)S(1)} fusion(bf16[4,128,128]{2,1,0:T(8,128)(2,1)} %param.19, f32[4,128]{1,0:T(4,128)S(1)} %broadcast_multiply_fusion.4), kind=kLoop, calls=%fused_computation.121 | loop fusion | flops 261632 | bytes 135168 | tf_op jit(solution)/shard_map/reduce_sum | solution.py:20
  2.9 1.3 %fusion.50 = bf16[4,4,128]{2,0,1:T(4,128)(2,1)S(1)} fusion(bf16[128,4]{0,1:T(4,128)(2,1)} %param.28, bf16[4,128,128]{2,1,0:T(8,128)(2,1)} %param.19, f32[4,128]{1,0:T(4,128)S(1)} %add_rsqrt_fusion.4, f32[4,128]{1,0:T(4,128)S(1)} %broadcast_multiply_fusion.4), kind=kOutput, calls=%fused_computation.80 | convolution fusion | flops 788480 | bytes 140288 | tf_op jit(solution)/shard_map/ijc,ch->hij/dot_general | solution.py:121
  4.3 0.7 broadcast_in_dim.11
  4.9 8.3 %all-to-all-start.2 = ((bf16[16,4,4,128]{3,2,1,0:T(4,128)(2,1)}), bf16[16,4,4,128]{3,2,1,0:T(4,128)(2,1)S(1)}, u32[]{:S(2)}, u32[]{:S(2)}) async-start(bf16[16,4,4,128]{3,2,1,0:T(4,128)(2,1)} %broadcast_in_dim.11), calls=%async_computation.2 | async-start | bytes 131072 | tf_op jit(solution)/shard_map/all_to_all | solution.py:58
  13.2 1.0 %convert_reduce_fusion = f32[2,128]{1,0:T(2,128)S(1)} fusion(bf16[2,128,256]{2,1,0:T(8,128)(2,1)} %param.18), kind=kLoop, calls=%fused_computation.93 | loop fusion | flops 130816 | bytes 132096 | tf_op jit(solution)/shard_map/reduce_sum | solution.py:19
  14.3 1.1 %fusion.69 = f32[2,128]{1,0:T(2,128)S(1)} fusion(bf16[2,128,256]{2,1,0:T(8,128)(2,1)} %param.18, f32[2,128]{1,0:T(2,128)S(1)} %broadcast_multiply_fusion.6), kind=kLoop, calls=%fused_computation.113 | loop fusion | flops 261888 | bytes 133120 | tf_op jit(solution)/shard_map/reduce_sum | solution.py:20
  15.4 1.2 %convolution_convert_fusion.11 = bf16[2,128,256]{2,1,0:T(8,128)(2,1)S(1)} fusion(bf16[4,256,256]{2,1,0:T(8,128)(2,1)} %param.22, bf16[2,128,256]{2,1,0:T(8,128)(2,1)} %param.18, f32[2,128]{1,0:T(2,128)S(1)} %add_rsqrt_fusion.6, f32[2,128]{1,0:T(2,128)S(1)} %broadcast_multiply_fusion.6), kind=kOutput, calls=%fused_computation.70 | convolution fusion | flops 33882112 | bytes 395264 | tf_op jit(solution)/shard_map/bqc,cf->bqf/dot_general | solution.py:29
  19.0 1.7 %all-to-all-done.2 = bf16[16,4,4,128]{3,2,1,0:T(4,128)(2,1)S(1)} async-done(((bf16[16,4,4,128]{3,2,1,0:T(4,128)(2,1)}), bf16[16,4,4,128]{3,2,1,0:T(4,128)(2,1)S(1)}, u32[]{:S(2)}, u32[]{:S(2)}) %all-to-all-start.2) | async-done | bytes 65568 | tf_op jit(solution)/shard_map/all_to_all | solution.py:58
  20.8 0.7 broadcast_in_dim.10
  21.4 5.2 %all-to-all-start = ((bf16[16,8,4,128]{3,1,2,0:T(8,128)(2,1)}), bf16[16,8,4,128]{3,1,2,0:T(8,128)(2,1)S(1)}, u32[]{:S(2)}, u32[]{:S(2)}) async-start(bf16[16,8,4,128]{3,1,2,0:T(8,128)(2,1)} %broadcast_in_dim.10), calls=%async_computation | async-start | bytes 262144 | tf_op jit(solution)/shard_map/all_to_all | solution.py:58
  26.8 0.7 convert_reduce_fusion.4
  28.5 0.6 fusion.190
  31.0 3.4 %all-to-all-done = bf16[16,8,4,128]{3,1,2,0:T(8,128)(2,1)S(1)} async-done(((bf16[16,8,4,128]{3,1,2,0:T(8,128)(2,1)}), bf16[16,8,4,128]{3,1,2,0:T(8,128)(2,1)S(1)}, u32[]{:S(2)}, u32[]{:S(2)}) %all-to-all-start) | async-done | bytes 131104 | tf_op jit(solution)/shard_map/all_to_all | solution.py:58
  34.4 1.3 %collective-permute-done = bf16[16,8,4,128]{3,1,2,0:T(8,128)(2,1)S(1)} collective-permute-done((bf16[16,8,4,128]{3,1,2,0:T(8,128)(2,1)S(1)}, bf16[16,8,4,128]{3,1,2,0:T(8,128)(2,1)S(1)}, u32[]{:S(2)}, u32[]{:S(2)}) %collective-permute-start) | collective-permute-done | bytes 131104 | tf_op jit(solution)/shard_map/ppermute | solution.py:59
  38.0 1.3 %fusion.44 = bf16[2,128,256]{2,1,0:T(8,128)(2,1)S(1)} fusion(f32[2,128,256]{2,1,0:T(8,128)S(1)} %copy.238, bf16[2,128,256]{2,1,0:T(8,128)(2,1)S(1)} %copy-done.2, bf16[256,256]{1,0:T(8,128)(2,1)S(1)} %copy-done.7, bf16[4,256,256]{2,1,0:T(8,128)(2,1)} %param.22, f32[2,128]{1,0:T(2,128)S(1)} %add_rsqrt_fusion.6, f32[2,128]{1,0:T(2,128)S(1)} %broadcast_multiply_fusion.6), kind=kOutput, calls=%fused_computation.57 | convolution fusion | flops 67895296 | bytes 919552 | tf_op jit(solution)/shard_map/bqf,fc->bqc/dot_general | solution.py:52
  39.3 0.8 copy.239
  40.1 2.6 %all-to-all-start.1 = ((bf16[2,128,256]{2,0,1:T(2,128)(2,1)}), bf16[2,128,256]{2,0,1:T(2,128)(2,1)S(1)}, u32[]{:S(2)}, u32[]{:S(2)}) async-start(bf16[2,128,256]{2,0,1:T(2,128)(2,1)} %copy.239), calls=%async_computation.1 | async-start | bytes 262144 | tf_op jit(solution)/shard_map/all_to_all | solution.py:127
  43.1 0.8 copy.267
  43.9 7.0 %all-to-all-done.1 = bf16[2,128,256]{2,0,1:T(2,128)(2,1)S(1)} async-done(((bf16[2,128,256]{2,0,1:T(2,128)(2,1)}), bf16[2,128,256]{2,0,1:T(2,128)(2,1)S(1)}, u32[]{:S(2)}, u32[]{:S(2)}) %all-to-all-start.1) | async-done | bytes 131104 | tf_op jit(solution)/shard_map/all_to_all | solution.py:127
  50.9 2.8 %all-to-all-start.3 = ((bf16[32,32,128]{2,1,0:T(8,128)(2,1)}), bf16[32,32,128]{2,1,0:T(8,128)(2,1)S(1)}, u32[]{:S(2)}, u32[]{:S(2)}) async-start(bf16[32,32,128]{2,1,0:T(8,128)(2,1)} %copy.267), calls=%async_computation.3 | async-start | bytes 524288 | tf_op jit(solution)/shard_map/all_to_all | solution.py:79
  56.0 0.6 fusion.185
  58.7 0.8 copy.287
  59.9 1.1 %reshape.307 = bf16[16,2,4096]{2,1,0:T(2,128)(2,1)} reshape(bf16[16,4,32,64]{3,2,1,0:T(8,128)(2,1)S(1)} %broadcast_bitcast_fusion) | data formatting | bytes 524288
  61.0 3.1 %all-to-all-done.3 = bf16[32,32,128]{2,1,0:T(8,128)(2,1)S(1)} async-done(((bf16[32,32,128]{2,1,0:T(8,128)(2,1)}), bf16[32,32,128]{2,1,0:T(8,128)(2,1)S(1)}, u32[]{:S(2)}, u32[]{:S(2)}) %all-to-all-start.3) | async-done | bytes 262176 | tf_op jit(solution)/shard_map/all_to_all | solution.py:79
  64.1 3.7 %all-to-all-start.4 = ((bf16[16,2,4096]{2,1,0:T(2,128)(2,1)}), bf16[16,2,4096]{2,1,0:T(2,128)(2,1)S(1)}, u32[]{:S(2)}, u32[]{:S(2)}) async-start(bf16[16,2,4096]{2,1,0:T(2,128)(2,1)} %reshape.307), calls=%async_computation.4 | async-start | bytes 524288 | tf_op jit(solution)/shard_map/all_to_all | solution.py:58
  69.8 0.6 fusion.195
  70.9 7.0 %all-to-all-done.4 = bf16[16,2,4096]{2,1,0:T(2,128)(2,1)S(1)} async-done(((bf16[16,2,4096]{2,1,0:T(2,128)(2,1)}), bf16[16,2,4096]{2,1,0:T(2,128)(2,1)S(1)}, u32[]{:S(2)}, u32[]{:S(2)}) %all-to-all-start.4) | async-done | bytes 262176 | tf_op jit(solution)/shard_map/all_to_all | solution.py:58
  78.9 1.4 %collective-permute-done.2 = bf16[16,64,4,32]{1,3,2,0:T(8,128)(2,1)S(1)} collective-permute-done((bf16[16,64,4,32]{1,3,2,0:T(8,128)(2,1)S(1)}, bf16[16,64,4,32]{1,3,2,0:T(8,128)(2,1)S(1)}, u32[]{:S(2)}, u32[]{:S(2)}) %collective-permute-start.2) | collective-permute-done | bytes 262176 | tf_op jit(solution)/shard_map/ppermute | solution.py:59
  80.7 1.1 %copy.285 = bf16[64,128,32]{1,0,2:T(8,128)(2,1)S(1)} copy(bf16[64,128,32]{0,2,1:T(8,128)(2,1)S(1)} %bitcast.275) | data formatting | bytes 1048576 | tf_op jit(solution)/shard_map/reshape | solution.py:68
  81.8 1.3 %divide_convert_fusion = bf16[4,32,128,32]{2,1,3,0:T(8,128)(2,1)S(1)} fusion(f32[]{:T(128)} %get-tuple-element.18, bf16[64,128,32]{1,0,2:T(8,128)(2,1)S(1)} %copy.285, bf16[64,4,256]{2,0,1:T(8,128)(2,1)S(1)} %get-tuple-element.21, f32[64,4]{0,1:T(4,128)S(1)} %add_rsqrt_fusion.2, f32[64,4]{0,1:T(4,128)S(1)} %broadcast_multiply_fusion.2, ...), kind=kOutput, calls=%fused_computation.4 | convolution fusion | flops 72630272 | bytes 1722628 | tf_op jit(solution)/shard_map/sic,sje->ijce/dot_general | solution.py:157
  84.2 0.8 copy.288
  (135 shorter events, 17.5 us)
Async XLA Ops:
  0.6 82.5 %copy-start = (bf16[1024,128]{1,0:T(8,128)(2,1)S(1)}, bf16[1024,128]{1,0:T(8,128)(2,1)}, u32[]{:S(2)}) copy-start(bf16[1024,128]{1,0:T(8,128)(2,1)} %param.35) | copy-start | bytes 786436
  0.6 15.9 %copy-start.2 = (bf16[2,128,256]{2,1,0:T(8,128)(2,1)S(1)}, bf16[2,128,256]{2,1,0:T(8,128)(2,1)}, u32[]{:S(2)}) copy-start(bf16[2,128,256]{2,1,0:T(8,128)(2,1)} %param.18) | copy-start | bytes 393220
  0.7 15.9 %copy-start.6 = (bf16[4,256,256]{2,1,0:T(8,128)(2,1)S(1)}, bf16[4,256,256]{2,1,0:T(8,128)(2,1)}, u32[]{:S(2)}) copy-start(bf16[4,256,256]{2,1,0:T(8,128)(2,1)} %param.22) | copy-start | bytes 1572868
  2.9 14.2 %copy-start.1 = (bf16[4,128,128]{2,1,0:T(8,128)(2,1)S(1)}, bf16[4,128,128]{2,1,0:T(8,128)(2,1)}, u32[]{:S(2)}) copy-start(bf16[4,128,128]{2,1,0:T(8,128)(2,1)} %param.19) | copy-start | bytes 393220
  4.2 13.1 %copy-start.4 = (bf16[4,128,128]{2,1,0:T(8,128)(2,1)S(1)}, bf16[4,128,128]{2,1,0:T(8,128)(2,1)}, u32[]{:S(2)}) copy-start(bf16[4,128,128]{2,1,0:T(8,128)(2,1)} %param.27) | copy-start | bytes 393220
  4.9 15.9 %all-to-all-start.2 = ((bf16[16,4,4,128]{3,2,1,0:T(4,128)(2,1)}), bf16[16,4,4,128]{3,2,1,0:T(4,128)(2,1)S(1)}, u32[]{:S(2)}, u32[]{:S(2)}) async-start(bf16[16,4,4,128]{3,2,1,0:T(4,128)(2,1)} %broadcast_in_dim.11), calls=%async_computation.2 | async-start | bytes 131072 | tf_op jit(solution)/shard_map/all_to_all | solution.py:58
  16.6 2.1 %copy-start.13 = (bf16[128,8]{0,1:T(8,128)(2,1)S(1)}, bf16[128,8]{0,1:T(8,128)(2,1)}, u32[]{:S(2)}) copy-start(bf16[128,8]{0,1:T(8,128)(2,1)} %param.23) | copy-start | bytes 6148
  16.9 2.2 %copy-start.15 = (s32[128]{0:T(128)S(1)}, s32[128]{0:T(128)}, u32[]{:S(2)}) copy-start(s32[128]{0:T(128)} %param.21) | copy-start | bytes 1540
  17.2 9.6 %copy-start.16 = (s32[64]{0:T(128)S(1)}, s32[64]{0:T(128)}, u32[]{:S(2)}) copy-start(s32[64]{0:T(128)} %param.20) | copy-start | bytes 772
  21.4 13.0 %all-to-all-start = ((bf16[16,8,4,128]{3,1,2,0:T(8,128)(2,1)}), bf16[16,8,4,128]{3,1,2,0:T(8,128)(2,1)S(1)}, u32[]{:S(2)}, u32[]{:S(2)}) async-start(bf16[16,8,4,128]{3,1,2,0:T(8,128)(2,1)} %broadcast_in_dim.10), calls=%async_computation | async-start | bytes 262144 | tf_op jit(solution)/shard_map/all_to_all | solution.py:58
  26.7 1.3 %collective-permute-start.1 = (bf16[16,4,4,128]{3,0,2,1:T(8,128)(2,1)S(1)}, bf16[16,4,4,128]{3,0,2,1:T(8,128)(2,1)S(1)}, u32[]{:S(2)}, u32[]{:S(2)}) collective-permute-start(bf16[16,4,4,128]{3,0,2,1:T(8,128)(2,1)S(1)} %copy.327), channel_id=1, source_target_pairs={{0,1},{1,0},{2,3},{3,2},{4,5},{5,4},{6,7},{7,6},{8,9},{9,8},{10,11... | collective-permute-start | bytes 196616 | tf_op jit(solution)/shard_map/ppermute | solution.py:59
  29.5 0.8 copy-start.9
  34.4 1.3 %collective-permute-start = (bf16[16,8,4,128]{3,1,2,0:T(8,128)(2,1)S(1)}, bf16[16,8,4,128]{3,1,2,0:T(8,128)(2,1)S(1)}, u32[]{:S(2)}, u32[]{:S(2)}) collective-permute-start(bf16[16,8,4,128]{3,1,2,0:T(8,128)(2,1)S(1)} %all-to-all-done), channel_id=1, source_target_pairs={{0,1},{1,0},{2,3},{3,2},{4,5},{5,4},{6,7},{7,6},{8,9},{9,8},{10,11... | collective-permute-start | bytes 393224 | tf_op jit(solution)/shard_map/ppermute | solution.py:59
  37.0 0.9 %copy-start.7 = (bf16[256,256]{1,0:T(8,128)(2,1)S(1)}, bf16[256,256]{1,0:T(8,128)(2,1)}, u32[]{:S(2)}) copy-start(bf16[256,256]{1,0:T(8,128)(2,1)} %param.24) | copy-start | bytes 393220
  38.0 4.7 %copy-start.14 = (bf16[128,4]{0,1:T(4,128)(2,1)S(1)}, bf16[128,4]{0,1:T(4,128)(2,1)}, u32[]{:S(2)}) copy-start(bf16[128,4]{0,1:T(4,128)(2,1)} %param.31) | copy-start | bytes 3076
  40.1 10.8 %all-to-all-start.1 = ((bf16[2,128,256]{2,0,1:T(2,128)(2,1)}), bf16[2,128,256]{2,0,1:T(2,128)(2,1)S(1)}, u32[]{:S(2)}, u32[]{:S(2)}) async-start(bf16[2,128,256]{2,0,1:T(2,128)(2,1)} %copy.239), calls=%async_computation.1 | async-start | bytes 262144 | tf_op jit(solution)/shard_map/all_to_all | solution.py:127
  50.9 13.2 %all-to-all-start.3 = ((bf16[32,32,128]{2,1,0:T(8,128)(2,1)}), bf16[32,32,128]{2,1,0:T(8,128)(2,1)S(1)}, u32[]{:S(2)}, u32[]{:S(2)}) async-start(bf16[32,32,128]{2,1,0:T(8,128)(2,1)} %copy.267), calls=%async_computation.3 | async-start | bytes 524288 | tf_op jit(solution)/shard_map/all_to_all | solution.py:79
  53.8 1.1 %copy-start.3 = (bf16[4,256,256]{2,1,0:T(8,128)(2,1)S(1)}, bf16[4,256,256]{2,1,0:T(8,128)(2,1)}, u32[]{:S(2)}) copy-start(bf16[4,256,256]{2,1,0:T(8,128)(2,1)} %param.25) | copy-start | bytes 1572868
  57.1 0.9 %copy-start.8 = (bf16[256,256]{1,0:T(8,128)(2,1)S(1)}, bf16[256,256]{1,0:T(8,128)(2,1)}, u32[]{:S(2)}) copy-start(bf16[256,256]{1,0:T(8,128)(2,1)} %param.26) | copy-start | bytes 393220
  58.0 1.5 %copy-start.11 = (bf16[256,32]{0,1:T(8,128)(2,1)S(1)}, bf16[256,32]{0,1:T(8,128)(2,1)}, u32[]{:S(2)}) copy-start(bf16[256,32]{0,1:T(8,128)(2,1)} %param.33) | copy-start | bytes 49156
  61.0 8.1 %copy-start.5 = (bf16[4,128,128]{2,1,0:T(8,128)(2,1)S(1)}, bf16[4,128,128]{2,1,0:T(8,128)(2,1)}, u32[]{:S(2)}) copy-start(bf16[4,128,128]{2,1,0:T(8,128)(2,1)} %param.30) | copy-start | bytes 393220
  64.1 13.9 %all-to-all-start.4 = ((bf16[16,2,4096]{2,1,0:T(2,128)(2,1)}), bf16[16,2,4096]{2,1,0:T(2,128)(2,1)S(1)}, u32[]{:S(2)}, u32[]{:S(2)}) async-start(bf16[16,2,4096]{2,1,0:T(2,128)(2,1)} %reshape.307), calls=%async_computation.4 | async-start | bytes 524288 | tf_op jit(solution)/shard_map/all_to_all | solution.py:58
  78.3 2.0 %collective-permute-start.2 = (bf16[16,64,4,32]{1,3,2,0:T(8,128)(2,1)S(1)}, bf16[16,64,4,32]{1,3,2,0:T(8,128)(2,1)S(1)}, u32[]{:S(2)}, u32[]{:S(2)}) collective-permute-start(bf16[16,64,4,32]{1,3,2,0:T(8,128)(2,1)S(1)} %bitcast.276), channel_id=1, source_target_pairs={{0,1},{1,0},{2,3},{3,2},{4,5},{5,4},{6,7},{7,6},{8,9},{9,8},{10,11... | collective-permute-start | bytes 786440 | tf_op jit(solution)/shard_map/ppermute | solution.py:59
  80.6 1.1 %copy-start.12 = (bf16[256,32]{0,1:T(8,128)(2,1)S(1)}, bf16[256,32]{0,1:T(8,128)(2,1)}, u32[]{:S(2)}) copy-start(bf16[256,32]{0,1:T(8,128)(2,1)} %param.34) | copy-start | bytes 49156
  83.1 0.8 copy-start.10

commit v12 on v6

--- a/solution.py
+++ b/solution.py
@@ -149,19 +149,34 @@
         * weighting
     ).astype(jnp.bfloat16)
     row_count = jnp.sum(sequence_mask.astype(jnp.float32))
-    outer_sum = (
-        jnp.einsum(
-            "sic,sje->ijce",
-            gather_blocks(left, 1, count),
-            right,
-            preferred_element_type=jnp.float32,
+    half = count // 2
+    same_core = lax.all_to_all(
+        jnp.broadcast_to(left[None], (half,) + left.shape), "chip", 0, 0, tiled=True
+    )
+    other_core = lax.ppermute(same_core, "core", [(0, 1), (1, 0)])
+
+    def outer_rows(received):
+        gathered = jnp.moveaxis(received, 0, 1).reshape(
+            left.shape[0], half * left.shape[1], left.shape[2]
         )
-        / row_count
-    )
-    flattened = outer_sum.astype(jnp.bfloat16).reshape(outer_sum.shape[0], outer_sum.shape[1], -1)
-    outer_update = jnp.einsum(
-        "ijf,fc->ijc", flattened, outer_output, preferred_element_type=jnp.float32
-    )
+        outer_sum = (
+            jnp.einsum("sic,sje->ijce", gathered, right, preferred_element_type=jnp.float32)
+            / row_count
+        )
+        flattened = outer_sum.astype(jnp.bfloat16).reshape(
+            outer_sum.shape[0], outer_sum.shape[1], -1
+        )
+        rows = jnp.einsum("ijf,fc->ijc", flattened, outer_output, preferred_element_type=jnp.float32)
+        return rows.reshape((half, left.shape[1]) + rows.shape[1:])
+
+    own_rows = outer_rows(same_core)
+    partner_rows = outer_rows(other_core)
+    first = lax.axis_index("core") == 0
+    outer_update = jnp.where(
+        first,
+        jnp.stack([own_rows, partner_rows], axis=1),
+        jnp.stack([partner_rows, own_rows], axis=1),
+    ).reshape(pair_cols.shape)
     pairwise_out = (pair_cols.astype(jnp.float32) + end_update + outer_update).astype(jnp.bfloat16)
     return (alignment_out, pairwise_out)
 

time: 77.2 us -> 97 us (1.26)
  local copies, waits for them, and re-layouts: 13.2 us -> 25 us
  matrix products: 16.7 us -> 24 us
  waiting for transfers between devices: 20.4 us -> 15.5 us
  starting transfers between devices: 18.2 us -> 21.1 us
  other arithmetic: 6.61 us -> 8.96 us
    all_to_all x2 -> x1, waiting for transfers between devices: 9.89 us -> 0.01 us  [gather_blocks(): same_core = lax.all_to_all(spread, 'chip', 0, 0, tiled=True)]
    convert_element_type x0 -> x2, local copies, waits for them, and re-layouts: none -> 7.43 us  [outer_rows(): outer_sum.astype(jnp.bfloat16)]
    all_to_all x0 -> x1, waiting for transfers between devices: none -> 5.85 us  [per_device(): lax.all_to_all(jnp.broadcast_to(left[None], (half,) + left.shape), 'chip'...]
    another operation x1 -> x2, local copies, waits for them, and re-layouts: 0.04 us -> 4.24 us  [gather_blocks(): jnp.stack([same_core, other_core], axis=1)]
    all_to_all x0 -> x1, starting transfers between devices: none -> 3.9 us  [per_device(): lax.all_to_all(jnp.broadcast_to(left[None], (half,) + left.shape), 'chip'...]
    dot_general x2 -> x5, matrix products: 1.81 us -> 5.56 us  [the longest x2 3.81 us: outer_rows(): jnp.einsum('sic,sje->ijce', gathered, right, preferred_element_type=jnp.f...]
    all_to_all x2 -> x1, starting transfers between devices: 12.2 us -> 8.44 us  [gather_blocks(): same_core = lax.all_to_all(spread, 'chip', 0, 0, tiled=True)]
    all_to_all x1, starting transfers between devices: 3.06 us -> 5.89 us  [per_device(): alignment_cols = lax.all_to_all(alignment_one, DAP, 1, 0, tiled=True)]
  transfers between devices with their start and end apart: 6 -> 6, of which waited for: 6 -> 4; matrix products, arithmetic and copies ran while one was open for 25% -> 34% of each run, Pallas kernels for 0% -> 0%
where the time goes in v12:
time: 97 us; the launch traced here: 96 us
  local copies, waits for them, and re-layouts  25 us (26%)
  matrix products  24 us (25%)
  starting transfers between devices  21.1 us (22%)
  waiting for transfers between devices  15.5 us (16%)
  other arithmetic  8.96 us (9%)
  between operations  1.53 us (2%)
    all_to_all x1, starting transfers between devices, gather_blocks(): same_core = lax.all_to_all(spread, 'chip', 0, 0, tiled=True)  8.44 us
    convert_element_type x2, local copies, waits for them, and re-layouts, outer_rows(): outer_sum.astype(jnp.bfloat16)  7.43 us
    dot_general x12, matrix products, project(): jnp.einsum('bqc,cf->bqf', inputs, weight_table, preferred_element_type=jn...  6.16 us
    all_to_all x1, starting transfers between devices, per_device(): alignment_cols = lax.all_to_all(alignment_one, DAP, 1, 0, tiled=True)  5.89 us
    all_to_all x1, waiting for transfers between devices, per_device(): lax.all_to_all(jnp.broadcast_to(left[None], (half,) + left.shape), 'chip'...  5.85 us
    all_to_all x1, waiting for transfers between devices, per_device(): alignment_cols = lax.all_to_all(alignment_one, DAP, 1, 0, tiled=True)  5.41 us
    another operation x2, local copies, waits for them, and re-layouts  4.24 us
    unnamed x50, local copies, waits for them, and re-layouts  3.93 us
  transfers between devices with their start and end apart: 6, of which 4 were waited for; matrix products, arithmetic and copies ran while one was open for 34% of the time, Pallas kernels for 0%

profile of v12, /device:TPU:0, one launch (start us, length us, event | category | flops | bytes accessed | tf_op | source)
XLA Modules:
  0.0 96.0 jit_solution(16617023224163425565)
XLA Ops:
  0.7 1.1 %convert_reduce_fusion = f32[4,128]{1,0:T(4,128)S(1)} fusion(bf16[4,128,128]{2,1,0:T(8,128)(2,1)} %param.19), kind=kLoop, calls=%fused_computation.98 | loop fusion | flops 130560 | bytes 133120 | tf_op jit(solution)/shard_map/reduce_sum | solution.py:19
  1.8 1.1 %fusion.68 = f32[4,128]{1,0:T(4,128)S(1)} fusion(bf16[4,128,128]{2,1,0:T(8,128)(2,1)} %param.19, f32[4,128]{1,0:T(4,128)S(1)} %broadcast_multiply_fusion.4), kind=kLoop, calls=%fused_computation.113 | loop fusion | flops 261632 | bytes 135168 | tf_op jit(solution)/shard_map/reduce_sum | solution.py:20
  3.0 1.3 %convolution_convert_fusion.12 = bf16[12,4,128]{2,0,1:T(8,128)(2,1)S(1)} fusion(bf16[4,128,128]{2,1,0:T(8,128)(2,1)} %param.19, f32[4,128]{1,0:T(4,128)S(1)} %add_rsqrt_fusion.4, f32[4,128]{1,0:T(4,128)S(1)} %broadcast_multiply_fusion.4, bf16[128,4]{0,1:T(4,128)(2,1)} %param.28, bf16[128,8]{0,1:T(8,128)(2,1)} %param.23), kind=kOutput, calls=%fused_computation.81 | convolution fusion | flops 1847296 | bytes 150528 | tf_op jit(solution)/shard_map/ijc,ch->hij/dot_general | solution.py:115
  5.0 8.4 %all-to-all-start = ((bf16[16,12,4,128]{3,2,1,0:T(4,128)(2,1)}), bf16[16,12,4,128]{3,2,1,0:T(4,128)(2,1)S(1)}, u32[]{:S(2)}, u32[]{:S(2)}) async-start(bf16[16,12,4,128]{3,2,1,0:T(4,128)(2,1)} %broadcast_in_dim.8), calls=%async_computation | async-start | bytes 393216 | tf_op jit(solution)/shard_map/all_to_all | solution.py:58
  13.4 1.0 %convert_reduce_fusion.1 = f32[2,128]{1,0:T(2,128)S(1)} fusion(bf16[2,128,256]{2,1,0:T(8,128)(2,1)} %param.18), kind=kLoop, calls=%fused_computation.100 | loop fusion | flops 130816 | bytes 132096 | tf_op jit(solution)/shard_map/reduce_sum | solution.py:19
  14.5 1.1 %fusion.70 = f32[2,128]{1,0:T(2,128)S(1)} fusion(bf16[2,128,256]{2,1,0:T(8,128)(2,1)} %param.18, f32[2,128]{1,0:T(2,128)S(1)} %broadcast_multiply_fusion.5), kind=kLoop, calls=%fused_computation.115 | loop fusion | flops 261888 | bytes 133120 | tf_op jit(solution)/shard_map/reduce_sum | solution.py:20
  15.6 1.2 %convolution_convert_fusion.11 = bf16[2,128,256]{2,1,0:T(8,128)(2,1)S(1)} fusion(bf16[4,256,256]{2,1,0:T(8,128)(2,1)} %param.22, bf16[2,128,256]{2,1,0:T(8,128)(2,1)} %param.18, f32[2,128]{1,0:T(2,128)S(1)} %add_rsqrt_fusion.5, f32[2,128]{1,0:T(2,128)S(1)} %broadcast_multiply_fusion.5), kind=kOutput, calls=%fused_computation.73 | convolution fusion | flops 33882112 | bytes 395264 | tf_op jit(solution)/shard_map/bqc,cf->bqf/dot_general | solution.py:29
  16.8 1.2 %convolution_convert_fusion.10 = bf16[2,128,256]{2,1,0:T(8,128)(2,1)S(1)} fusion(bf16[4,256,256]{2,1,0:T(8,128)(2,1)} %param.22, bf16[2,128,256]{2,1,0:T(8,128)(2,1)} %param.18, f32[2,128]{1,0:T(2,128)S(1)} %add_rsqrt_fusion.5, f32[2,128]{1,0:T(2,128)S(1)} %broadcast_multiply_fusion.5), kind=kOutput, calls=%fused_computation.72 | convolution fusion | flops 33882112 | bytes 395264 | tf_op jit(solution)/shard_map/bqc,cf->bqf/dot_general | solution.py:29
  18.0 1.2 %convolution_convert_fusion.9 = bf16[2,128,256]{2,1,0:T(8,128)(2,1)S(1)} fusion(bf16[4,256,256]{2,1,0:T(8,128)(2,1)} %param.22, bf16[2,128,256]{2,1,0:T(8,128)(2,1)S(1)} %copy-done.4, f32[2,128]{1,0:T(2,128)S(1)} %add_rsqrt_fusion.5, f32[2,128]{1,0:T(2,128)S(1)} %broadcast_multiply_fusion.5), kind=kOutput, calls=%fused_computation.71 | convolution fusion | flops 33882112 | bytes 395264 | tf_op jit(solution)/shard_map/bqc,cf->bqf/dot_general | solution.py:29
  20.9 1.1 %convert_reduce_fusion.4 = (f32[]{:T(128)}, f32[64]{0:T(128)}) fusion(s32[64]{0:T(128)S(1)} %copy-done.16), kind=kLoop, calls=%fused_computation.208 | loop fusion | flops 255 | bytes 516 | tf_op jit(solution)/shard_map/reduce_sum | solution.py:151
  22.6 1.4 %collective-permute-done = bf16[16,12,4,128]{3,0,2,1:T(8,128)(2,1)S(1)} collective-permute-done((bf16[16,12,4,128]{3,0,2,1:T(8,128)(2,1)S(1)}, bf16[16,12,4,128]{3,0,2,1:T(8,128)(2,1)S(1)}, u32[]{:S(2)}, u32[]{:S(2)}) %collective-permute-start) | collective-permute-done | bytes 196640 | tf_op jit(solution)/shard_map/ppermute | solution.py:59
  25.1 1.2 %fusion.175 = f32[2,8,128]{2,1,0:T(8,128)} fusion(bf16[2,128,8,32]{1,3,2,0:T(8,128)(2,1)S(1)} %bitcast.286, bf16[2,128,8,32]{1,3,2,0:T(8,128)(2,1)S(1)} %bitcast.288, f32[128]{0:T(128)S(1)} %add_multiply_fusion.1, f32[8,128,128]{1,2,0:T(8,128)S(1)} %copy.260), kind=kOutput, calls=%fused_computation.220 | convolution fusion | flops 18088064 | bytes 795136 | tf_op jit(solution)/shard_map/sub | solution.py:48
  26.9 1.2 %fusion.181 = f32[4,4,128]{2,1,0:T(4,128)} fusion(bf16[4,128,4,32]{1,3,2,0:T(8,128)(2,1)S(1)} %bitcast.274, bf16[4,128,4,32]{1,3,2,0:T(8,128)(2,1)S(1)} %bitcast.276, f32[128]{0:T(128)S(1)} %add_multiply_fusion.1, f32[4,128,128]{1,2,0:T(8,128)S(1)} %copy.282), kind=kOutput, calls=%fused_computation.222 | convolution fusion | flops 18088064 | bytes 532992 | tf_op jit(solution)/shard_map/sub | solution.py:48
  28.5 1.0 %fusion.57 = f32[2,8,32,128]{3,2,1,0:T(8,128)S(1)} fusion(bf16[2,128,8,32]{1,3,2,0:T(8,128)(2,1)S(1)} %bitcast.297, f32[2,8,128]{2,1,0:T(8,128)} %fusion.175, f32[2,8,128,128]{2,3,1,0:T(8,128)S(1)} %fusion.15), kind=kOutput, calls=%fused_computation.93 | convolution fusion | flops 17565824 | bytes 1449984 | tf_op jit(solution)/shard_map/bhqk,bkhd->bqhd/dot_general | solution.py:49
  29.6 1.4 %fusion.46 = bf16[2,128,256]{2,1,0:T(8,128)(2,1)S(1)} fusion(f32[2,128,256]{2,1,0:T(8,128)S(1)} %copy.262, bf16[2,128,256]{2,1,0:T(8,128)(2,1)S(1)} %copy-done.4, bf16[256,256]{1,0:T(8,128)(2,1)} %param.24, bf16[4,256,256]{2,1,0:T(8,128)(2,1)} %param.22, f32[2,128]{1,0:T(2,128)} %copy-done.9, f32[2,128]{1,0:T(2,128)S(1)} %broadcast_multiply_fusion.5), kind=kOutput, calls=%fused_computation.60 | convolution fusion | flops 67895296 | bytes 919552 | tf_op jit(solution)/shard_map/bqf,fc->bqc/dot_general | solution.py:52
  31.8 5.9 %all-to-all-start.1 = ((bf16[2,128,256]{2,0,1:T(2,128)(2,1)}), bf16[2,128,256]{2,0,1:T(2,128)(2,1)S(1)}, u32[]{:S(2)}, u32[]{:S(2)}) async-start(bf16[2,128,256]{2,0,1:T(2,128)(2,1)} %copy.263), calls=%async_computation.1 | async-start | bytes 262144 | tf_op jit(solution)/shard_map/all_to_all | solution.py:123
  40.5 5.4 %all-to-all-done.1 = bf16[2,128,256]{2,0,1:T(2,128)(2,1)S(1)} async-done(((bf16[2,128,256]{2,0,1:T(2,128)(2,1)}), bf16[2,128,256]{2,0,1:T(2,128)(2,1)S(1)}, u32[]{:S(2)}, u32[]{:S(2)}) %all-to-all-start.1) | async-done | bytes 131104 | tf_op jit(solution)/shard_map/all_to_all | solution.py:123
  45.9 2.8 %all-to-all-start.2 = ((bf16[32,32,128]{2,1,0:T(8,128)(2,1)}), bf16[32,32,128]{2,1,0:T(8,128)(2,1)S(1)}, u32[]{:S(2)}, u32[]{:S(2)}) async-start(bf16[32,32,128]{2,1,0:T(8,128)(2,1)} %copy.287), calls=%async_computation.2 | async-start | bytes 524288 | tf_op jit(solution)/shard_map/all_to_all | solution.py:79
  54.9 1.1 %reshape.302 = bf16[16,2,4096]{2,1,0:T(2,128)(2,1)} reshape(bf16[16,4,32,64]{3,2,1,0:T(8,128)(2,1)S(1)} %broadcast_bitcast_fusion) | data formatting | bytes 524288
  56.3 2.8 %all-to-all-done.2 = bf16[32,32,128]{2,1,0:T(8,128)(2,1)S(1)} async-done(((bf16[32,32,128]{2,1,0:T(8,128)(2,1)}), bf16[32,32,128]{2,1,0:T(8,128)(2,1)S(1)}, u32[]{:S(2)}, u32[]{:S(2)}) %all-to-all-start.2) | async-done | bytes 262176 | tf_op jit(solution)/shard_map/all_to_all | solution.py:79
  59.1 3.9 %all-to-all-start.3 = ((bf16[16,2,4096]{2,1,0:T(2,128)(2,1)}), bf16[16,2,4096]{2,1,0:T(2,128)(2,1)S(1)}, u32[]{:S(2)}, u32[]{:S(2)}) async-start(bf16[16,2,4096]{2,1,0:T(2,128)(2,1)} %reshape.302), calls=%async_computation.3 | async-start | bytes 524288 | tf_op jit(solution)/shard_map/all_to_all | solution.py:153
  67.4 5.8 %all-to-all-done.3 = bf16[16,2,4096]{2,1,0:T(2,128)(2,1)S(1)} async-done(((bf16[16,2,4096]{2,1,0:T(2,128)(2,1)}), bf16[16,2,4096]{2,1,0:T(2,128)(2,1)S(1)}, u32[]{:S(2)}, u32[]{:S(2)}) %all-to-all-start.3) | async-done | bytes 262176 | tf_op jit(solution)/shard_map/all_to_all | solution.py:153
  74.3 2.0 %fusion.12 = bf16[64,4,32,32]{0,3,2,1:T(8,128)(2,1)} fusion(bf16[64,4,32,1]{0,2,3,1:T(8,128)(2,1)S(1)} %fusion.50, f32[]{:T(128)} %get-tuple-element.18, bf16[64,64,32]{1,0,2:T(8,128)(2,1)S(1)} %copy.305), kind=kOutput, calls=%fused_computation.14 | convolution fusion | flops 34078720 | bytes 802820 | tf_op jit(solution)/shard_map/sic,sje->ijce/dot_general | solution.py:163
  76.3 4.2 %copy.306 = bf16[64,4,32,32]{3,2,1,0:T(8,128)(2,1)S(1)} copy(bf16[64,4,32,32]{0,3,2,1:T(8,128)(2,1)} %fusion.12) | data formatting | bytes 1048576 | tf_op jit(solution)/shard_map/convert_element_type | solution.py:166
  80.5 2.1 %reshape.263 = bf16[16,4,4,1024]{3,2,1,0:T(4,128)(2,1)S(1)} reshape(bf16[64,4,32,32]{3,2,1,0:T(8,128)(2,1)S(1)} %copy.306) | data formatting | bytes 1048576 | tf_op jit(solution)/shard_map/reshape.105
  82.6 1.1 %convolution_bitcast_fusion.3 = f32[16,1,4,4,128]{4,0,3,2,1:T(8,128)} fusion(bf16[16,4,4,1024]{3,2,1,0:T(4,128)(2,1)S(1)} %reshape.263, bf16[1024,128]{1,0:T(8,128)(2,1)S(1)} %copy-done), kind=kOutput, calls=%fused_computation.75 | convolution fusion | flops 67108864 | bytes 917504 | tf_op jit(solution)/shard_map/ijf,fc->ijc/dot_general | solution.py:169
  83.7 1.6 %copy.308 = bf16[64,64,32]{1,0,2:T(8,128)(2,1)S(1)} copy(bf16[64,64,32]{0,2,1:T(8,128)(2,1)} %bitcast.96) | data formatting | bytes 524288 | tf_op jit(solution)/shard_map/reshape | solution.py:159
  85.3 1.8 %fusion.13 = bf16[64,4,32,32]{0,3,2,1:T(8,128)(2,1)S(1)} fusion(bf16[64,4,32,1]{0,2,3,1:T(8,128)(2,1)} %copy-done.19, f32[]{:T(128)} %get-tuple-element.18, bf16[64,64,32]{1,0,2:T(8,128)(2,1)S(1)} %copy.308), kind=kOutput, calls=%fused_computation.15 | convolution fusion | flops 34078720 | bytes 802820 | tf_op jit(solution)/shard_map/sic,sje->ijce/dot_general | solution.py:163
  87.1 3.2 %copy.309 = bf16[64,4,32,32]{3,2,1,0:T(8,128)(2,1)S(1)} copy(bf16[64,4,32,32]{0,3,2,1:T(8,128)(2,1)S(1)} %fusion.13) | data formatting | bytes 1048576 | tf_op jit(solution)/shard_map/convert_element_type | solution.py:166
  90.4 2.1 %reshape.265 = bf16[16,4,4,1024]{3,2,1,0:T(4,128)(2,1)S(1)} reshape(bf16[64,4,32,32]{3,2,1,0:T(8,128)(2,1)S(1)} %copy.309) | data formatting | bytes 1048576 | tf_op jit(solution)/shard_map/reshape.108
  92.9 1.0 %maximum_select_fusion.1 = f32[16,2,4,4,128]{4,0,3,2,1:T(8,128)S(1)} fusion(f32[16,1,4,4,128]{4,0,3,2,1:T(8,128)S(1)} %convolution_bitcast_fusion.2, f32[16,1,4,4,128]{4,0,3,2,1:T(8,128)} %convolution_bitcast_fusion.3, pred[]{:T(512)S(6)} %eq.4), kind=kLoop, calls=%fused_computation.123 | loop fusion | flops 196608 | bytes 524289 | tf_op jit(solution)/shard_map/jit(_where)/select_n | solution.py:175
  94.1 1.1 %fusion.45 = bf16[128,4,128]{2,0,1:T(8,128)(2,1)S(1)} fusion(f32[128,4,128]{2,0,1:T(8,128)S(1)} %bitcast.291, f32[4,128,128]{2,1,0:T(8,128)S(1)} %copy-done.6, f32[128,4,128]{2,1,0:T(4,128)S(1)} %bitcast.264, bf16[4,128,128]{2,0,1:T(4,128)(2,1)S(1)} %fusion.79, bf16[128,128]{1,0:T(8,128)(2,1)} %param.32, bf16[4,128,128]{2,1,0:T(8,128)(2,1)} %param.30), kind=kOutput, calls=%fused_computation.59 | convolution fusion | flops 34078720 | bytes 1114112 | tf_op jit(solution)/shard_map/bqf,fc->bqc/dot_general | solution.py:52
  (142 shorter events, 21.6 us)
Async XLA Ops:
  0.6 82.0 %copy-start = (bf16[1024,128]{1,0:T(8,128)(2,1)S(1)}, bf16[1024,128]{1,0:T(8,128)(2,1)}, u32[]{:S(2)}) copy-start(bf16[1024,128]{1,0:T(8,128)(2,1)} %param.35) | copy-start | bytes 786436
  0.6 18.6 %copy-start.1 = (bf16[4,128,128]{2,1,0:T(8,128)(2,1)S(1)}, bf16[4,128,128]{2,1,0:T(8,128)(2,1)}, u32[]{:S(2)}) copy-start(bf16[4,128,128]{2,1,0:T(8,128)(2,1)} %param.19) | copy-start | bytes 393220
  0.7 17.4 %copy-start.4 = (bf16[2,128,256]{2,1,0:T(8,128)(2,1)S(1)}, bf16[2,128,256]{2,1,0:T(8,128)(2,1)}, u32[]{:S(2)}) copy-start(bf16[2,128,256]{2,1,0:T(8,128)(2,1)} %param.18) | copy-start | bytes 393220
  0.7 18.6 %copy-start.7 = (bf16[4,128,128]{2,1,0:T(8,128)(2,1)S(1)}, bf16[4,128,128]{2,1,0:T(8,128)(2,1)}, u32[]{:S(2)}) copy-start(bf16[4,128,128]{2,1,0:T(8,128)(2,1)} %param.27) | copy-start | bytes 393220
  0.7 19.7 %copy-start.16 = (s32[64]{0:T(128)S(1)}, s32[64]{0:T(128)}, u32[]{:S(2)}) copy-start(s32[64]{0:T(128)} %param.20) | copy-start | bytes 772
  5.0 17.6 %copy-start.17 = (s32[128]{0:T(128)S(1)}, s32[128]{0:T(128)}, u32[]{:S(2)}) copy-start(s32[128]{0:T(128)} %param.21) | copy-start | bytes 1540
  5.0 17.5 %all-to-all-start = ((bf16[16,12,4,128]{3,2,1,0:T(4,128)(2,1)}), bf16[16,12,4,128]{3,2,1,0:T(4,128)(2,1)S(1)}, u32[]{:S(2)}, u32[]{:S(2)}) async-start(bf16[16,12,4,128]{3,2,1,0:T(4,128)(2,1)} %broadcast_in_dim.8), calls=%async_computation | async-start | bytes 393216 | tf_op jit(solution)/shard_map/all_to_all | solution.py:58
  15.6 3.6 %copy-start.9 = (f32[2,128]{1,0:T(2,128)}, f32[2,128]{1,0:T(2,128)S(1)}, u32[]{:S(2)}) copy-start(f32[2,128]{1,0:T(2,128)S(1)} %add_rsqrt_fusion.5) | copy-start | bytes 3076
  22.5 1.5 %collective-permute-start = (bf16[16,12,4,128]{3,0,2,1:T(8,128)(2,1)S(1)}, bf16[16,12,4,128]{3,0,2,1:T(8,128)(2,1)S(1)}, u32[]{:S(2)}, u32[]{:S(2)}) collective-permute-start(bf16[16,12,4,128]{3,0,2,1:T(8,128)(2,1)S(1)} %copy.355), channel_id=1, source_target_pairs={{0,1},{1,0},{2,3},{3,2},{4,5},{5,4},{6,7},{7,6},{8,9},{9,8},{10,11... | collective-permute-start | bytes 589832 | tf_op jit(solution)/shard_map/ppermute | solution.py:59
  29.5 8.2 %copy-start.20 = (f32[4,4,128]{2,1,0:T(4,128)S(1)}, f32[4,4,128]{2,1,0:T(4,128)}, u32[]{:S(2)}) copy-start(f32[4,4,128]{2,1,0:T(4,128)} %fusion.181) | copy-start | bytes 24580
  31.8 14.1 %all-to-all-start.1 = ((bf16[2,128,256]{2,0,1:T(2,128)(2,1)}), bf16[2,128,256]{2,0,1:T(2,128)(2,1)S(1)}, u32[]{:S(2)}, u32[]{:S(2)}) async-start(bf16[2,128,256]{2,0,1:T(2,128)(2,1)} %copy.263), calls=%async_computation.1 | async-start | bytes 262144 | tf_op jit(solution)/shard_map/all_to_all | solution.py:123
  37.7 0.8 copy-start.12
  38.1 1.2 %copy-start.15 = (bf16[128,4]{0,1:T(4,128)(2,1)S(1)}, bf16[128,4]{0,1:T(4,128)(2,1)}, u32[]{:S(2)}) copy-start(bf16[128,4]{0,1:T(4,128)(2,1)} %param.31) | copy-start | bytes 3076
  39.7 10.2 %copy-start.5 = (bf16[4,256,256]{2,1,0:T(8,128)(2,1)S(1)}, bf16[4,256,256]{2,1,0:T(8,128)(2,1)}, u32[]{:S(2)}) copy-start(bf16[4,256,256]{2,1,0:T(8,128)(2,1)} %param.25) | copy-start | bytes 1572868
  45.9 13.2 %all-to-all-start.2 = ((bf16[32,32,128]{2,1,0:T(8,128)(2,1)}), bf16[32,32,128]{2,1,0:T(8,128)(2,1)S(1)}, u32[]{:S(2)}, u32[]{:S(2)}) async-start(bf16[32,32,128]{2,1,0:T(8,128)(2,1)} %copy.287), calls=%async_computation.2 | async-start | bytes 524288 | tf_op jit(solution)/shard_map/all_to_all | solution.py:79
  49.0 2.1 %copy-start.10 = (f32[64]{0:T(128)S(1)}, f32[64]{0:T(128)}, u32[]{:S(2)}) copy-start(f32[64]{0:T(128)} %get-tuple-element.19) | copy-start | bytes 772
  52.2 0.9 copy-start.11
  52.6 2.0 %copy-start.13 = (bf16[256,32]{0,1:T(8,128)(2,1)S(1)}, bf16[256,32]{0,1:T(8,128)(2,1)}, u32[]{:S(2)}) copy-start(bf16[256,32]{0,1:T(8,128)(2,1)} %param.33) | copy-start | bytes 49156
  52.6 2.0 %copy-start.18 = (f32[64]{0:T(128)S(1)}, f32[64]{0:T(128)}, u32[]{:S(2)}) copy-start(f32[64]{0:T(128)} %convert_element_type.227) | copy-start | bytes 772
  53.1 2.9 %copy-start.14 = (bf16[256,32]{0,1:T(8,128)(2,1)S(1)}, bf16[256,32]{0,1:T(8,128)(2,1)}, u32[]{:S(2)}) copy-start(bf16[256,32]{0,1:T(8,128)(2,1)} %param.34) | copy-start | bytes 49156
  54.6 9.7 %copy-start.8 = (bf16[4,128,128]{2,1,0:T(8,128)(2,1)S(1)}, bf16[4,128,128]{2,1,0:T(8,128)(2,1)}, u32[]{:S(2)}) copy-start(bf16[4,128,128]{2,1,0:T(8,128)(2,1)} %param.30) | copy-start | bytes 393220
  56.3 17.9 %copy-start.19 = (bf16[64,4,32,1]{0,2,3,1:T(8,128)(2,1)}, bf16[64,4,32,1]{0,2,3,1:T(8,128)(2,1)S(1)}, u32[]{:S(2)}) copy-start(bf16[64,4,32,1]{0,2,3,1:T(8,128)(2,1)S(1)} %fusion.50) | copy-start | bytes 49156
  59.1 14.1 %all-to-all-start.3 = ((bf16[16,2,4096]{2,1,0:T(2,128)(2,1)}), bf16[16,2,4096]{2,1,0:T(2,128)(2,1)S(1)}, u32[]{:S(2)}, u32[]{:S(2)}) async-start(bf16[16,2,4096]{2,1,0:T(2,128)(2,1)} %reshape.302), calls=%async_computation.3 | async-start | bytes 524288 | tf_op jit(solution)/shard_map/all_to_all | solution.py:153
  63.9 1.9 %copy-start.2 = (f32[32,16,128]{2,1,0:T(8,128)}, f32[32,16,128]{2,1,0:T(8,128)S(1)}, u32[]{:S(2)}) copy-start(f32[32,16,128]{2,1,0:T(8,128)S(1)} %get-tuple-element.15) | copy-start | bytes 786436
  73.6 10.1 %collective-permute-start.1 = (bf16[16,64,4,32]{1,3,2,0:T(8,128)(2,1)S(1)}, bf16[16,64,4,32]{1,3,2,0:T(8,128)(2,1)}, u32[]{:S(2)}, u32[]{:S(2)}) collective-permute-start(bf16[16,64,4,32]{1,3,2,0:T(8,128)(2,1)S(1)} %bitcast.258), channel_id=1, source_target_pairs={{0,1},{1,0},{2,3},{3,2},{4,5},{5,4},{6,7},{7,6},{8,9},{9,8},{10,11... | collective-permute-start | bytes 786440 | tf_op jit(solution)/shard_map/ppermute | solution.py:156
  90.3 3.8 %copy-start.3 = (f32[32,16,128]{2,1,0:T(8,128)S(1)}, f32[32,16,128]{2,1,0:T(8,128)}, u32[]{:S(2)}) copy-start(f32[32,16,128]{2,1,0:T(8,128)} %copy-done.2) | copy-start | bytes 786436
  90.4 3.8 %copy-start.6 = (f32[4,128,128]{2,1,0:T(8,128)S(1)}, f32[4,128,128]{2,1,0:T(8,128)}, u32[]{:S(2)}) copy-start(f32[4,128,128]{2,1,0:T(8,128)} %copy.303) | copy-start | bytes 786436

commit v13 on v6

--- a/solution.py
+++ b/solution.py
@@ -52,20 +52,23 @@
     return jnp.einsum("bqf,fc->bqc", gated, output_map, preferred_element_type=jnp.float32)
 
 
-def gather_blocks(block, axis, count):
-    half = count // 2
-    spread = jnp.broadcast_to(block[None], (half,) + block.shape)
+def gather_spread(spread, axis, count):
     same_core = lax.all_to_all(spread, "chip", 0, 0, tiled=True)
     other_core = lax.ppermute(same_core, "core", [(0, 1), (1, 0)])
     first = lax.axis_index("core") == 0
+    block = spread.shape[1:]
     received = jnp.where(
         first,
         jnp.stack([same_core, other_core], axis=1),
         jnp.stack([other_core, same_core], axis=1),
-    ).reshape((count,) + block.shape)
+    ).reshape((count,) + block)
     received = jnp.moveaxis(received, 0, axis)
-    shape = block.shape[:axis] + (count * block.shape[axis],) + block.shape[axis + 1 :]
+    shape = block[:axis] + (count * block[axis],) + block[axis + 1 :]
     return received.reshape(shape)
+
+
+def spread_maps(maps, count):
+    return jnp.broadcast_to(maps[None], (count // 2,) + maps.shape)
 
 
 def exchange_pair(pair_one, end_local, count):
@@ -112,10 +115,10 @@
     sequence_keys = key_offsets(sequence_mask)
     pair_norm = layer_norm(pairwise)
     both_maps = jnp.concatenate([row_bias_map, start_bias_map], axis=1)
-    both_local = jnp.einsum(
-        "ijc,ch->hij", pair_norm, both_maps, preferred_element_type=jnp.float32
-    ).astype(jnp.bfloat16)
-    both_bias = gather_blocks(both_local, 1, count)
+    both_spread = jnp.einsum(
+        "ijc,dch->dhij", pair_norm, spread_maps(both_maps, count), preferred_element_type=jnp.float32
+    ).astype(jnp.bfloat16)
+    both_bias = gather_spread(both_spread, 1, count)
     row_bias = both_bias[:H_M]
     start_bias = both_bias[H_M:]
     row_update = attend(layer_norm(alignment), row_project, row_bias, residue_keys, row_output, H_M)
@@ -140,8 +143,10 @@
     )
     last_norm = layer_norm(alignment_out)
     weighting = sequence_mask.astype(jnp.float32)[:, None, None]
-    left = (
-        jnp.einsum("sic,co->sio", last_norm, outer_left, preferred_element_type=jnp.float32)
+    left_spread = (
+        jnp.einsum(
+            "sic,dco->dsio", last_norm, spread_maps(outer_left, count), preferred_element_type=jnp.float32
+        )
         * weighting
     ).astype(jnp.bfloat16)
     right = (
@@ -152,7 +157,7 @@
     outer_sum = (
         jnp.einsum(
             "sic,sje->ijce",
-            gather_blocks(left, 1, count),
+            gather_spread(left_spread, 1, count),
             right,
             preferred_element_type=jnp.float32,
         )

time: 77.2 us -> 78.3 us (1.014)
  other arithmetic: 6.61 us -> 7.56 us
    unnamed x54 -> x53, local copies, waits for them, and re-layouts: 5.16 us -> 5.06 us
where the time goes in v13:
time: 78.3 us; the launch traced here: 77.5 us
  waiting for transfers between devices  20.3 us (26%)
  starting transfers between devices  18.2 us (23%)
  matrix products  16.8 us (21%)
  local copies, waits for them, and re-layouts  13.1 us (17%)
  other arithmetic  7.56 us (10%)
  between operations  1.4 us (2%)
    all_to_all x2, starting transfers between devices, gather_spread(): same_core = lax.all_to_all(spread, 'chip', 0, 0, tiled=True)  12.3 us
    all_to_all x2, waiting for transfers between devices, gather_spread(): same_core = lax.all_to_all(spread, 'chip', 0, 0, tiled=True)  9.9 us
    unnamed x53, local copies, waits for them, and re-layouts  5.06 us
    all_to_all x1, waiting for transfers between devices, per_device(): alignment_cols = lax.all_to_all(alignment_one, DAP, 1, 0, tiled=True)  4.67 us
    dot_general x12, matrix products, project(): jnp.einsum('bqc,cf->bqf', inputs, weight_table, preferred_element_type=jn...  3.98 us
    dot_general x4, matrix products, attend(): jnp.einsum('bqf,fc->bqc', gated, output_map, preferred_element_type=jnp.f...  3.42 us
    all_to_all x1, starting transfers between devices, per_device(): alignment_cols = lax.all_to_all(alignment_one, DAP, 1, 0, tiled=True)  3.11 us
    all_to_all x1, waiting for transfers between devices, exchange_pair(): lax.all_to_all(jnp.concatenate([pair_part, end_part], axis=1), DAP, 0, 0,...  2.98 us
  transfers between devices with their start and end apart: 6, of which 6 were waited for; matrix products, arithmetic and copies ran while one was open for 25% of the time, Pallas kernels for 0%

profile of v13, /device:TPU:0, one launch (start us, length us, event | category | flops | bytes accessed | tf_op | source)
XLA Modules:
  0.0 77.5 jit_solution(14729871759094828806)
XLA Ops:
  0.7 1.1 %convert_reduce_fusion = f32[4,128]{1,0:T(4,128)S(1)} fusion(bf16[4,128,128]{2,1,0:T(8,128)(2,1)} %param.19), kind=kLoop, calls=%fused_computation.92 | loop fusion | flops 130560 | bytes 133120 | tf_op jit(solution)/shard_map/reduce_sum | solution.py:19
  1.8 1.1 %fusion.64 = f32[4,128]{1,0:T(4,128)S(1)} fusion(bf16[4,128,128]{2,1,0:T(8,128)(2,1)} %param.19, f32[4,128]{1,0:T(4,128)S(1)} %broadcast_multiply_fusion.4), kind=kLoop, calls=%fused_computation.107 | loop fusion | flops 261632 | bytes 135168 | tf_op jit(solution)/shard_map/reduce_sum | solution.py:20
  2.9 0.7 pad_maximum_fusion.1
  3.6 1.3 %convolution_convert_fusion = bf16[16,12,4,128]{3,0,2,1:T(8,128)(2,1)S(1)} fusion(bf16[4,128,128]{2,1,0:T(8,128)(2,1)} %param.19, f32[4,128]{1,0:T(4,128)S(1)} %add_rsqrt_fusion.4, f32[4,128]{1,0:T(4,128)S(1)} %broadcast_multiply_fusion.4, bf16[128,12]{0,1:T(8,128)(2,1)S(1)} %pad_maximum_fusion.1), kind=kOutput, calls=%fused_computation.27 | convolution fusion | flops 25526272 | bytes 334848 | tf_op jit(solution)/shard_map/ijc,dch->dhij/dot_general | solution.py:118
  4.9 0.7 copy.232
  5.7 8.4 %all-to-all-start = ((bf16[16,12,4,128]{3,2,1,0:T(4,128)(2,1)}), bf16[16,12,4,128]{3,2,1,0:T(4,128)(2,1)S(1)}, u32[]{:S(2)}, u32[]{:S(2)}) async-start(bf16[16,12,4,128]{3,2,1,0:T(4,128)(2,1)} %copy.232), calls=%async_computation | async-start | bytes 393216 | tf_op jit(solution)/shard_map/all_to_all | solution.py:56
  15.3 1.0 %convolution_convert_fusion.6 = bf16[4,128,128]{1,2,0:T(8,128)(2,1)} fusion(bf16[4,128,128]{2,1,0:T(8,128)(2,1)S(1)} %copy-done.1, f32[4,128]{1,0:T(4,128)S(1)} %add_rsqrt_fusion.4, f32[4,128]{1,0:T(4,128)S(1)} %broadcast_multiply_fusion.4, bf16[4,128,128]{2,1,0:T(8,128)(2,1)S(1)} %copy-done.6), kind=kOutput, calls=%fused_computation.68 | convolution fusion | flops 17104896 | bytes 299008 | tf_op jit(solution)/shard_map/bqc,cf->bqf/dot_general | solution.py:29
  16.7 0.8 copy.229
  17.8 0.6 convert_element_type.224
  18.3 1.2 %convert_reduce_fusion.4 = (f32[]{:T(128)}, f32[64]{0:T(128)}) fusion(s32[64]{0:T(128)S(1)} %copy-done.19), kind=kLoop, calls=%fused_computation.203 | loop fusion | flops 255 | bytes 516 | tf_op jit(solution)/shard_map/reduce_sum | solution.py:156
  19.9 2.9 %all-to-all-done = bf16[16,12,4,128]{3,2,1,0:T(4,128)(2,1)S(1)} async-done(((bf16[16,12,4,128]{3,2,1,0:T(4,128)(2,1)}), bf16[16,12,4,128]{3,2,1,0:T(4,128)(2,1)S(1)}, u32[]{:S(2)}, u32[]{:S(2)}) %all-to-all-start) | async-done | bytes 196640 | tf_op jit(solution)/shard_map/all_to_all | solution.py:56
  22.8 1.4 %collective-permute-done = bf16[16,12,4,128]{3,2,1,0:T(4,128)(2,1)S(1)} collective-permute-done((bf16[16,12,4,128]{3,2,1,0:T(4,128)(2,1)S(1)}, bf16[16,12,4,128]{3,2,1,0:T(4,128)(2,1)S(1)}, u32[]{:S(2)}, u32[]{:S(2)}) %collective-permute-start) | collective-permute-done | bytes 196640 | tf_op jit(solution)/shard_map/ppermute | solution.py:57
  25.5 1.1 %fusion.175 = f32[2,8,128]{2,1,0:T(8,128)} fusion(bf16[2,128,8,32]{1,3,2,0:T(8,128)(2,1)S(1)} %bitcast.283, bf16[2,128,8,32]{1,3,2,0:T(8,128)(2,1)S(1)} %bitcast.285, f32[128]{0:T(128)S(1)} %add_multiply_fusion.1, f32[8,128,128]{1,2,0:T(8,128)S(1)} %copy.235), kind=kOutput, calls=%fused_computation.214 | convolution fusion | flops 18088064 | bytes 795136 | tf_op jit(solution)/shard_map/sub | solution.py:48
  27.4 0.6 fusion.181
  29.8 1.3 %fusion.46 = bf16[2,128,256]{2,1,0:T(8,128)(2,1)S(1)} fusion(f32[2,128,256]{2,1,0:T(8,128)S(1)} %copy.237, bf16[2,128,256]{2,1,0:T(8,128)(2,1)S(1)} %copy-done.2, bf16[256,256]{1,0:T(8,128)(2,1)S(1)} %copy-done.12, bf16[4,256,256]{2,1,0:T(8,128)(2,1)} %param.22, f32[2,128]{1,0:T(2,128)S(1)} %copy-done.9, f32[2,128]{1,0:T(2,128)S(1)} %broadcast_multiply_fusion.5), kind=kOutput, calls=%fused_computation.61 | convolution fusion | flops 67895296 | bytes 919552 | tf_op jit(solution)/shard_map/bqf,fc->bqc/dot_general | solution.py:52
  31.1 0.8 %copy.238 = bf16[2,128,256]{2,0,1:T(2,128)(2,1)} copy(bf16[2,128,256]{2,1,0:T(8,128)(2,1)S(1)} %fusion.46) | data formatting | bytes 262144 | tf_op jit(solution)/shard_map/convert_element_type | solution.py:125
  31.9 3.1 %all-to-all-start.1 = ((bf16[2,128,256]{2,0,1:T(2,128)(2,1)}), bf16[2,128,256]{2,0,1:T(2,128)(2,1)S(1)}, u32[]{:S(2)}, u32[]{:S(2)}) async-start(bf16[2,128,256]{2,0,1:T(2,128)(2,1)} %copy.238), calls=%async_computation.1 | async-start | bytes 262144 | tf_op jit(solution)/shard_map/all_to_all | solution.py:126
  35.8 1.3 %convert_reduce_fusion.3 = (f32[4,128]{1,0:T(4,128)S(1)}, bf16[4,128,128]{2,1,0:T(8,128)(2,1)S(1)}) fusion(bf16[128,128]{1,0:T(8,128)(2,1)S(1)} %copy-done.14, f32[4,128,128]{2,1,0:T(8,128)S(1)} %copy.259, bf16[4,128,128]{2,1,0:T(8,128)(2,1)S(1)} %copy-done.1, f32[4,128]{1,0:T(4,128)S(1)} %add_rsqrt_fusion.4, f32[4,128]{1,0:T(4,128)S(1)} %broadcast_multiply_fusion.4, ...), kind=kOutput, calls=%fused_computation.98 | convolution fusion | flops 34471424 | bytes 727040 | tf_op jit(solution)/shard_map/bqf,fc->bqc/dot_general | solution.py:52
  37.8 0.8 %copy.262 = bf16[32,32,128]{2,1,0:T(8,128)(2,1)} copy(bf16[32,32,128]{2,0,1:T(8,128)(2,1)S(1)} %pad_maximum_fusion) | data formatting | bytes 524288 | tf_op jit(solution)/shard_map/concatenate | solution.py:83
  38.6 4.7 %all-to-all-done.1 = bf16[2,128,256]{2,0,1:T(2,128)(2,1)S(1)} async-done(((bf16[2,128,256]{2,0,1:T(2,128)(2,1)}), bf16[2,128,256]{2,0,1:T(2,128)(2,1)S(1)}, u32[]{:S(2)}, u32[]{:S(2)}) %all-to-all-start.1) | async-done | bytes 131104 | tf_op jit(solution)/shard_map/all_to_all | solution.py:126
  43.2 2.8 %all-to-all-start.2 = ((bf16[32,32,128]{2,1,0:T(8,128)(2,1)}), bf16[32,32,128]{2,1,0:T(8,128)(2,1)S(1)}, u32[]{:S(2)}, u32[]{:S(2)}) async-start(bf16[32,32,128]{2,1,0:T(8,128)(2,1)} %copy.262), calls=%async_computation.2 | async-start | bytes 524288 | tf_op jit(solution)/shard_map/all_to_all | solution.py:82
  48.4 0.6 fusion.176
  51.1 0.8 copy.283
  52.3 1.1 %reshape.286 = bf16[16,2,4096]{2,1,0:T(2,128)(2,1)} reshape(bf16[16,4,32,64]{3,2,1,0:T(8,128)(2,1)S(1)} %bitcast.255) | data formatting | bytes 524288
  53.5 3.0 %all-to-all-done.2 = bf16[32,32,128]{2,1,0:T(8,128)(2,1)S(1)} async-done(((bf16[32,32,128]{2,1,0:T(8,128)(2,1)}), bf16[32,32,128]{2,1,0:T(8,128)(2,1)S(1)}, u32[]{:S(2)}, u32[]{:S(2)}) %all-to-all-start.2) | async-done | bytes 262176 | tf_op jit(solution)/shard_map/all_to_all | solution.py:82
  56.4 3.8 %all-to-all-start.3 = ((bf16[16,2,4096]{2,1,0:T(2,128)(2,1)}), bf16[16,2,4096]{2,1,0:T(2,128)(2,1)S(1)}, u32[]{:S(2)}, u32[]{:S(2)}) async-start(bf16[16,2,4096]{2,1,0:T(2,128)(2,1)} %reshape.286), calls=%async_computation.3 | async-start | bytes 524288 | tf_op jit(solution)/shard_map/all_to_all | solution.py:56
  62.3 0.6 fusion.186
  63.4 7.0 %all-to-all-done.3 = bf16[16,2,4096]{2,1,0:T(2,128)(2,1)S(1)} async-done(((bf16[16,2,4096]{2,1,0:T(2,128)(2,1)}), bf16[16,2,4096]{2,1,0:T(2,128)(2,1)S(1)}, u32[]{:S(2)}, u32[]{:S(2)}) %all-to-all-start.3) | async-done | bytes 262176 | tf_op jit(solution)/shard_map/all_to_all | solution.py:56
  71.4 1.4 %collective-permute-done.1 = bf16[16,64,4,32]{1,3,2,0:T(8,128)(2,1)S(1)} collective-permute-done((bf16[16,64,4,32]{1,3,2,0:T(8,128)(2,1)S(1)}, bf16[16,64,4,32]{1,3,2,0:T(8,128)(2,1)S(1)}, u32[]{:S(2)}, u32[]{:S(2)}) %collective-permute-start.1) | collective-permute-done | bytes 262176 | tf_op jit(solution)/shard_map/ppermute | solution.py:57
  73.1 1.1 %copy.281 = bf16[64,128,32]{1,0,2:T(8,128)(2,1)S(1)} copy(bf16[64,128,32]{0,2,1:T(8,128)(2,1)S(1)} %bitcast.252) | data formatting | bytes 1048576 | tf_op jit(solution)/shard_map/reshape | solution.py:67
  74.3 1.3 %divide_convert_fusion = bf16[4,32,128,32]{2,1,3,0:T(8,128)(2,1)S(1)} fusion(f32[]{:T(128)} %get-tuple-element.16, bf16[64,128,32]{1,0,2:T(8,128)(2,1)S(1)} %copy.281, bf16[64,4,256]{2,0,1:T(8,128)(2,1)S(1)} %get-tuple-element.19, f32[64,4]{0,1:T(4,128)S(1)} %add_rsqrt_fusion.2, f32[64,4]{0,1:T(4,128)S(1)} %broadcast_multiply_fusion.2, ...), kind=kOutput, calls=%fused_computation.4 | convolution fusion | flops 72630272 | bytes 1722628 | tf_op jit(solution)/shard_map/sic,sje->ijce/dot_general | solution.py:158
  76.7 0.8 copy.284
  (137 shorter events, 16.9 us)
Async XLA Ops:
  0.6 75.0 %copy-start = (bf16[1024,128]{1,0:T(8,128)(2,1)S(1)}, bf16[1024,128]{1,0:T(8,128)(2,1)}, u32[]{:S(2)}) copy-start(bf16[1024,128]{1,0:T(8,128)(2,1)} %param.35) | copy-start | bytes 786436
  0.6 13.5 %copy-start.2 = (bf16[2,128,256]{2,1,0:T(8,128)(2,1)S(1)}, bf16[2,128,256]{2,1,0:T(8,128)(2,1)}, u32[]{:S(2)}) copy-start(bf16[2,128,256]{2,1,0:T(8,128)(2,1)} %param.18) | copy-start | bytes 393220
  0.7 13.8 %copy-start.11 = (bf16[4,256,256]{2,1,0:T(8,128)(2,1)S(1)}, bf16[4,256,256]{2,1,0:T(8,128)(2,1)}, u32[]{:S(2)}) copy-start(bf16[4,256,256]{2,1,0:T(8,128)(2,1)} %param.22) | copy-start | bytes 1572868
  5.7 9.6 %copy-start.1 = (bf16[4,128,128]{2,1,0:T(8,128)(2,1)S(1)}, bf16[4,128,128]{2,1,0:T(8,128)(2,1)}, u32[]{:S(2)}) copy-start(bf16[4,128,128]{2,1,0:T(8,128)(2,1)} %param.19) | copy-start | bytes 393220
  5.7 9.6 %copy-start.6 = (bf16[4,128,128]{2,1,0:T(8,128)(2,1)S(1)}, bf16[4,128,128]{2,1,0:T(8,128)(2,1)}, u32[]{:S(2)}) copy-start(bf16[4,128,128]{2,1,0:T(8,128)(2,1)} %param.27) | copy-start | bytes 393220
  5.7 17.1 %all-to-all-start = ((bf16[16,12,4,128]{3,2,1,0:T(4,128)(2,1)}), bf16[16,12,4,128]{3,2,1,0:T(4,128)(2,1)S(1)}, u32[]{:S(2)}, u32[]{:S(2)}) async-start(bf16[16,12,4,128]{3,2,1,0:T(4,128)(2,1)} %copy.232), calls=%async_computation | async-start | bytes 393216 | tf_op jit(solution)/shard_map/all_to_all | solution.py:56
  14.5 2.2 %copy-start.8 = (f32[2,128]{1,0:T(2,128)}, f32[2,128]{1,0:T(2,128)S(1)}, u32[]{:S(2)}) copy-start(f32[2,128]{1,0:T(2,128)S(1)} %add_rsqrt_fusion.5) | copy-start | bytes 3076
  14.7 3.0 %copy-start.19 = (s32[64]{0:T(128)S(1)}, s32[64]{0:T(128)}, u32[]{:S(2)}) copy-start(s32[64]{0:T(128)} %param.20) | copy-start | bytes 772
  15.0 7.8 %copy-start.20 = (s32[128]{0:T(128)S(1)}, s32[128]{0:T(128)}, u32[]{:S(2)}) copy-start(s32[128]{0:T(128)} %param.21) | copy-start | bytes 1540
  22.8 1.4 %collective-permute-start = (bf16[16,12,4,128]{3,2,1,0:T(4,128)(2,1)S(1)}, bf16[16,12,4,128]{3,2,1,0:T(4,128)(2,1)S(1)}, u32[]{:S(2)}, u32[]{:S(2)}) collective-permute-start(bf16[16,12,4,128]{3,2,1,0:T(4,128)(2,1)S(1)} %all-to-all-done), channel_id=1, source_target_pairs={{0,1},{1,0},{2,3},{3,2},{4,5},{5,4},{6,7},{7,6},{8,9},{9,8},{10,11... | collective-permute-start | bytes 589832 | tf_op jit(solution)/shard_map/ppermute | solution.py:57
  27.9 0.9 %copy-start.5 = (bf16[2,128,256]{1,2,0:T(8,128)(2,1)S(1)}, bf16[2,128,256]{1,2,0:T(8,128)(2,1)}, u32[]{:S(2)}) copy-start(bf16[2,128,256]{1,2,0:T(8,128)(2,1)} %copy.229) | copy-start | bytes 393220
  28.0 0.9 %copy-start.22 = (f32[2,8,128]{2,1,0:T(8,128)S(1)}, f32[2,8,128]{2,1,0:T(8,128)}, u32[]{:S(2)}) copy-start(f32[2,8,128]{2,1,0:T(8,128)} %fusion.175) | copy-start | bytes 24580
  28.9 0.7 copy-start.9
  28.9 0.9 %copy-start.12 = (bf16[256,256]{1,0:T(8,128)(2,1)S(1)}, bf16[256,256]{1,0:T(8,128)(2,1)}, u32[]{:S(2)}) copy-start(bf16[256,256]{1,0:T(8,128)(2,1)} %param.24) | copy-start | bytes 393220
  29.8 5.2 %copy-start.4 = (bf16[4,128,128]{1,2,0:T(8,128)(2,1)S(1)}, bf16[4,128,128]{1,2,0:T(8,128)(2,1)}, u32[]{:S(2)}) copy-start(bf16[4,128,128]{1,2,0:T(8,128)(2,1)} %convolution_convert_fusion.6) | copy-start | bytes 393220
  31.9 11.3 %all-to-all-start.1 = ((bf16[2,128,256]{2,0,1:T(2,128)(2,1)}), bf16[2,128,256]{2,0,1:T(2,128)(2,1)S(1)}, u32[]{:S(2)}, u32[]{:S(2)}) async-start(bf16[2,128,256]{2,0,1:T(2,128)(2,1)} %copy.238), calls=%async_computation.1 | async-start | bytes 262144 | tf_op jit(solution)/shard_map/all_to_all | solution.py:126
  35.0 0.8 copy-start.14
  35.4 2.0 %copy-start.18 = (bf16[128,4]{0,1:T(4,128)(2,1)S(1)}, bf16[128,4]{0,1:T(4,128)(2,1)}, u32[]{:S(2)}) copy-start(bf16[128,4]{0,1:T(4,128)(2,1)} %param.31) | copy-start | bytes 3076
  43.2 13.2 %all-to-all-start.2 = ((bf16[32,32,128]{2,1,0:T(8,128)(2,1)}), bf16[32,32,128]{2,1,0:T(8,128)(2,1)S(1)}, u32[]{:S(2)}, u32[]{:S(2)}) async-start(bf16[32,32,128]{2,1,0:T(8,128)(2,1)} %copy.262), calls=%async_computation.2 | async-start | bytes 524288 | tf_op jit(solution)/shard_map/all_to_all | solution.py:82
  46.2 1.1 %copy-start.3 = (bf16[4,256,256]{2,1,0:T(8,128)(2,1)S(1)}, bf16[4,256,256]{2,1,0:T(8,128)(2,1)}, u32[]{:S(2)}) copy-start(bf16[4,256,256]{2,1,0:T(8,128)(2,1)} %param.25) | copy-start | bytes 1572868
  47.5 0.9 %copy-start.10 = (f32[64]{0:T(128)S(1)}, f32[64]{0:T(128)}, u32[]{:S(2)}) copy-start(f32[64]{0:T(128)} %get-tuple-element.17) | copy-start | bytes 772
  49.5 0.9 %copy-start.13 = (bf16[256,256]{1,0:T(8,128)(2,1)S(1)}, bf16[256,256]{1,0:T(8,128)(2,1)}, u32[]{:S(2)}) copy-start(bf16[256,256]{1,0:T(8,128)(2,1)} %param.26) | copy-start | bytes 393220
  50.4 1.4 %copy-start.16 = (bf16[256,32]{0,1:T(8,128)(2,1)S(1)}, bf16[256,32]{0,1:T(8,128)(2,1)}, u32[]{:S(2)}) copy-start(bf16[256,32]{0,1:T(8,128)(2,1)} %param.33) | copy-start | bytes 49156
  50.4 1.4 %copy-start.21 = (f32[64]{0:T(128)S(1)}, f32[64]{0:T(128)}, u32[]{:S(2)}) copy-start(f32[64]{0:T(128)} %convert_element_type.224) | copy-start | bytes 772
  53.5 8.1 %copy-start.7 = (bf16[4,128,128]{2,1,0:T(8,128)(2,1)S(1)}, bf16[4,128,128]{2,1,0:T(8,128)(2,1)}, u32[]{:S(2)}) copy-start(bf16[4,128,128]{2,1,0:T(8,128)(2,1)} %param.30) | copy-start | bytes 393220
  56.4 14.0 %all-to-all-start.3 = ((bf16[16,2,4096]{2,1,0:T(2,128)(2,1)}), bf16[16,2,4096]{2,1,0:T(2,128)(2,1)S(1)}, u32[]{:S(2)}, u32[]{:S(2)}) async-start(bf16[16,2,4096]{2,1,0:T(2,128)(2,1)} %reshape.286), calls=%async_computation.3 | async-start | bytes 524288 | tf_op jit(solution)/shard_map/all_to_all | solution.py:56
  70.8 2.0 %collective-permute-start.1 = (bf16[16,64,4,32]{1,3,2,0:T(8,128)(2,1)S(1)}, bf16[16,64,4,32]{1,3,2,0:T(8,128)(2,1)S(1)}, u32[]{:S(2)}, u32[]{:S(2)}) collective-permute-start(bf16[16,64,4,32]{1,3,2,0:T(8,128)(2,1)S(1)} %bitcast.253), channel_id=1, source_target_pairs={{0,1},{1,0},{2,3},{3,2},{4,5},{5,4},{6,7},{7,6},{8,9},{9,8},{10,11... | collective-permute-start | bytes 786440 | tf_op jit(solution)/shard_map/ppermute | solution.py:57
  73.1 1.1 %copy-start.17 = (bf16[256,32]{0,1:T(8,128)(2,1)S(1)}, bf16[256,32]{0,1:T(8,128)(2,1)}, u32[]{:S(2)}) copy-start(bf16[256,32]{0,1:T(8,128)(2,1)} %param.34) | copy-start | bytes 49156
  75.6 0.8 copy-start.15

commit v14 on v6

--- a/solution.py
+++ b/solution.py
@@ -57,12 +57,9 @@
     spread = jnp.broadcast_to(block[None], (half,) + block.shape)
     same_core = lax.all_to_all(spread, "chip", 0, 0, tiled=True)
     other_core = lax.ppermute(same_core, "core", [(0, 1), (1, 0)])
-    first = lax.axis_index("core") == 0
-    received = jnp.where(
-        first,
-        jnp.stack([same_core, other_core], axis=1),
-        jnp.stack([other_core, same_core], axis=1),
-    ).reshape((count,) + block.shape)
+    both = jnp.stack([other_core, same_core, other_core], axis=1)
+    received = lax.dynamic_slice_in_dim(both, 1 - lax.axis_index("core"), 2, axis=1)
+    received = received.reshape((count,) + block.shape)
     received = jnp.moveaxis(received, 0, axis)
     shape = block.shape[:axis] + (count * block.shape[axis],) + block.shape[axis + 1 :]
     return received.reshape(shape)

time: 77.2 us -> 77.7 us (level)
    another operation x0 -> x2, other arithmetic: none -> 0.84 us  [gather_blocks(): both = jnp.stack([other_core, same_core, other_core], axis=1)]
where the time goes in v14:
time: 77.7 us; the launch traced here: 76.9 us
  waiting for transfers between devices  20.4 us (26%)
  starting transfers between devices  18.2 us (23%)
  matrix products  16.7 us (21%)
  local copies, waits for them, and re-layouts  13.2 us (17%)
  other arithmetic  7.05 us (9%)
  between operations  1.43 us (2%)
    all_to_all x2, starting transfers between devices, gather_blocks(): same_core = lax.all_to_all(spread, 'chip', 0, 0, tiled=True)  12.2 us
    all_to_all x2, waiting for transfers between devices, gather_blocks(): same_core = lax.all_to_all(spread, 'chip', 0, 0, tiled=True)  9.89 us
    unnamed x54, local copies, waits for them, and re-layouts  5.16 us
    all_to_all x1, waiting for transfers between devices, per_device(): alignment_cols = lax.all_to_all(alignment_one, DAP, 1, 0, tiled=True)  4.67 us
    dot_general x12, matrix products, project(): jnp.einsum('bqc,cf->bqf', inputs, weight_table, preferred_element_type=jn...  3.98 us
    dot_general x4, matrix products, attend(): jnp.einsum('bqf,fc->bqc', gated, output_map, preferred_element_type=jnp.f...  3.42 us
    all_to_all x1, waiting for transfers between devices, exchange_pair(): lax.all_to_all(jnp.concatenate([pair_part, end_part], axis=1), DAP, 0, 0,...  3.07 us
    all_to_all x1, starting transfers between devices, per_device(): alignment_cols = lax.all_to_all(alignment_one, DAP, 1, 0, tiled=True)  3.06 us
  transfers between devices with their start and end apart: 6, of which 6 were waited for; matrix products, arithmetic and copies ran while one was open for 25% of the time, Pallas kernels for 0%

profile of v14, /device:TPU:0, one launch (start us, length us, event | category | flops | bytes accessed | tf_op | source)
XLA Modules:
  0.0 76.9 jit_solution(6904033605989884384)
XLA Ops:
  0.7 1.1 %convert_reduce_fusion = f32[4,128]{1,0:T(4,128)S(1)} fusion(bf16[4,128,128]{2,1,0:T(8,128)(2,1)} %param.19), kind=kLoop, calls=%fused_computation.99 | loop fusion | flops 130560 | bytes 133120 | tf_op jit(solution)/shard_map/reduce_sum | solution.py:19
  1.8 1.1 %fusion.67 = f32[4,128]{1,0:T(4,128)S(1)} fusion(bf16[4,128,128]{2,1,0:T(8,128)(2,1)} %param.19, f32[4,128]{1,0:T(4,128)S(1)} %broadcast_multiply_fusion.4), kind=kLoop, calls=%fused_computation.114 | loop fusion | flops 261632 | bytes 135168 | tf_op jit(solution)/shard_map/reduce_sum | solution.py:20
  2.9 1.3 %convolution_convert_fusion.12 = bf16[12,4,128]{2,0,1:T(8,128)(2,1)S(1)} fusion(bf16[4,128,128]{2,1,0:T(8,128)(2,1)} %param.19, f32[4,128]{1,0:T(4,128)S(1)} %add_rsqrt_fusion.4, f32[4,128]{1,0:T(4,128)S(1)} %broadcast_multiply_fusion.4, bf16[128,4]{0,1:T(4,128)(2,1)} %param.28, bf16[128,8]{0,1:T(8,128)(2,1)} %param.23), kind=kOutput, calls=%fused_computation.79 | convolution fusion | flops 1847296 | bytes 150528 | tf_op jit(solution)/shard_map/ijc,ch->hij/dot_general | solution.py:112
  4.2 0.7 broadcast_in_dim.8
  4.9 8.4 %all-to-all-start = ((bf16[16,12,4,128]{3,2,1,0:T(4,128)(2,1)}), bf16[16,12,4,128]{3,2,1,0:T(4,128)(2,1)S(1)}, u32[]{:S(2)}, u32[]{:S(2)}) async-start(bf16[16,12,4,128]{3,2,1,0:T(4,128)(2,1)} %broadcast_in_dim.8), calls=%async_computation | async-start | bytes 393216 | tf_op jit(solution)/shard_map/all_to_all | solution.py:58
  14.6 1.0 %convolution_convert_fusion.5 = bf16[4,128,128]{1,2,0:T(8,128)(2,1)} fusion(bf16[4,128,128]{2,1,0:T(8,128)(2,1)S(1)} %copy-done.1, f32[4,128]{1,0:T(4,128)S(1)} %add_rsqrt_fusion.4, f32[4,128]{1,0:T(4,128)S(1)} %broadcast_multiply_fusion.4, bf16[4,128,128]{2,1,0:T(8,128)(2,1)S(1)} %copy-done.6), kind=kOutput, calls=%fused_computation.67 | convolution fusion | flops 17104896 | bytes 299008 | tf_op jit(solution)/shard_map/bqc,cf->bqf/dot_general | solution.py:29
  16.0 0.8 copy.232
  17.0 0.6 convert_element_type.221
  17.6 1.2 %convert_reduce_fusion.4 = (f32[]{:T(128)}, f32[64]{0:T(128)}) fusion(s32[64]{0:T(128)S(1)} %copy-done.19), kind=kLoop, calls=%fused_computation.209 | loop fusion | flops 255 | bytes 516 | tf_op jit(solution)/shard_map/reduce_sum | solution.py:148
  19.2 2.8 %all-to-all-done = bf16[16,12,4,128]{3,2,1,0:T(4,128)(2,1)S(1)} async-done(((bf16[16,12,4,128]{3,2,1,0:T(4,128)(2,1)}), bf16[16,12,4,128]{3,2,1,0:T(4,128)(2,1)S(1)}, u32[]{:S(2)}, u32[]{:S(2)}) %all-to-all-start) | async-done | bytes 196640 | tf_op jit(solution)/shard_map/all_to_all | solution.py:58
  22.2 1.4 %collective-permute-done = bf16[16,12,4,128]{3,0,2,1:T(8,128)(2,1)S(1)} collective-permute-done((bf16[16,12,4,128]{3,0,2,1:T(8,128)(2,1)S(1)}, bf16[16,12,4,128]{3,0,2,1:T(8,128)(2,1)S(1)}, u32[]{:S(2)}, u32[]{:S(2)}) %collective-permute-start) | collective-permute-done | bytes 196640 | tf_op jit(solution)/shard_map/ppermute | solution.py:59
  24.8 1.1 %fusion.177 = f32[2,8,128]{2,1,0:T(8,128)} fusion(bf16[2,128,8,32]{1,3,2,0:T(8,128)(2,1)S(1)} %bitcast.276, bf16[2,128,8,32]{1,3,2,0:T(8,128)(2,1)S(1)} %bitcast.278, f32[128]{0:T(128)S(1)} %add_multiply_fusion.1, f32[8,128,128]{1,2,0:T(8,128)S(1)} %copy.240), kind=kOutput, calls=%fused_computation.221 | convolution fusion | flops 18088064 | bytes 795136 | tf_op jit(solution)/shard_map/sub | solution.py:48
  26.7 0.6 fusion.183
  29.1 1.3 %fusion.44 = bf16[2,128,256]{2,1,0:T(8,128)(2,1)S(1)} fusion(f32[2,128,256]{2,1,0:T(8,128)S(1)} %copy.242, bf16[2,128,256]{2,1,0:T(8,128)(2,1)S(1)} %copy-done.2, bf16[256,256]{1,0:T(8,128)(2,1)S(1)} %copy-done.12, bf16[4,256,256]{2,1,0:T(8,128)(2,1)} %param.22, f32[2,128]{1,0:T(2,128)S(1)} %copy-done.9, f32[2,128]{1,0:T(2,128)S(1)} %broadcast_multiply_fusion.5), kind=kOutput, calls=%fused_computation.60 | convolution fusion | flops 67895296 | bytes 919552 | tf_op jit(solution)/shard_map/bqf,fc->bqc/dot_general | solution.py:52
  30.4 0.8 %copy.243 = bf16[2,128,256]{2,0,1:T(2,128)(2,1)} copy(bf16[2,128,256]{2,1,0:T(8,128)(2,1)S(1)} %fusion.44) | data formatting | bytes 262144 | tf_op jit(solution)/shard_map/convert_element_type | solution.py:119
  31.2 3.1 %all-to-all-start.1 = ((bf16[2,128,256]{2,0,1:T(2,128)(2,1)}), bf16[2,128,256]{2,0,1:T(2,128)(2,1)S(1)}, u32[]{:S(2)}, u32[]{:S(2)}) async-start(bf16[2,128,256]{2,0,1:T(2,128)(2,1)} %copy.243), calls=%async_computation.1 | async-start | bytes 262144 | tf_op jit(solution)/shard_map/all_to_all | solution.py:120
  35.0 1.3 %convert_reduce_fusion.3 = (f32[4,128]{1,0:T(4,128)S(1)}, bf16[4,128,128]{2,1,0:T(8,128)(2,1)S(1)}) fusion(bf16[128,128]{1,0:T(8,128)(2,1)S(1)} %copy-done.14, f32[4,128,128]{2,1,0:T(8,128)S(1)} %copy.264, bf16[4,128,128]{2,1,0:T(8,128)(2,1)S(1)} %copy-done.1, f32[4,128]{1,0:T(4,128)S(1)} %add_rsqrt_fusion.4, f32[4,128]{1,0:T(4,128)S(1)} %broadcast_multiply_fusion.4, ...), kind=kOutput, calls=%fused_computation.105 | convolution fusion | flops 34471424 | bytes 727040 | tf_op jit(solution)/shard_map/bqf,fc->bqc/dot_general | solution.py:52
  37.0 0.8 %copy.267 = bf16[32,32,128]{2,1,0:T(8,128)(2,1)} copy(bf16[32,32,128]{2,0,1:T(8,128)(2,1)S(1)} %pad_maximum_fusion) | data formatting | bytes 524288 | tf_op jit(solution)/shard_map/concatenate | solution.py:77
  37.8 4.7 %all-to-all-done.1 = bf16[2,128,256]{2,0,1:T(2,128)(2,1)S(1)} async-done(((bf16[2,128,256]{2,0,1:T(2,128)(2,1)}), bf16[2,128,256]{2,0,1:T(2,128)(2,1)S(1)}, u32[]{:S(2)}, u32[]{:S(2)}) %all-to-all-start.1) | async-done | bytes 131104 | tf_op jit(solution)/shard_map/all_to_all | solution.py:120
  42.5 2.8 %all-to-all-start.2 = ((bf16[32,32,128]{2,1,0:T(8,128)(2,1)}), bf16[32,32,128]{2,1,0:T(8,128)(2,1)S(1)}, u32[]{:S(2)}, u32[]{:S(2)}) async-start(bf16[32,32,128]{2,1,0:T(8,128)(2,1)} %copy.267), calls=%async_computation.2 | async-start | bytes 524288 | tf_op jit(solution)/shard_map/all_to_all | solution.py:76
  47.7 0.6 fusion.178
  50.4 0.8 copy.287
  51.5 1.1 %reshape.281 = bf16[16,2,4096]{2,1,0:T(2,128)(2,1)} reshape(bf16[16,4,32,64]{3,2,1,0:T(8,128)(2,1)S(1)} %broadcast_bitcast_fusion) | data formatting | bytes 524288
  52.6 3.1 %all-to-all-done.2 = bf16[32,32,128]{2,1,0:T(8,128)(2,1)S(1)} async-done(((bf16[32,32,128]{2,1,0:T(8,128)(2,1)}), bf16[32,32,128]{2,1,0:T(8,128)(2,1)S(1)}, u32[]{:S(2)}, u32[]{:S(2)}) %all-to-all-start.2) | async-done | bytes 262176 | tf_op jit(solution)/shard_map/all_to_all | solution.py:76
  55.7 3.7 %all-to-all-start.3 = ((bf16[16,2,4096]{2,1,0:T(2,128)(2,1)}), bf16[16,2,4096]{2,1,0:T(2,128)(2,1)S(1)}, u32[]{:S(2)}, u32[]{:S(2)}) async-start(bf16[16,2,4096]{2,1,0:T(2,128)(2,1)} %reshape.281), calls=%async_computation.3 | async-start | bytes 524288 | tf_op jit(solution)/shard_map/all_to_all | solution.py:58
  61.4 0.6 fusion.188
  62.6 7.0 %all-to-all-done.3 = bf16[16,2,4096]{2,1,0:T(2,128)(2,1)S(1)} async-done(((bf16[16,2,4096]{2,1,0:T(2,128)(2,1)}), bf16[16,2,4096]{2,1,0:T(2,128)(2,1)S(1)}, u32[]{:S(2)}, u32[]{:S(2)}) %all-to-all-start.3) | async-done | bytes 262176 | tf_op jit(solution)/shard_map/all_to_all | solution.py:58
  70.6 1.4 %collective-permute-done.1 = bf16[16,64,4,32]{1,3,2,0:T(8,128)(2,1)S(1)} collective-permute-done((bf16[16,64,4,32]{1,3,2,0:T(8,128)(2,1)S(1)}, bf16[16,64,4,32]{1,3,2,0:T(8,128)(2,1)S(1)}, u32[]{:S(2)}, u32[]{:S(2)}) %collective-permute-start.1) | collective-permute-done | bytes 262176 | tf_op jit(solution)/shard_map/ppermute | solution.py:59
  71.9 0.6 fusion.51
  72.6 1.1 %copy.285 = bf16[64,128,32]{1,0,2:T(8,128)(2,1)S(1)} copy(bf16[64,128,32]{0,2,1:T(8,128)(2,1)S(1)} %bitcast.246) | data formatting | bytes 1048576 | tf_op jit(solution)/shard_map/reshape | solution.py:65
  73.7 1.3 %divide_convert_fusion = bf16[4,32,128,32]{2,1,3,0:T(8,128)(2,1)S(1)} fusion(f32[]{:T(128)} %get-tuple-element.18, bf16[64,128,32]{1,0,2:T(8,128)(2,1)S(1)} %copy.285, bf16[64,4,256]{2,0,1:T(8,128)(2,1)S(1)} %get-tuple-element.21, f32[64,4]{0,1:T(4,128)S(1)} %add_rsqrt_fusion.2, f32[64,4]{0,1:T(4,128)S(1)} %broadcast_multiply_fusion.2, ...), kind=kOutput, calls=%fused_computation.4 | convolution fusion | flops 72630272 | bytes 1722628 | tf_op jit(solution)/shard_map/sic,sje->ijce/dot_general | solution.py:150
  76.1 0.8 copy.288
  (138 shorter events, 16.5 us)
Async XLA Ops:
  0.6 74.4 %copy-start = (bf16[1024,128]{1,0:T(8,128)(2,1)S(1)}, bf16[1024,128]{1,0:T(8,128)(2,1)}, u32[]{:S(2)}) copy-start(bf16[1024,128]{1,0:T(8,128)(2,1)} %param.35) | copy-start | bytes 786436
  0.6 12.7 %copy-start.2 = (bf16[2,128,256]{2,1,0:T(8,128)(2,1)S(1)}, bf16[2,128,256]{2,1,0:T(8,128)(2,1)}, u32[]{:S(2)}) copy-start(bf16[2,128,256]{2,1,0:T(8,128)(2,1)} %param.18) | copy-start | bytes 393220
  0.7 13.1 %copy-start.11 = (bf16[4,256,256]{2,1,0:T(8,128)(2,1)S(1)}, bf16[4,256,256]{2,1,0:T(8,128)(2,1)}, u32[]{:S(2)}) copy-start(bf16[4,256,256]{2,1,0:T(8,128)(2,1)} %param.22) | copy-start | bytes 1572868
  4.9 9.6 %copy-start.1 = (bf16[4,128,128]{2,1,0:T(8,128)(2,1)S(1)}, bf16[4,128,128]{2,1,0:T(8,128)(2,1)}, u32[]{:S(2)}) copy-start(bf16[4,128,128]{2,1,0:T(8,128)(2,1)} %param.19) | copy-start | bytes 393220
  4.9 9.6 %copy-start.6 = (bf16[4,128,128]{2,1,0:T(8,128)(2,1)S(1)}, bf16[4,128,128]{2,1,0:T(8,128)(2,1)}, u32[]{:S(2)}) copy-start(bf16[4,128,128]{2,1,0:T(8,128)(2,1)} %param.27) | copy-start | bytes 393220
  4.9 17.1 %all-to-all-start = ((bf16[16,12,4,128]{3,2,1,0:T(4,128)(2,1)}), bf16[16,12,4,128]{3,2,1,0:T(4,128)(2,1)S(1)}, u32[]{:S(2)}, u32[]{:S(2)}) async-start(bf16[16,12,4,128]{3,2,1,0:T(4,128)(2,1)} %broadcast_in_dim.8), calls=%async_computation | async-start | bytes 393216 | tf_op jit(solution)/shard_map/all_to_all | solution.py:58
  13.7 2.2 %copy-start.8 = (f32[2,128]{1,0:T(2,128)}, f32[2,128]{1,0:T(2,128)S(1)}, u32[]{:S(2)}) copy-start(f32[2,128]{1,0:T(2,128)S(1)} %add_rsqrt_fusion.5) | copy-start | bytes 3076
  14.0 3.0 %copy-start.19 = (s32[64]{0:T(128)S(1)}, s32[64]{0:T(128)}, u32[]{:S(2)}) copy-start(s32[64]{0:T(128)} %param.20) | copy-start | bytes 772
  14.5 7.6 %copy-start.20 = (s32[128]{0:T(128)S(1)}, s32[128]{0:T(128)}, u32[]{:S(2)}) copy-start(s32[128]{0:T(128)} %param.21) | copy-start | bytes 1540
  22.1 1.5 %collective-permute-start = (bf16[16,12,4,128]{3,0,2,1:T(8,128)(2,1)S(1)}, bf16[16,12,4,128]{3,0,2,1:T(8,128)(2,1)S(1)}, u32[]{:S(2)}, u32[]{:S(2)}) collective-permute-start(bf16[16,12,4,128]{3,0,2,1:T(8,128)(2,1)S(1)} %copy.326), channel_id=1, source_target_pairs={{0,1},{1,0},{2,3},{3,2},{4,5},{5,4},{6,7},{7,6},{8,9},{9,8},{10,11... | collective-permute-start | bytes 589832 | tf_op jit(solution)/shard_map/ppermute | solution.py:59
  27.2 0.9 %copy-start.5 = (bf16[2,128,256]{1,2,0:T(8,128)(2,1)S(1)}, bf16[2,128,256]{1,2,0:T(8,128)(2,1)}, u32[]{:S(2)}) copy-start(bf16[2,128,256]{1,2,0:T(8,128)(2,1)} %copy.232) | copy-start | bytes 393220
  27.2 0.9 %copy-start.22 = (f32[2,8,128]{2,1,0:T(8,128)S(1)}, f32[2,8,128]{2,1,0:T(8,128)}, u32[]{:S(2)}) copy-start(f32[2,8,128]{2,1,0:T(8,128)} %fusion.177) | copy-start | bytes 24580
  28.1 0.7 copy-start.9
  28.1 0.9 %copy-start.12 = (bf16[256,256]{1,0:T(8,128)(2,1)S(1)}, bf16[256,256]{1,0:T(8,128)(2,1)}, u32[]{:S(2)}) copy-start(bf16[256,256]{1,0:T(8,128)(2,1)} %param.24) | copy-start | bytes 393220
  29.1 5.2 %copy-start.4 = (bf16[4,128,128]{1,2,0:T(8,128)(2,1)S(1)}, bf16[4,128,128]{1,2,0:T(8,128)(2,1)}, u32[]{:S(2)}) copy-start(bf16[4,128,128]{1,2,0:T(8,128)(2,1)} %convolution_convert_fusion.5) | copy-start | bytes 393220
  31.2 11.3 %all-to-all-start.1 = ((bf16[2,128,256]{2,0,1:T(2,128)(2,1)}), bf16[2,128,256]{2,0,1:T(2,128)(2,1)S(1)}, u32[]{:S(2)}, u32[]{:S(2)}) async-start(bf16[2,128,256]{2,0,1:T(2,128)(2,1)} %copy.243), calls=%async_computation.1 | async-start | bytes 262144 | tf_op jit(solution)/shard_map/all_to_all | solution.py:120
  34.3 0.8 copy-start.14
  34.6 2.0 %copy-start.18 = (bf16[128,4]{0,1:T(4,128)(2,1)S(1)}, bf16[128,4]{0,1:T(4,128)(2,1)}, u32[]{:S(2)}) copy-start(bf16[128,4]{0,1:T(4,128)(2,1)} %param.31) | copy-start | bytes 3076
  42.5 13.2 %all-to-all-start.2 = ((bf16[32,32,128]{2,1,0:T(8,128)(2,1)}), bf16[32,32,128]{2,1,0:T(8,128)(2,1)S(1)}, u32[]{:S(2)}, u32[]{:S(2)}) async-start(bf16[32,32,128]{2,1,0:T(8,128)(2,1)} %copy.267), calls=%async_computation.2 | async-start | bytes 524288 | tf_op jit(solution)/shard_map/all_to_all | solution.py:76
  45.4 1.1 %copy-start.3 = (bf16[4,256,256]{2,1,0:T(8,128)(2,1)S(1)}, bf16[4,256,256]{2,1,0:T(8,128)(2,1)}, u32[]{:S(2)}) copy-start(bf16[4,256,256]{2,1,0:T(8,128)(2,1)} %param.25) | copy-start | bytes 1572868
  46.8 0.9 %copy-start.10 = (f32[64]{0:T(128)S(1)}, f32[64]{0:T(128)}, u32[]{:S(2)}) copy-start(f32[64]{0:T(128)} %get-tuple-element.19) | copy-start | bytes 772
  48.8 0.9 %copy-start.13 = (bf16[256,256]{1,0:T(8,128)(2,1)S(1)}, bf16[256,256]{1,0:T(8,128)(2,1)}, u32[]{:S(2)}) copy-start(bf16[256,256]{1,0:T(8,128)(2,1)} %param.26) | copy-start | bytes 393220
  49.7 1.5 %copy-start.16 = (bf16[256,32]{0,1:T(8,128)(2,1)S(1)}, bf16[256,32]{0,1:T(8,128)(2,1)}, u32[]{:S(2)}) copy-start(bf16[256,32]{0,1:T(8,128)(2,1)} %param.33) | copy-start | bytes 49156
  49.7 1.5 %copy-start.21 = (f32[64]{0:T(128)S(1)}, f32[64]{0:T(128)}, u32[]{:S(2)}) copy-start(f32[64]{0:T(128)} %convert_element_type.221) | copy-start | bytes 772
  52.6 8.1 %copy-start.7 = (bf16[4,128,128]{2,1,0:T(8,128)(2,1)S(1)}, bf16[4,128,128]{2,1,0:T(8,128)(2,1)}, u32[]{:S(2)}) copy-start(bf16[4,128,128]{2,1,0:T(8,128)(2,1)} %param.30) | copy-start | bytes 393220
  55.7 13.9 %all-to-all-start.3 = ((bf16[16,2,4096]{2,1,0:T(2,128)(2,1)}), bf16[16,2,4096]{2,1,0:T(2,128)(2,1)S(1)}, u32[]{:S(2)}, u32[]{:S(2)}) async-start(bf16[16,2,4096]{2,1,0:T(2,128)(2,1)} %reshape.281), calls=%async_computation.3 | async-start | bytes 524288 | tf_op jit(solution)/shard_map/all_to_all | solution.py:58
  70.0 2.0 %collective-permute-start.1 = (bf16[16,64,4,32]{1,3,2,0:T(8,128)(2,1)S(1)}, bf16[16,64,4,32]{1,3,2,0:T(8,128)(2,1)S(1)}, u32[]{:S(2)}, u32[]{:S(2)}) collective-permute-start(bf16[16,64,4,32]{1,3,2,0:T(8,128)(2,1)S(1)} %bitcast.247), channel_id=1, source_target_pairs={{0,1},{1,0},{2,3},{3,2},{4,5},{5,4},{6,7},{7,6},{8,9},{9,8},{10,11... | collective-permute-start | bytes 786440 | tf_op jit(solution)/shard_map/ppermute | solution.py:59
  72.6 1.1 %copy-start.17 = (bf16[256,32]{0,1:T(8,128)(2,1)S(1)}, bf16[256,32]{0,1:T(8,128)(2,1)}, u32[]{:S(2)}) copy-start(bf16[256,32]{0,1:T(8,128)(2,1)} %param.34) | copy-start | bytes 49156
  75.0 0.8 copy-start.15

commit v15 on v6

--- a/solution.py
+++ b/solution.py
@@ -29,7 +29,7 @@
     return jnp.einsum("bqc,cf->bqf", inputs, weight_table, preferred_element_type=jnp.float32)
 
 
-def attend(inputs, weights, bias_table, key_bias, output_map, head_count):
+def attend(inputs, weights, bias_table, key_bias, output_map, head_count, early=False):
     batch_size, query_count, width = inputs.shape
     query_all = project(inputs, weights[0]).astype(jnp.bfloat16)
     key_all = project(inputs, weights[1]).astype(jnp.bfloat16)
@@ -42,6 +42,8 @@
     scores = jnp.einsum(
         "bqhd,bkhd->bhqk", query_heads, key_heads, preferred_element_type=jnp.float32
     ) * head_size ** (-0.5)
+    if early:
+        scores = lax.optimization_barrier(scores)
     if bias_table is not None:
         scores = scores + bias_table.astype(jnp.float32)[None]
     scores = scores + key_bias
@@ -118,7 +120,9 @@
     both_bias = gather_blocks(both_local, 1, count)
     row_bias = both_bias[:H_M]
     start_bias = both_bias[H_M:]
-    row_update = attend(layer_norm(alignment), row_project, row_bias, residue_keys, row_output, H_M)
+    row_update = attend(
+        layer_norm(alignment), row_project, row_bias, residue_keys, row_output, H_M, True
+    )
     alignment_one = (alignment.astype(jnp.float32) + row_update).astype(jnp.bfloat16)
     alignment_cols = lax.all_to_all(alignment_one, DAP, 1, 0, tiled=True)
     start_update = attend(pair_norm, start_project, start_bias, residue_keys, start_output, H_Z)

time: 77.2 us -> 81.2 us (1.052)
  matrix products: 16.7 us -> 20.1 us
  other arithmetic: 6.61 us -> 7.48 us
    dot_general x4, matrix products: 1.39 us -> 5.31 us  [attend(): jnp.einsum('bhqk,bkhd->bqhd', softened, value_heads, preferred_element_ty...]
    sub x4 -> x3, matrix products: 2.83 us -> 2.28 us  [attend(): softened = jax.nn.softmax(scores, axis=-1).astype(jnp.bfloat16)]
    unnamed x54 -> x60, local copies, waits for them, and re-layouts: 5.16 us -> 4.97 us
  transfers between devices with their start and end apart: 6 -> 6, of which waited for: 6 -> 6; matrix products, arithmetic and copies ran while one was open for 25% -> 24% of each run, Pallas kernels for 0% -> 0%
where the time goes in v15:
time: 81.2 us; the launch traced here: 80.4 us
  matrix products  20.1 us (25%)
  waiting for transfers between devices  20 us (25%)
  starting transfers between devices  18.5 us (23%)
  local copies, waits for them, and re-layouts  12.8 us (16%)
  other arithmetic  7.48 us (9%)
  between operations  1.47 us (2%)
    all_to_all x2, starting transfers between devices, gather_blocks(): same_core = lax.all_to_all(spread, 'chip', 0, 0, tiled=True)  12.2 us
    all_to_all x2, waiting for transfers between devices, gather_blocks(): same_core = lax.all_to_all(spread, 'chip', 0, 0, tiled=True)  9.49 us
    dot_general x4, matrix products, attend(): jnp.einsum('bhqk,bkhd->bqhd', softened, value_heads, preferred_element_ty...  5.31 us
    unnamed x60, local copies, waits for them, and re-layouts  4.97 us
    all_to_all x1, waiting for transfers between devices, per_device(): alignment_cols = lax.all_to_all(alignment_one, DAP, 1, 0, tiled=True)  4.66 us
    dot_general x12, matrix products, project(): jnp.einsum('bqc,cf->bqf', inputs, weight_table, preferred_element_type=jn...  3.98 us
    dot_general x4, matrix products, attend(): jnp.einsum('bqf,fc->bqc', gated, output_map, preferred_element_type=jnp.f...  3.49 us
    all_to_all x1, starting transfers between devices, per_device(): alignment_cols = lax.all_to_all(alignment_one, DAP, 1, 0, tiled=True)  3.47 us
  transfers between devices with their start and end apart: 6, of which 6 were waited for; matrix products, arithmetic and copies ran while one was open for 24% of the time, Pallas kernels for 0%

profile of v15, /device:TPU:0, one launch (start us, length us, event | category | flops | bytes accessed | tf_op | source)
XLA Modules:
  0.0 80.4 jit_solution(7814238678815593217)
XLA Ops:
  0.7 1.1 %convert_reduce_fusion = f32[4,128]{1,0:T(4,128)S(1)} fusion(bf16[4,128,128]{2,1,0:T(8,128)(2,1)} %param.19), kind=kLoop, calls=%fused_computation.93 | loop fusion | flops 130560 | bytes 133120 | tf_op jit(solution)/shard_map/reduce_sum | solution.py:19
  1.8 1.1 %fusion.64 = f32[4,128]{1,0:T(4,128)S(1)} fusion(bf16[4,128,128]{2,1,0:T(8,128)(2,1)} %param.19, f32[4,128]{1,0:T(4,128)S(1)} %broadcast_multiply_fusion.4), kind=kLoop, calls=%fused_computation.108 | loop fusion | flops 261632 | bytes 135168 | tf_op jit(solution)/shard_map/reduce_sum | solution.py:20
  2.9 1.3 %convolution_convert_fusion.12 = bf16[12,4,128]{2,0,1:T(8,128)(2,1)S(1)} fusion(bf16[4,128,128]{2,1,0:T(8,128)(2,1)} %param.19, f32[4,128]{1,0:T(4,128)S(1)} %add_rsqrt_fusion.4, f32[4,128]{1,0:T(4,128)S(1)} %broadcast_multiply_fusion.4, bf16[128,4]{0,1:T(4,128)(2,1)} %param.28, bf16[128,8]{0,1:T(8,128)(2,1)} %param.23), kind=kOutput, calls=%fused_computation.74 | convolution fusion | flops 1847296 | bytes 150528 | tf_op jit(solution)/shard_map/ijc,ch->hij/dot_general | solution.py:117
  4.2 0.7 broadcast_in_dim.8
  4.9 8.4 %all-to-all-start = ((bf16[16,12,4,128]{3,2,1,0:T(4,128)(2,1)}), bf16[16,12,4,128]{3,2,1,0:T(4,128)(2,1)S(1)}, u32[]{:S(2)}, u32[]{:S(2)}) async-start(bf16[16,12,4,128]{3,2,1,0:T(4,128)(2,1)} %broadcast_in_dim.8), calls=%async_computation | async-start | bytes 393216 | tf_op jit(solution)/shard_map/all_to_all | solution.py:60
  14.6 1.0 %convolution_convert_fusion.5 = bf16[4,128,128]{1,2,0:T(8,128)(2,1)} fusion(bf16[4,128,128]{2,1,0:T(8,128)(2,1)S(1)} %copy-done.1, f32[4,128]{1,0:T(4,128)S(1)} %add_rsqrt_fusion.4, f32[4,128]{1,0:T(4,128)S(1)} %broadcast_multiply_fusion.4, bf16[4,128,128]{2,1,0:T(8,128)(2,1)S(1)} %copy-done.7), kind=kOutput, calls=%fused_computation.62 | convolution fusion | flops 17104896 | bytes 299008 | tf_op jit(solution)/shard_map/bqc,cf->bqf/dot_general | solution.py:29
  16.0 0.8 copy.310
  17.4 0.6 convert_element_type.221
  18.0 1.2 %convert_reduce_fusion.4 = (f32[]{:T(128)}, f32[64]{0:T(128)}) fusion(s32[64]{0:T(128)S(1)} %copy-done.22), kind=kLoop, calls=%fused_computation.203 | loop fusion | flops 255 | bytes 516 | tf_op jit(solution)/shard_map/reduce_sum | solution.py:155
  19.6 2.5 %all-to-all-done = bf16[16,12,4,128]{3,2,1,0:T(4,128)(2,1)S(1)} async-done(((bf16[16,12,4,128]{3,2,1,0:T(4,128)(2,1)}), bf16[16,12,4,128]{3,2,1,0:T(4,128)(2,1)S(1)}, u32[]{:S(2)}, u32[]{:S(2)}) %all-to-all-start) | async-done | bytes 196640 | tf_op jit(solution)/shard_map/all_to_all | solution.py:60
  22.1 1.4 %collective-permute-done = bf16[16,12,4,128]{3,2,1,0:T(4,128)(2,1)S(1)} collective-permute-done((bf16[16,12,4,128]{3,2,1,0:T(4,128)(2,1)S(1)}, bf16[16,12,4,128]{3,2,1,0:T(4,128)(2,1)S(1)}, u32[]{:S(2)}, u32[]{:S(2)}) %collective-permute-start) | collective-permute-done | bytes 196640 | tf_op jit(solution)/shard_map/ppermute | solution.py:61
  24.6 1.2 %fusion.179 = f32[4,4,128]{2,1,0:T(4,128)} fusion(bf16[4,128,4,32]{1,3,2,0:T(8,128)(2,1)S(1)} %bitcast.259, bf16[4,128,4,32]{1,3,2,0:T(8,128)(2,1)S(1)} %bitcast.261, f32[128]{0:T(128)S(1)} %add_multiply_fusion.1, f32[4,128,128]{1,2,0:T(8,128)S(1)} %copy.337), kind=kOutput, calls=%fused_computation.215 | convolution fusion | flops 18088064 | bytes 532992 | tf_op jit(solution)/shard_map/sub | solution.py:50
  27.0 0.6 fusion.173
  27.9 4.3 %fusion.53 = f32[2,8,32,128]{3,2,1,0:T(8,128)S(1)} fusion(bf16[2,128,8,32]{1,3,2,0:T(8,128)(2,1)S(1)} %bitcast.279, f32[2,8,128]{2,1,0:T(8,128)S(1)} %fusion.173, f32[2,8,128,128]{3,2,1,0:T(8,128)S(1)} %convolution_multiply_fusion.2, f32[128]{0:T(128)} %copy-done.9, f32[8,128,128]{2,1,0:T(8,128)S(1)} %copy.316), kind=kOutput, calls=%fused_computation.88 | convolution fusion | flops 18090112 | bytes 1974784 | tf_op jit(solution)/shard_map/bhqk,bkhd->bqhd/dot_general | solution.py:51
  32.4 1.4 %fusion.42 = bf16[2,128,256]{2,1,0:T(8,128)(2,1)S(1)} fusion(f32[2,128,256]{2,1,0:T(8,128)S(1)} %copy.317, bf16[2,128,256]{2,1,0:T(8,128)(2,1)S(1)} %copy-done.3, bf16[256,256]{1,0:T(8,128)(2,1)} %param.24, bf16[4,256,256]{2,1,0:T(8,128)(2,1)} %param.22, f32[2,128]{1,0:T(2,128)} %copy-done.13, f32[2,128]{1,0:T(2,128)} %copy-done.12), kind=kOutput, calls=%fused_computation.55 | convolution fusion | flops 67895296 | bytes 919552 | tf_op jit(solution)/shard_map/bqf,fc->bqc/dot_general | solution.py:54
  33.8 0.8 copy.318
  34.6 3.5 %all-to-all-start.1 = ((bf16[2,128,256]{2,0,1:T(2,128)(2,1)}), bf16[2,128,256]{2,0,1:T(2,128)(2,1)S(1)}, u32[]{:S(2)}, u32[]{:S(2)}) async-start(bf16[2,128,256]{2,0,1:T(2,128)(2,1)} %copy.318), calls=%async_computation.1 | async-start | bytes 262144 | tf_op jit(solution)/shard_map/all_to_all | solution.py:127
  38.8 1.3 %convert_reduce_fusion.3 = (f32[4,128]{1,0:T(4,128)S(1)}, bf16[4,128,128]{2,1,0:T(8,128)(2,1)S(1)}) fusion(bf16[128,128]{1,0:T(8,128)(2,1)S(1)} %copy-done.17, f32[4,128,128]{2,1,0:T(8,128)S(1)} %copy.339, bf16[4,128,128]{2,1,0:T(8,128)(2,1)S(1)} %copy-done.1, f32[4,128]{1,0:T(4,128)S(1)} %add_rsqrt_fusion.4, f32[4,128]{1,0:T(4,128)S(1)} %broadcast_multiply_fusion.4, ...), kind=kOutput, calls=%fused_computation.99 | convolution fusion | flops 34471424 | bytes 727040 | tf_op jit(solution)/shard_map/bqf,fc->bqc/dot_general | solution.py:54
  40.8 0.8 copy.342
  41.6 4.7 %all-to-all-done.1 = bf16[2,128,256]{2,0,1:T(2,128)(2,1)S(1)} async-done(((bf16[2,128,256]{2,0,1:T(2,128)(2,1)}), bf16[2,128,256]{2,0,1:T(2,128)(2,1)S(1)}, u32[]{:S(2)}, u32[]{:S(2)}) %all-to-all-start.1) | async-done | bytes 131104 | tf_op jit(solution)/shard_map/all_to_all | solution.py:127
  46.3 2.8 %all-to-all-start.2 = ((bf16[32,32,128]{2,1,0:T(8,128)(2,1)}), bf16[32,32,128]{2,1,0:T(8,128)(2,1)S(1)}, u32[]{:S(2)}, u32[]{:S(2)}) async-start(bf16[32,32,128]{2,1,0:T(8,128)(2,1)} %copy.342), calls=%async_computation.2 | async-start | bytes 524288 | tf_op jit(solution)/shard_map/all_to_all | solution.py:81
  51.5 0.6 fusion.174
  54.2 0.8 copy.362
  55.3 1.1 %reshape.283 = bf16[16,2,4096]{2,1,0:T(2,128)(2,1)} reshape(bf16[16,4,32,64]{3,2,1,0:T(8,128)(2,1)S(1)} %broadcast_bitcast_fusion) | data formatting | bytes 524288
  56.4 3.1 %all-to-all-done.2 = bf16[32,32,128]{2,1,0:T(8,128)(2,1)S(1)} async-done(((bf16[32,32,128]{2,1,0:T(8,128)(2,1)}), bf16[32,32,128]{2,1,0:T(8,128)(2,1)S(1)}, u32[]{:S(2)}, u32[]{:S(2)}) %all-to-all-start.2) | async-done | bytes 262176 | tf_op jit(solution)/shard_map/all_to_all | solution.py:81
  59.5 3.7 %all-to-all-start.3 = ((bf16[16,2,4096]{2,1,0:T(2,128)(2,1)}), bf16[16,2,4096]{2,1,0:T(2,128)(2,1)S(1)}, u32[]{:S(2)}, u32[]{:S(2)}) async-start(bf16[16,2,4096]{2,1,0:T(2,128)(2,1)} %reshape.283), calls=%async_computation.3 | async-start | bytes 524288 | tf_op jit(solution)/shard_map/all_to_all | solution.py:60
  65.2 0.6 fusion.184
  66.4 7.0 %all-to-all-done.3 = bf16[16,2,4096]{2,1,0:T(2,128)(2,1)S(1)} async-done(((bf16[16,2,4096]{2,1,0:T(2,128)(2,1)}), bf16[16,2,4096]{2,1,0:T(2,128)(2,1)S(1)}, u32[]{:S(2)}, u32[]{:S(2)}) %all-to-all-start.3) | async-done | bytes 262176 | tf_op jit(solution)/shard_map/all_to_all | solution.py:60
  74.4 1.4 %collective-permute-done.1 = bf16[16,64,4,32]{1,3,2,0:T(8,128)(2,1)S(1)} collective-permute-done((bf16[16,64,4,32]{1,3,2,0:T(8,128)(2,1)S(1)}, bf16[16,64,4,32]{1,3,2,0:T(8,128)(2,1)S(1)}, u32[]{:S(2)}, u32[]{:S(2)}) %collective-permute-start.1) | collective-permute-done | bytes 262176 | tf_op jit(solution)/shard_map/ppermute | solution.py:61
  76.1 1.1 %copy.360 = bf16[64,128,32]{1,0,2:T(8,128)(2,1)S(1)} copy(bf16[64,128,32]{0,2,1:T(8,128)(2,1)S(1)} %bitcast.241) | data formatting | bytes 1048576 | tf_op jit(solution)/shard_map/reshape | solution.py:70
  77.2 1.3 %divide_convert_fusion = bf16[4,32,128,32]{2,1,3,0:T(8,128)(2,1)S(1)} fusion(f32[]{:T(128)} %get-tuple-element.20, bf16[64,128,32]{1,0,2:T(8,128)(2,1)S(1)} %copy.360, bf16[64,4,256]{2,0,1:T(8,128)(2,1)S(1)} %get-tuple-element.23, f32[64,4]{0,1:T(4,128)S(1)} %add_rsqrt_fusion.2, f32[64,4]{0,1:T(4,128)S(1)} %broadcast_multiply_fusion.2, ...), kind=kOutput, calls=%fused_computation.4 | convolution fusion | flops 72630272 | bytes 1722628 | tf_op jit(solution)/shard_map/sic,sje->ijce/dot_general | solution.py:157
  79.7 0.8 copy.363
  (143 shorter events, 16.2 us)
Async XLA Ops:
  0.6 77.9 %copy-start = (bf16[1024,128]{1,0:T(8,128)(2,1)S(1)}, bf16[1024,128]{1,0:T(8,128)(2,1)}, u32[]{:S(2)}) copy-start(bf16[1024,128]{1,0:T(8,128)(2,1)} %param.35) | copy-start | bytes 786436
  0.6 12.7 %copy-start.2 = (bf16[2,128,256]{2,1,0:T(8,128)(2,1)S(1)}, bf16[2,128,256]{2,1,0:T(8,128)(2,1)}, u32[]{:S(2)}) copy-start(bf16[2,128,256]{2,1,0:T(8,128)(2,1)} %param.18) | copy-start | bytes 393220
  0.7 13.1 %copy-start.15 = (bf16[4,256,256]{2,1,0:T(8,128)(2,1)S(1)}, bf16[4,256,256]{2,1,0:T(8,128)(2,1)}, u32[]{:S(2)}) copy-start(bf16[4,256,256]{2,1,0:T(8,128)(2,1)} %param.22) | copy-start | bytes 1572868
  4.9 9.6 %copy-start.1 = (bf16[4,128,128]{2,1,0:T(8,128)(2,1)S(1)}, bf16[4,128,128]{2,1,0:T(8,128)(2,1)}, u32[]{:S(2)}) copy-start(bf16[4,128,128]{2,1,0:T(8,128)(2,1)} %param.19) | copy-start | bytes 393220
  4.9 9.6 %copy-start.7 = (bf16[4,128,128]{2,1,0:T(8,128)(2,1)S(1)}, bf16[4,128,128]{2,1,0:T(8,128)(2,1)}, u32[]{:S(2)}) copy-start(bf16[4,128,128]{2,1,0:T(8,128)(2,1)} %param.27) | copy-start | bytes 393220
  4.9 17.1 %all-to-all-start = ((bf16[16,12,4,128]{3,2,1,0:T(4,128)(2,1)}), bf16[16,12,4,128]{3,2,1,0:T(4,128)(2,1)S(1)}, u32[]{:S(2)}, u32[]{:S(2)}) async-start(bf16[16,12,4,128]{3,2,1,0:T(4,128)(2,1)} %broadcast_in_dim.8), calls=%async_computation | async-start | bytes 393216 | tf_op jit(solution)/shard_map/all_to_all | solution.py:60
  13.5 2.4 %copy-start.12 = (f32[2,128]{1,0:T(2,128)}, f32[2,128]{1,0:T(2,128)S(1)}, u32[]{:S(2)}) copy-start(f32[2,128]{1,0:T(2,128)S(1)} %broadcast_multiply_fusion.5) | copy-start | bytes 3076
  13.7 2.2 %copy-start.13 = (f32[2,128]{1,0:T(2,128)}, f32[2,128]{1,0:T(2,128)S(1)}, u32[]{:S(2)}) copy-start(f32[2,128]{1,0:T(2,128)S(1)} %add_rsqrt_fusion.5) | copy-start | bytes 3076
  16.0 1.4 %copy-start.22 = (s32[64]{0:T(128)S(1)}, s32[64]{0:T(128)}, u32[]{:S(2)}) copy-start(s32[64]{0:T(128)} %param.20) | copy-start | bytes 772
  16.8 5.3 %copy-start.23 = (s32[128]{0:T(128)S(1)}, s32[128]{0:T(128)}, u32[]{:S(2)}) copy-start(s32[128]{0:T(128)} %param.21) | copy-start | bytes 1540
  22.0 1.4 %collective-permute-start = (bf16[16,12,4,128]{3,2,1,0:T(4,128)(2,1)S(1)}, bf16[16,12,4,128]{3,2,1,0:T(4,128)(2,1)S(1)}, u32[]{:S(2)}, u32[]{:S(2)}) collective-permute-start(bf16[16,12,4,128]{3,2,1,0:T(4,128)(2,1)S(1)} %all-to-all-done), channel_id=1, source_target_pairs={{0,1},{1,0},{2,3},{3,2},{4,5},{5,4},{6,7},{7,6},{8,9},{9,8},{10,11... | collective-permute-start | bytes 589832 | tf_op jit(solution)/shard_map/ppermute | solution.py:61
  22.0 4.1 %copy-start.9 = (f32[128]{0:T(128)}, f32[128]{0:T(128)S(1)}, u32[]{:S(2)}) copy-start(f32[128]{0:T(128)S(1)} %add_multiply_fusion.1) | copy-start | bytes 1540
  26.4 0.6 copy-start.10
  27.0 0.9 %copy-start.6 = (bf16[2,128,256]{1,2,0:T(8,128)(2,1)S(1)}, bf16[2,128,256]{1,2,0:T(8,128)(2,1)}, u32[]{:S(2)}) copy-start(bf16[2,128,256]{1,2,0:T(8,128)(2,1)} %copy.310) | copy-start | bytes 393220
  27.9 4.4 %copy-start.3 = (bf16[2,128,256]{2,1,0:T(8,128)(2,1)S(1)}, bf16[2,128,256]{2,1,0:T(8,128)(2,1)}, u32[]{:S(2)}) copy-start(bf16[2,128,256]{2,1,0:T(8,128)(2,1)} %param.18) | copy-start | bytes 393220
  32.4 5.7 %copy-start.5 = (bf16[4,128,128]{1,2,0:T(8,128)(2,1)S(1)}, bf16[4,128,128]{1,2,0:T(8,128)(2,1)}, u32[]{:S(2)}) copy-start(bf16[4,128,128]{1,2,0:T(8,128)(2,1)} %convolution_convert_fusion.5) | copy-start | bytes 393220
  32.4 5.7 %copy-start.25 = (f32[4,4,128]{2,1,0:T(4,128)S(1)}, f32[4,4,128]{2,1,0:T(4,128)}, u32[]{:S(2)}) copy-start(f32[4,4,128]{2,1,0:T(4,128)} %fusion.179) | copy-start | bytes 24580
  34.6 11.7 %all-to-all-start.1 = ((bf16[2,128,256]{2,0,1:T(2,128)(2,1)}), bf16[2,128,256]{2,0,1:T(2,128)(2,1)S(1)}, u32[]{:S(2)}, u32[]{:S(2)}) async-start(bf16[2,128,256]{2,0,1:T(2,128)(2,1)} %copy.318), calls=%async_computation.1 | async-start | bytes 262144 | tf_op jit(solution)/shard_map/all_to_all | solution.py:127
  38.1 0.8 copy-start.17
  38.4 2.0 %copy-start.21 = (bf16[128,4]{0,1:T(4,128)(2,1)S(1)}, bf16[128,4]{0,1:T(4,128)(2,1)}, u32[]{:S(2)}) copy-start(bf16[128,4]{0,1:T(4,128)(2,1)} %param.31) | copy-start | bytes 3076
  46.3 13.2 %all-to-all-start.2 = ((bf16[32,32,128]{2,1,0:T(8,128)(2,1)}), bf16[32,32,128]{2,1,0:T(8,128)(2,1)S(1)}, u32[]{:S(2)}, u32[]{:S(2)}) async-start(bf16[32,32,128]{2,1,0:T(8,128)(2,1)} %copy.342), calls=%async_computation.2 | async-start | bytes 524288 | tf_op jit(solution)/shard_map/all_to_all | solution.py:81
  49.2 1.1 %copy-start.4 = (bf16[4,256,256]{2,1,0:T(8,128)(2,1)S(1)}, bf16[4,256,256]{2,1,0:T(8,128)(2,1)}, u32[]{:S(2)}) copy-start(bf16[4,256,256]{2,1,0:T(8,128)(2,1)} %param.25) | copy-start | bytes 1572868
  50.6 0.9 %copy-start.14 = (f32[64]{0:T(128)S(1)}, f32[64]{0:T(128)}, u32[]{:S(2)}) copy-start(f32[64]{0:T(128)} %get-tuple-element.21) | copy-start | bytes 772
  52.6 0.9 %copy-start.16 = (bf16[256,256]{1,0:T(8,128)(2,1)S(1)}, bf16[256,256]{1,0:T(8,128)(2,1)}, u32[]{:S(2)}) copy-start(bf16[256,256]{1,0:T(8,128)(2,1)} %param.26) | copy-start | bytes 393220
  53.5 1.5 %copy-start.19 = (bf16[256,32]{0,1:T(8,128)(2,1)S(1)}, bf16[256,32]{0,1:T(8,128)(2,1)}, u32[]{:S(2)}) copy-start(bf16[256,32]{0,1:T(8,128)(2,1)} %param.33) | copy-start | bytes 49156
  53.5 1.5 %copy-start.24 = (f32[64]{0:T(128)S(1)}, f32[64]{0:T(128)}, u32[]{:S(2)}) copy-start(f32[64]{0:T(128)} %convert_element_type.221) | copy-start | bytes 772
  56.4 8.1 %copy-start.8 = (bf16[4,128,128]{2,1,0:T(8,128)(2,1)S(1)}, bf16[4,128,128]{2,1,0:T(8,128)(2,1)}, u32[]{:S(2)}) copy-start(bf16[4,128,128]{2,1,0:T(8,128)(2,1)} %param.30) | copy-start | bytes 393220
  59.5 13.9 %all-to-all-start.3 = ((bf16[16,2,4096]{2,1,0:T(2,128)(2,1)}), bf16[16,2,4096]{2,1,0:T(2,128)(2,1)S(1)}, u32[]{:S(2)}, u32[]{:S(2)}) async-start(bf16[16,2,4096]{2,1,0:T(2,128)(2,1)} %reshape.283), calls=%async_computation.3 | async-start | bytes 524288 | tf_op jit(solution)/shard_map/all_to_all | solution.py:60
  64.1 1.1 %copy-start.11 = (f32[128]{0:T(128)S(1)}, f32[128]{0:T(128)}, u32[]{:S(2)}) copy-start(f32[128]{0:T(128)} %copy-done.9) | copy-start | bytes 1540
  73.8 2.0 %collective-permute-start.1 = (bf16[16,64,4,32]{1,3,2,0:T(8,128)(2,1)S(1)}, bf16[16,64,4,32]{1,3,2,0:T(8,128)(2,1)S(1)}, u32[]{:S(2)}, u32[]{:S(2)}) collective-permute-start(bf16[16,64,4,32]{1,3,2,0:T(8,128)(2,1)S(1)} %bitcast.242), channel_id=1, source_target_pairs={{0,1},{1,0},{2,3},{3,2},{4,5},{5,4},{6,7},{7,6},{8,9},{9,8},{10,11... | collective-permute-start | bytes 786440 | tf_op jit(solution)/shard_map/ppermute | solution.py:61
  76.1 1.1 %copy-start.20 = (bf16[256,32]{0,1:T(8,128)(2,1)S(1)}, bf16[256,32]{0,1:T(8,128)(2,1)}, u32[]{:S(2)}) copy-start(bf16[256,32]{0,1:T(8,128)(2,1)} %param.34) | copy-start | bytes 49156
  78.6 0.8 copy-start.18

commit v16 on v15

--- a/solution.py
+++ b/solution.py
@@ -29,7 +29,7 @@
     return jnp.einsum("bqc,cf->bqf", inputs, weight_table, preferred_element_type=jnp.float32)
 
 
-def attend(inputs, weights, bias_table, key_bias, output_map, head_count, early=False):
+def attend(inputs, weights, bias_table, key_bias, output_map, head_count, blocks=0):
     batch_size, query_count, width = inputs.shape
     query_all = project(inputs, weights[0]).astype(jnp.bfloat16)
     key_all = project(inputs, weights[1]).astype(jnp.bfloat16)
@@ -42,8 +42,6 @@
     scores = jnp.einsum(
         "bqhd,bkhd->bhqk", query_heads, key_heads, preferred_element_type=jnp.float32
     ) * head_size ** (-0.5)
-    if early:
-        scores = lax.optimization_barrier(scores)
     if bias_table is not None:
         scores = scores + bias_table.astype(jnp.float32)[None]
     scores = scores + key_bias
@@ -51,6 +49,9 @@
     mixed = jnp.einsum("bhqk,bkhd->bqhd", softened, value_heads, preferred_element_type=jnp.float32)
     mixed = mixed.reshape(batch_size, query_count, head_count * head_size)
     gated = (mixed * gating).astype(jnp.bfloat16)
+    if blocks:
+        gated = gated.reshape(batch_size, blocks, query_count // blocks, gated.shape[-1])
+        return jnp.einsum("bdqf,fc->dbqc", gated, output_map, preferred_element_type=jnp.float32)
     return jnp.einsum("bqf,fc->bqc", gated, output_map, preferred_element_type=jnp.float32)
 
 
@@ -121,10 +122,14 @@
     row_bias = both_bias[:H_M]
     start_bias = both_bias[H_M:]
     row_update = attend(
-        layer_norm(alignment), row_project, row_bias, residue_keys, row_output, H_M, True
-    )
-    alignment_one = (alignment.astype(jnp.float32) + row_update).astype(jnp.bfloat16)
-    alignment_cols = lax.all_to_all(alignment_one, DAP, 1, 0, tiled=True)
+        layer_norm(alignment), row_project, row_bias, residue_keys, row_output, H_M, count
+    )
+    by_device = jnp.moveaxis(
+        alignment.reshape(alignment.shape[0], count, -1, alignment.shape[2]), 1, 0
+    )
+    alignment_one = (by_device.astype(jnp.float32) + row_update).astype(jnp.bfloat16)
+    alignment_cols = lax.all_to_all(alignment_one, DAP, 0, 0, tiled=True)
+    alignment_cols = alignment_cols.reshape((-1,) + alignment_cols.shape[2:])
     start_update = attend(pair_norm, start_project, start_bias, residue_keys, start_output, H_Z)
     pair_one = (pairwise.astype(jnp.float32) + start_update).astype(jnp.bfloat16)
     rows_norm_one = layer_norm(pair_one)

time: 81.2 us -> 79.3 us (0.977)
  matrix products: 20.1 us -> 18.7 us
    dot_general x4, matrix products: 5.31 us -> 2.08 us  [attend(): jnp.einsum('bhqk,bkhd->bqhd', softened, value_heads, preferred_element_ty...]
    dot_general x4 -> x3, matrix products: 3.49 us -> 2.05 us  [attend(): jnp.einsum('bqf,fc->bqc', gated, output_map, preferred_element_type=jnp.f...]
    sub x3 -> x4, matrix products: 2.28 us -> 3.43 us  [attend(): softened = jax.nn.softmax(scores, axis=-1).astype(jnp.bfloat16)]
    dot_general x12 -> x13, matrix products: 3.98 us -> 4.95 us  [project(): jnp.einsum('bqc,cf->bqf', inputs, weight_table, preferred_element_type=jn...]
    dot_general x4, matrix products: 1.41 us -> 2.37 us  [attend(): jnp.einsum('bqhd,bkhd->bhqk', query_heads, key_heads, preferred_element_t...]
where the time goes in v16:
time: 79.3 us; the launch traced here: 78.5 us
  waiting for transfers between devices  20.3 us (26%)
  matrix products  18.7 us (24%)
  starting transfers between devices  18 us (23%)
  local copies, waits for them, and re-layouts  13 us (16%)
  other arithmetic  6.84 us (9%)
  between operations  1.5 us (2%)
    all_to_all x2, starting transfers between devices, gather_blocks(): same_core = lax.all_to_all(spread, 'chip', 0, 0, tiled=True)  12.1 us
    all_to_all x2, waiting for transfers between devices, gather_blocks(): same_core = lax.all_to_all(spread, 'chip', 0, 0, tiled=True)  9.64 us
    unnamed x60, local copies, waits for them, and re-layouts  5.29 us
    dot_general x13, matrix products, project(): jnp.einsum('bqc,cf->bqf', inputs, weight_table, preferred_element_type=jn...  4.95 us
    all_to_all x1, waiting for transfers between devices, per_device(): alignment_cols = lax.all_to_all(alignment_one, DAP, 0, 0, tiled=True)  4.65 us
    sub x4, matrix products, attend(): softened = jax.nn.softmax(scores, axis=-1).astype(jnp.bfloat16)  3.43 us
    all_to_all x1, waiting for transfers between devices, exchange_pair(): lax.all_to_all(jnp.concatenate([pair_part, end_part], axis=1), DAP, 0, 0,...  3.29 us
    all_to_all x1, starting transfers between devices, per_device(): alignment_cols = lax.all_to_all(alignment_one, DAP, 0, 0, tiled=True)  3.26 us
  transfers between devices with their start and end apart: 6, of which 6 were waited for; matrix products, arithmetic and copies ran while one was open for 24% of the time, Pallas kernels for 0%

profile of v16, /device:TPU:0, one launch (start us, length us, event | category | flops | bytes accessed | tf_op | source)
XLA Modules:
  0.0 78.5 jit_solution(14397530447395869805)
XLA Ops:
  0.7 1.1 %convert_reduce_fusion = f32[4,128]{1,0:T(4,128)S(1)} fusion(bf16[4,128,128]{2,1,0:T(8,128)(2,1)} %param.19), kind=kLoop, calls=%fused_computation.92 | loop fusion | flops 130560 | bytes 133120 | tf_op jit(solution)/shard_map/reduce_sum | solution.py:19
  1.8 1.1 %fusion.62 = f32[4,128]{1,0:T(4,128)S(1)} fusion(bf16[4,128,128]{2,1,0:T(8,128)(2,1)} %param.19, f32[4,128]{1,0:T(4,128)S(1)} %broadcast_multiply_fusion.4), kind=kLoop, calls=%fused_computation.103 | loop fusion | flops 261632 | bytes 135168 | tf_op jit(solution)/shard_map/reduce_sum | solution.py:20
  2.9 1.3 %convolution_convert_fusion.12 = bf16[12,4,128]{2,0,1:T(8,128)(2,1)S(1)} fusion(bf16[4,128,128]{2,1,0:T(8,128)(2,1)} %param.19, f32[4,128]{1,0:T(4,128)S(1)} %add_rsqrt_fusion.4, f32[4,128]{1,0:T(4,128)S(1)} %broadcast_multiply_fusion.4, bf16[128,4]{0,1:T(4,128)(2,1)} %param.28, bf16[128,8]{0,1:T(8,128)(2,1)} %param.23), kind=kOutput, calls=%fused_computation.77 | convolution fusion | flops 1847296 | bytes 150528 | tf_op jit(solution)/shard_map/ijc,ch->hij/dot_general | solution.py:118
  4.2 0.7 broadcast_in_dim.8
  4.9 8.3 %all-to-all-start = ((bf16[16,12,4,128]{3,2,1,0:T(4,128)(2,1)}), bf16[16,12,4,128]{3,2,1,0:T(4,128)(2,1)S(1)}, u32[]{:S(2)}, u32[]{:S(2)}) async-start(bf16[16,12,4,128]{3,2,1,0:T(4,128)(2,1)} %broadcast_in_dim.8), calls=%async_computation | async-start | bytes 393216 | tf_op jit(solution)/shard_map/all_to_all | solution.py:61
  14.6 1.0 %convolution_convert_fusion.5 = bf16[4,128,128]{1,2,0:T(8,128)(2,1)} fusion(bf16[4,128,128]{2,1,0:T(8,128)(2,1)S(1)} %copy-done.1, f32[4,128]{1,0:T(4,128)S(1)} %add_rsqrt_fusion.4, f32[4,128]{1,0:T(4,128)S(1)} %broadcast_multiply_fusion.4, bf16[4,128,128]{2,1,0:T(8,128)(2,1)S(1)} %copy-done.9), kind=kOutput, calls=%fused_computation.64 | convolution fusion | flops 17104896 | bytes 299008 | tf_op jit(solution)/shard_map/bqc,cf->bqf/dot_general | solution.py:29
  16.0 0.8 copy.192
  17.0 0.6 convert_element_type.223
  17.7 1.2 %convert_reduce_fusion.5 = (f32[]{:T(128)}, f32[64]{0:T(128)}) fusion(s32[64]{0:T(128)S(1)} %copy-done.21), kind=kLoop, calls=%fused_computation.203 | loop fusion | flops 255 | bytes 516 | tf_op jit(solution)/shard_map/reduce_sum | solution.py:160
  19.3 2.6 %all-to-all-done = bf16[16,12,4,128]{3,2,1,0:T(4,128)(2,1)S(1)} async-done(((bf16[16,12,4,128]{3,2,1,0:T(4,128)(2,1)}), bf16[16,12,4,128]{3,2,1,0:T(4,128)(2,1)S(1)}, u32[]{:S(2)}, u32[]{:S(2)}) %all-to-all-start) | async-done | bytes 196640 | tf_op jit(solution)/shard_map/all_to_all | solution.py:61
  22.1 1.4 %collective-permute-done = bf16[16,12,4,128]{3,0,2,1:T(8,128)(2,1)S(1)} collective-permute-done((bf16[16,12,4,128]{3,0,2,1:T(8,128)(2,1)S(1)}, bf16[16,12,4,128]{3,0,2,1:T(8,128)(2,1)S(1)}, u32[]{:S(2)}, u32[]{:S(2)}) %collective-permute-start) | collective-permute-done | bytes 196640 | tf_op jit(solution)/shard_map/ppermute | solution.py:62
  24.6 1.1 %fusion.161 = f32[2,8,128]{2,1,0:T(8,128)} fusion(bf16[2,128,8,32]{1,3,2,0:T(8,128)(2,1)S(1)} %bitcast.265, bf16[2,128,8,32]{1,3,2,0:T(8,128)(2,1)S(1)} %bitcast.267, f32[128]{0:T(128)S(1)} %add_multiply_fusion.1, f32[8,128,128]{1,2,0:T(8,128)S(1)} %copy.200), kind=kOutput, calls=%fused_computation.213 | convolution fusion | flops 18088064 | bytes 795136 | tf_op jit(solution)/shard_map/sub | solution.py:48
  25.7 1.3 %fusion.13 = f32[2,8,128,128]{2,3,1,0:T(8,128)S(1)} fusion(bf16[2,128,8,32]{1,3,2,0:T(8,128)(2,1)} %bitcast.266, bf16[2,128,8,32]{1,3,2,0:T(8,128)(2,1)} %bitcast.268, f32[128]{0:T(128)S(1)} %add_multiply_fusion.1, f32[8,128,128]{1,2,0:T(8,128)S(1)} %copy.200), kind=kOutput, calls=%fused_computation.17 | convolution fusion | flops 17563648 | bytes 1835520 | tf_op jit(solution)/shard_map/bqhd,bkhd->bhqk/dot_general | solution.py:42
  27.4 1.2 %fusion.167 = f32[4,4,128]{2,1,0:T(4,128)} fusion(bf16[4,128,4,32]{1,3,2,0:T(8,128)(2,1)S(1)} %bitcast.253, bf16[4,128,4,32]{1,3,2,0:T(8,128)(2,1)S(1)} %bitcast.255, f32[128]{0:T(128)S(1)} %add_multiply_fusion.1, f32[4,128,128]{1,2,0:T(8,128)S(1)} %copy.225), kind=kOutput, calls=%fused_computation.215 | convolution fusion | flops 18088064 | bytes 532992 | tf_op jit(solution)/shard_map/sub | solution.py:48
  29.4 1.0 %fusion.53 = f32[2,8,32,128]{3,2,1,0:T(8,128)S(1)} fusion(bf16[2,128,8,32]{1,3,2,0:T(8,128)(2,1)S(1)} %bitcast.277, f32[2,8,128]{2,1,0:T(8,128)} %fusion.161, f32[2,8,128,128]{2,3,1,0:T(8,128)S(1)} %fusion.13), kind=kOutput, calls=%fused_computation.87 | convolution fusion | flops 17565824 | bytes 1449984 | tf_op jit(solution)/shard_map/bhqk,bkhd->bqhd/dot_general | solution.py:49
  30.6 1.2 %fusion.38 = bf16[2,128,256]{2,1,0:T(8,128)(2,1)S(1)} fusion(f32[2,128,256]{2,1,0:T(8,128)S(1)} %copy.202, bf16[4,256,256]{2,1,0:T(8,128)(2,1)} %param.22, bf16[2,128,256]{2,1,0:T(8,128)(2,1)S(1)} %copy-done.2, f32[2,128]{1,0:T(2,128)S(1)} %copy-done.12, f32[2,128]{1,0:T(2,128)S(1)} %broadcast_multiply_fusion.5), kind=kOutput, calls=%fused_computation.51 | convolution fusion | flops 34144256 | bytes 657408 | tf_op jit(solution)/shard_map/bqc,cf->bqf/dot_general | solution.py:29
  32.1 0.8 copy.205
  32.9 3.3 %all-to-all-start.1 = ((bf16[32,2,4,256]{3,2,1,0:T(4,128)(2,1)}), bf16[32,2,4,256]{3,2,1,0:T(4,128)(2,1)S(1)}, u32[]{:S(2)}, u32[]{:S(2)}) async-start(bf16[32,2,4,256]{3,2,1,0:T(4,128)(2,1)} %copy.205), calls=%async_computation.1 | async-start | bytes 262144 | tf_op jit(solution)/shard_map/all_to_all | solution.py:131
  36.9 1.3 %convert_reduce_fusion.2 = (f32[4,128]{1,0:T(4,128)S(1)}, bf16[4,128,128]{2,1,0:T(8,128)(2,1)S(1)}) fusion(bf16[128,128]{1,0:T(8,128)(2,1)S(1)} %copy-done.16, f32[4,128,128]{2,1,0:T(8,128)S(1)} %copy.227, bf16[4,128,128]{2,1,0:T(8,128)(2,1)S(1)} %copy-done.1, f32[4,128]{1,0:T(4,128)S(1)} %add_rsqrt_fusion.4, f32[4,128]{1,0:T(4,128)S(1)} %broadcast_multiply_fusion.4, ...), kind=kOutput, calls=%fused_computation.96 | convolution fusion | flops 34471424 | bytes 727040 | tf_op jit(solution)/shard_map/bqf,fc->bqc/dot_general | solution.py:55
  38.9 0.8 %copy.230 = bf16[32,32,128]{2,1,0:T(8,128)(2,1)} copy(bf16[32,32,128]{2,0,1:T(8,128)(2,1)S(1)} %pad_maximum_fusion) | data formatting | bytes 524288 | tf_op jit(solution)/shard_map/concatenate | solution.py:83
  39.7 4.6 %all-to-all-done.1 = bf16[32,2,4,256]{3,2,1,0:T(4,128)(2,1)S(1)} async-done(((bf16[32,2,4,256]{3,2,1,0:T(4,128)(2,1)}), bf16[32,2,4,256]{3,2,1,0:T(4,128)(2,1)S(1)}, u32[]{:S(2)}, u32[]{:S(2)}) %all-to-all-start.1) | async-done | bytes 131104 | tf_op jit(solution)/shard_map/all_to_all | solution.py:131
  44.4 2.6 %all-to-all-start.2 = ((bf16[32,32,128]{2,1,0:T(8,128)(2,1)}), bf16[32,32,128]{2,1,0:T(8,128)(2,1)S(1)}, u32[]{:S(2)}, u32[]{:S(2)}) async-start(bf16[32,32,128]{2,1,0:T(8,128)(2,1)} %copy.230), calls=%async_computation.2 | async-start | bytes 524288 | tf_op jit(solution)/shard_map/all_to_all | solution.py:82
  50.7 0.7 copy-done.15
  52.1 0.8 copy.250
  53.2 1.1 %reshape.286 = bf16[16,2,4096]{2,1,0:T(2,128)(2,1)} reshape(bf16[16,4,32,64]{3,2,1,0:T(8,128)(2,1)S(1)} %broadcast_bitcast_fusion) | data formatting | bytes 524288
  54.3 3.3 %all-to-all-done.2 = bf16[32,32,128]{2,1,0:T(8,128)(2,1)S(1)} async-done(((bf16[32,32,128]{2,1,0:T(8,128)(2,1)}), bf16[32,32,128]{2,1,0:T(8,128)(2,1)S(1)}, u32[]{:S(2)}, u32[]{:S(2)}) %all-to-all-start.2) | async-done | bytes 262176 | tf_op jit(solution)/shard_map/all_to_all | solution.py:82
  57.6 3.7 %all-to-all-start.3 = ((bf16[16,2,4096]{2,1,0:T(2,128)(2,1)}), bf16[16,2,4096]{2,1,0:T(2,128)(2,1)S(1)}, u32[]{:S(2)}, u32[]{:S(2)}) async-start(bf16[16,2,4096]{2,1,0:T(2,128)(2,1)} %reshape.286), calls=%async_computation.3 | async-start | bytes 524288 | tf_op jit(solution)/shard_map/all_to_all | solution.py:61
  64.5 7.0 %all-to-all-done.3 = bf16[16,2,4096]{2,1,0:T(2,128)(2,1)S(1)} async-done(((bf16[16,2,4096]{2,1,0:T(2,128)(2,1)}), bf16[16,2,4096]{2,1,0:T(2,128)(2,1)S(1)}, u32[]{:S(2)}, u32[]{:S(2)}) %all-to-all-start.3) | async-done | bytes 262176 | tf_op jit(solution)/shard_map/all_to_all | solution.py:61
  72.4 1.4 %collective-permute-done.1 = bf16[16,64,4,32]{1,3,2,0:T(8,128)(2,1)S(1)} collective-permute-done((bf16[16,64,4,32]{1,3,2,0:T(8,128)(2,1)S(1)}, bf16[16,64,4,32]{1,3,2,0:T(8,128)(2,1)S(1)}, u32[]{:S(2)}, u32[]{:S(2)}) %collective-permute-start.1) | collective-permute-done | bytes 262176 | tf_op jit(solution)/shard_map/ppermute | solution.py:62
  74.2 1.1 %copy.248 = bf16[64,128,32]{1,0,2:T(8,128)(2,1)S(1)} copy(bf16[64,128,32]{0,2,1:T(8,128)(2,1)S(1)} %bitcast.234) | data formatting | bytes 1048576 | tf_op jit(solution)/shard_map/reshape | solution.py:71
  75.3 1.3 %divide_convert_fusion = bf16[4,32,128,32]{2,1,3,0:T(8,128)(2,1)S(1)} fusion(f32[]{:T(128)} %get-tuple-element.16, bf16[64,128,32]{1,0,2:T(8,128)(2,1)S(1)} %copy.248, bf16[64,4,256]{2,0,1:T(8,128)(2,1)S(1)} %get-tuple-element.19, f32[64,4]{0,1:T(4,128)S(1)} %add_rsqrt_fusion.2, f32[64,4]{0,1:T(4,128)S(1)} %broadcast_multiply_fusion.2, ...), kind=kOutput, calls=%fused_computation.4 | convolution fusion | flops 72630272 | bytes 1722628 | tf_op jit(solution)/shard_map/sic,sje->ijce/dot_general | solution.py:162
  77.7 0.8 copy.251
  (143 shorter events, 16.4 us)
Async XLA Ops:
  0.6 76.0 %copy-start = (bf16[1024,128]{1,0:T(8,128)(2,1)S(1)}, bf16[1024,128]{1,0:T(8,128)(2,1)}, u32[]{:S(2)}) copy-start(bf16[1024,128]{1,0:T(8,128)(2,1)} %param.35) | copy-start | bytes 786436
  0.6 12.6 %copy-start.2 = (bf16[2,128,256]{2,1,0:T(8,128)(2,1)S(1)}, bf16[2,128,256]{2,1,0:T(8,128)(2,1)}, u32[]{:S(2)}) copy-start(bf16[2,128,256]{2,1,0:T(8,128)(2,1)} %param.18) | copy-start | bytes 393220
  0.7 13.1 %copy-start.14 = (bf16[4,256,256]{2,1,0:T(8,128)(2,1)S(1)}, bf16[4,256,256]{2,1,0:T(8,128)(2,1)}, u32[]{:S(2)}) copy-start(bf16[4,256,256]{2,1,0:T(8,128)(2,1)} %param.22) | copy-start | bytes 1572868
  4.9 17.0 %all-to-all-start = ((bf16[16,12,4,128]{3,2,1,0:T(4,128)(2,1)}), bf16[16,12,4,128]{3,2,1,0:T(4,128)(2,1)S(1)}, u32[]{:S(2)}, u32[]{:S(2)}) async-start(bf16[16,12,4,128]{3,2,1,0:T(4,128)(2,1)} %broadcast_in_dim.8), calls=%async_computation | async-start | bytes 393216 | tf_op jit(solution)/shard_map/all_to_all | solution.py:61
  13.3 1.3 %copy-start.1 = (bf16[4,128,128]{2,1,0:T(8,128)(2,1)S(1)}, bf16[4,128,128]{2,1,0:T(8,128)(2,1)}, u32[]{:S(2)}) copy-start(bf16[4,128,128]{2,1,0:T(8,128)(2,1)} %param.19) | copy-start | bytes 393220
  13.3 1.3 %copy-start.9 = (bf16[4,128,128]{2,1,0:T(8,128)(2,1)S(1)}, bf16[4,128,128]{2,1,0:T(8,128)(2,1)}, u32[]{:S(2)}) copy-start(bf16[4,128,128]{2,1,0:T(8,128)(2,1)} %param.27) | copy-start | bytes 393220
  13.8 2.2 %copy-start.11 = (f32[2,128]{1,0:T(2,128)}, f32[2,128]{1,0:T(2,128)S(1)}, u32[]{:S(2)}) copy-start(f32[2,128]{1,0:T(2,128)S(1)} %add_rsqrt_fusion.5) | copy-start | bytes 3076
  14.0 3.0 %copy-start.21 = (s32[64]{0:T(128)S(1)}, s32[64]{0:T(128)}, u32[]{:S(2)}) copy-start(s32[64]{0:T(128)} %param.20) | copy-start | bytes 772
  14.6 7.5 %copy-start.22 = (s32[128]{0:T(128)S(1)}, s32[128]{0:T(128)}, u32[]{:S(2)}) copy-start(s32[128]{0:T(128)} %param.21) | copy-start | bytes 1540
  16.9 7.7 %copy-start.3 = (bf16[2,128,256]{1,2,0:T(8,128)(2,1)}, bf16[2,128,256]{1,2,0:T(8,128)(2,1)S(1)}, u32[]{:S(2)}) copy-start(bf16[2,128,256]{1,2,0:T(8,128)(2,1)S(1)} %copy.193) | copy-start | bytes 393220
  17.0 7.5 %copy-start.4 = (bf16[2,128,256]{1,2,0:T(8,128)(2,1)}, bf16[2,128,256]{1,2,0:T(8,128)(2,1)S(1)}, u32[]{:S(2)}) copy-start(bf16[2,128,256]{1,2,0:T(8,128)(2,1)S(1)} %copy.194) | copy-start | bytes 393220
  21.9 1.5 %collective-permute-start = (bf16[16,12,4,128]{3,0,2,1:T(8,128)(2,1)S(1)}, bf16[16,12,4,128]{3,0,2,1:T(8,128)(2,1)S(1)}, u32[]{:S(2)}, u32[]{:S(2)}) collective-permute-start(bf16[16,12,4,128]{3,0,2,1:T(8,128)(2,1)S(1)} %copy.297), channel_id=1, source_target_pairs={{0,1},{1,0},{2,3},{3,2},{4,5},{5,4},{6,7},{7,6},{8,9},{9,8},{10,11... | collective-permute-start | bytes 589832 | tf_op jit(solution)/shard_map/ppermute | solution.py:62
  28.5 0.9 %copy-start.8 = (bf16[2,128,256]{1,2,0:T(8,128)(2,1)S(1)}, bf16[2,128,256]{1,2,0:T(8,128)(2,1)}, u32[]{:S(2)}) copy-start(bf16[2,128,256]{1,2,0:T(8,128)(2,1)} %copy.192) | copy-start | bytes 393220
  29.4 1.2 %copy-start.12 = (f32[2,128]{1,0:T(2,128)S(1)}, f32[2,128]{1,0:T(2,128)}, u32[]{:S(2)}) copy-start(f32[2,128]{1,0:T(2,128)} %copy-done.11) | copy-start | bytes 3076
  30.6 1.3 %copy-start.6 = (bf16[256,256]{1,0:T(8,128)(2,1)S(1)}, bf16[256,256]{1,0:T(8,128)(2,1)}, u32[]{:S(2)}) copy-start(bf16[256,256]{1,0:T(8,128)(2,1)} %param.24) | copy-start | bytes 393220
  31.9 4.3 %copy-start.7 = (bf16[4,128,128]{1,2,0:T(8,128)(2,1)S(1)}, bf16[4,128,128]{1,2,0:T(8,128)(2,1)}, u32[]{:S(2)}) copy-start(bf16[4,128,128]{1,2,0:T(8,128)(2,1)} %convolution_convert_fusion.5) | copy-start | bytes 393220
  31.9 4.3 %copy-start.24 = (f32[4,4,128]{2,1,0:T(4,128)S(1)}, f32[4,4,128]{2,1,0:T(4,128)}, u32[]{:S(2)}) copy-start(f32[4,4,128]{2,1,0:T(4,128)} %fusion.167) | copy-start | bytes 24580
  32.9 11.5 %all-to-all-start.1 = ((bf16[32,2,4,256]{3,2,1,0:T(4,128)(2,1)}), bf16[32,2,4,256]{3,2,1,0:T(4,128)(2,1)S(1)}, u32[]{:S(2)}, u32[]{:S(2)}) async-start(bf16[32,2,4,256]{3,2,1,0:T(4,128)(2,1)} %copy.205), calls=%async_computation.1 | async-start | bytes 262144 | tf_op jit(solution)/shard_map/all_to_all | solution.py:131
  36.2 0.8 copy-start.16
  36.5 2.0 %copy-start.20 = (bf16[128,4]{0,1:T(4,128)(2,1)S(1)}, bf16[128,4]{0,1:T(4,128)(2,1)}, u32[]{:S(2)}) copy-start(bf16[128,4]{0,1:T(4,128)(2,1)} %param.31) | copy-start | bytes 3076
  38.9 9.1 %copy-start.5 = (bf16[4,256,256]{2,1,0:T(8,128)(2,1)S(1)}, bf16[4,256,256]{2,1,0:T(8,128)(2,1)}, u32[]{:S(2)}) copy-start(bf16[4,256,256]{2,1,0:T(8,128)(2,1)} %param.25) | copy-start | bytes 1572868
  44.4 13.2 %all-to-all-start.2 = ((bf16[32,32,128]{2,1,0:T(8,128)(2,1)}), bf16[32,32,128]{2,1,0:T(8,128)(2,1)S(1)}, u32[]{:S(2)}, u32[]{:S(2)}) async-start(bf16[32,32,128]{2,1,0:T(8,128)(2,1)} %copy.230), calls=%async_computation.2 | async-start | bytes 524288 | tf_op jit(solution)/shard_map/all_to_all | solution.py:82
  48.1 0.9 %copy-start.13 = (f32[64]{0:T(128)S(1)}, f32[64]{0:T(128)}, u32[]{:S(2)}) copy-start(f32[64]{0:T(128)} %get-tuple-element.17) | copy-start | bytes 772
  50.5 0.9 %copy-start.15 = (bf16[256,256]{1,0:T(8,128)(2,1)S(1)}, bf16[256,256]{1,0:T(8,128)(2,1)}, u32[]{:S(2)}) copy-start(bf16[256,256]{1,0:T(8,128)(2,1)} %param.26) | copy-start | bytes 393220
  51.4 1.4 %copy-start.18 = (bf16[256,32]{0,1:T(8,128)(2,1)S(1)}, bf16[256,32]{0,1:T(8,128)(2,1)}, u32[]{:S(2)}) copy-start(bf16[256,32]{0,1:T(8,128)(2,1)} %param.33) | copy-start | bytes 49156
  51.4 1.4 %copy-start.23 = (f32[64]{0:T(128)S(1)}, f32[64]{0:T(128)}, u32[]{:S(2)}) copy-start(f32[64]{0:T(128)} %convert_element_type.223) | copy-start | bytes 772
  54.3 8.3 %copy-start.10 = (bf16[4,128,128]{2,1,0:T(8,128)(2,1)S(1)}, bf16[4,128,128]{2,1,0:T(8,128)(2,1)}, u32[]{:S(2)}) copy-start(bf16[4,128,128]{2,1,0:T(8,128)(2,1)} %param.30) | copy-start | bytes 393220
  57.6 13.9 %all-to-all-start.3 = ((bf16[16,2,4096]{2,1,0:T(2,128)(2,1)}), bf16[16,2,4096]{2,1,0:T(2,128)(2,1)S(1)}, u32[]{:S(2)}, u32[]{:S(2)}) async-start(bf16[16,2,4096]{2,1,0:T(2,128)(2,1)} %reshape.286), calls=%async_computation.3 | async-start | bytes 524288 | tf_op jit(solution)/shard_map/all_to_all | solution.py:61
  71.8 2.0 %collective-permute-start.1 = (bf16[16,64,4,32]{1,3,2,0:T(8,128)(2,1)S(1)}, bf16[16,64,4,32]{1,3,2,0:T(8,128)(2,1)S(1)}, u32[]{:S(2)}, u32[]{:S(2)}) collective-permute-start(bf16[16,64,4,32]{1,3,2,0:T(8,128)(2,1)S(1)} %bitcast.236), channel_id=1, source_target_pairs={{0,1},{1,0},{2,3},{3,2},{4,5},{5,4},{6,7},{7,6},{8,9},{9,8},{10,11... | collective-permute-start | bytes 786440 | tf_op jit(solution)/shard_map/ppermute | solution.py:62
  74.1 1.1 %copy-start.19 = (bf16[256,32]{0,1:T(8,128)(2,1)S(1)}, bf16[256,32]{0,1:T(8,128)(2,1)}, u32[]{:S(2)}) copy-start(bf16[256,32]{0,1:T(8,128)(2,1)} %param.34) | copy-start | bytes 49156
  76.6 0.8 copy-start.17

commit v17 on v6

--- a/solution.py
+++ b/solution.py
@@ -127,16 +127,11 @@
     end_local = jnp.einsum(
         "kic,ch->hki", rows_norm_one, end_bias_map, preferred_element_type=jnp.float32
     ).astype(jnp.bfloat16)
-    pair_cols, end_all = exchange_pair(pair_one, end_local, count)
-    end_bias = jnp.swapaxes(end_all, 1, 2)
+    pair_cols = lax.all_to_all(pair_one, DAP, 1, 0, tiled=True)
     column_norm = jnp.swapaxes(layer_norm(alignment_cols), 0, 1)
     column_update = attend(column_norm, column_project, None, sequence_keys, column_output, H_M)
     alignment_out = (alignment_cols.astype(jnp.float32) + jnp.swapaxes(column_update, 0, 1)).astype(
         jnp.bfloat16
-    )
-    end_norm = jnp.swapaxes(layer_norm(pair_cols), 0, 1)
-    end_update = jnp.swapaxes(
-        attend(end_norm, end_project, end_bias, residue_keys, end_output, H_Z), 0, 1
     )
     last_norm = layer_norm(alignment_out)
     weighting = sequence_mask.astype(jnp.float32)[:, None, None]
@@ -149,13 +144,21 @@
         * weighting
     ).astype(jnp.bfloat16)
     row_count = jnp.sum(sequence_mask.astype(jnp.float32))
+    packed = jnp.concatenate([left.reshape(-1), end_local.reshape(-1)])
+    received = gather_blocks(packed[None], 0, count)
+    left_all = jnp.moveaxis(received[:, : left.size].reshape((count,) + left.shape), 0, 1)
+    left_all = left_all.reshape(left.shape[0], count * left.shape[1], left.shape[2])
+    end_all = jnp.moveaxis(received[:, left.size :].reshape((count,) + end_local.shape), 0, 1)
+    end_all = end_all.reshape(
+        (end_local.shape[0], count * end_local.shape[1]) + end_local.shape[2:]
+    )
+    end_bias = jnp.swapaxes(end_all, 1, 2)
+    end_norm = jnp.swapaxes(layer_norm(pair_cols), 0, 1)
+    end_update = jnp.swapaxes(
+        attend(end_norm, end_project, end_bias, residue_keys, end_output, H_Z), 0, 1
+    )
     outer_sum = (
-        jnp.einsum(
-            "sic,sje->ijce",
-            gather_blocks(left, 1, count),
-            right,
-            preferred_element_type=jnp.float32,
-        )
+        jnp.einsum("sic,sje->ijce", left_all, right, preferred_element_type=jnp.float32)
         / row_count
     )
     flattened = outer_sum.astype(jnp.bfloat16).reshape(outer_sum.shape[0], outer_sum.shape[1], -1)

time: 77.2 us -> 98.6 us (1.28)
  local copies, waits for them, and re-layouts: 13.2 us -> 21.2 us
  matrix products: 16.7 us -> 23.2 us
  starting transfers between devices: 18.2 us -> 21 us
  waiting for transfers between devices: 20.4 us -> 22.7 us
  other arithmetic: 6.61 us -> 7.92 us
    all_to_all x1, starting transfers between devices: 2.76 us -> 5.89 us  [per_device(): pair_cols = lax.all_to_all(pair_one, DAP, 1, 0, tiled=True)]
    broadcast_in_dim x0 -> x1, other arithmetic: none -> 2.57 us  [gather_blocks(): spread = jnp.broadcast_to(block[None], (half,) + block.shape)]
    dot_general x12, matrix products: 3.98 us -> 6.19 us  [project(): jnp.einsum('bqc,cf->bqf', inputs, weight_table, preferred_element_type=jn...]
    all_to_all x1, waiting for transfers between devices: 3.07 us -> 4.97 us  [per_device(): pair_cols = lax.all_to_all(pair_one, DAP, 1, 0, tiled=True)]
    reshape x2 -> x3, local copies, waits for them, and re-layouts: 1.13 us -> 2.83 us  [the longest x1 1.62 us: per_device(): received[:, :left.size].reshape((count,) + left.shape)]
    dot_general x4, matrix products: 3.42 us -> 5.07 us  [attend(): jnp.einsum('bqf,fc->bqc', gated, output_map, preferred_element_type=jnp.f...]
    sub x4, matrix products: 2.83 us -> 4.38 us  [attend(): softened = jax.nn.softmax(scores, axis=-1).astype(jnp.bfloat16)]
    ppermute x2, waiting for transfers between devices: 2.78 us -> 1.4 us  [gather_blocks(): other_core = lax.ppermute(same_core, 'core', [(0, 1), (1, 0)])]
  transfers between devices with their start and end apart: 6 -> 6, of which waited for: 6 -> 4; matrix products, arithmetic and copies ran while one was open for 25% -> 18% of each run, Pallas kernels for 0% -> 0%
where the time goes in v17:
time: 98.6 us; the launch traced here: 97.6 us
  matrix products  23.2 us (24%)
  waiting for transfers between devices  22.7 us (23%)
  local copies, waits for them, and re-layouts  21.2 us (22%)
  starting transfers between devices  21 us (21%)
  other arithmetic  7.92 us (8%)
  between operations  1.66 us (2%)
    all_to_all x2, starting transfers between devices, gather_blocks(): same_core = lax.all_to_all(spread, 'chip', 0, 0, tiled=True)  12.2 us
    all_to_all x2, waiting for transfers between devices, gather_blocks(): same_core = lax.all_to_all(spread, 'chip', 0, 0, tiled=True)  10.5 us
    dot_general x12, matrix products, project(): jnp.einsum('bqc,cf->bqf', inputs, weight_table, preferred_element_type=jn...  6.19 us
    all_to_all x1, starting transfers between devices, per_device(): pair_cols = lax.all_to_all(pair_one, DAP, 1, 0, tiled=True)  5.89 us
    all_to_all x1, waiting for transfers between devices, per_device(): alignment_cols = lax.all_to_all(alignment_one, DAP, 1, 0, tiled=True)  5.82 us
    dot_general x4, matrix products, attend(): jnp.einsum('bqf,fc->bqc', gated, output_map, preferred_element_type=jnp.f...  5.07 us
    unnamed x69, local copies, waits for them, and re-layouts  5.03 us
    all_to_all x1, waiting for transfers between devices, per_device(): pair_cols = lax.all_to_all(pair_one, DAP, 1, 0, tiled=True)  4.97 us
  transfers between devices with their start and end apart: 6, of which 4 were waited for; matrix products, arithmetic and copies ran while one was open for 18% of the time, Pallas kernels for 0%

profile of v17, /device:TPU:0, one launch (start us, length us, event | category | flops | bytes accessed | tf_op | source)
XLA Modules:
  0.0 97.6 jit_solution(10343247932285663444)
XLA Ops:
  0.7 1.1 %copy.264 = bf16[4,128,128]{1,2,0:T(8,128)(2,1)S(1)} copy(bf16[4,128,128]{2,1,0:T(8,128)(2,1)} %param.19) | data formatting | bytes 262144 | tf_op args[1]
  1.9 0.9 convolution_convert_fusion.12
  3.5 8.4 %all-to-all-start = ((bf16[16,12,4,128]{3,2,1,0:T(4,128)(2,1)}), bf16[16,12,4,128]{3,2,1,0:T(4,128)(2,1)S(1)}, u32[]{:S(2)}, u32[]{:S(2)}) async-start(bf16[16,12,4,128]{3,2,1,0:T(4,128)(2,1)} %broadcast_in_dim.4), calls=%async_computation | async-start | bytes 393216 | tf_op jit(solution)/shard_map/all_to_all | solution.py:58
  11.9 1.0 convolution_convert_fusion.1
  12.9 1.0 convolution_convert_fusion
  13.9 1.0 %convert_reduce_fusion.1 = f32[2,128]{1,0:T(2,128)S(1)} fusion(bf16[2,128,256]{2,1,0:T(8,128)(2,1)} %param.18), kind=kLoop, calls=%fused_computation.93 | loop fusion | flops 130816 | bytes 132096 | tf_op jit(solution)/shard_map/reduce_sum | solution.py:19
  18.8 1.2 %convert_reduce_fusion.4 = (f32[]{:T(128)}, f32[64]{0:T(128)}) fusion(s32[64]{0:T(128)S(1)} %copy-done.26), kind=kLoop, calls=%fused_computation.197 | loop fusion | flops 255 | bytes 516 | tf_op jit(solution)/shard_map/reduce_sum | solution.py:146
  20.0 1.6 %convolution_convert_fusion.2 = bf16[4,128,128]{1,2,0:T(8,128)(2,1)} fusion(bf16[4,128,128]{1,2,0:T(8,128)(2,1)S(1)} %copy.264, f32[4,128]{1,0:T(4,128)S(1)} %add_rsqrt_fusion.4, f32[4,128]{1,0:T(4,128)S(1)} %broadcast_multiply_fusion.4, bf16[4,128,128]{2,1,0:T(8,128)(2,1)} %param.27), kind=kOutput, calls=%fused_computation.61 | convolution fusion | flops 17104896 | bytes 299008 | tf_op jit(solution)/shard_map/bqc,cf->bqf/dot_general | solution.py:29
  21.8 1.4 %collective-permute-done = bf16[16,12,4,128]{3,0,2,1:T(8,128)(2,1)S(1)} collective-permute-done((bf16[16,12,4,128]{3,0,2,1:T(8,128)(2,1)S(1)}, bf16[16,12,4,128]{3,0,2,1:T(8,128)(2,1)S(1)}, u32[]{:S(2)}, u32[]{:S(2)}) %collective-permute-start) | collective-permute-done | bytes 196640 | tf_op jit(solution)/shard_map/ppermute | solution.py:59
  24.3 1.1 %fusion.174 = f32[4,4,128]{2,1,0:T(4,128)} fusion(bf16[4,128,4,32]{1,3,2,0:T(8,128)(2,1)S(1)} %bitcast.277, bf16[4,128,4,32]{1,3,2,0:T(8,128)(2,1)S(1)} %bitcast.279, f32[128]{0:T(128)S(1)} %add_multiply_fusion.1, f32[4,128,128]{1,2,0:T(8,128)S(1)} %copy.296), kind=kOutput, calls=%fused_computation.210 | convolution fusion | flops 18088064 | bytes 532992 | tf_op jit(solution)/shard_map/sub | solution.py:48
  26.1 1.4 %fusion.13 = f32[2,8,128,128]{2,3,1,0:T(8,128)S(1)} fusion(bf16[2,128,8,32]{1,3,2,0:T(8,128)(2,1)} %bitcast.285, bf16[2,128,8,32]{1,3,2,0:T(8,128)(2,1)} %bitcast.287, f32[128]{0:T(128)S(1)} %add_multiply_fusion.1, f32[8,128,128]{1,2,0:T(8,128)S(1)} %copy.271), kind=kOutput, calls=%fused_computation.17 | convolution fusion | flops 17563648 | bytes 1835520 | tf_op jit(solution)/shard_map/bqhd,bkhd->bhqk/dot_general | solution.py:42
  27.5 2.1 %fusion.172 = f32[2,8,128]{2,1,0:T(8,128)} fusion(bf16[2,128,8,32]{1,3,2,0:T(8,128)(2,1)} %bitcast.286, bf16[2,128,8,32]{1,3,2,0:T(8,128)(2,1)} %bitcast.288, f32[128]{0:T(128)S(1)} %add_multiply_fusion.1, f32[8,128,128]{1,2,0:T(8,128)S(1)} %copy.271), kind=kOutput, calls=%fused_computation.208 | convolution fusion | flops 18088064 | bytes 795136 | tf_op jit(solution)/shard_map/sub | solution.py:48
  30.4 1.2 %convert_reduce_fusion.2 = (f32[4,128]{1,0:T(4,128)S(1)}, bf16[4,128,128]{1,2,0:T(8,128)(2,1)S(1)}) fusion(bf16[128,128]{1,0:T(8,128)(2,1)S(1)} %copy-done.22, f32[4,128,128]{2,1,0:T(8,128)S(1)} %copy.299, bf16[4,128,128]{1,2,0:T(8,128)(2,1)S(1)} %copy.264, f32[4,128]{1,0:T(4,128)S(1)} %add_rsqrt_fusion.4, f32[4,128]{1,0:T(4,128)S(1)} %broadcast_multiply_fusion.4, ...), kind=kOutput, calls=%fused_computation.95 | convolution fusion | flops 34471424 | bytes 727040 | tf_op jit(solution)/shard_map/bqf,fc->bqc/dot_general | solution.py:52
  32.3 5.9 %all-to-all-start.2 = ((bf16[4,128,128]{2,0,1:T(4,128)(2,1)}), bf16[4,128,128]{2,0,1:T(4,128)(2,1)S(1)}, u32[]{:S(2)}, u32[]{:S(2)}) async-start(bf16[4,128,128]{2,0,1:T(4,128)(2,1)} %copy.301), calls=%async_computation.2 | async-start | bytes 262144 | tf_op jit(solution)/shard_map/all_to_all | solution.py:130
  39.2 1.3 %fusion.44 = bf16[2,128,256]{2,1,0:T(8,128)(2,1)S(1)} fusion(f32[2,128,256]{2,1,0:T(8,128)S(1)} %copy.273, bf16[2,128,256]{2,1,0:T(8,128)(2,1)S(1)} %copy-done.5, bf16[256,256]{1,0:T(8,128)(2,1)S(1)} %copy-done.21, bf16[4,256,256]{2,1,0:T(8,128)(2,1)} %param.22, f32[2,128]{1,0:T(2,128)S(1)} %copy-done.18, f32[2,128]{1,0:T(2,128)S(1)} %broadcast_multiply_fusion.5), kind=kOutput, calls=%fused_computation.57 | convolution fusion | flops 67895296 | bytes 919552 | tf_op jit(solution)/shard_map/bqf,fc->bqc/dot_general | solution.py:52
  40.5 0.8 copy.274
  41.5 5.0 %all-to-all-done.2 = bf16[4,128,128]{2,0,1:T(4,128)(2,1)S(1)} async-done(((bf16[4,128,128]{2,0,1:T(4,128)(2,1)}), bf16[4,128,128]{2,0,1:T(4,128)(2,1)S(1)}, u32[]{:S(2)}, u32[]{:S(2)}) %all-to-all-start.2) | async-done | bytes 131104 | tf_op jit(solution)/shard_map/all_to_all | solution.py:130
  46.5 2.8 %all-to-all-start.1 = ((bf16[2,128,256]{2,0,1:T(2,128)(2,1)}), bf16[2,128,256]{2,0,1:T(2,128)(2,1)S(1)}, u32[]{:S(2)}, u32[]{:S(2)}) async-start(bf16[2,128,256]{2,0,1:T(2,128)(2,1)} %copy.274), calls=%async_computation.1 | async-start | bytes 262144 | tf_op jit(solution)/shard_map/all_to_all | solution.py:123
  49.5 1.0 copy.305
  50.4 1.0 %multiply_reduce_fusion = f32[32,4,4]{2,0,1:T(8,128)} fusion(bf16[4,32,4,128]{3,2,1,0:T(4,128)(2,1)S(1)} %bitcast.259, f32[32,4,4]{2,0,1:T(8,128)S(1)} %broadcast_multiply_fusion), kind=kLoop, calls=%fused_computation.120 | loop fusion | flops 261632 | bytes 135168 | tf_op jit(solution)/shard_map/reduce_sum | solution.py:20
  51.5 5.8 %all-to-all-done.1 = bf16[2,128,256]{2,0,1:T(2,128)(2,1)S(1)} async-done(((bf16[2,128,256]{2,0,1:T(2,128)(2,1)}), bf16[2,128,256]{2,0,1:T(2,128)(2,1)S(1)}, u32[]{:S(2)}, u32[]{:S(2)}) %all-to-all-start.1) | async-done | bytes 131104 | tf_op jit(solution)/shard_map/all_to_all | solution.py:123
  61.3 1.4 %convert_reduce_fusion.3 = (f32[64,4]{0,1:T(4,128)S(1)}, bf16[64,4,256]{2,0,1:T(8,128)(2,1)S(1)}) fusion(f32[64,4,256]{2,0,1:T(8,128)S(1)} %reshape.272, bf16[256,256]{1,0:T(8,128)(2,1)} %param.26, f32[4,64,256]{2,1,0:T(8,128)S(1)} %copy.288, bf16[4,256,256]{2,1,0:T(8,128)(2,1)S(1)} %copy-done.6, f32[64,4]{0,1:T(4,128)S(1)} %copy.283, f32[64,4]{0,1:T(4,128)S(1)} %copy.279), kind=kOutput, calls=%fused_computation.97 | convolution fusion | flops 67895040 | bytes 1184768 | tf_op jit(solution)/shard_map/bqf,fc->bqc/dot_general | solution.py:52
  64.4 2.6 %reduce.4 = bf16[16,10240]{1,0:T(8,128)(2,1)S(1)} reduce(bf16[16,1,10240]{2,1,0:T(2,128)(2,1)S(1)} %broadcast_in_dim.5, bf16[]{:T(256)} %broadcast.251), dimensions={1}, to_apply=%broadcast_in_dim.5.reduce_sub_computation | reduce | bytes 655362 | tf_op jit(solution)/shard_map/broadcast_in_dim | solution.py:57
  67.0 0.9 reshape.308
  67.9 3.8 %all-to-all-start.3 = ((bf16[16,2,5120]{2,1,0:T(2,128)(2,1)}), bf16[16,2,5120]{2,1,0:T(2,128)(2,1)S(1)}, u32[]{:S(2)}, u32[]{:S(2)}) async-start(bf16[16,2,5120]{2,1,0:T(2,128)(2,1)} %reshape.308), calls=%async_computation.3 | async-start | bytes 655360 | tf_op jit(solution)/shard_map/all_to_all | solution.py:58
  72.9 10.5 %all-to-all-done.3 = bf16[16,2,5120]{2,1,0:T(2,128)(2,1)S(1)} async-done(((bf16[16,2,5120]{2,1,0:T(2,128)(2,1)}), bf16[16,2,5120]{2,1,0:T(2,128)(2,1)S(1)}, u32[]{:S(2)}, u32[]{:S(2)}) %all-to-all-start.3) | async-done | bytes 327712 | tf_op jit(solution)/shard_map/all_to_all | solution.py:58
  88.3 0.8 copy.319
  89.2 1.6 %reshape.268 = bf16[32,64,4,32]{3,2,1,0:T(4,128)(2,1)S(1)} reshape(bf16[32,8192]{1,0:T(8,128)(2,1)S(1)} %slice-done) | data formatting | bytes 1048576 | tf_op jit(solution)/shard_map/reshape | solution.py:149
  90.8 1.1 %copy.320 = bf16[64,32,4,32]{0,3,2,1:T(8,128)(2,1)S(1)} copy(bf16[64,32,4,32]{3,2,0,1:T(4,128)(2,1)S(1)} %bitcast.252) | data formatting | bytes 1048576 | tf_op jit(solution)/shard_map/transpose | solution.py:149
  91.9 1.1 %copy.321 = bf16[64,128,32]{1,0,2:T(8,128)(2,1)S(1)} copy(bf16[64,128,32]{0,2,1:T(8,128)(2,1)S(1)} %bitcast.253) | data formatting | bytes 1048576 | tf_op jit(solution)/shard_map/reshape | solution.py:150
  93.1 2.0 %divide_convert_fusion = bf16[4,32,128,32]{2,1,3,0:T(8,128)(2,1)S(1)} fusion(f32[]{:T(128)} %get-tuple-element.16, bf16[64,128,32]{1,0,2:T(8,128)(2,1)S(1)} %copy.321, bf16[64,4,256]{2,0,1:T(8,128)(2,1)S(1)} %get-tuple-element.21, f32[64,4]{0,1:T(4,128)S(1)} %copy-done.16, f32[64,4]{0,1:T(4,128)S(1)} %broadcast_multiply_fusion.2, ...), kind=kOutput, calls=%fused_computation.4 | convolution fusion | flops 72630272 | bytes 1722628 | tf_op jit(solution)/shard_map/sic,sje->ijce/dot_general | solution.py:161
  95.6 1.2 %fusion.43 = bf16[128,4,128]{2,0,1:T(8,128)(2,1)S(1)} fusion(f32[128,4,128]{2,0,1:T(8,128)S(1)} %fusion.71, f32[128,4,128]{2,0,1:T(8,128)S(1)} %bitcast.257, f32[4,128,128]{2,1,0:T(8,128)S(1)} %copy-done.7, bf16[128,128]{1,0:T(8,128)(2,1)S(1)} %copy-done.23, bf16[4,128,128]{2,1,0:T(8,128)(2,1)} %param.30, f32[128,4]{0,1:T(4,128)S(1)} %rsqrt.59, ...), kind=kOutput, calls=%fused_computation.56 | convolution fusion | flops 34275328 | bytes 1249280 | tf_op jit(solution)/shard_map/bqf,fc->bqc/dot_general | solution.py:52
  (163 shorter events, 22.0 us)
Async XLA Ops:
  0.6 94.5 %copy-start = (bf16[1024,128]{1,0:T(8,128)(2,1)S(1)}, bf16[1024,128]{1,0:T(8,128)(2,1)}, u32[]{:S(2)}) copy-start(bf16[1024,128]{1,0:T(8,128)(2,1)} %param.35) | copy-start | bytes 786436
  0.6 14.3 %copy-start.4 = (bf16[2,128,256]{2,1,0:T(8,128)(2,1)S(1)}, bf16[2,128,256]{2,1,0:T(8,128)(2,1)}, u32[]{:S(2)}) copy-start(bf16[2,128,256]{2,1,0:T(8,128)(2,1)} %param.18) | copy-start | bytes 393220
  0.7 14.5 %copy-start.20 = (bf16[4,256,256]{2,1,0:T(8,128)(2,1)S(1)}, bf16[4,256,256]{2,1,0:T(8,128)(2,1)}, u32[]{:S(2)}) copy-start(bf16[4,256,256]{2,1,0:T(8,128)(2,1)} %param.22) | copy-start | bytes 1572868
  1.8 16.4 %copy-start.26 = (s32[64]{0:T(128)S(1)}, s32[64]{0:T(128)}, u32[]{:S(2)}) copy-start(s32[64]{0:T(128)} %param.20) | copy-start | bytes 772
  3.5 18.2 %copy-start.27 = (s32[128]{0:T(128)S(1)}, s32[128]{0:T(128)}, u32[]{:S(2)}) copy-start(s32[128]{0:T(128)} %param.21) | copy-start | bytes 1540
  3.5 18.1 %all-to-all-start = ((bf16[16,12,4,128]{3,2,1,0:T(4,128)(2,1)}), bf16[16,12,4,128]{3,2,1,0:T(4,128)(2,1)S(1)}, u32[]{:S(2)}, u32[]{:S(2)}) async-start(bf16[16,12,4,128]{3,2,1,0:T(4,128)(2,1)} %broadcast_in_dim.4), calls=%async_computation | async-start | bytes 393216 | tf_op jit(solution)/shard_map/all_to_all | solution.py:58
  15.1 8.5 %copy-start.17 = (f32[2,128]{1,0:T(2,128)}, f32[2,128]{1,0:T(2,128)S(1)}, u32[]{:S(2)}) copy-start(f32[2,128]{1,0:T(2,128)S(1)} %add_rsqrt_fusion.5) | copy-start | bytes 3076
  21.6 1.5 %collective-permute-start = (bf16[16,12,4,128]{3,0,2,1:T(8,128)(2,1)S(1)}, bf16[16,12,4,128]{3,0,2,1:T(8,128)(2,1)S(1)}, u32[]{:S(2)}, u32[]{:S(2)}) collective-permute-start(bf16[16,12,4,128]{3,0,2,1:T(8,128)(2,1)S(1)} %copy.363), channel_id=1, source_target_pairs={{0,1},{1,0},{2,3},{3,2},{4,5},{5,4},{6,7},{7,6},{8,9},{9,8},{10,11... | collective-permute-start | bytes 589832 | tf_op jit(solution)/shard_map/ppermute | solution.py:59
  21.7 5.7 %copy-start.13 = (f32[128]{0:T(128)}, f32[128]{0:T(128)S(1)}, u32[]{:S(2)}) copy-start(f32[128]{0:T(128)S(1)} %add_multiply_fusion.1) | copy-start | bytes 1540
  26.1 3.5 %copy-start.10 = (bf16[4,128,128]{1,2,0:T(8,128)(2,1)S(1)}, bf16[4,128,128]{1,2,0:T(8,128)(2,1)}, u32[]{:S(2)}) copy-start(bf16[4,128,128]{1,2,0:T(8,128)(2,1)} %convolution_convert_fusion.2) | copy-start | bytes 393220
  26.1 3.5 %copy-start.30 = (f32[4,4,128]{2,1,0:T(4,128)S(1)}, f32[4,4,128]{2,1,0:T(4,128)}, u32[]{:S(2)}) copy-start(f32[4,4,128]{2,1,0:T(4,128)} %fusion.174) | copy-start | bytes 24580
  29.9 8.3 %copy-start.11 = (bf16[2,128,256]{1,2,0:T(8,128)(2,1)S(1)}, bf16[2,128,256]{1,2,0:T(8,128)(2,1)}, u32[]{:S(2)}) copy-start(bf16[2,128,256]{1,2,0:T(8,128)(2,1)} %copy.261) | copy-start | bytes 393220
  29.9 8.3 %copy-start.29 = (f32[2,8,128]{2,1,0:T(8,128)S(1)}, f32[2,8,128]{2,1,0:T(8,128)}, u32[]{:S(2)}) copy-start(f32[2,8,128]{2,1,0:T(8,128)} %fusion.172) | copy-start | bytes 24580
  32.3 14.1 %all-to-all-start.2 = ((bf16[4,128,128]{2,0,1:T(4,128)(2,1)}), bf16[4,128,128]{2,0,1:T(4,128)(2,1)S(1)}, u32[]{:S(2)}, u32[]{:S(2)}) async-start(bf16[4,128,128]{2,0,1:T(4,128)(2,1)} %copy.301), calls=%async_computation.2 | async-start | bytes 262144 | tf_op jit(solution)/shard_map/all_to_all | solution.py:130
  38.6 2.7 %copy-start.25 = (bf16[128,4]{0,1:T(4,128)(2,1)S(1)}, bf16[128,4]{0,1:T(4,128)(2,1)}, u32[]{:S(2)}) copy-start(bf16[128,4]{0,1:T(4,128)(2,1)} %param.31) | copy-start | bytes 3076
  41.5 17.0 %copy-start.6 = (bf16[4,256,256]{2,1,0:T(8,128)(2,1)S(1)}, bf16[4,256,256]{2,1,0:T(8,128)(2,1)}, u32[]{:S(2)}) copy-start(bf16[4,256,256]{2,1,0:T(8,128)(2,1)} %param.25) | copy-start | bytes 1572868
  46.5 10.8 %all-to-all-start.1 = ((bf16[2,128,256]{2,0,1:T(2,128)(2,1)}), bf16[2,128,256]{2,0,1:T(2,128)(2,1)S(1)}, u32[]{:S(2)}, u32[]{:S(2)}) async-start(bf16[2,128,256]{2,0,1:T(2,128)(2,1)} %copy.274), calls=%async_computation.1 | async-start | bytes 262144 | tf_op jit(solution)/shard_map/all_to_all | solution.py:123
  57.5 1.9 %copy-start.19 = (f32[64]{0:T(128)S(1)}, f32[64]{0:T(128)}, u32[]{:S(2)}) copy-start(f32[64]{0:T(128)} %get-tuple-element.17) | copy-start | bytes 772
  61.1 1.8 %copy-start.24 = (bf16[256,32]{0,1:T(8,128)(2,1)S(1)}, bf16[256,32]{0,1:T(8,128)(2,1)}, u32[]{:S(2)}) copy-start(bf16[256,32]{0,1:T(8,128)(2,1)} %param.33) | copy-start | bytes 49156
  61.1 1.8 %copy-start.28 = (f32[64]{0:T(128)S(1)}, f32[64]{0:T(128)}, u32[]{:S(2)}) copy-start(f32[64]{0:T(128)} %convert_element_type.229) | copy-start | bytes 772
  62.7 9.0 %copy-start.9 = (f32[32,4,4]{2,0,1:T(8,128)S(1)}, f32[32,4,4]{2,0,1:T(8,128)}, u32[]{:S(2)}) copy-start(f32[32,4,4]{2,0,1:T(8,128)} %multiply_reduce_fusion) | copy-start | bytes 6148
  62.9 9.3 %copy-start.15 = (f32[64,4]{0,1:T(4,128)}, f32[64,4]{0,1:T(4,128)S(1)}, u32[]{:S(2)}) copy-start(f32[64,4]{0,1:T(4,128)S(1)} %add_rsqrt_fusion.3) | copy-start | bytes 3076
  63.5 8.9 %copy-start.8 = (f32[32,4,4]{1,0,2:T(8,128)S(1)}, f32[32,4,4]{1,0,2:T(8,128)}, u32[]{:S(2)}) copy-start(f32[32,4,4]{1,0,2:T(8,128)} %copy.305) | copy-start | bytes 6148
  63.5 9.1 %copy-start.12 = (bf16[4,128,128]{2,1,0:T(8,128)(2,1)S(1)}, bf16[4,128,128]{2,1,0:T(8,128)(2,1)}, u32[]{:S(2)}) copy-start(bf16[4,128,128]{2,1,0:T(8,128)(2,1)} %param.30) | copy-start | bytes 393220
  67.9 15.5 %all-to-all-start.3 = ((bf16[16,2,5120]{2,1,0:T(2,128)(2,1)}), bf16[16,2,5120]{2,1,0:T(2,128)(2,1)S(1)}, u32[]{:S(2)}, u32[]{:S(2)}) async-start(bf16[16,2,5120]{2,1,0:T(2,128)(2,1)} %reshape.308), calls=%async_computation.3 | async-start | bytes 655360 | tf_op jit(solution)/shard_map/all_to_all | solution.py:58
  72.4 13.3 %copy-start.1 = (f32[32,4,4,128]{3,1,0,2:T(4,128)}, f32[32,4,4,128]{3,1,0,2:T(4,128)S(1)}, u32[]{:S(2)}) copy-start(f32[32,4,4,128]{3,1,0,2:T(4,128)S(1)} %copy.303) | copy-start | bytes 786436
  83.9 1.8 %collective-permute-start.1 = (bf16[16,1,10240]{2,0,1:T(8,128)(2,1)S(1)}, bf16[16,1,10240]{2,0,1:T(8,128)(2,1)S(1)}, u32[]{:S(2)}, u32[]{:S(2)}) collective-permute-start(bf16[16,1,10240]{2,0,1:T(8,128)(2,1)S(1)} %copy.339), channel_id=1, source_target_pairs={{0,1},{1,0},{2,3},{3,2},{4,5},{5,4},{6,7},{7,6},{8,9},{9,8},{10,11... | collective-permute-start | bytes 983048 | tf_op jit(solution)/shard_map/ppermute | solution.py:59
  85.8 1.2 %copy-start.14 = (f32[128]{0:T(128)S(1)}, f32[128]{0:T(128)}, u32[]{:S(2)}) copy-start(f32[128]{0:T(128)} %copy-done.13) | copy-start | bytes 1540
  90.8 2.2 %copy-start.16 = (f32[64,4]{0,1:T(4,128)S(1)}, f32[64,4]{0,1:T(4,128)}, u32[]{:S(2)}) copy-start(f32[64,4]{0,1:T(4,128)} %copy-done.15) | copy-start | bytes 3076
  93.0 2.6 %copy-start.2 = (f32[32,4,4,128]{3,1,0,2:T(4,128)S(1)}, f32[32,4,4,128]{3,1,0,2:T(4,128)}, u32[]{:S(2)}) copy-start(f32[32,4,4,128]{3,1,0,2:T(4,128)} %copy-done.1) | copy-start | bytes 786436
  93.0 2.6 %copy-start.7 = (f32[4,128,128]{2,1,0:T(8,128)S(1)}, f32[4,128,128]{2,1,0:T(8,128)}, u32[]{:S(2)}) copy-start(f32[4,128,128]{2,1,0:T(8,128)} %copy.319) | copy-start | bytes 786436
  93.1 2.6 %copy-start.23 = (bf16[128,128]{1,0:T(8,128)(2,1)S(1)}, bf16[128,128]{1,0:T(8,128)(2,1)}, u32[]{:S(2)}) copy-start(bf16[128,128]{1,0:T(8,128)(2,1)} %param.32) | copy-start | bytes 98308
  (6 other events, 5.9 us)
